TPU v7x, 512 devices: a whole 4x4x16 slice. The times are simulated.
512 devices in a mesh: row: 16 (over z), col: 32 (over y, x, core).
Axes of the slice: x: 4, y: 4, z: 16, core: 2. Of those that a mesh axis runs over, the one named last changes fastest.
Arguments:
- inputs: bfloat16 [2048, 8192], P('col', 'row'), may hold values from -6 to 6
- gate_pre: bfloat16 [2048, 14784], P('row', 'col'), may hold values from -6 to 6
- up_pre: bfloat16 [2048, 14784], P('row', 'col'), may hold values from -6 to 6
- w_gate: bfloat16 [8192, 14784], P('row', 'col'), may hold values from -0.0625 to 0.0625
- w_up: bfloat16 [8192, 14784], P('row', 'col'), may hold values from -0.0625 to 0.0625
- w_down: bfloat16 [14784, 8192], P('col', 'row'), may hold values from -0.046875 to 0.046875
- grad_out: bfloat16 [2048, 8192], P('col', 'row'), may hold values from -1.5 to 1.5
Outputs:
- grad_in: bfloat16 [2048, 8192], P('col', 'row')
- grad_gate: bfloat16 [8192, 14784], P('row', 'col')
- grad_up: bfloat16 [8192, 14784], P('row', 'col')
- grad_down: bfloat16 [14784, 8192], P('col', 'row')
All inputs are finite; a program needn't handle non-finite values.
Results may differ from a plain program's by a relative error of at most 0.025.
Values may be sent and summed in bfloat16 or wider, within the bound.
No kernel may reach another device: no remote copies, remote signals or barrier semaphores. Data moves between devices by JAX's collectives and lax.ppermute only.
A program may use at most 64 MiB of HBM per device.

v0:
```python
import jax
import jax.numpy as jnp
from jax import lax
from jax.sharding import PartitionSpec as P


def contract_rows(left, right):
    return lax.dot_general(
        left, right, (((0,), (0,)), ((), ())), preferred_element_type=jnp.float32
    )


def contract_cols(left, right):
    return lax.dot_general(
        left, right, (((1,), (1,)), ((), ())), preferred_element_type=jnp.float32
    )


def pointwise(gate_pre, up_pre, hidden_grad):
    gate_value = gate_pre.astype(jnp.float32)
    up_value = up_pre.astype(jnp.float32)
    sigmoid_gate = jax.nn.sigmoid(gate_value)
    activated = gate_value * sigmoid_gate
    hidden = (activated * up_value).astype(jnp.bfloat16)
    up_grad = (hidden_grad * activated).astype(jnp.bfloat16)
    gate_grad = (
        hidden_grad * up_value * sigmoid_gate * (1.0 + gate_value * (1.0 - sigmoid_gate))
    ).astype(jnp.bfloat16)
    return (hidden, gate_grad, up_grad)


def shards(inputs, gate_pre, up_pre, w_gate, w_up, w_down, grad_out):
    all_grad_out, all_inputs = (
        lax.all_gather(grad_out, "col", axis=0, tiled=True),
        lax.all_gather(inputs, "col", axis=0, tiled=True),
    )
    hidden_grad = lax.psum_scatter(
        contract_cols(all_grad_out, w_down).astype(jnp.bfloat16),
        "row",
        scatter_dimension=0,
        tiled=True,
    ).astype(jnp.float32)
    share_hidden, share_gate, share_up = pointwise(gate_pre, up_pre, hidden_grad)
    hidden, gate_grad, up_grad = (
        lax.all_gather(share_hidden, "row", axis=0, tiled=True),
        lax.all_gather(share_gate, "row", axis=0, tiled=True),
        lax.all_gather(share_up, "row", axis=0, tiled=True),
    )
    grad_down = contract_rows(hidden, all_grad_out).astype(jnp.bfloat16)
    grad_gate = contract_rows(all_inputs, gate_grad).astype(jnp.bfloat16)
    grad_up = contract_rows(all_inputs, up_grad).astype(jnp.bfloat16)
    grad_in = lax.psum_scatter(
        (contract_cols(gate_grad, w_gate) + contract_cols(up_grad, w_up)).astype(jnp.bfloat16),
        "col",
        scatter_dimension=0,
        tiled=True,
    )
    return (grad_in, grad_gate, grad_up, grad_down)


def solution(mesh):
    return jax.shard_map(
        shards,
        mesh=mesh,
        in_specs=(
            P("col", "row"),
            P("row", "col"),
            P("row", "col"),
            P("row", "col"),
            P("row", "col"),
            P("col", "row"),
            P("col", "row"),
        ),
        out_specs=(P("col", "row"), P("row", "col"), P("row", "col"), P("col", "row")),
        check_vma=False,
    )
```

profile of v0, /device:TPU:1, one launch (start us, length us, event | category | flops | bytes accessed | tf_op | source)
XLA Modules:
  0.0 552.8 jit_solution(13441405227481804049)
XLA Ops:
  7.2 0.0 copy-start
  7.2 0.0 all-gather.6.cloned.1.call-start
  7.2 0.7 all-gather.6.cloned.1.call-update
  7.9 0.0 reduce-scatter.7.cloned.1.call-start
  8.0 67.8 %all-gather.6.cloned.1.call-done = bf16[2048,512]{1,0:T(8,128)(2,1)} async-done(((bf16[64,512]{1,0:T(8,128)(2,1)}), bf16[2048,512]{1,0:T(8,128)(2,1)}) %all-gather.6.cloned.1.call-update) | async-done | bytes 2097168 | tf_op jit(solution)/shard_map/all_gather | solution.py:34
  75.7 2.8 convolution_convert_fusion
  78.6 2.5 copy.11
  81.0 0.0 copy-start.3
  81.0 0.0 copy-start.4
  81.0 0.0 reduce-scatter.7.cloned.1.call-update
  81.0 0.0 all-gather.8.cloned.1.call-start
  81.1 63.1 %reduce-scatter.7.cloned.1.call-done = bf16[128,462]{1,0:T(8,128)(2,1)} async-done(((bf16[2048,462]{1,0:T(8,128)(2,1)}), bf16[128,462]{1,0:T(8,128)(2,1)}) %reduce-scatter.7.cloned.1.call-update) | async-done | bytes 118288
  144.2 1.0 copy.12
  145.3 0.0 copy-done.3
  145.3 0.0 copy-done.4
  145.3 0.9 fusion.6
  146.1 0.0 all-gather.8.cloned.1.call-update
  146.2 0.0 all-gather.10.cloned.1.call-start
  146.2 0.5 all-gather.10.cloned.1.call-update
  146.7 0.0 all-gather.12.cloned.1.call-start
  146.8 0.5 all-gather.12.cloned.1.call-update
  147.3 0.0 all-gather.14.cloned.1.call-start
  147.4 0.5 all-gather.14.cloned.1.call-update
  147.9 0.0 copy-start.2
  147.9 0.0 reduce-scatter.5.cloned.1.call-start
  148.0 73.4 %all-gather.8.cloned.1.call-done = bf16[2048,462]{0,1:T(8,128)(2,1)} async-done(((bf16[128,462]{0,1:T(8,128)(2,1)}), bf16[2048,462]{0,1:T(8,128)(2,1)}) %all-gather.8.cloned.1.call-update) | async-done | bytes 1892368 | tf_op jit(solution)/shard_map/all_gather | solution.py:46
  221.4 0.0 copy-done
  221.4 4.8 fusion.11
  226.1 71.0 %all-gather.10.cloned.1.call-done = bf16[2048,462]{0,1:T(8,128)(2,1)} async-done(((bf16[128,462]{0,1:T(8,128)(2,1)}), bf16[2048,462]{0,1:T(8,128)(2,1)}) %all-gather.10.cloned.1.call-update) | async-done | bytes 1892368 | tf_op jit(solution)/shard_map/all_gather | solution.py:47
  297.1 0.0 copy-done.2
  297.1 5.5 add_convert_fusion
  302.6 0.0 reduce-scatter.5.cloned.1.call-update
  302.6 0.0 copy-start.1
  302.6 63.2 %all-gather.12.cloned.1.call-done = bf16[2048,512]{1,0:T(8,128)(2,1)} async-done(((bf16[64,512]{1,0:T(8,128)(2,1)}), bf16[2048,512]{1,0:T(8,128)(2,1)}) %all-gather.12.cloned.1.call-update) | async-done | bytes 2097168 | tf_op jit(solution)/shard_map/all_gather | solution.py:35
  365.8 0.0 copy-start.5
  365.8 4.2 fusion.1
  370.0 0.0 copy-done.1
  370.0 0.0 copy-done.5
  370.0 1.9 fusion
  372.0 62.3 %all-gather.14.cloned.1.call-done = bf16[2048,462]{0,1:T(8,128)(2,1)} async-done(((bf16[128,462]{0,1:T(8,128)(2,1)}), bf16[2048,462]{0,1:T(8,128)(2,1)}) %all-gather.14.cloned.1.call-update) | async-done | bytes 1892368 | tf_op jit(solution)/shard_map/all_gather | solution.py:45
  434.2 4.1 convolution_convert_fusion.1
  438.3 107.7 %reduce-scatter.5.cloned.1.call-done = bf16[64,512]{1,0:T(8,128)(2,1)} async-done(((bf16[2048,512]{1,0:T(8,128)(2,1)}), bf16[64,512]{1,0:T(8,128)(2,1)}) %reduce-scatter.5.cloned.1.call-update) | async-done | bytes 65552 | tf_op jit(solution)/shard_map/reduce_scatter | solution.py:52
Async XLA Ops:
  7.2 214.2 %copy-start = (bf16[512,462]{0,1:T(8,128)(2,1)S(1)}, bf16[512,462]{0,1:T(8,128)(2,1)}, u32[]{:S(2)}) copy-start(bf16[512,462]{0,1:T(8,128)(2,1)} %param.10) | copy-start | bytes 1419268
  7.2 68.5 %all-gather.6.cloned.1.call-start = ((), (), s32[]{:S(2)}) async-start(), calls=%async_computation.2 | async-start | bytes 2162688 | tf_op jit(solution)/shard_map/all_gather | solution.py:34
  7.9 136.3 %reduce-scatter.7.cloned.1.call-start = ((), (), s32[]{:S(2)}) async-start(), calls=%async_computation.8 | async-start | bytes 2228224
  81.0 64.2 %copy-start.3 = (bf16[128,462]{0,1:T(8,128)(2,1)S(1)}, bf16[128,462]{0,1:T(8,128)(2,1)}, u32[]{:S(2)}) copy-start(bf16[128,462]{0,1:T(8,128)(2,1)} %param.9) | copy-start | bytes 354820
  81.0 64.3 %copy-start.4 = (bf16[128,462]{0,1:T(8,128)(2,1)S(1)}, bf16[128,462]{0,1:T(8,128)(2,1)}, u32[]{:S(2)}) copy-start(bf16[128,462]{0,1:T(8,128)(2,1)} %param.8) | copy-start | bytes 354820
  81.0 140.3 %all-gather.8.cloned.1.call-start = ((), (), s32[]{:S(2)}) async-start(), calls=%async_computation.3 | async-start | bytes 2019328 | tf_op jit(solution)/shard_map/all_gather | solution.py:46
  146.2 151.0 %all-gather.10.cloned.1.call-start = ((), (), s32[]{:S(2)}) async-start(), calls=%async_computation.4 | async-start | bytes 2019328 | tf_op jit(solution)/shard_map/all_gather | solution.py:47
  146.7 219.1 %all-gather.12.cloned.1.call-start = ((), (), s32[]{:S(2)}) async-start(), calls=%async_computation.6 | async-start | bytes 2162688 | tf_op jit(solution)/shard_map/all_gather | solution.py:35
  147.3 286.9 %all-gather.14.cloned.1.call-start = ((), (), s32[]{:S(2)}) async-start(), calls=%async_computation.7 | async-start | bytes 2019328 | tf_op jit(solution)/shard_map/all_gather | solution.py:45
  147.9 149.2 %copy-start.2 = (bf16[512,462]{0,1:T(8,128)(2,1)S(1)}, bf16[512,462]{0,1:T(8,128)(2,1)}, u32[]{:S(2)}) copy-start(bf16[512,462]{0,1:T(8,128)(2,1)} %param.11) | copy-start | bytes 1419268
  147.9 398.1 %reduce-scatter.5.cloned.1.call-start = ((), (), s32[]{:S(2)}) async-start(), calls=%async_computation.5 | async-start | bytes 2162688 | tf_op jit(solution)/shard_map/reduce_scatter | solution.py:52
  302.6 67.4 %copy-start.1 = (bf16[2048,462]{0,1:T(8,128)(2,1)S(1)}, bf16[2048,462]{0,1:T(8,128)(2,1)}, u32[]{:S(2)}) copy-start(bf16[2048,462]{0,1:T(8,128)(2,1)} %all-gather.8.cloned.1.call-done) | copy-start | bytes 5677060
  365.8 4.2 copy-start.5
Sparse Core Ops, SparseCore 0:
  11.1 64.5 all-gather.5
  81.2 63.0 reduce-scatter.6
  146.8 74.5 all-gather.7
  223.8 73.2 all-gather.9
  300.1 65.6 all-gather.11
  368.2 65.9 all-gather.13
  439.2 106.7 reduce-scatter.4
where the time goes:
time: 554 us; the launch traced here: 553 us
  waiting for transfers between devices  511 us (92%)
  matrix products  23.3 us (4%)
  between operations  14.2 us (3%)
    reduce_scatter x1, waiting for transfers between devices, shards(): lax.psum_scatter((contract_cols(gate_grad, w_gate) + contract_cols(up_gra...  108 us
    all_gather x1, waiting for transfers between devices, shards(): lax.all_gather(share_gate, 'row', axis=0, tiled=True)  73.4 us
    all_gather x1, waiting for transfers between devices, shards(): lax.all_gather(share_up, 'row', axis=0, tiled=True)  71 us
    all_gather x1, waiting for transfers between devices, shards(): lax.all_gather(grad_out, 'col', axis=0, tiled=True)  67.8 us
    unnamed x8, waiting for transfers between devices  65.4 us
    all_gather x1, waiting for transfers between devices, shards(): lax.all_gather(inputs, 'col', axis=0, tiled=True)  63.2 us
    all_gather x1, waiting for transfers between devices, shards(): lax.all_gather(share_hidden, 'row', axis=0, tiled=True)  62.3 us
    dot_general x3, matrix products, contract_cols(): lax.dot_general(left, right, (((1,), (1,)), ((), ())), preferred_element_...  13.1 us
  transfers between devices with their start and end apart: 7, of which 7 were waited for; matrix products, arithmetic and copies ran while one was open for 4% of the time, Pallas kernels for 0%

commit v1 on v0

--- a/solution.py
+++ b/solution.py
@@ -29,22 +29,70 @@
     return (hidden, gate_grad, up_grad)
 
 
-def shards(inputs, gate_pre, up_pre, w_gate, w_up, w_down, grad_out):
-    all_grad_out, all_inputs = (
-        lax.all_gather(grad_out, "col", axis=0, tiled=True),
-        lax.all_gather(inputs, "col", axis=0, tiled=True),
+def _shifts(n):
+    up = [(j, (j + 1) % n) for j in range(n)]
+    down = [(j, (j - 1) % n) for j in range(n)]
+    return up, down
+
+
+def ring_all_gather(x, axis, n):
+    me = lax.axis_index(axis)
+    up, down = _shifts(n)
+    n_up = n // 2
+    n_down = n - 1 - n_up
+    out = jnp.zeros((n,) + x.shape, x.dtype)
+    out = lax.dynamic_update_index_in_dim(out, x, me, 0)
+    a = x
+    b = x
+    for s in range(1, n_up + 1):
+        a = lax.ppermute(a, axis, up)
+        out = lax.dynamic_update_index_in_dim(out, a, (me - s + n) % n, 0)
+        if s <= n_down:
+            b = lax.ppermute(b, axis, down)
+            out = lax.dynamic_update_index_in_dim(out, b, (me + s) % n, 0)
+    return out
+
+
+def ring_reduce_scatter(parts, axis, n, wire_dtype):
+    me = lax.axis_index(axis)
+    up, down = _shifts(n)
+    n_up = n // 2
+    n_down = n - 1 - n_up
+
+    def block(j):
+        return lax.dynamic_index_in_dim(parts, (j + 2 * n) % n, 0, keepdims=False).astype(
+            jnp.float32
+        )
+
+    a = block(me + n_up)
+    b = block(me - n_down)
+    for s in range(n_up):
+        a = lax.ppermute(a.astype(wire_dtype), axis, up).astype(jnp.float32)
+        if s < n_up - 1:
+            a = a + block(me + n_up - 1 - s)
+        if s < n_down:
+            b = lax.ppermute(b.astype(wire_dtype), axis, down).astype(jnp.float32)
+            if s < n_down - 1:
+                b = b + block(me - n_down + 1 + s)
+    return block(me) + a + b
+
+
+def shards(inputs, gate_pre, up_pre, w_gate, w_up, w_down, grad_out, n_row):
+    tokens_row, hidden_units = gate_pre.shape
+    pre = jnp.stack([gate_pre, up_pre], axis=1)
+    all_pre = ring_all_gather(pre, "row", n_row).reshape(
+        (n_row * tokens_row, 2, hidden_units)
     )
-    hidden_grad = lax.psum_scatter(
-        contract_cols(all_grad_out, w_down).astype(jnp.bfloat16),
-        "row",
-        scatter_dimension=0,
-        tiled=True,
-    ).astype(jnp.float32)
-    share_hidden, share_gate, share_up = pointwise(gate_pre, up_pre, hidden_grad)
-    hidden, gate_grad, up_grad = (
-        lax.all_gather(share_hidden, "row", axis=0, tiled=True),
-        lax.all_gather(share_gate, "row", axis=0, tiled=True),
-        lax.all_gather(share_up, "row", axis=0, tiled=True),
+    all_grad_out = lax.all_gather(grad_out, "col", axis=0, tiled=True)
+    all_inputs = lax.all_gather(inputs, "col", axis=0, tiled=True)
+    part = contract_cols(all_grad_out, w_down).astype(jnp.bfloat16)
+    part = part.reshape((n_row, tokens_row, hidden_units))
+    own = ring_reduce_scatter(part, "row", n_row, jnp.bfloat16).astype(jnp.bfloat16)
+    hidden_grad = ring_all_gather(own, "row", n_row).reshape(
+        (n_row * tokens_row, hidden_units)
+    )
+    hidden, gate_grad, up_grad = pointwise(
+        all_pre[:, 0], all_pre[:, 1], hidden_grad.astype(jnp.float32)
     )
     grad_down = contract_rows(hidden, all_grad_out).astype(jnp.bfloat16)
     grad_gate = contract_rows(all_inputs, gate_grad).astype(jnp.bfloat16)
@@ -59,8 +107,13 @@
 
 
 def solution(mesh):
+    n_row = mesh.shape["row"]
+
+    def body(*args):
+        return shards(*args, n_row=n_row)
+
     return jax.shard_map(
-        shards,
+        body,
         mesh=mesh,
         in_specs=(
             P("col", "row"),

time: 554 us -> 721 us (1.30); the launches traced: 553 us -> 707 us
  waiting for transfers between devices: 511 us -> 153 us
  local copies, waits for them, and re-layouts: 3.53 us -> 361 us
  starting transfers between devices: 0.27 us -> 152 us
    dynamic_update_slice x0 -> x32, local copies, waits for them, and re-layouts: none -> 328 us  [the longest x16 164 us: ring_all_gather(): out = lax.dynamic_update_index_in_dim(out, a, (me - s + n) % n, 0)]
    all_gather x5 -> x2, waiting for transfers between devices: 338 us -> 38.1 us  [the longest x1 38.1 us: shards(): all_grad_out = lax.all_gather(grad_out, 'col', axis=0, tiled=True)]
    ppermute x0 -> x45, starting transfers between devices: none -> 152 us  [the longest x14 69.8 us: ring_all_gather(): b = lax.ppermute(b, axis, down)]
    unnamed x8 -> x3, waiting for transfers between devices: 65.4 us -> 0.71 us
    broadcast_in_dim x0 -> x34, local copies, waits for them, and re-layouts: none -> 20.7 us  [the longest x16 9.06 us: ring_all_gather(): out = lax.dynamic_update_index_in_dim(out, a, (me - s + n) % n, 0)]
    ppermute x0 -> x45, waiting for transfers between devices: none -> 10.1 us  [the longest x16 8.65 us: ring_all_gather(): a = lax.ppermute(a, axis, up)]
  transfers between devices with their start and end apart: 7 -> 48, of which waited for: 7 -> 9; matrix products, arithmetic and copies ran while one was open for 4% -> 55% of each run, Pallas kernels for 0% -> 0%
where the time goes in v1:
time: 721 us; the launch traced here: 707 us
  local copies, waits for them, and re-layouts  361 us (50%)
  waiting for transfers between devices  153 us (21%)
  starting transfers between devices  152 us (21%)
  matrix products  17.2 us (2%)
  between operations  15.9 us (2%)
  other arithmetic  7.71 us (1%)
    dynamic_update_slice x16, local copies, waits for them, and re-layouts, ring_all_gather(): out = lax.dynamic_update_index_in_dim(out, a, (me - s + n) % n, 0)  164 us
    dynamic_update_slice x14, local copies, waits for them, and re-layouts, ring_all_gather(): out = lax.dynamic_update_index_in_dim(out, b, (me + s) % n, 0)  143 us
    reduce_scatter x1, waiting for transfers between devices, shards(): lax.psum_scatter((contract_cols(gate_grad, w_gate) + contract_cols(up_gra...  104 us
    ppermute x14, starting transfers between devices, ring_all_gather(): b = lax.ppermute(b, axis, down)  69.8 us
    all_gather x1, waiting for transfers between devices, shards(): all_grad_out = lax.all_gather(grad_out, 'col', axis=0, tiled=True)  38.1 us
    ppermute x16, starting transfers between devices, ring_all_gather(): a = lax.ppermute(a, axis, up)  33.1 us
    ppermute x7, starting transfers between devices, ring_reduce_scatter(): b = lax.ppermute(b.astype(wire_dtype), axis, down).astype(jnp.float32)  32.8 us
    dynamic_update_slice x2, local copies, waits for them, and re-layouts, ring_all_gather(): out = lax.dynamic_update_index_in_dim(out, x, me, 0)  20.6 us
  transfers between devices with their start and end apart: 48, of which 9 were waited for; matrix products, arithmetic and copies ran while one was open for 55% of the time, Pallas kernels for 0%

profile of v1, /device:TPU:1, one launch (start us, length us, event | category | flops | bytes accessed | tf_op | source)
XLA Modules:
  0.0 707.5 jit_solution(4396758375819040371)
XLA Ops:
  13.3 9.5 %collective-permute-start.31 = (bf16[128,2,462]{0,2,1:T(8,128)(2,1)S(1)}, bf16[128,2,462]{0,2,1:T(8,128)(2,1)}, u32[]{:S(2)}, u32[]{:S(2)}) collective-permute-start(bf16[128,2,462]{0,2,1:T(8,128)(2,1)S(1)} %get-tuple-element.22), channel_id=1, source_target_pairs={{0,480},{32,0},{64,32},{96,64},{128,96},{160,128},{192,160},{224,1... | collective-permute-start | bytes 709640 | tf_op jit(solution)/shard_map/ppermute | solution.py:51
  28.5 4.6 collective-permute-start.33
  37.6 38.1 %all-gather.3.cloned.1.call-done = bf16[2048,512]{1,0:T(8,128)(2,1)} async-done(((bf16[64,512]{1,0:T(8,128)(2,1)}), bf16[2048,512]{1,0:T(8,128)(2,1)}) %all-gather.3.cloned.1.call-update) | async-done | bytes 2097168 | tf_op jit(solution)/shard_map/all_gather | solution.py:86
  79.5 4.8 constant_dynamic-slice_fusion.15
  93.9 4.6 collective-permute-start.8
  117.5 4.8 collective-permute-start.11
  124.4 4.8 collective-permute-start.12
  131.2 4.8 collective-permute-start.13
  138.1 4.7 collective-permute-start.14
  175.6 4.8 collective-permute-start.20
  195.5 4.8 collective-permute-start.24
  202.2 4.6 collective-permute-start.43
  208.8 4.6 collective-permute-start.26
  216.0 5.1 collective-permute-start.28
  226.6 14.5 %dynamic_update_slice.114 = bf16[16,128,2,462]{1,0,3,2:T(8,128)(2,1)} dynamic-update-slice(bf16[16,128,2,462]{1,0,3,2:T(8,128)(2,1)} %broadcast_in_dim.121, bf16[1,128,2,462]{1,0,3,2:T(2,128)(2,1)S(1)} %copy.56, s32[]{:T(128)S(6)} %select_n.304, s32[]{:T(128)} %constant.338.clone.1, s32[]{:T(128)} %constant.338.clone.1, s32[]{:T(128)} %constant.338.clone.1) | dynamic-update-slice | bytes 473092 | tf_op jit(solution)/shard_map/jit(dynamic_update_index_in_dim)/dynamic_update_slice | solution.py:44
  242.7 14.3 %dynamic_update_slice.115 = bf16[16,128,2,462]{1,0,3,2:T(8,128)(2,1)} dynamic-update-slice(bf16[16,128,2,462]{1,0,3,2:T(8,128)(2,1)} %dynamic_update_slice.114, bf16[1,128,2,462]{1,0,3,2:T(2,128)(2,1)S(1)} %copy.57, s32[]{:T(128)S(6)} %select_n.306, s32[]{:T(128)} %constant.338.clone.1, s32[]{:T(128)} %constant.338.clone.1, s32[]{:T(128)} %constant.338.clone.1) | dynamic-update-slice | bytes 473092 | tf_op jit(solution)/shard_map/jit(dynamic_update_index_in_dim)/dynamic_update_slice | solution.py:49
  257.0 14.3 %dynamic_update_slice.116 = bf16[16,128,2,462]{1,0,3,2:T(8,128)(2,1)} dynamic-update-slice(bf16[16,128,2,462]{1,0,3,2:T(8,128)(2,1)} %dynamic_update_slice.115, bf16[1,128,2,462]{1,0,3,2:T(2,128)(2,1)S(1)} %copy.58, s32[]{:T(128)S(6)} %select_n.308, s32[]{:T(128)} %constant.338.clone.1, s32[]{:T(128)} %constant.338.clone.1, s32[]{:T(128)} %constant.338.clone.1) | dynamic-update-slice | bytes 473092 | tf_op jit(solution)/shard_map/jit(dynamic_update_index_in_dim)/dynamic_update_slice | solution.py:52
  274.0 14.3 %dynamic_update_slice.117 = bf16[16,128,2,462]{1,0,3,2:T(8,128)(2,1)} dynamic-update-slice(bf16[16,128,2,462]{1,0,3,2:T(8,128)(2,1)} %dynamic_update_slice.116, bf16[1,128,2,462]{1,0,3,2:T(2,128)(2,1)S(1)} %copy.59, s32[]{:T(128)S(6)} %select_n.310, s32[]{:T(128)} %constant.338.clone.1, s32[]{:T(128)} %constant.338.clone.1, s32[]{:T(128)} %constant.338.clone.1) | dynamic-update-slice | bytes 473092 | tf_op jit(solution)/shard_map/jit(dynamic_update_index_in_dim)/dynamic_update_slice | solution.py:49
  288.3 14.3 %dynamic_update_slice.118 = bf16[16,128,2,462]{1,0,3,2:T(8,128)(2,1)} dynamic-update-slice(bf16[16,128,2,462]{1,0,3,2:T(8,128)(2,1)} %dynamic_update_slice.117, bf16[1,128,2,462]{1,0,3,2:T(2,128)(2,1)S(1)} %copy.60, s32[]{:T(128)S(6)} %select_n.312, s32[]{:T(128)} %constant.338.clone.1, s32[]{:T(128)} %constant.338.clone.1, s32[]{:T(128)} %constant.338.clone.1) | dynamic-update-slice | bytes 473092 | tf_op jit(solution)/shard_map/jit(dynamic_update_index_in_dim)/dynamic_update_slice | solution.py:52
  304.3 14.3 %dynamic_update_slice.119 = bf16[16,128,2,462]{1,0,3,2:T(8,128)(2,1)} dynamic-update-slice(bf16[16,128,2,462]{1,0,3,2:T(8,128)(2,1)} %dynamic_update_slice.118, bf16[1,128,2,462]{1,0,3,2:T(2,128)(2,1)S(1)} %copy.61, s32[]{:T(128)S(6)} %select_n.314, s32[]{:T(128)} %constant.338.clone.1, s32[]{:T(128)} %constant.338.clone.1, s32[]{:T(128)} %constant.338.clone.1) | dynamic-update-slice | bytes 473092 | tf_op jit(solution)/shard_map/jit(dynamic_update_index_in_dim)/dynamic_update_slice | solution.py:49
  318.6 14.3 %dynamic_update_slice.120 = bf16[16,128,2,462]{1,0,3,2:T(8,128)(2,1)} dynamic-update-slice(bf16[16,128,2,462]{1,0,3,2:T(8,128)(2,1)} %dynamic_update_slice.119, bf16[1,128,2,462]{1,0,3,2:T(2,128)(2,1)S(1)} %copy.62, s32[]{:T(128)S(6)} %select_n.316, s32[]{:T(128)} %constant.338.clone.1, s32[]{:T(128)} %constant.338.clone.1, s32[]{:T(128)} %constant.338.clone.1) | dynamic-update-slice | bytes 473092 | tf_op jit(solution)/shard_map/jit(dynamic_update_index_in_dim)/dynamic_update_slice | solution.py:52
  333.6 14.3 %dynamic_update_slice.121 = bf16[16,128,2,462]{1,0,3,2:T(8,128)(2,1)} dynamic-update-slice(bf16[16,128,2,462]{1,0,3,2:T(8,128)(2,1)} %dynamic_update_slice.120, bf16[1,128,2,462]{1,0,3,2:T(2,128)(2,1)S(1)} %copy.63, s32[]{:T(128)S(6)} %select_n.318, s32[]{:T(128)} %constant.338.clone.1, s32[]{:T(128)} %constant.338.clone.1, s32[]{:T(128)} %constant.338.clone.1) | dynamic-update-slice | bytes 473092 | tf_op jit(solution)/shard_map/jit(dynamic_update_index_in_dim)/dynamic_update_slice | solution.py:49
  347.9 14.3 %dynamic_update_slice.122 = bf16[16,128,2,462]{1,0,3,2:T(8,128)(2,1)} dynamic-update-slice(bf16[16,128,2,462]{1,0,3,2:T(8,128)(2,1)} %dynamic_update_slice.121, bf16[1,128,2,462]{1,0,3,2:T(2,128)(2,1)S(1)} %copy.64, s32[]{:T(128)S(6)} %select_n.320, s32[]{:T(128)} %constant.338.clone.1, s32[]{:T(128)} %constant.338.clone.1, s32[]{:T(128)} %constant.338.clone.1) | dynamic-update-slice | bytes 473092 | tf_op jit(solution)/shard_map/jit(dynamic_update_index_in_dim)/dynamic_update_slice | solution.py:52
  362.9 14.3 %dynamic_update_slice.123 = bf16[16,128,2,462]{1,0,3,2:T(8,128)(2,1)} dynamic-update-slice(bf16[16,128,2,462]{1,0,3,2:T(8,128)(2,1)} %dynamic_update_slice.122, bf16[1,128,2,462]{1,0,3,2:T(2,128)(2,1)S(1)} %copy.65, s32[]{:T(128)S(6)} %select_n.322, s32[]{:T(128)} %constant.338.clone.1, s32[]{:T(128)} %constant.338.clone.1, s32[]{:T(128)} %constant.338.clone.1) | dynamic-update-slice | bytes 473092 | tf_op jit(solution)/shard_map/jit(dynamic_update_index_in_dim)/dynamic_update_slice | solution.py:49
  377.2 14.3 %dynamic_update_slice.124 = bf16[16,128,2,462]{1,0,3,2:T(8,128)(2,1)} dynamic-update-slice(bf16[16,128,2,462]{1,0,3,2:T(8,128)(2,1)} %dynamic_update_slice.123, bf16[1,128,2,462]{1,0,3,2:T(2,128)(2,1)S(1)} %copy.66, s32[]{:T(128)S(6)} %select_n.324, s32[]{:T(128)} %constant.338.clone.1, s32[]{:T(128)} %constant.338.clone.1, s32[]{:T(128)} %constant.338.clone.1) | dynamic-update-slice | bytes 473092 | tf_op jit(solution)/shard_map/jit(dynamic_update_index_in_dim)/dynamic_update_slice | solution.py:52
  392.2 14.5 %dynamic_update_slice.125 = bf16[16,128,2,462]{1,0,3,2:T(8,128)(2,1)} dynamic-update-slice(bf16[16,128,2,462]{1,0,3,2:T(8,128)(2,1)} %dynamic_update_slice.124, bf16[1,128,2,462]{1,0,3,2:T(2,128)(2,1)S(1)} %copy.67, s32[]{:T(128)S(6)} %select_n.326, s32[]{:T(128)} %constant.338.clone.1, s32[]{:T(128)} %constant.338.clone.1, s32[]{:T(128)} %constant.338.clone.1) | dynamic-update-slice | bytes 473092 | tf_op jit(solution)/shard_map/jit(dynamic_update_index_in_dim)/dynamic_update_slice | solution.py:49
  406.7 14.3 %dynamic_update_slice.126 = bf16[16,128,2,462]{1,0,3,2:T(8,128)(2,1)} dynamic-update-slice(bf16[16,128,2,462]{1,0,3,2:T(8,128)(2,1)} %dynamic_update_slice.125, bf16[1,128,2,462]{1,0,3,2:T(2,128)(2,1)S(1)} %copy.68, s32[]{:T(128)S(6)} %select_n.328, s32[]{:T(128)} %constant.338.clone.1, s32[]{:T(128)} %constant.338.clone.1, s32[]{:T(128)} %constant.338.clone.1) | dynamic-update-slice | bytes 473092 | tf_op jit(solution)/shard_map/jit(dynamic_update_index_in_dim)/dynamic_update_slice | solution.py:52
  422.7 14.3 %dynamic_update_slice.127 = bf16[16,128,2,462]{1,0,3,2:T(8,128)(2,1)} dynamic-update-slice(bf16[16,128,2,462]{1,0,3,2:T(8,128)(2,1)} %dynamic_update_slice.126, bf16[1,128,2,462]{1,0,3,2:T(2,128)(2,1)S(1)} %copy.69, s32[]{:T(128)S(6)} %select_n.330, s32[]{:T(128)} %constant.338.clone.1, s32[]{:T(128)} %constant.338.clone.1, s32[]{:T(128)} %constant.338.clone.1) | dynamic-update-slice | bytes 473092 | tf_op jit(solution)/shard_map/jit(dynamic_update_index_in_dim)/dynamic_update_slice | solution.py:49
  437.0 14.3 %dynamic_update_slice.128 = bf16[16,128,2,462]{1,0,3,2:T(8,128)(2,1)} dynamic-update-slice(bf16[16,128,2,462]{1,0,3,2:T(8,128)(2,1)} %dynamic_update_slice.127, bf16[1,128,2,462]{1,0,3,2:T(2,128)(2,1)S(1)} %copy.70, s32[]{:T(128)S(6)} %select_n.332, s32[]{:T(128)} %constant.338.clone.1, s32[]{:T(128)} %constant.338.clone.1, s32[]{:T(128)} %constant.338.clone.1) | dynamic-update-slice | bytes 473092 | tf_op jit(solution)/shard_map/jit(dynamic_update_index_in_dim)/dynamic_update_slice | solution.py:52
  452.6 14.3 %dynamic_update_slice.129 = bf16[16,128,2,462]{1,0,3,2:T(8,128)(2,1)} dynamic-update-slice(bf16[16,128,2,462]{1,0,3,2:T(8,128)(2,1)} %dynamic_update_slice.128, bf16[1,128,2,462]{1,0,3,2:T(2,128)(2,1)S(1)} %copy.71, s32[]{:T(128)S(6)} %select_n.334, s32[]{:T(128)} %constant.338.clone.1, s32[]{:T(128)} %constant.338.clone.1, s32[]{:T(128)} %constant.338.clone.1) | dynamic-update-slice | bytes 473092 | tf_op jit(solution)/shard_map/jit(dynamic_update_index_in_dim)/dynamic_update_slice | solution.py:49
  471.9 6.2 dynamic_update_slice.98
  478.5 6.2 dynamic_update_slice.99
  484.6 6.2 dynamic_update_slice.100
  491.2 6.2 dynamic_update_slice.101
  497.4 6.2 dynamic_update_slice.102
  503.9 6.2 dynamic_update_slice.103
  510.1 6.2 dynamic_update_slice.104
  516.7 6.6 dynamic_update_slice.105
  523.2 6.2 dynamic_update_slice.106
  529.8 6.2 dynamic_update_slice.107
  535.9 6.2 dynamic_update_slice.108
  543.4 6.2 dynamic_update_slice.109
  549.5 6.2 dynamic_update_slice.110
  557.9 6.2 dynamic_update_slice.111
  564.0 6.2 dynamic_update_slice.112
  571.3 6.2 dynamic_update_slice.113
  586.4 4.8 fusion.10
  596.7 104.0 %reduce-scatter.2.cloned.1.call-done = bf16[64,512]{1,0:T(8,128)(2,1)} async-done(((bf16[2048,512]{1,0:T(8,128)(2,1)}), bf16[64,512]{1,0:T(8,128)(2,1)}) %reduce-scatter.2.cloned.1.call-update) | async-done | bytes 65552 | tf_op jit(solution)/shard_map/reduce_scatter | solution.py:100
  (216 shorter events, 150.5 us)
Async XLA Ops:
  7.2 68.5 %all-gather.3.cloned.1.call-start = ((), (), s32[]{:S(2)}) async-start(), calls=%async_computation.1 | async-start | bytes 2162688 | tf_op jit(solution)/shard_map/all_gather | solution.py:86
  7.9 583.2 %all-gather.5.cloned.1.call-start = ((), (), s32[]{:S(2)}) async-start(), calls=%async_computation.3 | async-start | bytes 2162688 | tf_op jit(solution)/shard_map/all_gather | solution.py:87
  9.0 17.4 %collective-permute-start.30 = (bf16[128,2,462]{0,2,1:T(8,128)(2,1)S(1)}, bf16[128,2,462]{0,2,1:T(8,128)(2,1)S(1)}, u32[]{:S(2)}, u32[]{:S(2)}) collective-permute-start(bf16[128,2,462]{0,2,1:T(8,128)(2,1)S(1)} %get-tuple-element.22), channel_id=1, source_target_pairs={{0,32},{32,64},{64,96},{96,128},{128,160},{160,192},{192,224},{224... | collective-permute-start | bytes 709640 | tf_op jit(solution)/shard_map/ppermute | solution.py:48
  13.3 15.2 %collective-permute-start.31 = (bf16[128,2,462]{0,2,1:T(8,128)(2,1)S(1)}, bf16[128,2,462]{0,2,1:T(8,128)(2,1)}, u32[]{:S(2)}, u32[]{:S(2)}) collective-permute-start(bf16[128,2,462]{0,2,1:T(8,128)(2,1)S(1)} %get-tuple-element.22), channel_id=1, source_target_pairs={{0,480},{32,0},{64,32},{96,64},{128,96},{160,128},{192,160},{224,1... | collective-permute-start | bytes 709640 | tf_op jit(solution)/shard_map/ppermute | solution.py:51
  26.4 9.3 %collective-permute-start.32 = (bf16[128,2,462]{0,2,1:T(8,128)(2,1)S(1)}, bf16[128,2,462]{0,2,1:T(8,128)(2,1)}, u32[]{:S(2)}, u32[]{:S(2)}) collective-permute-start(bf16[128,2,462]{0,2,1:T(8,128)(2,1)S(1)} %collective-permute-done.30), channel_id=1, source_target_pairs={{0,32},{32,64},{64,96},{96,128},{128,160},{160,192},{192,224},{224... | collective-permute-start | bytes 709640 | tf_op jit(solution)/shard_map/ppermute | solution.py:48
  28.5 59.0 %collective-permute-start.33 = (bf16[128,2,462]{0,2,1:T(8,128)(2,1)}, bf16[128,2,462]{0,2,1:T(8,128)(2,1)}, u32[]{:S(2)}, u32[]{:S(2)}) collective-permute-start(bf16[128,2,462]{0,2,1:T(8,128)(2,1)} %collective-permute-done.31), channel_id=1, source_target_pairs={{0,480},{32,0},{64,32},{96,64},{128,96},{160,128},{192,160},{224,1... | collective-permute-start | bytes 709640 | tf_op jit(solution)/shard_map/ppermute | solution.py:51
  35.7 56.3 %collective-permute-start.34 = (bf16[128,2,462]{0,2,1:T(8,128)(2,1)}, bf16[128,2,462]{0,2,1:T(8,128)(2,1)}, u32[]{:S(2)}, u32[]{:S(2)}) collective-permute-start(bf16[128,2,462]{0,2,1:T(8,128)(2,1)} %collective-permute-done.32), channel_id=1, source_target_pairs={{0,32},{32,64},{64,96},{96,128},{128,160},{160,192},{192,224},{224... | collective-permute-start | bytes 709640 | tf_op jit(solution)/shard_map/ppermute | solution.py:48
  84.3 14.2 %collective-permute-start = (bf16[128,462]{0,1:T(8,128)(2,1)S(1)}, bf16[128,462]{0,1:T(8,128)(2,1)}, u32[]{:S(2)}, u32[]{:S(2)}) collective-permute-start(bf16[128,462]{0,1:T(8,128)(2,1)S(1)} %bitcast.191), channel_id=1, source_target_pairs={{0,32},{32,64},{64,96},{96,128},{128,160},{160,192},{192,224},{224... | collective-permute-start | bytes 354824 | tf_op jit(solution)/shard_map/ppermute | solution.py:70
  87.5 613.3 %reduce-scatter.2.cloned.1.call-start = ((), (), s32[]{:S(2)}) async-start(), calls=%async_computation.2 | async-start | bytes 2162688 | tf_op jit(solution)/shard_map/reduce_scatter | solution.py:100
  87.5 57.8 %collective-permute-start.35 = (bf16[128,2,462]{0,2,1:T(8,128)(2,1)}, bf16[128,2,462]{0,2,1:T(8,128)(2,1)S(1)}, u32[]{:S(2)}, u32[]{:S(2)}) collective-permute-start(bf16[128,2,462]{0,2,1:T(8,128)(2,1)} %collective-permute-done.33), channel_id=1, source_target_pairs={{0,480},{32,0},{64,32},{96,64},{128,96},{160,128},{192,160},{224,1... | collective-permute-start | bytes 709640 | tf_op jit(solution)/shard_map/ppermute | solution.py:51
  92.0 58.0 %collective-permute-start.36 = (bf16[128,2,462]{0,2,1:T(8,128)(2,1)}, bf16[128,2,462]{0,2,1:T(8,128)(2,1)S(1)}, u32[]{:S(2)}, u32[]{:S(2)}) collective-permute-start(bf16[128,2,462]{0,2,1:T(8,128)(2,1)} %collective-permute-done.34), channel_id=1, source_target_pairs={{0,32},{32,64},{64,96},{96,128},{128,160},{160,192},{192,224},{224... | collective-permute-start | bytes 709640 | tf_op jit(solution)/shard_map/ppermute | solution.py:48
  93.9 7.6 %collective-permute-start.8 = (bf16[128,462]{0,1:T(8,128)(2,1)S(1)}, bf16[128,462]{0,1:T(8,128)(2,1)S(1)}, u32[]{:S(2)}, u32[]{:S(2)}) collective-permute-start(bf16[128,462]{0,1:T(8,128)(2,1)S(1)} %bitcast.192), channel_id=1, source_target_pairs={{0,480},{32,0},{64,32},{96,64},{128,96},{160,128},{192,160},{224,1... | collective-permute-start | bytes 354824 | tf_op jit(solution)/shard_map/ppermute | solution.py:74
  99.5 7.5 %collective-permute-start.1 = (bf16[128,462]{0,1:T(8,128)(2,1)S(1)}, bf16[128,462]{0,1:T(8,128)(2,1)S(1)}, u32[]{:S(2)}, u32[]{:S(2)}) collective-permute-start(bf16[128,462]{0,1:T(8,128)(2,1)S(1)} %fusion.27), channel_id=1, source_target_pairs={{0,32},{32,64},{64,96},{96,128},{128,160},{160,192},{192,224},{224... | collective-permute-start | bytes 354824 | tf_op jit(solution)/shard_map/ppermute | solution.py:70
  102.5 7.5 %collective-permute-start.9 = (bf16[128,462]{0,1:T(8,128)(2,1)S(1)}, bf16[128,462]{0,1:T(8,128)(2,1)S(1)}, u32[]{:S(2)}, u32[]{:S(2)}) collective-permute-start(bf16[128,462]{0,1:T(8,128)(2,1)S(1)} %fusion.20), channel_id=1, source_target_pairs={{0,480},{32,0},{64,32},{96,64},{128,96},{160,128},{192,160},{224,1... | collective-permute-start | bytes 354824 | tf_op jit(solution)/shard_map/ppermute | solution.py:74
  108.0 7.5 %collective-permute-start.2 = (bf16[128,462]{0,1:T(8,128)(2,1)S(1)}, bf16[128,462]{0,1:T(8,128)(2,1)S(1)}, u32[]{:S(2)}, u32[]{:S(2)}) collective-permute-start(bf16[128,462]{0,1:T(8,128)(2,1)S(1)} %fusion.26), channel_id=1, source_target_pairs={{0,32},{32,64},{64,96},{96,128},{128,160},{160,192},{192,224},{224... | collective-permute-start | bytes 354824 | tf_op jit(solution)/shard_map/ppermute | solution.py:70
  110.9 6.6 collective-permute-start.10
  115.6 6.8 collective-permute-start.3
  117.5 6.8 collective-permute-start.11
  122.4 6.8 collective-permute-start.4
  124.4 6.8 collective-permute-start.12
  129.2 6.9 collective-permute-start.5
  131.2 6.9 collective-permute-start.13
  136.2 7.2 %collective-permute-start.6 = (bf16[128,462]{0,1:T(8,128)(2,1)S(1)}, bf16[128,462]{0,1:T(8,128)(2,1)S(1)}, u32[]{:S(2)}, u32[]{:S(2)}) collective-permute-start(bf16[128,462]{0,1:T(8,128)(2,1)S(1)} %fusion.22), channel_id=1, source_target_pairs={{0,32},{32,64},{64,96},{96,128},{128,160},{160,192},{192,224},{224... | collective-permute-start | bytes 354824 | tf_op jit(solution)/shard_map/ppermute | solution.py:70
  138.1 13.7 %collective-permute-start.14 = (bf16[128,462]{0,1:T(8,128)(2,1)S(1)}, bf16[128,462]{0,1:T(8,128)(2,1)S(1)}, u32[]{:S(2)}, u32[]{:S(2)}) collective-permute-start(bf16[128,462]{0,1:T(8,128)(2,1)S(1)} %fusion.15), channel_id=1, source_target_pairs={{0,480},{32,0},{64,32},{96,64},{128,96},{160,128},{192,160},{224,1... | collective-permute-start | bytes 354824 | tf_op jit(solution)/shard_map/ppermute | solution.py:74
  143.4 8.5 %collective-permute-start.7 = (bf16[128,462]{0,1:T(8,128)(2,1)S(1)}, bf16[128,462]{0,1:T(8,128)(2,1)S(1)}, u32[]{:S(2)}, u32[]{:S(2)}) collective-permute-start(bf16[128,462]{0,1:T(8,128)(2,1)S(1)} %fusion.21), channel_id=1, source_target_pairs={{0,32},{32,64},{64,96},{96,128},{128,160},{160,192},{192,224},{224... | collective-permute-start | bytes 354824 | tf_op jit(solution)/shard_map/ppermute | solution.py:70
  145.4 17.1 %collective-permute-start.37 = (bf16[128,2,462]{0,2,1:T(8,128)(2,1)S(1)}, bf16[128,2,462]{0,2,1:T(8,128)(2,1)S(1)}, u32[]{:S(2)}, u32[]{:S(2)}) collective-permute-start(bf16[128,2,462]{0,2,1:T(8,128)(2,1)S(1)} %collective-permute-done.35), channel_id=1, source_target_pairs={{0,480},{32,0},{64,32},{96,64},{128,96},{160,128},{192,160},{224,1... | collective-permute-start | bytes 709640 | tf_op jit(solution)/shard_map/ppermute | solution.py:51
  150.0 17.1 %collective-permute-start.38 = (bf16[128,2,462]{0,2,1:T(8,128)(2,1)S(1)}, bf16[128,2,462]{0,2,1:T(8,128)(2,1)S(1)}, u32[]{:S(2)}, u32[]{:S(2)}) collective-permute-start(bf16[128,2,462]{0,2,1:T(8,128)(2,1)S(1)} %collective-permute-done.36), channel_id=1, source_target_pairs={{0,32},{32,64},{64,96},{96,128},{128,160},{160,192},{192,224},{224... | collective-permute-start | bytes 709640 | tf_op jit(solution)/shard_map/ppermute | solution.py:48
  152.0 8.6 %collective-permute-start.15 = (bf16[128,462]{0,1:T(8,128)(2,1)S(1)}, bf16[128,462]{0,1:T(8,128)(2,1)S(1)}, u32[]{:S(2)}, u32[]{:S(2)}) collective-permute-start(bf16[128,462]{0,1:T(8,128)(2,1)S(1)} %fusion.29), channel_id=1, source_target_pairs={{0,32},{32,64},{64,96},{96,128},{128,160},{160,192},{192,224},{224... | collective-permute-start | bytes 354824 | tf_op jit(solution)/shard_map/ppermute | solution.py:48
  153.9 15.1 %collective-permute-start.16 = (bf16[128,462]{0,1:T(8,128)(2,1)S(1)}, bf16[128,462]{0,1:T(8,128)(2,1)S(1)}, u32[]{:S(2)}, u32[]{:S(2)}) collective-permute-start(bf16[128,462]{0,1:T(8,128)(2,1)S(1)} %fusion.29), channel_id=1, source_target_pairs={{0,480},{32,0},{64,32},{96,64},{128,96},{160,128},{192,160},{224,1... | collective-permute-start | bytes 354824 | tf_op jit(solution)/shard_map/ppermute | solution.py:51
  160.6 13.1 %collective-permute-start.17 = (bf16[128,462]{0,1:T(8,128)(2,1)S(1)}, bf16[128,462]{0,1:T(8,128)(2,1)S(1)}, u32[]{:S(2)}, u32[]{:S(2)}) collective-permute-start(bf16[128,462]{0,1:T(8,128)(2,1)S(1)} %collective-permute-done.15), channel_id=1, source_target_pairs={{0,32},{32,64},{64,96},{96,128},{128,160},{160,192},{192,224},{224... | collective-permute-start | bytes 354824 | tf_op jit(solution)/shard_map/ppermute | solution.py:48
  162.5 19.9 %collective-permute-start.39 = (bf16[128,2,462]{0,2,1:T(8,128)(2,1)S(1)}, bf16[128,2,462]{0,2,1:T(8,128)(2,1)S(1)}, u32[]{:S(2)}, u32[]{:S(2)}) collective-permute-start(bf16[128,2,462]{0,2,1:T(8,128)(2,1)S(1)} %collective-permute-done.37), channel_id=1, source_target_pairs={{0,480},{32,0},{64,32},{96,64},{128,96},{160,128},{192,160},{224,1... | collective-permute-start | bytes 709640 | tf_op jit(solution)/shard_map/ppermute | solution.py:51
  167.1 19.9 %collective-permute-start.40 = (bf16[128,2,462]{0,2,1:T(8,128)(2,1)S(1)}, bf16[128,2,462]{0,2,1:T(8,128)(2,1)S(1)}, u32[]{:S(2)}, u32[]{:S(2)}) collective-permute-start(bf16[128,2,462]{0,2,1:T(8,128)(2,1)S(1)} %collective-permute-done.38), channel_id=1, source_target_pairs={{0,32},{32,64},{64,96},{96,128},{128,160},{160,192},{192,224},{224... | collective-permute-start | bytes 709640 | tf_op jit(solution)/shard_map/ppermute | solution.py:48
  169.0 6.5 collective-permute-start.18
  173.7 6.8 collective-permute-start.19
  175.6 13.3 %collective-permute-start.20 = (bf16[128,462]{0,1:T(8,128)(2,1)S(1)}, bf16[128,462]{0,1:T(8,128)(2,1)S(1)}, u32[]{:S(2)}, u32[]{:S(2)}) collective-permute-start(bf16[128,462]{0,1:T(8,128)(2,1)S(1)} %collective-permute-done.18), channel_id=1, source_target_pairs={{0,480},{32,0},{64,32},{96,64},{128,96},{160,128},{192,160},{224,1... | collective-permute-start | bytes 354824 | tf_op jit(solution)/shard_map/ppermute | solution.py:51
  180.5 13.1 %collective-permute-start.21 = (bf16[128,462]{0,1:T(8,128)(2,1)S(1)}, bf16[128,462]{0,1:T(8,128)(2,1)S(1)}, u32[]{:S(2)}, u32[]{:S(2)}) collective-permute-start(bf16[128,462]{0,1:T(8,128)(2,1)S(1)} %collective-permute-done.19), channel_id=1, source_target_pairs={{0,32},{32,64},{64,96},{96,128},{128,160},{160,192},{192,224},{224... | collective-permute-start | bytes 354824 | tf_op jit(solution)/shard_map/ppermute | solution.py:48
  182.4 19.9 %collective-permute-start.41 = (bf16[128,2,462]{0,2,1:T(8,128)(2,1)S(1)}, bf16[128,2,462]{0,2,1:T(8,128)(2,1)S(1)}, u32[]{:S(2)}, u32[]{:S(2)}) collective-permute-start(bf16[128,2,462]{0,2,1:T(8,128)(2,1)S(1)} %collective-permute-done.39), channel_id=1, source_target_pairs={{0,480},{32,0},{64,32},{96,64},{128,96},{160,128},{192,160},{224,1... | collective-permute-start | bytes 709640 | tf_op jit(solution)/shard_map/ppermute | solution.py:51
  187.0 19.9 %collective-permute-start.42 = (bf16[128,2,462]{0,2,1:T(8,128)(2,1)S(1)}, bf16[128,2,462]{0,2,1:T(8,128)(2,1)S(1)}, u32[]{:S(2)}, u32[]{:S(2)}) collective-permute-start(bf16[128,2,462]{0,2,1:T(8,128)(2,1)S(1)} %collective-permute-done.40), channel_id=1, source_target_pairs={{0,32},{32,64},{64,96},{96,128},{128,160},{160,192},{192,224},{224... | collective-permute-start | bytes 709640 | tf_op jit(solution)/shard_map/ppermute | solution.py:48
  188.9 6.5 collective-permute-start.22
  193.5 6.8 collective-permute-start.23
  195.5 13.3 %collective-permute-start.24 = (bf16[128,462]{0,1:T(8,128)(2,1)S(1)}, bf16[128,462]{0,1:T(8,128)(2,1)S(1)}, u32[]{:S(2)}, u32[]{:S(2)}) collective-permute-start(bf16[128,462]{0,1:T(8,128)(2,1)S(1)} %collective-permute-done.22), channel_id=1, source_target_pairs={{0,480},{32,0},{64,32},{96,64},{128,96},{160,128},{192,160},{224,1... | collective-permute-start | bytes 354824 | tf_op jit(solution)/shard_map/ppermute | solution.py:51
  200.3 13.1 %collective-permute-start.25 = (bf16[128,462]{0,1:T(8,128)(2,1)S(1)}, bf16[128,462]{0,1:T(8,128)(2,1)S(1)}, u32[]{:S(2)}, u32[]{:S(2)}) collective-permute-start(bf16[128,462]{0,1:T(8,128)(2,1)S(1)} %collective-permute-done.23), channel_id=1, source_target_pairs={{0,32},{32,64},{64,96},{96,128},{128,160},{160,192},{192,224},{224... | collective-permute-start | bytes 354824 | tf_op jit(solution)/shard_map/ppermute | solution.py:48
  202.2 219.2 %collective-permute-start.43 = (bf16[128,2,462]{0,2,1:T(8,128)(2,1)S(1)}, bf16[128,2,462]{0,2,1:T(8,128)(2,1)}, u32[]{:S(2)}, u32[]{:S(2)}) collective-permute-start(bf16[128,2,462]{0,2,1:T(8,128)(2,1)S(1)} %collective-permute-done.41), channel_id=1, source_target_pairs={{0,480},{32,0},{64,32},{96,64},{128,96},{160,128},{192,160},{224,1... | collective-permute-start | bytes 709640 | tf_op jit(solution)/shard_map/ppermute | solution.py:51
  206.8 244.5 %collective-permute-start.44 = (bf16[128,2,462]{0,2,1:T(8,128)(2,1)S(1)}, bf16[128,2,462]{0,2,1:T(8,128)(2,1)}, u32[]{:S(2)}, u32[]{:S(2)}) collective-permute-start(bf16[128,2,462]{0,2,1:T(8,128)(2,1)S(1)} %collective-permute-done.42), channel_id=1, source_target_pairs={{0,32},{32,64},{64,96},{96,128},{128,160},{160,192},{192,224},{224... | collective-permute-start | bytes 709640 | tf_op jit(solution)/shard_map/ppermute | solution.py:48
  208.8 7.2 %collective-permute-start.26 = (bf16[128,462]{0,1:T(8,128)(2,1)S(1)}, bf16[128,462]{0,1:T(8,128)(2,1)}, u32[]{:S(2)}, u32[]{:S(2)}) collective-permute-start(bf16[128,462]{0,1:T(8,128)(2,1)S(1)} %collective-permute-done.24), channel_id=1, source_target_pairs={{0,480},{32,0},{64,32},{96,64},{128,96},{160,128},{192,160},{224,1... | collective-permute-start | bytes 354824 | tf_op jit(solution)/shard_map/ppermute | solution.py:51
  213.4 8.1 %collective-permute-start.27 = (bf16[128,462]{0,1:T(8,128)(2,1)S(1)}, bf16[128,462]{0,1:T(8,128)(2,1)}, u32[]{:S(2)}, u32[]{:S(2)}) collective-permute-start(bf16[128,462]{0,1:T(8,128)(2,1)S(1)} %collective-permute-done.25), channel_id=1, source_target_pairs={{0,32},{32,64},{64,96},{96,128},{128,160},{160,192},{192,224},{224... | collective-permute-start | bytes 354824 | tf_op jit(solution)/shard_map/ppermute | solution.py:48
  216.0 340.8 %collective-permute-start.28 = (bf16[128,462]{0,1:T(8,128)(2,1)}, bf16[128,462]{0,1:T(8,128)(2,1)}, u32[]{:S(2)}, u32[]{:S(2)}) collective-permute-start(bf16[128,462]{0,1:T(8,128)(2,1)} %collective-permute-done.26), channel_id=1, source_target_pairs={{0,480},{32,0},{64,32},{96,64},{128,96},{160,128},{192,160},{224,1... | collective-permute-start | bytes 354824 | tf_op jit(solution)/shard_map/ppermute | solution.py:51
  221.5 348.7 %collective-permute-start.29 = (bf16[128,462]{0,1:T(8,128)(2,1)}, bf16[128,462]{0,1:T(8,128)(2,1)}, u32[]{:S(2)}, u32[]{:S(2)}) collective-permute-start(bf16[128,462]{0,1:T(8,128)(2,1)} %collective-permute-done.27), channel_id=1, source_target_pairs={{0,32},{32,64},{64,96},{96,128},{128,160},{160,192},{192,224},{224... | collective-permute-start | bytes 354824 | tf_op jit(solution)/shard_map/ppermute | solution.py:48
  (34 other events, 1485.4 us)
Sparse Core Ops, SparseCore 0:
  11.1 64.5 all-gather.2
  87.6 57.6 all-gather.4
  586.5 114.2 reduce-scatter.1

commit v2 on v1

--- a/solution.py
+++ b/solution.py
@@ -40,17 +40,17 @@
     up, down = _shifts(n)
     n_up = n // 2
     n_down = n - 1 - n_up
-    out = jnp.zeros((n,) + x.shape, x.dtype)
-    out = lax.dynamic_update_index_in_dim(out, x, me, 0)
+    held = {0: x}
     a = x
     b = x
     for s in range(1, n_up + 1):
         a = lax.ppermute(a, axis, up)
-        out = lax.dynamic_update_index_in_dim(out, a, (me - s + n) % n, 0)
+        held[-s] = a
         if s <= n_down:
             b = lax.ppermute(b, axis, down)
-            out = lax.dynamic_update_index_in_dim(out, b, (me + s) % n, 0)
-    return out
+            held[s] = b
+    ring_order = jnp.stack([held[d] for d in range(-n_up, n_down + 1)])
+    return jnp.take(ring_order, (jnp.arange(n) - me + n_up) % n, axis=0)
 
 
 def ring_reduce_scatter(parts, axis, n, wire_dtype):
@@ -79,21 +79,16 @@
 
 def shards(inputs, gate_pre, up_pre, w_gate, w_up, w_down, grad_out, n_row):
     tokens_row, hidden_units = gate_pre.shape
-    pre = jnp.stack([gate_pre, up_pre], axis=1)
-    all_pre = ring_all_gather(pre, "row", n_row).reshape(
-        (n_row * tokens_row, 2, hidden_units)
-    )
     all_grad_out = lax.all_gather(grad_out, "col", axis=0, tiled=True)
     all_inputs = lax.all_gather(inputs, "col", axis=0, tiled=True)
     part = contract_cols(all_grad_out, w_down).astype(jnp.bfloat16)
     part = part.reshape((n_row, tokens_row, hidden_units))
-    own = ring_reduce_scatter(part, "row", n_row, jnp.bfloat16).astype(jnp.bfloat16)
-    hidden_grad = ring_all_gather(own, "row", n_row).reshape(
-        (n_row * tokens_row, hidden_units)
+    own_grad = ring_reduce_scatter(part, "row", n_row, jnp.bfloat16)
+    own = jnp.stack(pointwise(gate_pre, up_pre, own_grad), axis=1)
+    gathered = ring_all_gather(own, "row", n_row).reshape(
+        (n_row * tokens_row, 3, hidden_units)
     )
-    hidden, gate_grad, up_grad = pointwise(
-        all_pre[:, 0], all_pre[:, 1], hidden_grad.astype(jnp.float32)
-    )
+    hidden, gate_grad, up_grad = gathered[:, 0], gathered[:, 1], gathered[:, 2]
     grad_down = contract_rows(hidden, all_grad_out).astype(jnp.bfloat16)
     grad_gate = contract_rows(all_inputs, gate_grad).astype(jnp.bfloat16)
     grad_up = contract_rows(all_inputs, up_grad).astype(jnp.bfloat16)

time: 721 us -> 400 us (0.55); the launches traced: 707 us -> 398 us
  local copies, waits for them, and re-layouts: 361 us -> 43.5 us
  waiting for transfers between devices: 153 us -> 222 us
  starting transfers between devices: 152 us -> 96.1 us
    dynamic_update_slice x32 -> x0, local copies, waits for them, and re-layouts: 328 us -> none  [the longest x16 164 us: ring_all_gather(): out = lax.dynamic_update_index_in_dim(out, a, (me - s + n) % n, 0)]
    ppermute x14 -> x7, starting transfers between devices: 69.8 us -> 32.2 us  [ring_all_gather(): b = lax.ppermute(b, axis, down)]
    ppermute x16 -> x8, waiting for transfers between devices: 8.65 us -> 40.1 us  [ring_all_gather(): a = lax.ppermute(a, axis, up)]
    all_gather x1, waiting for transfers between devices: 38.1 us -> 67.5 us  [shards(): all_grad_out = lax.all_gather(grad_out, 'col', axis=0, tiled=True)]
    broadcast_in_dim x34 -> x1, local copies, waits for them, and re-layouts: 20.7 us -> 0.07 us  [ring_all_gather(): return jnp.take(ring_order, (jnp.arange(n) - me + n_up) % n, axis=0)]
    gather x0 -> x3, local copies, waits for them, and re-layouts: none -> 20.2 us  [ring_all_gather(): return jnp.take(ring_order, (jnp.arange(n) - me + n_up) % n, axis=0)]
    ppermute x16 -> x8, starting transfers between devices: 33.1 us -> 15.3 us  [ring_all_gather(): a = lax.ppermute(a, axis, up)]
    unnamed x73 -> x35, local copies, waits for them, and re-layouts: 3.1 us -> 17.5 us
  transfers between devices with their start and end apart: 48 -> 33, of which waited for: 9 -> 19; matrix products, arithmetic and copies ran while one was open for 55% -> 14% of each run, Pallas kernels for 0% -> 0%
where the time goes in v2:
time: 400 us; the launch traced here: 398 us
  waiting for transfers between devices  222 us (56%)
  starting transfers between devices  96.1 us (24%)
  local copies, waits for them, and re-layouts  43.5 us (11%)
  matrix products  18 us (4%)
  between operations  14.5 us (4%)
  other arithmetic  4.62 us (1%)
    reduce_scatter x1, waiting for transfers between devices, shards(): lax.psum_scatter((contract_cols(gate_grad, w_gate) + contract_cols(up_gra...  98.5 us
    all_gather x1, waiting for transfers between devices, shards(): all_grad_out = lax.all_gather(grad_out, 'col', axis=0, tiled=True)  67.5 us
    ppermute x8, waiting for transfers between devices, ring_all_gather(): a = lax.ppermute(a, axis, up)  40.1 us
    ppermute x7, starting transfers between devices, ring_all_gather(): b = lax.ppermute(b, axis, down)  32.2 us
    ppermute x7, starting transfers between devices, ring_reduce_scatter(): b = lax.ppermute(b.astype(wire_dtype), axis, down).astype(jnp.float32)  31.8 us
    gather x3, local copies, waits for them, and re-layouts, ring_all_gather(): return jnp.take(ring_order, (jnp.arange(n) - me + n_up) % n, axis=0)  20.2 us
    unnamed x35, local copies, waits for them, and re-layouts  17.5 us
    ppermute x8, starting transfers between devices, ring_reduce_scatter(): a = lax.ppermute(a.astype(wire_dtype), axis, up).astype(jnp.float32)  16.6 us
  transfers between devices with their start and end apart: 33, of which 19 were waited for; matrix products, arithmetic and copies ran while one was open for 14% of the time, Pallas kernels for 0%

profile of v2, /device:TPU:1, one launch (start us, length us, event | category | flops | bytes accessed | tf_op | source)
XLA Modules:
  0.0 398.3 jit_solution(15042089465494132816)
XLA Ops:
  8.2 67.5 %all-gather.3.cloned.1.call-done = bf16[2048,512]{1,0:T(8,128)(2,1)} async-done(((bf16[64,512]{1,0:T(8,128)(2,1)}), bf16[2048,512]{1,0:T(8,128)(2,1)}) %all-gather.3.cloned.1.call-update) | async-done | bytes 2097168 | tf_op jit(solution)/shard_map/all_gather | solution.py:82
  75.7 2.8 convolution_convert_fusion
  79.5 4.6 %constant_dynamic-slice_fusion.15 = (bf16[1,128,462]{1,0,2:T(2,128)(2,1)S(1)}, bf16[1,128,462]{1,0,2:T(2,128)(2,1)S(1)}, bf16[1,128,462]{1,0,2:T(2,128)(2,1)S(1)...) fusion(bf16[16,128,462]{1,0,2:T(8,128)(2,1)S(1)} %slice_bitcast, ...), kind=kLoop, calls=%fused_computation.111 | loop fusion | bytes 3784768 | tf_op jit(solution)/shard_map/jit(dynamic_index_in_dim)/dynamic_slice | solution.py:63
  84.1 3.2 collective-permute-start
  87.3 4.4 %collective-permute-start.8 = (bf16[128,462]{0,1:T(8,128)(2,1)S(1)}, bf16[128,462]{0,1:T(8,128)(2,1)S(1)}, u32[]{:S(2)}, u32[]{:S(2)}) collective-permute-start(bf16[128,462]{0,1:T(8,128)(2,1)S(1)} %bitcast.164), channel_id=1, source_target_pairs={{0,480},{32,0},{64,32},{96,64},{128,96},{160,128},{192,160},{224,1... | collective-permute-start | bytes 354824 | tf_op jit(solution)/shard_map/ppermute | solution.py:74
  93.2 1.9 collective-permute-start.1
  95.1 4.6 %collective-permute-start.9 = (bf16[128,462]{0,1:T(8,128)(2,1)S(1)}, bf16[128,462]{0,1:T(8,128)(2,1)S(1)}, u32[]{:S(2)}, u32[]{:S(2)}) collective-permute-start(bf16[128,462]{0,1:T(8,128)(2,1)S(1)} %fusion.22), channel_id=1, source_target_pairs={{0,480},{32,0},{64,32},{96,64},{128,96},{160,128},{192,160},{224,1... | collective-permute-start | bytes 354824 | tf_op jit(solution)/shard_map/ppermute | solution.py:74
  100.0 1.9 collective-permute-start.2
  102.0 4.6 %collective-permute-start.10 = (bf16[128,462]{0,1:T(8,128)(2,1)S(1)}, bf16[128,462]{0,1:T(8,128)(2,1)S(1)}, u32[]{:S(2)}, u32[]{:S(2)}) collective-permute-start(bf16[128,462]{0,1:T(8,128)(2,1)S(1)} %fusion.21), channel_id=1, source_target_pairs={{0,480},{32,0},{64,32},{96,64},{128,96},{160,128},{192,160},{224,1... | collective-permute-start | bytes 354824 | tf_op jit(solution)/shard_map/ppermute | solution.py:74
  106.8 1.9 collective-permute-start.3
  108.8 4.6 %collective-permute-start.11 = (bf16[128,462]{0,1:T(8,128)(2,1)S(1)}, bf16[128,462]{0,1:T(8,128)(2,1)S(1)}, u32[]{:S(2)}, u32[]{:S(2)}) collective-permute-start(bf16[128,462]{0,1:T(8,128)(2,1)S(1)} %fusion.20), channel_id=1, source_target_pairs={{0,480},{32,0},{64,32},{96,64},{128,96},{160,128},{192,160},{224,1... | collective-permute-start | bytes 354824 | tf_op jit(solution)/shard_map/ppermute | solution.py:74
  113.6 1.9 collective-permute-start.4
  115.6 4.6 %collective-permute-start.12 = (bf16[128,462]{0,1:T(8,128)(2,1)S(1)}, bf16[128,462]{0,1:T(8,128)(2,1)S(1)}, u32[]{:S(2)}, u32[]{:S(2)}) collective-permute-start(bf16[128,462]{0,1:T(8,128)(2,1)S(1)} %fusion.19), channel_id=1, source_target_pairs={{0,480},{32,0},{64,32},{96,64},{128,96},{160,128},{192,160},{224,1... | collective-permute-start | bytes 354824 | tf_op jit(solution)/shard_map/ppermute | solution.py:74
  120.5 1.9 collective-permute-start.5
  122.4 4.6 %collective-permute-start.13 = (bf16[128,462]{0,1:T(8,128)(2,1)S(1)}, bf16[128,462]{0,1:T(8,128)(2,1)S(1)}, u32[]{:S(2)}, u32[]{:S(2)}) collective-permute-start(bf16[128,462]{0,1:T(8,128)(2,1)S(1)} %fusion.18), channel_id=1, source_target_pairs={{0,480},{32,0},{64,32},{96,64},{128,96},{160,128},{192,160},{224,1... | collective-permute-start | bytes 354824 | tf_op jit(solution)/shard_map/ppermute | solution.py:74
  127.3 1.9 collective-permute-start.6
  129.3 4.6 %collective-permute-start.14 = (bf16[128,462]{0,1:T(8,128)(2,1)S(1)}, bf16[128,462]{0,1:T(8,128)(2,1)S(1)}, u32[]{:S(2)}, u32[]{:S(2)}) collective-permute-start(bf16[128,462]{0,1:T(8,128)(2,1)S(1)} %fusion.17), channel_id=1, source_target_pairs={{0,480},{32,0},{64,32},{96,64},{128,96},{160,128},{192,160},{224,1... | collective-permute-start | bytes 354824 | tf_op jit(solution)/shard_map/ppermute | solution.py:74
  134.5 1.9 collective-permute-start.7
  136.4 6.2 %collective-permute-done.7 = bf16[128,462]{0,1:T(8,128)(2,1)S(1)} collective-permute-done((bf16[128,462]{0,1:T(8,128)(2,1)S(1)}, bf16[128,462]{0,1:T(8,128)(2,1)S(1)}, u32[]{:S(2)}, u32[]{:S(2)}) %collective-permute-start.7) | collective-permute-done | bytes 118304 | tf_op jit(solution)/shard_map/ppermute | solution.py:70
  142.8 1.9 collective-permute-start.15
  144.8 8.7 %collective-permute-done.15 = bf16[128,3,462]{0,2,1:T(8,128)(2,1)S(1)} collective-permute-done((bf16[128,3,462]{0,2,1:T(8,128)(2,1)S(1)}, bf16[128,3,462]{0,2,1:T(8,128)(2,1)S(1)}, u32[]{:S(2)}, u32[]{:S(2)}) %collective-permute-start.15) | collective-permute-done | bytes 354848 | tf_op jit(solution)/shard_map/ppermute | solution.py:47
  155.4 4.6 %collective-permute-start.23 = (bf16[128,3,462]{0,2,1:T(8,128)(2,1)S(1)}, bf16[128,3,462]{0,2,1:T(8,128)(2,1)S(1)}, u32[]{:S(2)}, u32[]{:S(2)}) collective-permute-start(bf16[128,3,462]{0,2,1:T(8,128)(2,1)S(1)} %pad_maximum_fusion), channel_id=1, source_target_pairs={{0,480},{32,0},{64,32},{96,64},{128,96},{160,128},{192,160},{224,1... | collective-permute-start | bytes 1064456 | tf_op jit(solution)/shard_map/ppermute | solution.py:50
  159.9 6.4 %collective-permute-done.16 = bf16[128,3,462]{0,2,1:T(8,128)(2,1)S(1)} collective-permute-done((bf16[128,3,462]{0,2,1:T(8,128)(2,1)S(1)}, bf16[128,3,462]{0,2,1:T(8,128)(2,1)S(1)}, u32[]{:S(2)}, u32[]{:S(2)}) %collective-permute-start.16) | collective-permute-done | bytes 354848 | tf_op jit(solution)/shard_map/ppermute | solution.py:47
  166.4 1.9 collective-permute-start.17
  168.3 4.6 %collective-permute-start.24 = (bf16[128,3,462]{0,2,1:T(8,128)(2,1)S(1)}, bf16[128,3,462]{0,2,1:T(8,128)(2,1)S(1)}, u32[]{:S(2)}, u32[]{:S(2)}) collective-permute-start(bf16[128,3,462]{0,2,1:T(8,128)(2,1)S(1)} %collective-permute-done.23), channel_id=1, source_target_pairs={{0,480},{32,0},{64,32},{96,64},{128,96},{160,128},{192,160},{224,1... | collective-permute-start | bytes 1064456 | tf_op jit(solution)/shard_map/ppermute | solution.py:50
  172.9 6.1 %collective-permute-done.17 = bf16[128,3,462]{0,2,1:T(8,128)(2,1)S(1)} collective-permute-done((bf16[128,3,462]{0,2,1:T(8,128)(2,1)S(1)}, bf16[128,3,462]{0,2,1:T(8,128)(2,1)S(1)}, u32[]{:S(2)}, u32[]{:S(2)}) %collective-permute-start.17) | collective-permute-done | bytes 354848 | tf_op jit(solution)/shard_map/ppermute | solution.py:47
  180.9 4.6 %collective-permute-start.25 = (bf16[128,3,462]{0,2,1:T(8,128)(2,1)S(1)}, bf16[128,3,462]{0,2,1:T(8,128)(2,1)S(1)}, u32[]{:S(2)}, u32[]{:S(2)}) collective-permute-start(bf16[128,3,462]{0,2,1:T(8,128)(2,1)S(1)} %collective-permute-done.24), channel_id=1, source_target_pairs={{0,480},{32,0},{64,32},{96,64},{128,96},{160,128},{192,160},{224,1... | collective-permute-start | bytes 1064456 | tf_op jit(solution)/shard_map/ppermute | solution.py:50
  185.5 5.2 %collective-permute-done.18 = bf16[128,3,462]{0,2,1:T(8,128)(2,1)S(1)} collective-permute-done((bf16[128,3,462]{0,2,1:T(8,128)(2,1)S(1)}, bf16[128,3,462]{0,2,1:T(8,128)(2,1)S(1)}, u32[]{:S(2)}, u32[]{:S(2)}) %collective-permute-start.18) | collective-permute-done | bytes 354848 | tf_op jit(solution)/shard_map/ppermute | solution.py:47
  192.6 4.6 %collective-permute-start.26 = (bf16[128,3,462]{0,2,1:T(8,128)(2,1)S(1)}, bf16[128,3,462]{0,2,1:T(8,128)(2,1)S(1)}, u32[]{:S(2)}, u32[]{:S(2)}) collective-permute-start(bf16[128,3,462]{0,2,1:T(8,128)(2,1)S(1)} %collective-permute-done.25), channel_id=1, source_target_pairs={{0,480},{32,0},{64,32},{96,64},{128,96},{160,128},{192,160},{224,1... | collective-permute-start | bytes 1064456 | tf_op jit(solution)/shard_map/ppermute | solution.py:50
  197.2 4.4 %collective-permute-done.19 = bf16[128,3,462]{0,2,1:T(8,128)(2,1)S(1)} collective-permute-done((bf16[128,3,462]{0,2,1:T(8,128)(2,1)S(1)}, bf16[128,3,462]{0,2,1:T(8,128)(2,1)S(1)}, u32[]{:S(2)}, u32[]{:S(2)}) %collective-permute-start.19) | collective-permute-done | bytes 354848 | tf_op jit(solution)/shard_map/ppermute | solution.py:47
  201.6 1.9 collective-permute-start.20
  203.5 4.6 %collective-permute-start.27 = (bf16[128,3,462]{0,2,1:T(8,128)(2,1)S(1)}, bf16[128,3,462]{0,2,1:T(8,128)(2,1)}, u32[]{:S(2)}, u32[]{:S(2)}) collective-permute-start(bf16[128,3,462]{0,2,1:T(8,128)(2,1)S(1)} %collective-permute-done.26), channel_id=1, source_target_pairs={{0,480},{32,0},{64,32},{96,64},{128,96},{160,128},{192,160},{224,1... | collective-permute-start | bytes 1064456 | tf_op jit(solution)/shard_map/ppermute | solution.py:50
  208.1 3.5 collective-permute-done.20
  211.6 1.9 collective-permute-start.21
  213.6 4.6 %collective-permute-start.28 = (bf16[128,3,462]{0,2,1:T(8,128)(2,1)}, bf16[128,3,462]{0,2,1:T(8,128)(2,1)S(1)}, u32[]{:S(2)}, u32[]{:S(2)}) collective-permute-start(bf16[128,3,462]{0,2,1:T(8,128)(2,1)} %collective-permute-done.27), channel_id=1, source_target_pairs={{0,480},{32,0},{64,32},{96,64},{128,96},{160,128},{192,160},{224,1... | collective-permute-start | bytes 1064456 | tf_op jit(solution)/shard_map/ppermute | solution.py:50
  218.2 3.0 collective-permute-done.21
  223.3 4.7 %collective-permute-start.29 = (bf16[128,3,462]{0,2,1:T(8,128)(2,1)S(1)}, bf16[128,3,462]{0,2,1:T(8,128)(2,1)S(1)}, u32[]{:S(2)}, u32[]{:S(2)}) collective-permute-start(bf16[128,3,462]{0,2,1:T(8,128)(2,1)S(1)} %collective-permute-done.28), channel_id=1, source_target_pairs={{0,480},{32,0},{64,32},{96,64},{128,96},{160,128},{192,160},{224,1... | collective-permute-start | bytes 1064456 | tf_op jit(solution)/shard_map/ppermute | solution.py:50
  228.0 2.8 collective-permute-done.22
  248.1 6.4 %gather_fusion = bf16[16,128,3,462]{1,3,2,0:T(8,128)(2,1)} fusion(bf16[16,128,3,462]{1,3,2,0:T(8,128)(2,1)} %bitcast_dynamic-update-slice_fusion, s32[1024]{0:T(1024)S(1)} %pad_clamp_fusion), kind=kCustom, calls=%fused_computation | custom fusion | bytes 11354176 | tf_op jit(solution)/shard_map/jit(_take)/gather | solution.py:53
  254.4 6.5 %copy.41 = bf16[16,128,3,462]{1,0,3,2:T(8,128)(2,1)} copy(bf16[16,128,3,462]{1,3,2,0:T(8,128)(2,1)} %gather_fusion) | data formatting | bytes 11354112 | tf_op jit(solution)/shard_map/jit(_take)/gather | solution.py:53
  261.0 7.3 %gather.7 = bf16[2048,3,462]{0,2,1:T(8,128)(2,1)} reshape(bf16[16,128,3,462]{1,0,3,2:T(8,128)(2,1)} %copy.41) | data formatting | bytes 11354112 | tf_op jit(solution)/shard_map/jit(_take)/gather | solution.py:53
  268.3 3.2 broadcast_select_fusion
  274.0 2.7 add_convert_fusion
  276.7 3.5 fusion.6
  280.2 5.5 %all-gather.5.cloned.1.call-done = bf16[2048,512]{1,0:T(8,128)(2,1)} async-done(((bf16[64,512]{1,0:T(8,128)(2,1)}), bf16[2048,512]{1,0:T(8,128)(2,1)}) %all-gather.5.cloned.1.call-update) | async-done | bytes 2097168 | tf_op jit(solution)/shard_map/all_gather | solution.py:83
  285.7 4.2 %fusion.7 = bf16[512,462]{0,1:T(8,128)(2,1)} fusion(bf16[2048,512]{1,0:T(8,128)(2,1)} %all-gather.5.cloned.1.call-done, bf16[2048,3,462]{0,2,1:T(8,128)(2,1)} %copy-done.1), kind=kOutput, calls=%fused_computation.15 | convolution fusion | flops 969120768 | bytes 4470784 | tf_op jit(solution)/shard_map/dot_general | solution.py:8
  289.9 3.5 fusion.8
  293.3 98.5 %reduce-scatter.2.cloned.1.call-done = bf16[64,512]{1,0:T(8,128)(2,1)} async-done(((bf16[2048,512]{1,0:T(8,128)(2,1)}), bf16[64,512]{1,0:T(8,128)(2,1)}) %reduce-scatter.2.cloned.1.call-update) | async-done | bytes 65552 | tf_op jit(solution)/shard_map/reduce_scatter | solution.py:95
  (89 shorter events, 33.1 us)
Async XLA Ops:
  7.2 264.3 %copy-start = (bf16[512,462]{0,1:T(8,128)(2,1)S(1)}, bf16[512,462]{0,1:T(8,128)(2,1)}, u32[]{:S(2)}) copy-start(bf16[512,462]{0,1:T(8,128)(2,1)} %param.10) | copy-start | bytes 1419268
  7.2 68.5 %all-gather.3.cloned.1.call-start = ((), (), s32[]{:S(2)}) async-start(), calls=%async_computation.1 | async-start | bytes 2162688 | tf_op jit(solution)/shard_map/all_gather | solution.py:82
  7.9 277.7 %all-gather.5.cloned.1.call-start = ((), (), s32[]{:S(2)}) async-start(), calls=%async_computation.3 | async-start | bytes 2162688 | tf_op jit(solution)/shard_map/all_gather | solution.py:83
  79.4 63.2 %copy-start.5 = (bf16[128,462]{0,1:T(8,128)(2,1)S(1)}, bf16[128,462]{0,1:T(8,128)(2,1)}, u32[]{:S(2)}) copy-start(bf16[128,462]{0,1:T(8,128)(2,1)} %param.8) | copy-start | bytes 354820
  79.5 63.1 %copy-start.6 = (bf16[128,462]{0,1:T(8,128)(2,1)S(1)}, bf16[128,462]{0,1:T(8,128)(2,1)}, u32[]{:S(2)}) copy-start(bf16[128,462]{0,1:T(8,128)(2,1)} %param.9) | copy-start | bytes 354820
  84.1 9.0 %collective-permute-start = (bf16[128,462]{0,1:T(8,128)(2,1)S(1)}, bf16[128,462]{0,1:T(8,128)(2,1)S(1)}, u32[]{:S(2)}, u32[]{:S(2)}) collective-permute-start(bf16[128,462]{0,1:T(8,128)(2,1)S(1)} %bitcast.165), channel_id=1, source_target_pairs={{0,32},{32,64},{64,96},{96,128},{128,160},{160,192},{192,224},{224... | collective-permute-start | bytes 354824 | tf_op jit(solution)/shard_map/ppermute | solution.py:70
  87.3 7.7 %collective-permute-start.8 = (bf16[128,462]{0,1:T(8,128)(2,1)S(1)}, bf16[128,462]{0,1:T(8,128)(2,1)S(1)}, u32[]{:S(2)}, u32[]{:S(2)}) collective-permute-start(bf16[128,462]{0,1:T(8,128)(2,1)S(1)} %bitcast.164), channel_id=1, source_target_pairs={{0,480},{32,0},{64,32},{96,64},{128,96},{160,128},{192,160},{224,1... | collective-permute-start | bytes 354824 | tf_op jit(solution)/shard_map/ppermute | solution.py:74
  93.2 6.8 %collective-permute-start.1 = (bf16[128,462]{0,1:T(8,128)(2,1)S(1)}, bf16[128,462]{0,1:T(8,128)(2,1)S(1)}, u32[]{:S(2)}, u32[]{:S(2)}) collective-permute-start(bf16[128,462]{0,1:T(8,128)(2,1)S(1)} %fusion.29), channel_id=1, source_target_pairs={{0,32},{32,64},{64,96},{96,128},{128,160},{160,192},{192,224},{224... | collective-permute-start | bytes 354824 | tf_op jit(solution)/shard_map/ppermute | solution.py:70
  95.1 6.8 %collective-permute-start.9 = (bf16[128,462]{0,1:T(8,128)(2,1)S(1)}, bf16[128,462]{0,1:T(8,128)(2,1)S(1)}, u32[]{:S(2)}, u32[]{:S(2)}) collective-permute-start(bf16[128,462]{0,1:T(8,128)(2,1)S(1)} %fusion.22), channel_id=1, source_target_pairs={{0,480},{32,0},{64,32},{96,64},{128,96},{160,128},{192,160},{224,1... | collective-permute-start | bytes 354824 | tf_op jit(solution)/shard_map/ppermute | solution.py:74
  100.0 6.8 %collective-permute-start.2 = (bf16[128,462]{0,1:T(8,128)(2,1)S(1)}, bf16[128,462]{0,1:T(8,128)(2,1)S(1)}, u32[]{:S(2)}, u32[]{:S(2)}) collective-permute-start(bf16[128,462]{0,1:T(8,128)(2,1)S(1)} %fusion.28), channel_id=1, source_target_pairs={{0,32},{32,64},{64,96},{96,128},{128,160},{160,192},{192,224},{224... | collective-permute-start | bytes 354824 | tf_op jit(solution)/shard_map/ppermute | solution.py:70
  102.0 6.8 %collective-permute-start.10 = (bf16[128,462]{0,1:T(8,128)(2,1)S(1)}, bf16[128,462]{0,1:T(8,128)(2,1)S(1)}, u32[]{:S(2)}, u32[]{:S(2)}) collective-permute-start(bf16[128,462]{0,1:T(8,128)(2,1)S(1)} %fusion.21), channel_id=1, source_target_pairs={{0,480},{32,0},{64,32},{96,64},{128,96},{160,128},{192,160},{224,1... | collective-permute-start | bytes 354824 | tf_op jit(solution)/shard_map/ppermute | solution.py:74
  106.8 6.8 %collective-permute-start.3 = (bf16[128,462]{0,1:T(8,128)(2,1)S(1)}, bf16[128,462]{0,1:T(8,128)(2,1)S(1)}, u32[]{:S(2)}, u32[]{:S(2)}) collective-permute-start(bf16[128,462]{0,1:T(8,128)(2,1)S(1)} %fusion.27), channel_id=1, source_target_pairs={{0,32},{32,64},{64,96},{96,128},{128,160},{160,192},{192,224},{224... | collective-permute-start | bytes 354824 | tf_op jit(solution)/shard_map/ppermute | solution.py:70
  108.8 6.8 %collective-permute-start.11 = (bf16[128,462]{0,1:T(8,128)(2,1)S(1)}, bf16[128,462]{0,1:T(8,128)(2,1)S(1)}, u32[]{:S(2)}, u32[]{:S(2)}) collective-permute-start(bf16[128,462]{0,1:T(8,128)(2,1)S(1)} %fusion.20), channel_id=1, source_target_pairs={{0,480},{32,0},{64,32},{96,64},{128,96},{160,128},{192,160},{224,1... | collective-permute-start | bytes 354824 | tf_op jit(solution)/shard_map/ppermute | solution.py:74
  113.6 6.8 %collective-permute-start.4 = (bf16[128,462]{0,1:T(8,128)(2,1)S(1)}, bf16[128,462]{0,1:T(8,128)(2,1)S(1)}, u32[]{:S(2)}, u32[]{:S(2)}) collective-permute-start(bf16[128,462]{0,1:T(8,128)(2,1)S(1)} %fusion.26), channel_id=1, source_target_pairs={{0,32},{32,64},{64,96},{96,128},{128,160},{160,192},{192,224},{224... | collective-permute-start | bytes 354824 | tf_op jit(solution)/shard_map/ppermute | solution.py:70
  115.6 6.8 %collective-permute-start.12 = (bf16[128,462]{0,1:T(8,128)(2,1)S(1)}, bf16[128,462]{0,1:T(8,128)(2,1)S(1)}, u32[]{:S(2)}, u32[]{:S(2)}) collective-permute-start(bf16[128,462]{0,1:T(8,128)(2,1)S(1)} %fusion.19), channel_id=1, source_target_pairs={{0,480},{32,0},{64,32},{96,64},{128,96},{160,128},{192,160},{224,1... | collective-permute-start | bytes 354824 | tf_op jit(solution)/shard_map/ppermute | solution.py:74
  120.5 6.8 %collective-permute-start.5 = (bf16[128,462]{0,1:T(8,128)(2,1)S(1)}, bf16[128,462]{0,1:T(8,128)(2,1)S(1)}, u32[]{:S(2)}, u32[]{:S(2)}) collective-permute-start(bf16[128,462]{0,1:T(8,128)(2,1)S(1)} %fusion.25), channel_id=1, source_target_pairs={{0,32},{32,64},{64,96},{96,128},{128,160},{160,192},{192,224},{224... | collective-permute-start | bytes 354824 | tf_op jit(solution)/shard_map/ppermute | solution.py:70
  122.4 6.8 %collective-permute-start.13 = (bf16[128,462]{0,1:T(8,128)(2,1)S(1)}, bf16[128,462]{0,1:T(8,128)(2,1)S(1)}, u32[]{:S(2)}, u32[]{:S(2)}) collective-permute-start(bf16[128,462]{0,1:T(8,128)(2,1)S(1)} %fusion.18), channel_id=1, source_target_pairs={{0,480},{32,0},{64,32},{96,64},{128,96},{160,128},{192,160},{224,1... | collective-permute-start | bytes 354824 | tf_op jit(solution)/shard_map/ppermute | solution.py:74
  127.3 7.2 %collective-permute-start.6 = (bf16[128,462]{0,1:T(8,128)(2,1)S(1)}, bf16[128,462]{0,1:T(8,128)(2,1)S(1)}, u32[]{:S(2)}, u32[]{:S(2)}) collective-permute-start(bf16[128,462]{0,1:T(8,128)(2,1)S(1)} %fusion.24), channel_id=1, source_target_pairs={{0,32},{32,64},{64,96},{96,128},{128,160},{160,192},{192,224},{224... | collective-permute-start | bytes 354824 | tf_op jit(solution)/shard_map/ppermute | solution.py:70
  129.3 7.2 %collective-permute-start.14 = (bf16[128,462]{0,1:T(8,128)(2,1)S(1)}, bf16[128,462]{0,1:T(8,128)(2,1)S(1)}, u32[]{:S(2)}, u32[]{:S(2)}) collective-permute-start(bf16[128,462]{0,1:T(8,128)(2,1)S(1)} %fusion.17), channel_id=1, source_target_pairs={{0,480},{32,0},{64,32},{96,64},{128,96},{160,128},{192,160},{224,1... | collective-permute-start | bytes 354824 | tf_op jit(solution)/shard_map/ppermute | solution.py:74
  134.5 8.1 %collective-permute-start.7 = (bf16[128,462]{0,1:T(8,128)(2,1)S(1)}, bf16[128,462]{0,1:T(8,128)(2,1)S(1)}, u32[]{:S(2)}, u32[]{:S(2)}) collective-permute-start(bf16[128,462]{0,1:T(8,128)(2,1)S(1)} %fusion.23), channel_id=1, source_target_pairs={{0,32},{32,64},{64,96},{96,128},{128,160},{160,192},{192,224},{224... | collective-permute-start | bytes 354824 | tf_op jit(solution)/shard_map/ppermute | solution.py:70
  142.8 10.6 %collective-permute-start.15 = (bf16[128,3,462]{0,2,1:T(8,128)(2,1)S(1)}, bf16[128,3,462]{0,2,1:T(8,128)(2,1)S(1)}, u32[]{:S(2)}, u32[]{:S(2)}) collective-permute-start(bf16[128,3,462]{0,2,1:T(8,128)(2,1)S(1)} %pad_maximum_fusion), channel_id=1, source_target_pairs={{0,32},{32,64},{64,96},{96,128},{128,160},{160,192},{192,224},{224... | collective-permute-start | bytes 1064456 | tf_op jit(solution)/shard_map/ppermute | solution.py:47
  153.4 12.9 %collective-permute-start.16 = (bf16[128,3,462]{0,2,1:T(8,128)(2,1)S(1)}, bf16[128,3,462]{0,2,1:T(8,128)(2,1)S(1)}, u32[]{:S(2)}, u32[]{:S(2)}) collective-permute-start(bf16[128,3,462]{0,2,1:T(8,128)(2,1)S(1)} %collective-permute-done.15), channel_id=1, source_target_pairs={{0,32},{32,64},{64,96},{96,128},{128,160},{160,192},{192,224},{224... | collective-permute-start | bytes 1064456 | tf_op jit(solution)/shard_map/ppermute | solution.py:47
  155.4 12.9 %collective-permute-start.23 = (bf16[128,3,462]{0,2,1:T(8,128)(2,1)S(1)}, bf16[128,3,462]{0,2,1:T(8,128)(2,1)S(1)}, u32[]{:S(2)}, u32[]{:S(2)}) collective-permute-start(bf16[128,3,462]{0,2,1:T(8,128)(2,1)S(1)} %pad_maximum_fusion), channel_id=1, source_target_pairs={{0,480},{32,0},{64,32},{96,64},{128,96},{160,128},{192,160},{224,1... | collective-permute-start | bytes 1064456 | tf_op jit(solution)/shard_map/ppermute | solution.py:50
  166.4 12.6 %collective-permute-start.17 = (bf16[128,3,462]{0,2,1:T(8,128)(2,1)S(1)}, bf16[128,3,462]{0,2,1:T(8,128)(2,1)S(1)}, u32[]{:S(2)}, u32[]{:S(2)}) collective-permute-start(bf16[128,3,462]{0,2,1:T(8,128)(2,1)S(1)} %collective-permute-done.16), channel_id=1, source_target_pairs={{0,32},{32,64},{64,96},{96,128},{128,160},{160,192},{192,224},{224... | collective-permute-start | bytes 1064456 | tf_op jit(solution)/shard_map/ppermute | solution.py:47
  168.3 12.6 %collective-permute-start.24 = (bf16[128,3,462]{0,2,1:T(8,128)(2,1)S(1)}, bf16[128,3,462]{0,2,1:T(8,128)(2,1)S(1)}, u32[]{:S(2)}, u32[]{:S(2)}) collective-permute-start(bf16[128,3,462]{0,2,1:T(8,128)(2,1)S(1)} %collective-permute-done.23), channel_id=1, source_target_pairs={{0,480},{32,0},{64,32},{96,64},{128,96},{160,128},{192,160},{224,1... | collective-permute-start | bytes 1064456 | tf_op jit(solution)/shard_map/ppermute | solution.py:50
  179.0 11.7 %collective-permute-start.18 = (bf16[128,3,462]{0,2,1:T(8,128)(2,1)S(1)}, bf16[128,3,462]{0,2,1:T(8,128)(2,1)S(1)}, u32[]{:S(2)}, u32[]{:S(2)}) collective-permute-start(bf16[128,3,462]{0,2,1:T(8,128)(2,1)S(1)} %collective-permute-done.17), channel_id=1, source_target_pairs={{0,32},{32,64},{64,96},{96,128},{128,160},{160,192},{192,224},{224... | collective-permute-start | bytes 1064456 | tf_op jit(solution)/shard_map/ppermute | solution.py:47
  180.9 11.7 %collective-permute-start.25 = (bf16[128,3,462]{0,2,1:T(8,128)(2,1)S(1)}, bf16[128,3,462]{0,2,1:T(8,128)(2,1)S(1)}, u32[]{:S(2)}, u32[]{:S(2)}) collective-permute-start(bf16[128,3,462]{0,2,1:T(8,128)(2,1)S(1)} %collective-permute-done.24), channel_id=1, source_target_pairs={{0,480},{32,0},{64,32},{96,64},{128,96},{160,128},{192,160},{224,1... | collective-permute-start | bytes 1064456 | tf_op jit(solution)/shard_map/ppermute | solution.py:50
  190.7 12.8 %copy-start.3 = (bf16[128,3,462]{0,2,1:T(8,128)(2,1)}, bf16[128,3,462]{0,2,1:T(8,128)(2,1)S(1)}, u32[]{:S(2)}) copy-start(bf16[128,3,462]{0,2,1:T(8,128)(2,1)S(1)} %collective-permute-done.18) | copy-start | bytes 1064452
  190.7 10.9 %collective-permute-start.19 = (bf16[128,3,462]{0,2,1:T(8,128)(2,1)S(1)}, bf16[128,3,462]{0,2,1:T(8,128)(2,1)S(1)}, u32[]{:S(2)}, u32[]{:S(2)}) collective-permute-start(bf16[128,3,462]{0,2,1:T(8,128)(2,1)S(1)} %collective-permute-done.18), channel_id=1, source_target_pairs={{0,32},{32,64},{64,96},{96,128},{128,160},{160,192},{192,224},{224... | collective-permute-start | bytes 1064456 | tf_op jit(solution)/shard_map/ppermute | solution.py:47
  192.6 10.9 %collective-permute-start.26 = (bf16[128,3,462]{0,2,1:T(8,128)(2,1)S(1)}, bf16[128,3,462]{0,2,1:T(8,128)(2,1)S(1)}, u32[]{:S(2)}, u32[]{:S(2)}) collective-permute-start(bf16[128,3,462]{0,2,1:T(8,128)(2,1)S(1)} %collective-permute-done.25), channel_id=1, source_target_pairs={{0,480},{32,0},{64,32},{96,64},{128,96},{160,128},{192,160},{224,1... | collective-permute-start | bytes 1064456 | tf_op jit(solution)/shard_map/ppermute | solution.py:50
  201.6 6.5 %copy-start.4 = (bf16[128,3,462]{0,2,1:T(8,128)(2,1)}, bf16[128,3,462]{0,2,1:T(8,128)(2,1)S(1)}, u32[]{:S(2)}) copy-start(bf16[128,3,462]{0,2,1:T(8,128)(2,1)S(1)} %collective-permute-done.19) | copy-start | bytes 1064452
  201.6 10.0 %collective-permute-start.20 = (bf16[128,3,462]{0,2,1:T(8,128)(2,1)S(1)}, bf16[128,3,462]{0,2,1:T(8,128)(2,1)}, u32[]{:S(2)}, u32[]{:S(2)}) collective-permute-start(bf16[128,3,462]{0,2,1:T(8,128)(2,1)S(1)} %collective-permute-done.19), channel_id=1, source_target_pairs={{0,32},{32,64},{64,96},{96,128},{128,160},{160,192},{192,224},{224... | collective-permute-start | bytes 1064456 | tf_op jit(solution)/shard_map/ppermute | solution.py:47
  203.5 10.1 %collective-permute-start.27 = (bf16[128,3,462]{0,2,1:T(8,128)(2,1)S(1)}, bf16[128,3,462]{0,2,1:T(8,128)(2,1)}, u32[]{:S(2)}, u32[]{:S(2)}) collective-permute-start(bf16[128,3,462]{0,2,1:T(8,128)(2,1)S(1)} %collective-permute-done.26), channel_id=1, source_target_pairs={{0,480},{32,0},{64,32},{96,64},{128,96},{160,128},{192,160},{224,1... | collective-permute-start | bytes 1064456 | tf_op jit(solution)/shard_map/ppermute | solution.py:50
  211.6 9.6 %collective-permute-start.21 = (bf16[128,3,462]{0,2,1:T(8,128)(2,1)}, bf16[128,3,462]{0,2,1:T(8,128)(2,1)}, u32[]{:S(2)}, u32[]{:S(2)}) collective-permute-start(bf16[128,3,462]{0,2,1:T(8,128)(2,1)} %collective-permute-done.20), channel_id=1, source_target_pairs={{0,32},{32,64},{64,96},{96,128},{128,160},{160,192},{192,224},{224... | collective-permute-start | bytes 1064456 | tf_op jit(solution)/shard_map/ppermute | solution.py:47
  213.5 178.3 %reduce-scatter.2.cloned.1.call-start = ((), (), s32[]{:S(2)}) async-start(), calls=%async_computation.2 | async-start | bytes 2162688 | tf_op jit(solution)/shard_map/reduce_scatter | solution.py:95
  213.6 9.6 %collective-permute-start.28 = (bf16[128,3,462]{0,2,1:T(8,128)(2,1)}, bf16[128,3,462]{0,2,1:T(8,128)(2,1)S(1)}, u32[]{:S(2)}, u32[]{:S(2)}) collective-permute-start(bf16[128,3,462]{0,2,1:T(8,128)(2,1)} %collective-permute-done.27), channel_id=1, source_target_pairs={{0,480},{32,0},{64,32},{96,64},{128,96},{160,128},{192,160},{224,1... | collective-permute-start | bytes 1064456 | tf_op jit(solution)/shard_map/ppermute | solution.py:50
  221.2 9.5 %collective-permute-start.22 = (bf16[128,3,462]{0,2,1:T(8,128)(2,1)}, bf16[128,3,462]{0,2,1:T(8,128)(2,1)S(1)}, u32[]{:S(2)}, u32[]{:S(2)}) collective-permute-start(bf16[128,3,462]{0,2,1:T(8,128)(2,1)} %collective-permute-done.21), channel_id=1, source_target_pairs={{0,32},{32,64},{64,96},{96,128},{128,160},{160,192},{192,224},{224... | collective-permute-start | bytes 1064456 | tf_op jit(solution)/shard_map/ppermute | solution.py:47
  223.3 24.0 %collective-permute-start.29 = (bf16[128,3,462]{0,2,1:T(8,128)(2,1)S(1)}, bf16[128,3,462]{0,2,1:T(8,128)(2,1)S(1)}, u32[]{:S(2)}, u32[]{:S(2)}) collective-permute-start(bf16[128,3,462]{0,2,1:T(8,128)(2,1)S(1)} %collective-permute-done.28), channel_id=1, source_target_pairs={{0,480},{32,0},{64,32},{96,64},{128,96},{160,128},{192,160},{224,1... | collective-permute-start | bytes 1064456 | tf_op jit(solution)/shard_map/ppermute | solution.py:50
  271.5 2.5 copy-start.1
  271.5 2.5 copy-start.2
  274.0 2.8 copy-start.7
  285.7 4.2 %copy-start.8 = (bf16[2048,512]{1,0:T(8,128)(2,1)S(1)}, bf16[2048,512]{1,0:T(8,128)(2,1)}, u32[]{:S(2)}) copy-start(bf16[2048,512]{1,0:T(8,128)(2,1)} %all-gather.5.cloned.1.call-done) | copy-start | bytes 6291460
Sparse Core Ops, SparseCore 0:
  11.1 64.5 all-gather.2
  213.6 71.9 all-gather.4
  290.7 101.1 reduce-scatter.1

commit v3 on v2

--- a/solution.py
+++ b/solution.py
@@ -49,13 +49,14 @@
         if s <= n_down:
             b = lax.ppermute(b, axis, down)
             held[s] = b
-    ring_order = jnp.stack([held[d] for d in range(-n_up, n_down + 1)])
-    return jnp.take(ring_order, (jnp.arange(n) - me + n_up) % n, axis=0)
+    ring_order = jnp.stack([held[d] for d in range(-n_up, n_down + 1)], axis=1)
+    return jnp.take(ring_order, (jnp.arange(n) - me + n_up) % n, axis=1)
 
 
-def ring_reduce_scatter(parts, axis, n, wire_dtype):
-    me = lax.axis_index(axis)
-    up, down = _shifts(n)
+def ring_reduce_scatter(parts, axis, n, wire_dtype, me=None, up=None, down=None):
+    if me is None:
+        me = lax.axis_index(axis)
+        up, down = _shifts(n)
     n_up = n // 2
     n_down = n - 1 - n_up
 
@@ -77,35 +78,75 @@
     return block(me) + a + b
 
 
-def shards(inputs, gate_pre, up_pre, w_gate, w_up, w_down, grad_out, n_row):
+def col_reduce_scatter(blocks, n_x, n_y):
+    n_col = 2 * n_x * n_y
+    c = lax.axis_index("col")
+    core = c % 2
+    x = (c // 2) % n_x
+    y = c // (2 * n_x)
+    m = blocks.shape[1] // 2
+    halves = blocks.reshape((n_y * n_x, 2, m) + blocks.shape[2:]).astype(jnp.float32)
+    keep = lax.dynamic_index_in_dim(halves, core, 1, keepdims=False)
+    give = lax.dynamic_index_in_dim(halves, 1 - core, 1, keepdims=False)
+    pair = [(j, j ^ 1) for j in range(n_col)]
+    summed = keep + lax.ppermute(give, "col", pair)
+
+    def idx(yy, xx, cc):
+        return (yy * n_x + xx) * 2 + cc
+
+    def ring(step, size, coord):
+        pairs = []
+        for yy in range(n_y):
+            for xx in range(n_x):
+                for cc in range(2):
+                    if coord == "x":
+                        pairs.append((idx(yy, xx, cc), idx(yy, (xx + step) % size, cc)))
+                    else:
+                        pairs.append((idx(yy, xx, cc), idx((yy + step) % size, xx, cc)))
+        return pairs
+
+    by_x = jnp.swapaxes(summed.reshape((n_y, n_x, m) + blocks.shape[2:]), 0, 1)
+    over_x = ring_reduce_scatter(
+        by_x, "col", n_x, jnp.bfloat16, me=x, up=ring(1, n_x, "x"), down=ring(-1, n_x, "x")
+    )
+    return ring_reduce_scatter(
+        over_x, "col", n_y, jnp.bfloat16, me=y, up=ring(1, n_y, "y"), down=ring(-1, n_y, "y")
+    )
+
+
+def shards(inputs, gate_pre, up_pre, w_gate, w_up, w_down, grad_out, n_row, n_x, n_y):
     tokens_row, hidden_units = gate_pre.shape
     all_grad_out = lax.all_gather(grad_out, "col", axis=0, tiled=True)
     all_inputs = lax.all_gather(inputs, "col", axis=0, tiled=True)
     part = contract_cols(all_grad_out, w_down).astype(jnp.bfloat16)
     part = part.reshape((n_row, tokens_row, hidden_units))
     own_grad = ring_reduce_scatter(part, "row", n_row, jnp.bfloat16)
-    own = jnp.stack(pointwise(gate_pre, up_pre, own_grad), axis=1)
+    own = jnp.stack(pointwise(gate_pre, up_pre, own_grad), axis=0)
     gathered = ring_all_gather(own, "row", n_row).reshape(
-        (n_row * tokens_row, 3, hidden_units)
+        (3, n_row * tokens_row, hidden_units)
     )
-    hidden, gate_grad, up_grad = gathered[:, 0], gathered[:, 1], gathered[:, 2]
+    hidden, gate_grad, up_grad = gathered[0], gathered[1], gathered[2]
     grad_down = contract_rows(hidden, all_grad_out).astype(jnp.bfloat16)
     grad_gate = contract_rows(all_inputs, gate_grad).astype(jnp.bfloat16)
     grad_up = contract_rows(all_inputs, up_grad).astype(jnp.bfloat16)
-    grad_in = lax.psum_scatter(
-        (contract_cols(gate_grad, w_gate) + contract_cols(up_grad, w_up)).astype(jnp.bfloat16),
-        "col",
-        scatter_dimension=0,
-        tiled=True,
-    )
+    grad_in_terms = (
+        contract_cols(gate_grad, w_gate) + contract_cols(up_grad, w_up)
+    ).astype(jnp.bfloat16)
+    grad_in_terms = grad_in_terms.reshape((n_y * n_x, -1, grad_in_terms.shape[1]))
+    grad_in = col_reduce_scatter(grad_in_terms, n_x, n_y).astype(jnp.bfloat16)
     return (grad_in, grad_gate, grad_up, grad_down)
 
 
 def solution(mesh):
     n_row = mesh.shape["row"]
+    try:
+        n_x = len({d.coords[0] for d in mesh.devices.flat})
+    except AttributeError:
+        n_x = int(round((mesh.shape["col"] // 2) ** 0.5))
+    n_y = mesh.shape["col"] // (2 * n_x)
 
     def body(*args):
-        return shards(*args, n_row=n_row)
+        return shards(*args, n_row=n_row, n_x=n_x, n_y=n_y)
 
     return jax.shard_map(
         body,

time: 400 us -> 346 us (0.86)
  waiting for transfers between devices: 222 us -> 131 us
  starting transfers between devices: 96.1 us -> 133 us
  other arithmetic: 4.62 us -> 11.7 us
  matrix products: 18 us -> 13.6 us
    reduce_scatter x1 -> x0, waiting for transfers between devices: 98.5 us -> none  [shards(): lax.psum_scatter((contract_cols(gate_grad, w_gate) + contract_cols(up_gra...]
    ppermute x0 -> x1, starting transfers between devices: none -> 18.5 us  [col_reduce_scatter(): summed = keep + lax.ppermute(give, 'col', pair)]
    gather x3 -> x1, local copies, waits for them, and re-layouts: 20.2 us -> 6.31 us  [ring_all_gather(): return jnp.take(ring_order, (jnp.arange(n) - me + n_up) % n, axis=1)]
    ppermute x8 -> x12, starting transfers between devices: 16.6 us -> 26.2 us  [ring_reduce_scatter(): a = lax.ppermute(a.astype(wire_dtype), axis, up).astype(jnp.float32)]
    ppermute x8 -> x12, waiting for transfers between devices: 9.31 us -> 18.4 us  [ring_reduce_scatter(): a = lax.ppermute(a.astype(wire_dtype), axis, up).astype(jnp.float32)]
    ppermute x7 -> x9, starting transfers between devices: 31.8 us -> 40.4 us  [ring_reduce_scatter(): b = lax.ppermute(b.astype(wire_dtype), axis, down).astype(jnp.float32)]
    unnamed x35 -> x52, local copies, waits for them, and re-layouts: 17.5 us -> 25.4 us
    all_gather x1, waiting for transfers between devices: 5.46 us -> 0.02 us  [shards(): all_inputs = lax.all_gather(inputs, 'col', axis=0, tiled=True)]
  transfers between devices with their start and end apart: 33 -> 39, of which waited for: 19 -> 21; matrix products, arithmetic and copies ran while one was open for 14% -> 15% of each run, Pallas kernels for 0% -> 0%
where the time goes in v3:
time: 346 us; the launch traced here: 344 us
  starting transfers between devices  133 us (38%)
  waiting for transfers between devices  131 us (38%)
  local copies, waits for them, and re-layouts  39.9 us (12%)
  between operations  15.3 us (4%)
  matrix products  13.6 us (4%)
  other arithmetic  11.7 us (3%)
    all_gather x1, waiting for transfers between devices, shards(): all_grad_out = lax.all_gather(grad_out, 'col', axis=0, tiled=True)  67.5 us
    ppermute x9, starting transfers between devices, ring_reduce_scatter(): b = lax.ppermute(b.astype(wire_dtype), axis, down).astype(jnp.float32)  40.4 us
    ppermute x8, waiting for transfers between devices, ring_all_gather(): a = lax.ppermute(a, axis, up)  39.9 us
    ppermute x7, starting transfers between devices, ring_all_gather(): b = lax.ppermute(b, axis, down)  32.3 us
    ppermute x12, starting transfers between devices, ring_reduce_scatter(): a = lax.ppermute(a.astype(wire_dtype), axis, up).astype(jnp.float32)  26.2 us
    unnamed x52, local copies, waits for them, and re-layouts  25.4 us
    ppermute x1, starting transfers between devices, col_reduce_scatter(): summed = keep + lax.ppermute(give, 'col', pair)  18.5 us
    ppermute x12, waiting for transfers between devices, ring_reduce_scatter(): a = lax.ppermute(a.astype(wire_dtype), axis, up).astype(jnp.float32)  18.4 us
  transfers between devices with their start and end apart: 39, of which 21 were waited for; matrix products, arithmetic and copies ran while one was open for 15% of the time, Pallas kernels for 0%

profile of v3, /device:TPU:1, one launch (start us, length us, event | category | flops | bytes accessed | tf_op | source)
XLA Modules:
  0.0 344.4 jit_solution(6927628350432120359)
XLA Ops:
  8.2 67.5 %all-gather.3.cloned.1.call-done = bf16[2048,512]{1,0:T(8,128)(2,1)} async-done(((bf16[64,512]{1,0:T(8,128)(2,1)}), bf16[2048,512]{1,0:T(8,128)(2,1)}) %all-gather.3.cloned.1.call-update) | async-done | bytes 2097168 | tf_op jit(solution)/shard_map/all_gather | solution.py:119
  75.7 2.8 convolution_convert_fusion
  79.4 4.6 %constant_dynamic-slice_fusion.15 = (bf16[1,128,462]{1,0,2:T(2,128)(2,1)S(1)}, bf16[1,128,462]{1,0,2:T(2,128)(2,1)S(1)}, bf16[1,128,462]{1,0,2:T(2,128)(2,1)S(1)...) fusion(bf16[16,128,462]{1,0,2:T(8,128)(2,1)S(1)} %slice_bitcast, ...), kind=kLoop, calls=%fused_computation.125 | loop fusion | bytes 3784768 | tf_op jit(solution)/shard_map/jit(dynamic_index_in_dim)/dynamic_slice | solution.py:64
  84.1 3.2 collective-permute-start
  87.3 4.4 %collective-permute-start.8 = (bf16[128,462]{0,1:T(8,128)(2,1)S(1)}, bf16[128,462]{0,1:T(8,128)(2,1)S(1)}, u32[]{:S(2)}, u32[]{:S(2)}) collective-permute-start(bf16[128,462]{0,1:T(8,128)(2,1)S(1)} %bitcast.216), channel_id=1, source_target_pairs={{0,480},{32,0},{64,32},{96,64},{128,96},{160,128},{192,160},{224,1... | collective-permute-start | bytes 354824 | tf_op jit(solution)/shard_map/ppermute | solution.py:75
  93.1 1.9 collective-permute-start.1
  95.1 4.7 %collective-permute-start.9 = (bf16[128,462]{0,1:T(8,128)(2,1)S(1)}, bf16[128,462]{0,1:T(8,128)(2,1)S(1)}, u32[]{:S(2)}, u32[]{:S(2)}) collective-permute-start(bf16[128,462]{0,1:T(8,128)(2,1)S(1)} %fusion.19), channel_id=1, source_target_pairs={{0,480},{32,0},{64,32},{96,64},{128,96},{160,128},{192,160},{224,1... | collective-permute-start | bytes 354824 | tf_op jit(solution)/shard_map/ppermute | solution.py:75
  100.0 1.9 collective-permute-start.2
  101.9 4.7 %collective-permute-start.10 = (bf16[128,462]{0,1:T(8,128)(2,1)S(1)}, bf16[128,462]{0,1:T(8,128)(2,1)S(1)}, u32[]{:S(2)}, u32[]{:S(2)}) collective-permute-start(bf16[128,462]{0,1:T(8,128)(2,1)S(1)} %fusion.18), channel_id=1, source_target_pairs={{0,480},{32,0},{64,32},{96,64},{128,96},{160,128},{192,160},{224,1... | collective-permute-start | bytes 354824 | tf_op jit(solution)/shard_map/ppermute | solution.py:75
  106.8 1.9 collective-permute-start.3
  108.8 4.7 %collective-permute-start.11 = (bf16[128,462]{0,1:T(8,128)(2,1)S(1)}, bf16[128,462]{0,1:T(8,128)(2,1)S(1)}, u32[]{:S(2)}, u32[]{:S(2)}) collective-permute-start(bf16[128,462]{0,1:T(8,128)(2,1)S(1)} %fusion.17), channel_id=1, source_target_pairs={{0,480},{32,0},{64,32},{96,64},{128,96},{160,128},{192,160},{224,1... | collective-permute-start | bytes 354824 | tf_op jit(solution)/shard_map/ppermute | solution.py:75
  113.6 1.9 collective-permute-start.4
  115.6 4.7 %collective-permute-start.12 = (bf16[128,462]{0,1:T(8,128)(2,1)S(1)}, bf16[128,462]{0,1:T(8,128)(2,1)S(1)}, u32[]{:S(2)}, u32[]{:S(2)}) collective-permute-start(bf16[128,462]{0,1:T(8,128)(2,1)S(1)} %fusion.16), channel_id=1, source_target_pairs={{0,480},{32,0},{64,32},{96,64},{128,96},{160,128},{192,160},{224,1... | collective-permute-start | bytes 354824 | tf_op jit(solution)/shard_map/ppermute | solution.py:75
  120.5 1.9 collective-permute-start.5
  122.4 4.7 %collective-permute-start.13 = (bf16[128,462]{0,1:T(8,128)(2,1)S(1)}, bf16[128,462]{0,1:T(8,128)(2,1)S(1)}, u32[]{:S(2)}, u32[]{:S(2)}) collective-permute-start(bf16[128,462]{0,1:T(8,128)(2,1)S(1)} %fusion.15), channel_id=1, source_target_pairs={{0,480},{32,0},{64,32},{96,64},{128,96},{160,128},{192,160},{224,1... | collective-permute-start | bytes 354824 | tf_op jit(solution)/shard_map/ppermute | solution.py:75
  127.3 1.9 collective-permute-start.6
  129.3 4.7 %collective-permute-start.14 = (bf16[128,462]{0,1:T(8,128)(2,1)S(1)}, bf16[128,462]{0,1:T(8,128)(2,1)S(1)}, u32[]{:S(2)}, u32[]{:S(2)}) collective-permute-start(bf16[128,462]{0,1:T(8,128)(2,1)S(1)} %fusion.14), channel_id=1, source_target_pairs={{0,480},{32,0},{64,32},{96,64},{128,96},{160,128},{192,160},{224,1... | collective-permute-start | bytes 354824 | tf_op jit(solution)/shard_map/ppermute | solution.py:75
  136.4 6.2 %collective-permute-done.7 = bf16[128,462]{0,1:T(8,128)(2,1)S(1)} collective-permute-done((bf16[128,462]{0,1:T(8,128)(2,1)S(1)}, bf16[128,462]{0,1:T(8,128)(2,1)S(1)}, u32[]{:S(2)}, u32[]{:S(2)}) %collective-permute-start.7) | collective-permute-done | bytes 118304 | tf_op jit(solution)/shard_map/ppermute | solution.py:71
  144.8 8.7 %collective-permute-done.15 = bf16[3,128,462]{1,2,0:T(8,128)(2,1)S(1)} collective-permute-done((bf16[3,128,462]{1,2,0:T(8,128)(2,1)S(1)}, bf16[3,128,462]{1,2,0:T(8,128)(2,1)S(1)}, u32[]{:S(2)}, u32[]{:S(2)}) %collective-permute-start.15) | collective-permute-done | bytes 354848 | tf_op jit(solution)/shard_map/ppermute | solution.py:47
  155.4 4.6 %collective-permute-start.23 = (bf16[3,128,462]{1,2,0:T(8,128)(2,1)S(1)}, bf16[3,128,462]{1,2,0:T(8,128)(2,1)S(1)}, u32[]{:S(2)}, u32[]{:S(2)}) collective-permute-start(bf16[3,128,462]{1,2,0:T(8,128)(2,1)S(1)} %pad_maximum_fusion), channel_id=1, source_target_pairs={{0,480},{32,0},{64,32},{96,64},{128,96},{160,128},{192,160},{224,1... | collective-permute-start | bytes 1064456 | tf_op jit(solution)/shard_map/ppermute | solution.py:50
  160.0 6.4 %collective-permute-done.16 = bf16[3,128,462]{1,2,0:T(8,128)(2,1)S(1)} collective-permute-done((bf16[3,128,462]{1,2,0:T(8,128)(2,1)S(1)}, bf16[3,128,462]{1,2,0:T(8,128)(2,1)S(1)}, u32[]{:S(2)}, u32[]{:S(2)}) %collective-permute-start.16) | collective-permute-done | bytes 354848 | tf_op jit(solution)/shard_map/ppermute | solution.py:47
  168.3 4.6 %collective-permute-start.24 = (bf16[3,128,462]{1,2,0:T(8,128)(2,1)S(1)}, bf16[3,128,462]{1,2,0:T(8,128)(2,1)S(1)}, u32[]{:S(2)}, u32[]{:S(2)}) collective-permute-start(bf16[3,128,462]{1,2,0:T(8,128)(2,1)S(1)} %collective-permute-done.23), channel_id=1, source_target_pairs={{0,480},{32,0},{64,32},{96,64},{128,96},{160,128},{192,160},{224,1... | collective-permute-start | bytes 1064456 | tf_op jit(solution)/shard_map/ppermute | solution.py:50
  172.9 6.1 %collective-permute-done.17 = bf16[3,128,462]{1,2,0:T(8,128)(2,1)S(1)} collective-permute-done((bf16[3,128,462]{1,2,0:T(8,128)(2,1)S(1)}, bf16[3,128,462]{1,2,0:T(8,128)(2,1)S(1)}, u32[]{:S(2)}, u32[]{:S(2)}) %collective-permute-start.17) | collective-permute-done | bytes 354848 | tf_op jit(solution)/shard_map/ppermute | solution.py:47
  180.9 4.6 %collective-permute-start.25 = (bf16[3,128,462]{1,2,0:T(8,128)(2,1)S(1)}, bf16[3,128,462]{1,2,0:T(8,128)(2,1)S(1)}, u32[]{:S(2)}, u32[]{:S(2)}) collective-permute-start(bf16[3,128,462]{1,2,0:T(8,128)(2,1)S(1)} %collective-permute-done.24), channel_id=1, source_target_pairs={{0,480},{32,0},{64,32},{96,64},{128,96},{160,128},{192,160},{224,1... | collective-permute-start | bytes 1064456 | tf_op jit(solution)/shard_map/ppermute | solution.py:50
  185.5 5.2 %collective-permute-done.18 = bf16[3,128,462]{1,2,0:T(8,128)(2,1)S(1)} collective-permute-done((bf16[3,128,462]{1,2,0:T(8,128)(2,1)S(1)}, bf16[3,128,462]{1,2,0:T(8,128)(2,1)S(1)}, u32[]{:S(2)}, u32[]{:S(2)}) %collective-permute-start.18) | collective-permute-done | bytes 354848 | tf_op jit(solution)/shard_map/ppermute | solution.py:47
  192.6 4.6 %collective-permute-start.26 = (bf16[3,128,462]{1,2,0:T(8,128)(2,1)S(1)}, bf16[3,128,462]{1,2,0:T(8,128)(2,1)S(1)}, u32[]{:S(2)}, u32[]{:S(2)}) collective-permute-start(bf16[3,128,462]{1,2,0:T(8,128)(2,1)S(1)} %collective-permute-done.25), channel_id=1, source_target_pairs={{0,480},{32,0},{64,32},{96,64},{128,96},{160,128},{192,160},{224,1... | collective-permute-start | bytes 1064456 | tf_op jit(solution)/shard_map/ppermute | solution.py:50
  197.2 4.4 %collective-permute-done.19 = bf16[3,128,462]{1,2,0:T(8,128)(2,1)S(1)} collective-permute-done((bf16[3,128,462]{1,2,0:T(8,128)(2,1)S(1)}, bf16[3,128,462]{1,2,0:T(8,128)(2,1)S(1)}, u32[]{:S(2)}, u32[]{:S(2)}) %collective-permute-start.19) | collective-permute-done | bytes 354848 | tf_op jit(solution)/shard_map/ppermute | solution.py:47
  203.5 4.6 %collective-permute-start.27 = (bf16[3,128,462]{1,2,0:T(8,128)(2,1)S(1)}, bf16[3,128,462]{1,2,0:T(8,128)(2,1)}, u32[]{:S(2)}, u32[]{:S(2)}) collective-permute-start(bf16[3,128,462]{1,2,0:T(8,128)(2,1)S(1)} %collective-permute-done.26), channel_id=1, source_target_pairs={{0,480},{32,0},{64,32},{96,64},{128,96},{160,128},{192,160},{224,1... | collective-permute-start | bytes 1064456 | tf_op jit(solution)/shard_map/ppermute | solution.py:50
  208.1 3.5 %collective-permute-done.20 = bf16[3,128,462]{1,2,0:T(8,128)(2,1)S(1)} collective-permute-done((bf16[3,128,462]{1,2,0:T(8,128)(2,1)S(1)}, bf16[3,128,462]{1,2,0:T(8,128)(2,1)S(1)}, u32[]{:S(2)}, u32[]{:S(2)}) %collective-permute-start.20) | collective-permute-done | bytes 354848 | tf_op jit(solution)/shard_map/ppermute | solution.py:47
  213.5 4.6 %collective-permute-start.28 = (bf16[3,128,462]{1,2,0:T(8,128)(2,1)}, bf16[3,128,462]{1,2,0:T(8,128)(2,1)}, u32[]{:S(2)}, u32[]{:S(2)}) collective-permute-start(bf16[3,128,462]{1,2,0:T(8,128)(2,1)} %collective-permute-done.27), channel_id=1, source_target_pairs={{0,480},{32,0},{64,32},{96,64},{128,96},{160,128},{192,160},{224,1... | collective-permute-start | bytes 1064456 | tf_op jit(solution)/shard_map/ppermute | solution.py:50
  218.1 2.9 collective-permute-done.21
  223.1 4.9 %collective-permute-start.29 = (bf16[3,128,462]{1,2,0:T(8,128)(2,1)}, bf16[3,128,462]{1,2,0:T(8,128)(2,1)S(1)}, u32[]{:S(2)}, u32[]{:S(2)}) collective-permute-start(bf16[3,128,462]{1,2,0:T(8,128)(2,1)} %collective-permute-done.28), channel_id=1, source_target_pairs={{0,480},{32,0},{64,32},{96,64},{128,96},{160,128},{192,160},{224,1... | collective-permute-start | bytes 1064456 | tf_op jit(solution)/shard_map/ppermute | solution.py:50
  227.9 2.7 collective-permute-done.22
  248.9 6.3 %gather_fusion = bf16[16,3,128,462]{2,3,1,0:T(8,128)(2,1)} fusion(bf16[3,16,128,462]{2,3,0,1:T(8,128)(2,1)} %bitcast_dynamic-update-slice_fusion, s32[1024]{0:T(1024)S(1)} %pad_clamp_fusion), kind=kCustom, calls=%fused_computation | custom fusion | bytes 11354176 | tf_op jit(solution)/shard_map/jit(_take)/gather | solution.py:53
  255.2 3.2 select_bitcast_fusion
  258.8 2.3 copy_bitcast_fusion
  266.6 2.0 copy-done.1
  270.1 18.5 %collective-permute-start.30 = (f32[16,64,512]{2,1,0:T(8,128)}, f32[16,64,512]{2,1,0:T(8,128)}, u32[]{:S(2)}, u32[]{:S(2)}) collective-permute-start(f32[16,64,512]{2,1,0:T(8,128)} %dynamic-slice_bitcast_fusion), channel_id=1, source_target_pairs={{0,1},{1,0},{2,3},{3,2},{4,5},{5,4},{6,7},{7,6},{8,9},{9,8},{10,11... | collective-permute-start | bytes 6291464 | tf_op jit(solution)/shard_map/ppermute | solution.py:92
  288.6 4.6 %collective-permute-done.30 = f32[16,64,512]{2,1,0:T(8,128)} collective-permute-done((f32[16,64,512]{2,1,0:T(8,128)}, f32[16,64,512]{2,1,0:T(8,128)}, u32[]{:S(2)}, u32[]{:S(2)}) %collective-permute-start.30) | collective-permute-done | bytes 2097184 | tf_op jit(solution)/shard_map/ppermute | solution.py:92
  293.2 2.7 bitcast_add_fusion
  297.4 2.7 collective-permute-start.31
  300.2 3.8 %collective-permute-start.33 = (bf16[4,64,512]{2,1,0:T(8,128)(2,1)S(1)}, bf16[4,64,512]{2,1,0:T(8,128)(2,1)S(1)}, u32[]{:S(2)}, u32[]{:S(2)}) collective-permute-start(bf16[4,64,512]{2,1,0:T(8,128)(2,1)S(1)} %get-tuple-element.8), channel_id=1, source_target_pairs={{0,6},{1,7},{2,0},{3,1},{4,2},{5,3},{6,4},{7,5},{8,14},{9,15},{10,... | collective-permute-start | bytes 786440 | tf_op jit(solution)/shard_map/ppermute | solution.py:75
  304.0 3.9 %collective-permute-done.31 = bf16[4,64,512]{2,1,0:T(8,128)(2,1)S(1)} collective-permute-done((bf16[4,64,512]{2,1,0:T(8,128)(2,1)S(1)}, bf16[4,64,512]{2,1,0:T(8,128)(2,1)S(1)}, u32[]{:S(2)}, u32[]{:S(2)}) %collective-permute-start.31) | collective-permute-done | bytes 262176 | tf_op jit(solution)/shard_map/ppermute | solution.py:71
  311.7 4.2 %fusion.1 = bf16[512,462]{0,1:T(8,128)(2,1)} fusion(bf16[2048,462]{0,1:T(8,128)(2,1)} %bitcast.208, bf16[2048,512]{1,0:T(8,128)(2,1)} %all-gather.5.cloned.1.call-done), kind=kOutput, calls=%fused_computation.14 | convolution fusion | flops 969120768 | bytes 4462592 | tf_op jit(solution)/shard_map/dot_general | solution.py:8
  315.9 3.7 %collective-permute-done.32 = bf16[4,64,512]{2,1,0:T(8,128)(2,1)S(1)} collective-permute-done((bf16[4,64,512]{2,1,0:T(8,128)(2,1)}, bf16[4,64,512]{2,1,0:T(8,128)(2,1)S(1)}, u32[]{:S(2)}, u32[]{:S(2)}) %collective-permute-start.32) | collective-permute-done | bytes 262176 | tf_op jit(solution)/shard_map/ppermute | solution.py:71
  320.8 3.1 collective-permute-start.34
  326.7 3.9 %collective-permute-start.36 = (bf16[64,512]{1,0:T(8,128)(2,1)S(1)}, bf16[64,512]{1,0:T(8,128)(2,1)S(1)}, u32[]{:S(2)}, u32[]{:S(2)}) collective-permute-start(bf16[64,512]{1,0:T(8,128)(2,1)S(1)} %get-tuple-element.28), channel_id=1, source_target_pairs={{0,24},{1,25},{2,26},{3,27},{4,28},{5,29},{6,30},{7,31},{8,0},{9,1... | collective-permute-start | bytes 196616 | tf_op jit(solution)/shard_map/ppermute | solution.py:75
  334.5 2.4 collective-permute-done.35
  (125 shorter events, 61.1 us)
Async XLA Ops:
  7.2 256.1 %copy-start = (bf16[512,462]{0,1:T(8,128)(2,1)S(1)}, bf16[512,462]{0,1:T(8,128)(2,1)}, u32[]{:S(2)}) copy-start(bf16[512,462]{0,1:T(8,128)(2,1)} %param.10) | copy-start | bytes 1419268
  7.2 68.5 %all-gather.3.cloned.1.call-start = ((), (), s32[]{:S(2)}) async-start(), calls=%async_computation | async-start | bytes 2162688 | tf_op jit(solution)/shard_map/all_gather | solution.py:119
  7.9 303.8 %all-gather.5.cloned.1.call-start = ((), (), s32[]{:S(2)}) async-start(), calls=%async_computation.1 | async-start | bytes 2162688 | tf_op jit(solution)/shard_map/all_gather | solution.py:120
  84.1 9.0 %collective-permute-start = (bf16[128,462]{0,1:T(8,128)(2,1)S(1)}, bf16[128,462]{0,1:T(8,128)(2,1)S(1)}, u32[]{:S(2)}, u32[]{:S(2)}) collective-permute-start(bf16[128,462]{0,1:T(8,128)(2,1)S(1)} %bitcast.217), channel_id=1, source_target_pairs={{0,32},{32,64},{64,96},{96,128},{128,160},{160,192},{192,224},{224... | collective-permute-start | bytes 354824 | tf_op jit(solution)/shard_map/ppermute | solution.py:71
  87.3 7.7 %collective-permute-start.8 = (bf16[128,462]{0,1:T(8,128)(2,1)S(1)}, bf16[128,462]{0,1:T(8,128)(2,1)S(1)}, u32[]{:S(2)}, u32[]{:S(2)}) collective-permute-start(bf16[128,462]{0,1:T(8,128)(2,1)S(1)} %bitcast.216), channel_id=1, source_target_pairs={{0,480},{32,0},{64,32},{96,64},{128,96},{160,128},{192,160},{224,1... | collective-permute-start | bytes 354824 | tf_op jit(solution)/shard_map/ppermute | solution.py:75
  93.1 6.8 %collective-permute-start.1 = (bf16[128,462]{0,1:T(8,128)(2,1)S(1)}, bf16[128,462]{0,1:T(8,128)(2,1)S(1)}, u32[]{:S(2)}, u32[]{:S(2)}) collective-permute-start(bf16[128,462]{0,1:T(8,128)(2,1)S(1)} %fusion.26), channel_id=1, source_target_pairs={{0,32},{32,64},{64,96},{96,128},{128,160},{160,192},{192,224},{224... | collective-permute-start | bytes 354824 | tf_op jit(solution)/shard_map/ppermute | solution.py:71
  95.1 47.5 %copy-start.10 = (bf16[128,462]{0,1:T(8,128)(2,1)S(1)}, bf16[128,462]{0,1:T(8,128)(2,1)}, u32[]{:S(2)}) copy-start(bf16[128,462]{0,1:T(8,128)(2,1)} %param.8) | copy-start | bytes 354820
  95.1 47.5 %copy-start.11 = (bf16[128,462]{0,1:T(8,128)(2,1)S(1)}, bf16[128,462]{0,1:T(8,128)(2,1)}, u32[]{:S(2)}) copy-start(bf16[128,462]{0,1:T(8,128)(2,1)} %param.9) | copy-start | bytes 354820
  95.1 6.8 %collective-permute-start.9 = (bf16[128,462]{0,1:T(8,128)(2,1)S(1)}, bf16[128,462]{0,1:T(8,128)(2,1)S(1)}, u32[]{:S(2)}, u32[]{:S(2)}) collective-permute-start(bf16[128,462]{0,1:T(8,128)(2,1)S(1)} %fusion.19), channel_id=1, source_target_pairs={{0,480},{32,0},{64,32},{96,64},{128,96},{160,128},{192,160},{224,1... | collective-permute-start | bytes 354824 | tf_op jit(solution)/shard_map/ppermute | solution.py:75
  100.0 6.8 %collective-permute-start.2 = (bf16[128,462]{0,1:T(8,128)(2,1)S(1)}, bf16[128,462]{0,1:T(8,128)(2,1)S(1)}, u32[]{:S(2)}, u32[]{:S(2)}) collective-permute-start(bf16[128,462]{0,1:T(8,128)(2,1)S(1)} %fusion.25), channel_id=1, source_target_pairs={{0,32},{32,64},{64,96},{96,128},{128,160},{160,192},{192,224},{224... | collective-permute-start | bytes 354824 | tf_op jit(solution)/shard_map/ppermute | solution.py:71
  101.9 6.8 %collective-permute-start.10 = (bf16[128,462]{0,1:T(8,128)(2,1)S(1)}, bf16[128,462]{0,1:T(8,128)(2,1)S(1)}, u32[]{:S(2)}, u32[]{:S(2)}) collective-permute-start(bf16[128,462]{0,1:T(8,128)(2,1)S(1)} %fusion.18), channel_id=1, source_target_pairs={{0,480},{32,0},{64,32},{96,64},{128,96},{160,128},{192,160},{224,1... | collective-permute-start | bytes 354824 | tf_op jit(solution)/shard_map/ppermute | solution.py:75
  106.8 6.8 %collective-permute-start.3 = (bf16[128,462]{0,1:T(8,128)(2,1)S(1)}, bf16[128,462]{0,1:T(8,128)(2,1)S(1)}, u32[]{:S(2)}, u32[]{:S(2)}) collective-permute-start(bf16[128,462]{0,1:T(8,128)(2,1)S(1)} %fusion.24), channel_id=1, source_target_pairs={{0,32},{32,64},{64,96},{96,128},{128,160},{160,192},{192,224},{224... | collective-permute-start | bytes 354824 | tf_op jit(solution)/shard_map/ppermute | solution.py:71
  108.8 6.8 %collective-permute-start.11 = (bf16[128,462]{0,1:T(8,128)(2,1)S(1)}, bf16[128,462]{0,1:T(8,128)(2,1)S(1)}, u32[]{:S(2)}, u32[]{:S(2)}) collective-permute-start(bf16[128,462]{0,1:T(8,128)(2,1)S(1)} %fusion.17), channel_id=1, source_target_pairs={{0,480},{32,0},{64,32},{96,64},{128,96},{160,128},{192,160},{224,1... | collective-permute-start | bytes 354824 | tf_op jit(solution)/shard_map/ppermute | solution.py:75
  113.6 6.8 %collective-permute-start.4 = (bf16[128,462]{0,1:T(8,128)(2,1)S(1)}, bf16[128,462]{0,1:T(8,128)(2,1)S(1)}, u32[]{:S(2)}, u32[]{:S(2)}) collective-permute-start(bf16[128,462]{0,1:T(8,128)(2,1)S(1)} %fusion.23), channel_id=1, source_target_pairs={{0,32},{32,64},{64,96},{96,128},{128,160},{160,192},{192,224},{224... | collective-permute-start | bytes 354824 | tf_op jit(solution)/shard_map/ppermute | solution.py:71
  115.6 6.8 %collective-permute-start.12 = (bf16[128,462]{0,1:T(8,128)(2,1)S(1)}, bf16[128,462]{0,1:T(8,128)(2,1)S(1)}, u32[]{:S(2)}, u32[]{:S(2)}) collective-permute-start(bf16[128,462]{0,1:T(8,128)(2,1)S(1)} %fusion.16), channel_id=1, source_target_pairs={{0,480},{32,0},{64,32},{96,64},{128,96},{160,128},{192,160},{224,1... | collective-permute-start | bytes 354824 | tf_op jit(solution)/shard_map/ppermute | solution.py:75
  120.5 6.8 %collective-permute-start.5 = (bf16[128,462]{0,1:T(8,128)(2,1)S(1)}, bf16[128,462]{0,1:T(8,128)(2,1)S(1)}, u32[]{:S(2)}, u32[]{:S(2)}) collective-permute-start(bf16[128,462]{0,1:T(8,128)(2,1)S(1)} %fusion.22), channel_id=1, source_target_pairs={{0,32},{32,64},{64,96},{96,128},{128,160},{160,192},{192,224},{224... | collective-permute-start | bytes 354824 | tf_op jit(solution)/shard_map/ppermute | solution.py:71
  122.4 6.8 %collective-permute-start.13 = (bf16[128,462]{0,1:T(8,128)(2,1)S(1)}, bf16[128,462]{0,1:T(8,128)(2,1)S(1)}, u32[]{:S(2)}, u32[]{:S(2)}) collective-permute-start(bf16[128,462]{0,1:T(8,128)(2,1)S(1)} %fusion.15), channel_id=1, source_target_pairs={{0,480},{32,0},{64,32},{96,64},{128,96},{160,128},{192,160},{224,1... | collective-permute-start | bytes 354824 | tf_op jit(solution)/shard_map/ppermute | solution.py:75
  127.3 7.2 %collective-permute-start.6 = (bf16[128,462]{0,1:T(8,128)(2,1)S(1)}, bf16[128,462]{0,1:T(8,128)(2,1)S(1)}, u32[]{:S(2)}, u32[]{:S(2)}) collective-permute-start(bf16[128,462]{0,1:T(8,128)(2,1)S(1)} %fusion.21), channel_id=1, source_target_pairs={{0,32},{32,64},{64,96},{96,128},{128,160},{160,192},{192,224},{224... | collective-permute-start | bytes 354824 | tf_op jit(solution)/shard_map/ppermute | solution.py:71
  129.3 7.2 %collective-permute-start.14 = (bf16[128,462]{0,1:T(8,128)(2,1)S(1)}, bf16[128,462]{0,1:T(8,128)(2,1)S(1)}, u32[]{:S(2)}, u32[]{:S(2)}) collective-permute-start(bf16[128,462]{0,1:T(8,128)(2,1)S(1)} %fusion.14), channel_id=1, source_target_pairs={{0,480},{32,0},{64,32},{96,64},{128,96},{160,128},{192,160},{224,1... | collective-permute-start | bytes 354824 | tf_op jit(solution)/shard_map/ppermute | solution.py:75
  134.5 8.1 %collective-permute-start.7 = (bf16[128,462]{0,1:T(8,128)(2,1)S(1)}, bf16[128,462]{0,1:T(8,128)(2,1)S(1)}, u32[]{:S(2)}, u32[]{:S(2)}) collective-permute-start(bf16[128,462]{0,1:T(8,128)(2,1)S(1)} %fusion.20), channel_id=1, source_target_pairs={{0,32},{32,64},{64,96},{96,128},{128,160},{160,192},{192,224},{224... | collective-permute-start | bytes 354824 | tf_op jit(solution)/shard_map/ppermute | solution.py:71
  142.9 10.6 %collective-permute-start.15 = (bf16[3,128,462]{1,2,0:T(8,128)(2,1)S(1)}, bf16[3,128,462]{1,2,0:T(8,128)(2,1)S(1)}, u32[]{:S(2)}, u32[]{:S(2)}) collective-permute-start(bf16[3,128,462]{1,2,0:T(8,128)(2,1)S(1)} %pad_maximum_fusion), channel_id=1, source_target_pairs={{0,32},{32,64},{64,96},{96,128},{128,160},{160,192},{192,224},{224... | collective-permute-start | bytes 1064456 | tf_op jit(solution)/shard_map/ppermute | solution.py:47
  153.5 12.9 %collective-permute-start.16 = (bf16[3,128,462]{1,2,0:T(8,128)(2,1)S(1)}, bf16[3,128,462]{1,2,0:T(8,128)(2,1)S(1)}, u32[]{:S(2)}, u32[]{:S(2)}) collective-permute-start(bf16[3,128,462]{1,2,0:T(8,128)(2,1)S(1)} %collective-permute-done.15), channel_id=1, source_target_pairs={{0,32},{32,64},{64,96},{96,128},{128,160},{160,192},{192,224},{224... | collective-permute-start | bytes 1064456 | tf_op jit(solution)/shard_map/ppermute | solution.py:47
  155.4 12.9 %collective-permute-start.23 = (bf16[3,128,462]{1,2,0:T(8,128)(2,1)S(1)}, bf16[3,128,462]{1,2,0:T(8,128)(2,1)S(1)}, u32[]{:S(2)}, u32[]{:S(2)}) collective-permute-start(bf16[3,128,462]{1,2,0:T(8,128)(2,1)S(1)} %pad_maximum_fusion), channel_id=1, source_target_pairs={{0,480},{32,0},{64,32},{96,64},{128,96},{160,128},{192,160},{224,1... | collective-permute-start | bytes 1064456 | tf_op jit(solution)/shard_map/ppermute | solution.py:50
  166.4 12.6 %collective-permute-start.17 = (bf16[3,128,462]{1,2,0:T(8,128)(2,1)S(1)}, bf16[3,128,462]{1,2,0:T(8,128)(2,1)S(1)}, u32[]{:S(2)}, u32[]{:S(2)}) collective-permute-start(bf16[3,128,462]{1,2,0:T(8,128)(2,1)S(1)} %collective-permute-done.16), channel_id=1, source_target_pairs={{0,32},{32,64},{64,96},{96,128},{128,160},{160,192},{192,224},{224... | collective-permute-start | bytes 1064456 | tf_op jit(solution)/shard_map/ppermute | solution.py:47
  168.3 12.6 %collective-permute-start.24 = (bf16[3,128,462]{1,2,0:T(8,128)(2,1)S(1)}, bf16[3,128,462]{1,2,0:T(8,128)(2,1)S(1)}, u32[]{:S(2)}, u32[]{:S(2)}) collective-permute-start(bf16[3,128,462]{1,2,0:T(8,128)(2,1)S(1)} %collective-permute-done.23), channel_id=1, source_target_pairs={{0,480},{32,0},{64,32},{96,64},{128,96},{160,128},{192,160},{224,1... | collective-permute-start | bytes 1064456 | tf_op jit(solution)/shard_map/ppermute | solution.py:50
  179.0 11.7 %collective-permute-start.18 = (bf16[3,128,462]{1,2,0:T(8,128)(2,1)S(1)}, bf16[3,128,462]{1,2,0:T(8,128)(2,1)S(1)}, u32[]{:S(2)}, u32[]{:S(2)}) collective-permute-start(bf16[3,128,462]{1,2,0:T(8,128)(2,1)S(1)} %collective-permute-done.17), channel_id=1, source_target_pairs={{0,32},{32,64},{64,96},{96,128},{128,160},{160,192},{192,224},{224... | collective-permute-start | bytes 1064456 | tf_op jit(solution)/shard_map/ppermute | solution.py:47
  180.9 11.7 %collective-permute-start.25 = (bf16[3,128,462]{1,2,0:T(8,128)(2,1)S(1)}, bf16[3,128,462]{1,2,0:T(8,128)(2,1)S(1)}, u32[]{:S(2)}, u32[]{:S(2)}) collective-permute-start(bf16[3,128,462]{1,2,0:T(8,128)(2,1)S(1)} %collective-permute-done.24), channel_id=1, source_target_pairs={{0,480},{32,0},{64,32},{96,64},{128,96},{160,128},{192,160},{224,1... | collective-permute-start | bytes 1064456 | tf_op jit(solution)/shard_map/ppermute | solution.py:50
  190.7 22.8 %copy-start.6 = (bf16[3,128,462]{1,2,0:T(8,128)(2,1)}, bf16[3,128,462]{1,2,0:T(8,128)(2,1)S(1)}, u32[]{:S(2)}) copy-start(bf16[3,128,462]{1,2,0:T(8,128)(2,1)S(1)} %collective-permute-done.18) | copy-start | bytes 1064452
  190.7 10.9 %collective-permute-start.19 = (bf16[3,128,462]{1,2,0:T(8,128)(2,1)S(1)}, bf16[3,128,462]{1,2,0:T(8,128)(2,1)S(1)}, u32[]{:S(2)}, u32[]{:S(2)}) collective-permute-start(bf16[3,128,462]{1,2,0:T(8,128)(2,1)S(1)} %collective-permute-done.18), channel_id=1, source_target_pairs={{0,32},{32,64},{64,96},{96,128},{128,160},{160,192},{192,224},{224... | collective-permute-start | bytes 1064456 | tf_op jit(solution)/shard_map/ppermute | solution.py:47
  192.6 10.9 %collective-permute-start.26 = (bf16[3,128,462]{1,2,0:T(8,128)(2,1)S(1)}, bf16[3,128,462]{1,2,0:T(8,128)(2,1)S(1)}, u32[]{:S(2)}, u32[]{:S(2)}) collective-permute-start(bf16[3,128,462]{1,2,0:T(8,128)(2,1)S(1)} %collective-permute-done.25), channel_id=1, source_target_pairs={{0,480},{32,0},{64,32},{96,64},{128,96},{160,128},{192,160},{224,1... | collective-permute-start | bytes 1064456 | tf_op jit(solution)/shard_map/ppermute | solution.py:50
  201.6 16.5 %copy-start.8 = (bf16[3,128,462]{1,2,0:T(8,128)(2,1)}, bf16[3,128,462]{1,2,0:T(8,128)(2,1)S(1)}, u32[]{:S(2)}) copy-start(bf16[3,128,462]{1,2,0:T(8,128)(2,1)S(1)} %collective-permute-done.19) | copy-start | bytes 1064452
  201.6 10.0 %collective-permute-start.20 = (bf16[3,128,462]{1,2,0:T(8,128)(2,1)S(1)}, bf16[3,128,462]{1,2,0:T(8,128)(2,1)S(1)}, u32[]{:S(2)}, u32[]{:S(2)}) collective-permute-start(bf16[3,128,462]{1,2,0:T(8,128)(2,1)S(1)} %collective-permute-done.19), channel_id=1, source_target_pairs={{0,32},{32,64},{64,96},{96,128},{128,160},{160,192},{192,224},{224... | collective-permute-start | bytes 1064456 | tf_op jit(solution)/shard_map/ppermute | solution.py:47
  203.5 10.0 %collective-permute-start.27 = (bf16[3,128,462]{1,2,0:T(8,128)(2,1)S(1)}, bf16[3,128,462]{1,2,0:T(8,128)(2,1)}, u32[]{:S(2)}, u32[]{:S(2)}) collective-permute-start(bf16[3,128,462]{1,2,0:T(8,128)(2,1)S(1)} %collective-permute-done.26), channel_id=1, source_target_pairs={{0,480},{32,0},{64,32},{96,64},{128,96},{160,128},{192,160},{224,1... | collective-permute-start | bytes 1064456 | tf_op jit(solution)/shard_map/ppermute | solution.py:50
  211.6 9.4 %copy-start.9 = (bf16[3,128,462]{1,2,0:T(8,128)(2,1)}, bf16[3,128,462]{1,2,0:T(8,128)(2,1)S(1)}, u32[]{:S(2)}) copy-start(bf16[3,128,462]{1,2,0:T(8,128)(2,1)S(1)} %collective-permute-done.20) | copy-start | bytes 1064452
  211.6 9.4 %collective-permute-start.21 = (bf16[3,128,462]{1,2,0:T(8,128)(2,1)S(1)}, bf16[3,128,462]{1,2,0:T(8,128)(2,1)}, u32[]{:S(2)}, u32[]{:S(2)}) collective-permute-start(bf16[3,128,462]{1,2,0:T(8,128)(2,1)S(1)} %collective-permute-done.20), channel_id=1, source_target_pairs={{0,32},{32,64},{64,96},{96,128},{128,160},{160,192},{192,224},{224... | collective-permute-start | bytes 1064456 | tf_op jit(solution)/shard_map/ppermute | solution.py:47
  213.5 9.5 %collective-permute-start.28 = (bf16[3,128,462]{1,2,0:T(8,128)(2,1)}, bf16[3,128,462]{1,2,0:T(8,128)(2,1)}, u32[]{:S(2)}, u32[]{:S(2)}) collective-permute-start(bf16[3,128,462]{1,2,0:T(8,128)(2,1)} %collective-permute-done.27), channel_id=1, source_target_pairs={{0,480},{32,0},{64,32},{96,64},{128,96},{160,128},{192,160},{224,1... | collective-permute-start | bytes 1064456 | tf_op jit(solution)/shard_map/ppermute | solution.py:50
  221.0 9.6 %collective-permute-start.22 = (bf16[3,128,462]{1,2,0:T(8,128)(2,1)}, bf16[3,128,462]{1,2,0:T(8,128)(2,1)}, u32[]{:S(2)}, u32[]{:S(2)}) collective-permute-start(bf16[3,128,462]{1,2,0:T(8,128)(2,1)} %collective-permute-done.21), channel_id=1, source_target_pairs={{0,32},{32,64},{64,96},{96,128},{128,160},{160,192},{192,224},{224... | collective-permute-start | bytes 1064456 | tf_op jit(solution)/shard_map/ppermute | solution.py:47
  223.0 14.7 %copy-start.7 = (bf16[3,128,462]{1,2,0:T(8,128)(2,1)S(1)}, bf16[3,128,462]{1,2,0:T(8,128)(2,1)}, u32[]{:S(2)}) copy-start(bf16[3,128,462]{1,2,0:T(8,128)(2,1)} %copy-done.6) | copy-start | bytes 1064452
  223.1 25.1 %collective-permute-start.29 = (bf16[3,128,462]{1,2,0:T(8,128)(2,1)}, bf16[3,128,462]{1,2,0:T(8,128)(2,1)S(1)}, u32[]{:S(2)}, u32[]{:S(2)}) collective-permute-start(bf16[3,128,462]{1,2,0:T(8,128)(2,1)} %collective-permute-done.28), channel_id=1, source_target_pairs={{0,480},{32,0},{64,32},{96,64},{128,96},{160,128},{192,160},{224,1... | collective-permute-start | bytes 1064456 | tf_op jit(solution)/shard_map/ppermute | solution.py:50
  270.1 23.2 %collective-permute-start.30 = (f32[16,64,512]{2,1,0:T(8,128)}, f32[16,64,512]{2,1,0:T(8,128)}, u32[]{:S(2)}, u32[]{:S(2)}) collective-permute-start(f32[16,64,512]{2,1,0:T(8,128)} %dynamic-slice_bitcast_fusion), channel_id=1, source_target_pairs={{0,1},{1,0},{2,3},{3,2},{4,5},{5,4},{6,7},{7,6},{8,9},{9,8},{10,11... | collective-permute-start | bytes 6291464 | tf_op jit(solution)/shard_map/ppermute | solution.py:92
  297.4 10.5 %collective-permute-start.31 = (bf16[4,64,512]{2,1,0:T(8,128)(2,1)S(1)}, bf16[4,64,512]{2,1,0:T(8,128)(2,1)S(1)}, u32[]{:S(2)}, u32[]{:S(2)}) collective-permute-start(bf16[4,64,512]{2,1,0:T(8,128)(2,1)S(1)} %get-tuple-element.7), channel_id=1, source_target_pairs={{0,2},{1,3},{2,4},{3,5},{4,6},{5,7},{6,0},{7,1},{8,10},{9,11},{10,... | collective-permute-start | bytes 786440 | tf_op jit(solution)/shard_map/ppermute | solution.py:71
  300.2 15.7 %collective-permute-start.33 = (bf16[4,64,512]{2,1,0:T(8,128)(2,1)S(1)}, bf16[4,64,512]{2,1,0:T(8,128)(2,1)S(1)}, u32[]{:S(2)}, u32[]{:S(2)}) collective-permute-start(bf16[4,64,512]{2,1,0:T(8,128)(2,1)S(1)} %get-tuple-element.8), channel_id=1, source_target_pairs={{0,6},{1,7},{2,0},{3,1},{4,2},{5,3},{6,4},{7,5},{8,14},{9,15},{10,... | collective-permute-start | bytes 786440 | tf_op jit(solution)/shard_map/ppermute | solution.py:75
  309.8 9.9 %collective-permute-start.32 = (bf16[4,64,512]{2,1,0:T(8,128)(2,1)}, bf16[4,64,512]{2,1,0:T(8,128)(2,1)S(1)}, u32[]{:S(2)}, u32[]{:S(2)}) collective-permute-start(bf16[4,64,512]{2,1,0:T(8,128)(2,1)} %fusion.2), channel_id=1, source_target_pairs={{0,2},{1,3},{2,4},{3,5},{4,6},{5,7},{6,0},{7,1},{8,10},{9,11},{10,... | collective-permute-start | bytes 786440 | tf_op jit(solution)/shard_map/ppermute | solution.py:71
  311.7 12.2 %copy-start.13 = (bf16[2048,512]{1,0:T(8,128)(2,1)S(1)}, bf16[2048,512]{1,0:T(8,128)(2,1)}, u32[]{:S(2)}) copy-start(bf16[2048,512]{1,0:T(8,128)(2,1)} %all-gather.5.cloned.1.call-done) | copy-start | bytes 6291460
  320.8 9.8 %collective-permute-start.34 = (bf16[64,512]{1,0:T(8,128)(2,1)S(1)}, bf16[64,512]{1,0:T(8,128)(2,1)S(1)}, u32[]{:S(2)}, u32[]{:S(2)}) collective-permute-start(bf16[64,512]{1,0:T(8,128)(2,1)S(1)} %get-tuple-element.27), channel_id=1, source_target_pairs={{0,8},{1,9},{2,10},{3,11},{4,12},{5,13},{6,14},{7,15},{8,16},{9,17... | collective-permute-start | bytes 196616 | tf_op jit(solution)/shard_map/ppermute | solution.py:71
  326.2 6.4 %copy-start.12 = (bf16[2048,512]{1,0:T(8,128)(2,1)S(1)}, bf16[2048,512]{1,0:T(8,128)(2,1)}, u32[]{:S(2)}) copy-start(bf16[2048,512]{1,0:T(8,128)(2,1)} %all-gather.3.cloned.1.call-done) | copy-start | bytes 6291460
  326.7 7.8 %collective-permute-start.36 = (bf16[64,512]{1,0:T(8,128)(2,1)S(1)}, bf16[64,512]{1,0:T(8,128)(2,1)S(1)}, u32[]{:S(2)}, u32[]{:S(2)}) collective-permute-start(bf16[64,512]{1,0:T(8,128)(2,1)S(1)} %get-tuple-element.28), channel_id=1, source_target_pairs={{0,24},{1,25},{2,26},{3,27},{4,28},{5,29},{6,30},{7,31},{8,0},{9,1... | collective-permute-start | bytes 196616 | tf_op jit(solution)/shard_map/ppermute | solution.py:75
  330.6 6.2 %collective-permute-start.35 = (bf16[64,512]{1,0:T(8,128)(2,1)S(1)}, bf16[64,512]{1,0:T(8,128)(2,1)S(1)}, u32[]{:S(2)}, u32[]{:S(2)}) collective-permute-start(bf16[64,512]{1,0:T(8,128)(2,1)S(1)} %fusion.28), channel_id=1, source_target_pairs={{0,8},{1,9},{2,10},{3,11},{4,12},{5,13},{6,14},{7,15},{8,16},{9,17... | collective-permute-start | bytes 196616 | tf_op jit(solution)/shard_map/ppermute | solution.py:71
  (5 other events, 12.4 us)
Sparse Core Ops, SparseCore 0:
  11.1 64.5 all-gather.2
  223.1 73.0 all-gather.4

commit v4 on v3

--- a/solution.py
+++ b/solution.py
@@ -114,39 +114,65 @@
     )
 
 
-def shards(inputs, gate_pre, up_pre, w_gate, w_up, w_down, grad_out, n_row, n_x, n_y):
+def shards(inputs, gate_pre, up_pre, w_gate, w_up, w_down, grad_out, n_row, n_col):
     tokens_row, hidden_units = gate_pre.shape
-    all_grad_out = lax.all_gather(grad_out, "col", axis=0, tiled=True)
+    tokens_col, width = grad_out.shape
+    spread = jnp.broadcast_to(grad_out[None], (n_col, tokens_col, width))
+    all_grad_out = lax.all_to_all(spread, "col", 0, 0).reshape((n_col * tokens_col, width))
     all_inputs = lax.all_gather(inputs, "col", axis=0, tiled=True)
     part = contract_cols(all_grad_out, w_down).astype(jnp.bfloat16)
     part = part.reshape((n_row, tokens_row, hidden_units))
     own_grad = ring_reduce_scatter(part, "row", n_row, jnp.bfloat16)
     own = jnp.stack(pointwise(gate_pre, up_pre, own_grad), axis=0)
-    gathered = ring_all_gather(own, "row", n_row).reshape(
-        (3, n_row * tokens_row, hidden_units)
-    )
-    hidden, gate_grad, up_grad = gathered[0], gathered[1], gathered[2]
-    grad_down = contract_rows(hidden, all_grad_out).astype(jnp.bfloat16)
-    grad_gate = contract_rows(all_inputs, gate_grad).astype(jnp.bfloat16)
-    grad_up = contract_rows(all_inputs, up_grad).astype(jnp.bfloat16)
-    grad_in_terms = (
-        contract_cols(gate_grad, w_gate) + contract_cols(up_grad, w_up)
-    ).astype(jnp.bfloat16)
-    grad_in_terms = grad_in_terms.reshape((n_y * n_x, -1, grad_in_terms.shape[1]))
-    grad_in = col_reduce_scatter(grad_in_terms, n_x, n_y).astype(jnp.bfloat16)
+
+    me = lax.axis_index("row")
+    up, down = _shifts(n_row)
+    n_up = n_row // 2
+    n_down = n_row - 1 - n_up
+    sums = [None, None, None]
+    terms = {}
+
+    def use(block, offset):
+        k = (me + offset + n_row) % n_row
+        rows_out = lax.dynamic_slice_in_dim(all_grad_out, k * tokens_row, tokens_row, 0)
+        rows_in = lax.dynamic_slice_in_dim(all_inputs, k * tokens_row, tokens_row, 0)
+        hidden, gate_grad, up_grad = block[0], block[1], block[2]
+        new = (
+            contract_rows(hidden, rows_out),
+            contract_rows(rows_in, gate_grad),
+            contract_rows(rows_in, up_grad),
+        )
+        for i in range(3):
+            sums[i] = new[i] if sums[i] is None else sums[i] + new[i]
+        terms[offset] = (
+            contract_cols(gate_grad, w_gate) + contract_cols(up_grad, w_up)
+        ).astype(jnp.bfloat16)
+
+    a = own
+    b = own
+    use(own, 0)
+    for s in range(1, n_up + 1):
+        a = lax.ppermute(a, "row", up)
+        if s <= n_down:
+            b = lax.ppermute(b, "row", down)
+        use(a, -s)
+        if s <= n_down:
+            use(b, s)
+    grad_down, grad_gate, grad_up = (v.astype(jnp.bfloat16) for v in sums)
+    ring_order = jnp.stack([terms[d] for d in range(-n_up, n_down + 1)])
+    natural = jnp.take(ring_order, (jnp.arange(n_row) - me + n_up) % n_row, axis=0)
+    natural = natural.reshape((n_col, -1, width))
+    received = lax.all_to_all(natural, "col", 0, 0)
+    grad_in = received.astype(jnp.float32).sum(axis=0).astype(jnp.bfloat16)
     return (grad_in, grad_gate, grad_up, grad_down)
 
 
 def solution(mesh):
     n_row = mesh.shape["row"]
-    try:
-        n_x = len({d.coords[0] for d in mesh.devices.flat})
-    except AttributeError:
-        n_x = int(round((mesh.shape["col"] // 2) ** 0.5))
-    n_y = mesh.shape["col"] // (2 * n_x)
+    n_col = mesh.shape["col"]
 
     def body(*args):
-        return shards(*args, n_row=n_row, n_x=n_x, n_y=n_y)
+        return shards(*args, n_row=n_row, n_col=n_col)
 
     return jax.shard_map(
         body,

time: 346 us -> 325 us (0.939)
  waiting for transfers between devices: 131 us -> 68.1 us
  matrix products: 13.6 us -> 71.6 us
  local copies, waits for them, and re-layouts: 39.9 us -> 17 us
  starting transfers between devices: 133 us -> 138 us
    all_gather x1 -> x0, waiting for transfers between devices: 67.5 us -> none  [shards(): all_grad_out = lax.all_gather(grad_out, 'col', axis=0, tiled=True)]
    all_to_all x0 -> x2, waiting for transfers between devices: none -> 47.1 us  [the longest x1 27.3 us: shards(): lax.all_to_all(spread, 'col', 0, 0).reshape((n_col * tokens_col, width))]
    all_to_all x0 -> x2, starting transfers between devices: none -> 34.3 us  [the longest x1 23.6 us: shards(): received = lax.all_to_all(natural, 'col', 0, 0)]
    dot_general x3 -> x48, matrix products: 8.07 us -> 40.4 us  [contract_rows(): lax.dot_general(left, right, (((0,), (0,)), ((), ())), preferred_element_...]
    ppermute x16 -> x15, waiting for transfers between devices: 44.5 us -> 13.9 us  [the longest x8 7.66 us: shards(): a = lax.ppermute(a, 'row', up)]
    dot_general x3 -> x33, matrix products: 5.52 us -> 31.2 us  [contract_cols(): lax.dot_general(left, right, (((1,), (1,)), ((), ())), preferred_element_...]
    unnamed x52 -> x81, local copies, waits for them, and re-layouts: 25.4 us -> 5.45 us
    ppermute x16 -> x15, starting transfers between devices: 66.1 us -> 50 us  [the longest x7 34.5 us: shards(): b = lax.ppermute(b, 'row', down)]
  transfers between devices with their start and end apart: 39 -> 33, of which waited for: 21 -> 12; matrix products, arithmetic and copies ran while one was open for 15% -> 21% of each run, Pallas kernels for 0% -> 0%
where the time goes in v4:
time: 325 us; the launch traced here: 323 us
  starting transfers between devices  138 us (42%)
  matrix products  71.6 us (22%)
  waiting for transfers between devices  68.1 us (21%)
  local copies, waits for them, and re-layouts  17 us (5%)
  between operations  15.7 us (5%)
  other arithmetic  12.9 us (4%)
    dot_general x48, matrix products, contract_rows(): lax.dot_general(left, right, (((0,), (0,)), ((), ())), preferred_element_...  40.4 us
    ppermute x7, starting transfers between devices, ring_reduce_scatter(): b = lax.ppermute(b.astype(wire_dtype), axis, down).astype(jnp.float32)  38 us
    ppermute x7, starting transfers between devices, shards(): b = lax.ppermute(b, 'row', down)  34.5 us
    dot_general x33, matrix products, contract_cols(): lax.dot_general(left, right, (((1,), (1,)), ((), ())), preferred_element_...  31.2 us
    all_to_all x1, waiting for transfers between devices, shards(): lax.all_to_all(spread, 'col', 0, 0).reshape((n_col * tokens_col, width))  27.3 us
    all_to_all x1, starting transfers between devices, shards(): received = lax.all_to_all(natural, 'col', 0, 0)  23.6 us
    all_to_all x1, waiting for transfers between devices, shards(): received = lax.all_to_all(natural, 'col', 0, 0)  19.8 us
    ppermute x8, starting transfers between devices, shards(): a = lax.ppermute(a, 'row', up)  15.5 us
  transfers between devices with their start and end apart: 33, of which 12 were waited for; matrix products, arithmetic and copies ran while one was open for 21% of the time, Pallas kernels for 0%

profile of v4, /device:TPU:1, one launch (start us, length us, event | category | flops | bytes accessed | tf_op | source)
XLA Modules:
  0.0 323.1 jit_solution(11378830527596383205)
XLA Ops:
  7.2 2.4 broadcast_in_dim.23
  9.6 10.6 %all-to-all-start = ((bf16[32,64,512]{2,1,0:T(8,128)(2,1)}), bf16[32,64,512]{2,1,0:T(8,128)(2,1)S(1)}, u32[]{:S(2)}, u32[]{:S(2)}) async-start(bf16[32,64,512]{2,1,0:T(8,128)(2,1)} %broadcast_in_dim.23), calls=%async_computation | async-start | bytes 4194304 | tf_op jit(solution)/shard_map/all_to_all | solution.py:121
  21.3 27.3 %all-to-all-done = bf16[32,64,512]{2,1,0:T(8,128)(2,1)S(1)} async-done(((bf16[32,64,512]{2,1,0:T(8,128)(2,1)}), bf16[32,64,512]{2,1,0:T(8,128)(2,1)S(1)}, u32[]{:S(2)}, u32[]{:S(2)}) %all-to-all-start) | async-done | bytes 2097184 | tf_op jit(solution)/shard_map/all_to_all | solution.py:121
  50.7 5.0 %constant_dynamic-slice_fusion.15 = (bf16[1,128,462]{1,0,2:T(2,128)(2,1)S(1)}, bf16[1,128,462]{1,0,2:T(2,128)(2,1)}, bf16[1,128,462]{1,0,2:T(2,128)(2,1)}, bf16[...) fusion(bf16[16,128,462]{1,0,2:T(8,128)(2,1)S(1)} %slice_bitcast, ...), kind=kLoop, calls=%fused_computation.367 | loop fusion | bytes 3784768 | tf_op jit(solution)/shard_map/jit(dynamic_index_in_dim)/dynamic_slice | solution.py:64
  56.4 1.9 collective-permute-start
  58.5 9.7 %collective-permute-start.8 = (bf16[128,462]{0,1:T(8,128)(2,1)S(1)}, bf16[128,462]{0,1:T(8,128)(2,1)S(1)}, u32[]{:S(2)}, u32[]{:S(2)}) collective-permute-start(bf16[128,462]{0,1:T(8,128)(2,1)S(1)} %bitcast.381), channel_id=1, source_target_pairs={{0,480},{32,0},{64,32},{96,64},{128,96},{160,128},{192,160},{224,1... | collective-permute-start | bytes 354824 | tf_op jit(solution)/shard_map/ppermute | solution.py:75
  69.5 1.9 collective-permute-start.1
  72.6 4.5 %collective-permute-start.9 = (bf16[128,462]{0,1:T(8,128)(2,1)S(1)}, bf16[128,462]{0,1:T(8,128)(2,1)S(1)}, u32[]{:S(2)}, u32[]{:S(2)}) collective-permute-start(bf16[128,462]{0,1:T(8,128)(2,1)S(1)} %fusion.82), channel_id=1, source_target_pairs={{0,480},{32,0},{64,32},{96,64},{128,96},{160,128},{192,160},{224,1... | collective-permute-start | bytes 354824 | tf_op jit(solution)/shard_map/ppermute | solution.py:75
  78.1 1.9 collective-permute-start.2
  81.0 4.6 %collective-permute-start.10 = (bf16[128,462]{0,1:T(8,128)(2,1)S(1)}, bf16[128,462]{0,1:T(8,128)(2,1)S(1)}, u32[]{:S(2)}, u32[]{:S(2)}) collective-permute-start(bf16[128,462]{0,1:T(8,128)(2,1)S(1)} %fusion.81), channel_id=1, source_target_pairs={{0,480},{32,0},{64,32},{96,64},{128,96},{160,128},{192,160},{224,1... | collective-permute-start | bytes 354824 | tf_op jit(solution)/shard_map/ppermute | solution.py:75
  85.7 1.9 collective-permute-start.3
  87.6 4.8 %collective-permute-start.11 = (bf16[128,462]{0,1:T(8,128)(2,1)S(1)}, bf16[128,462]{0,1:T(8,128)(2,1)S(1)}, u32[]{:S(2)}, u32[]{:S(2)}) collective-permute-start(bf16[128,462]{0,1:T(8,128)(2,1)S(1)} %fusion.80), channel_id=1, source_target_pairs={{0,480},{32,0},{64,32},{96,64},{128,96},{160,128},{192,160},{224,1... | collective-permute-start | bytes 354824 | tf_op jit(solution)/shard_map/ppermute | solution.py:75
  92.5 1.9 collective-permute-start.4
  94.5 4.8 %collective-permute-start.12 = (bf16[128,462]{0,1:T(8,128)(2,1)S(1)}, bf16[128,462]{0,1:T(8,128)(2,1)S(1)}, u32[]{:S(2)}, u32[]{:S(2)}) collective-permute-start(bf16[128,462]{0,1:T(8,128)(2,1)S(1)} %fusion.79), channel_id=1, source_target_pairs={{0,480},{32,0},{64,32},{96,64},{128,96},{160,128},{192,160},{224,1... | collective-permute-start | bytes 354824 | tf_op jit(solution)/shard_map/ppermute | solution.py:75
  99.3 1.9 collective-permute-start.5
  101.3 4.8 %collective-permute-start.13 = (bf16[128,462]{0,1:T(8,128)(2,1)S(1)}, bf16[128,462]{0,1:T(8,128)(2,1)S(1)}, u32[]{:S(2)}, u32[]{:S(2)}) collective-permute-start(bf16[128,462]{0,1:T(8,128)(2,1)S(1)} %fusion.78), channel_id=1, source_target_pairs={{0,480},{32,0},{64,32},{96,64},{128,96},{160,128},{192,160},{224,1... | collective-permute-start | bytes 354824 | tf_op jit(solution)/shard_map/ppermute | solution.py:75
  106.2 1.9 collective-permute-start.6
  109.2 5.0 %collective-permute-start.14 = (bf16[128,462]{0,1:T(8,128)(2,1)}, bf16[128,462]{0,1:T(8,128)(2,1)}, u32[]{:S(2)}, u32[]{:S(2)}) collective-permute-start(bf16[128,462]{0,1:T(8,128)(2,1)} %fusion.77), channel_id=1, source_target_pairs={{0,480},{32,0},{64,32},{96,64},{128,96},{160,128},{192,160},{224,1... | collective-permute-start | bytes 354824 | tf_op jit(solution)/shard_map/ppermute | solution.py:75
  115.0 1.9 collective-permute-start.7
  117.4 5.6 %collective-permute-done.7 = bf16[128,462]{0,1:T(8,128)(2,1)S(1)} collective-permute-done((bf16[128,462]{0,1:T(8,128)(2,1)}, bf16[128,462]{0,1:T(8,128)(2,1)S(1)}, u32[]{:S(2)}, u32[]{:S(2)}) %collective-permute-start.7) | collective-permute-done | bytes 118304 | tf_op jit(solution)/shard_map/ppermute | solution.py:71
  124.9 1.9 collective-permute-start.15
  126.8 4.6 %collective-permute-start.23 = (bf16[3,128,462]{1,2,0:T(8,128)(2,1)S(1)}, bf16[3,128,462]{1,2,0:T(8,128)(2,1)S(1)}, u32[]{:S(2)}, u32[]{:S(2)}) collective-permute-start(bf16[3,128,462]{1,2,0:T(8,128)(2,1)S(1)} %pad_maximum_fusion), channel_id=1, source_target_pairs={{0,480},{32,0},{64,32},{96,64},{128,96},{160,128},{192,160},{224,1... | collective-permute-start | bytes 1064456 | tf_op jit(solution)/shard_map/ppermute | solution.py:157
  132.9 2.8 collective-permute-done.23
  135.7 5.0 %collective-permute-start.24 = (bf16[3,128,462]{1,2,0:T(8,128)(2,1)S(1)}, bf16[3,128,462]{1,2,0:T(8,128)(2,1)S(1)}, u32[]{:S(2)}, u32[]{:S(2)}) collective-permute-start(bf16[3,128,462]{1,2,0:T(8,128)(2,1)S(1)} %collective-permute-done.23), channel_id=1, source_target_pairs={{0,480},{32,0},{64,32},{96,64},{128,96},{160,128},{192,160},{224,1... | collective-permute-start | bytes 1064456 | tf_op jit(solution)/shard_map/ppermute | solution.py:157
  140.7 1.9 collective-permute-start.16
  146.6 5.3 %collective-permute-start.25 = (bf16[3,128,462]{1,2,0:T(8,128)(2,1)S(1)}, bf16[3,128,462]{1,2,0:T(8,128)(2,1)}, u32[]{:S(2)}, u32[]{:S(2)}) collective-permute-start(bf16[3,128,462]{1,2,0:T(8,128)(2,1)S(1)} %collective-permute-done.24), channel_id=1, source_target_pairs={{0,480},{32,0},{64,32},{96,64},{128,96},{160,128},{192,160},{224,1... | collective-permute-start | bytes 1064456 | tf_op jit(solution)/shard_map/ppermute | solution.py:157
  151.9 1.9 collective-permute-start.17
  156.9 5.3 %collective-permute-start.26 = (bf16[3,128,462]{1,2,0:T(8,128)(2,1)}, bf16[3,128,462]{1,2,0:T(8,128)(2,1)}, u32[]{:S(2)}, u32[]{:S(2)}) collective-permute-start(bf16[3,128,462]{1,2,0:T(8,128)(2,1)} %collective-permute-done.25), channel_id=1, source_target_pairs={{0,480},{32,0},{64,32},{96,64},{128,96},{160,128},{192,160},{224,1... | collective-permute-start | bytes 1064456 | tf_op jit(solution)/shard_map/ppermute | solution.py:157
  162.2 2.1 collective-permute-start.18
  166.2 1.9 fusion.170
  169.2 2.1 fusion.4
  181.9 4.7 %collective-permute-start.27 = (bf16[3,128,462]{1,2,0:T(8,128)(2,1)}, bf16[3,128,462]{1,2,0:T(8,128)(2,1)S(1)}, u32[]{:S(2)}, u32[]{:S(2)}) collective-permute-start(bf16[3,128,462]{1,2,0:T(8,128)(2,1)} %collective-permute-done.26), channel_id=1, source_target_pairs={{0,480},{32,0},{64,32},{96,64},{128,96},{160,128},{192,160},{224,1... | collective-permute-start | bytes 1064456 | tf_op jit(solution)/shard_map/ppermute | solution.py:157
  190.2 1.9 collective-permute-start.19
  198.1 4.6 %collective-permute-start.28 = (bf16[3,128,462]{1,2,0:T(8,128)(2,1)S(1)}, bf16[3,128,462]{1,2,0:T(8,128)(2,1)S(1)}, u32[]{:S(2)}, u32[]{:S(2)}) collective-permute-start(bf16[3,128,462]{1,2,0:T(8,128)(2,1)S(1)} %collective-permute-done.27), channel_id=1, source_target_pairs={{0,480},{32,0},{64,32},{96,64},{128,96},{160,128},{192,160},{224,1... | collective-permute-start | bytes 1064456 | tf_op jit(solution)/shard_map/ppermute | solution.py:157
  204.4 1.9 collective-permute-start.20
  210.1 5.0 %collective-permute-start.29 = (bf16[3,128,462]{1,2,0:T(8,128)(2,1)S(1)}, bf16[3,128,462]{1,2,0:T(8,128)(2,1)S(1)}, u32[]{:S(2)}, u32[]{:S(2)}) collective-permute-start(bf16[3,128,462]{1,2,0:T(8,128)(2,1)S(1)} %collective-permute-done.28), channel_id=1, source_target_pairs={{0,480},{32,0},{64,32},{96,64},{128,96},{160,128},{192,160},{224,1... | collective-permute-start | bytes 1064456 | tf_op jit(solution)/shard_map/ppermute | solution.py:157
  216.9 1.9 collective-permute-start.21
  218.8 2.1 fusion.1
  223.9 2.9 collective-permute-done.21
  226.8 1.9 collective-permute-start.22
  229.2 2.1 fusion.92
  231.3 4.8 %collective-permute-done.22 = bf16[3,128,462]{1,2,0:T(8,128)(2,1)S(1)} collective-permute-done((bf16[3,128,462]{1,2,0:T(8,128)(2,1)S(1)}, bf16[3,128,462]{1,2,0:T(8,128)(2,1)S(1)}, u32[]{:S(2)}, u32[]{:S(2)}) %collective-permute-start.22) | collective-permute-done | bytes 354848 | tf_op jit(solution)/shard_map/ppermute | solution.py:155
  254.5 3.6 %gather_fusion = bf16[16,128,512]{2,1,0:T(8,128)(2,1)} fusion(bf16[16,128,512]{2,1,0:T(8,128)(2,1)} %fusion.38, s32[1024]{0:T(1024)S(1)} %pad_clamp_fusion), kind=kCustom, calls=%fused_computation | custom fusion | bytes 4194368 | tf_op jit(solution)/shard_map/jit(_take)/gather | solution.py:163
  258.1 3.2 broadcast_select_fusion
  261.3 23.6 %all-to-all-start.1 = ((bf16[32,64,512]{2,1,0:T(8,128)(2,1)}), bf16[32,64,512]{2,1,0:T(8,128)(2,1)}, u32[]{:S(2)}, u32[]{:S(2)}) async-start(bf16[32,64,512]{2,1,0:T(8,128)(2,1)} %broadcast_select_fusion), calls=%async_computation.1 | async-start | bytes 4194304 | tf_op jit(solution)/shard_map/all_to_all | solution.py:165
  289.9 1.9 fusion.20
  293.9 19.8 %all-to-all-done.1 = bf16[32,64,512]{2,1,0:T(8,128)(2,1)} async-done(((bf16[32,64,512]{2,1,0:T(8,128)(2,1)}), bf16[32,64,512]{2,1,0:T(8,128)(2,1)}, u32[]{:S(2)}, u32[]{:S(2)}) %all-to-all-start.1) | async-done | bytes 2097184 | tf_op jit(solution)/shard_map/all_to_all | solution.py:165
  313.7 2.5 reduce_sum.12
  (207 shorter events, 79.7 us)
Async XLA Ops:
  7.2 125.5 %copy-start = (bf16[512,462]{0,1:T(8,128)(2,1)S(1)}, bf16[512,462]{0,1:T(8,128)(2,1)}, u32[]{:S(2)}) copy-start(bf16[512,462]{0,1:T(8,128)(2,1)} %param.10) | copy-start | bytes 1419268
  9.6 39.0 %copy-start.38 = (bf16[462,512]{1,0:T(8,128)(2,1)S(1)}, bf16[462,512]{1,0:T(8,128)(2,1)}, u32[]{:S(2)}) copy-start(bf16[462,512]{1,0:T(8,128)(2,1)} %param.12) | copy-start | bytes 1419268
  9.6 38.9 %all-to-all-start = ((bf16[32,64,512]{2,1,0:T(8,128)(2,1)}), bf16[32,64,512]{2,1,0:T(8,128)(2,1)S(1)}, u32[]{:S(2)}, u32[]{:S(2)}) async-start(bf16[32,64,512]{2,1,0:T(8,128)(2,1)} %broadcast_in_dim.23), calls=%async_computation | async-start | bytes 4194304 | tf_op jit(solution)/shard_map/all_to_all | solution.py:121
  20.3 151.0 %all-gather.2.cloned.1.call-start = ((), (), s32[]{:S(2)}) async-start(), calls=%async_computation.2 | async-start | bytes 2162688 | tf_op jit(solution)/shard_map/all_gather | solution.py:122
  48.6 120.6 %copy-start.3 = (bf16[32,64,512]{2,1,0:T(8,128)(2,1)}, bf16[32,64,512]{2,1,0:T(8,128)(2,1)S(1)}, u32[]{:S(2)}) copy-start(bf16[32,64,512]{2,1,0:T(8,128)(2,1)S(1)} %all-to-all-done) | copy-start | bytes 6291460
  56.4 12.1 %collective-permute-start = (bf16[128,462]{0,1:T(8,128)(2,1)}, bf16[128,462]{0,1:T(8,128)(2,1)}, u32[]{:S(2)}, u32[]{:S(2)}) collective-permute-start(bf16[128,462]{0,1:T(8,128)(2,1)} %bitcast.358), channel_id=1, source_target_pairs={{0,32},{32,64},{64,96},{96,128},{128,160},{160,192},{192,224},{224... | collective-permute-start | bytes 354824 | tf_op jit(solution)/shard_map/ppermute | solution.py:71
  58.4 40.9 %copy-start.32 = (bf16[1,128,462]{1,0,2:T(2,128)(2,1)S(1)}, bf16[1,128,462]{1,0,2:T(2,128)(2,1)}, u32[]{:S(2)}) copy-start(bf16[1,128,462]{1,0,2:T(2,128)(2,1)} %get-tuple-element.13) | copy-start | bytes 354820
  58.4 27.2 %copy-start.36 = (bf16[1,128,462]{1,0,2:T(2,128)(2,1)S(1)}, bf16[1,128,462]{1,0,2:T(2,128)(2,1)}, u32[]{:S(2)}) copy-start(bf16[1,128,462]{1,0,2:T(2,128)(2,1)} %get-tuple-element.15) | copy-start | bytes 354820
  58.4 29.2 %copy-start.35 = (bf16[1,128,462]{1,0,2:T(2,128)(2,1)S(1)}, bf16[1,128,462]{1,0,2:T(2,128)(2,1)}, u32[]{:S(2)}) copy-start(bf16[1,128,462]{1,0,2:T(2,128)(2,1)} %get-tuple-element.7) | copy-start | bytes 354820
  58.4 34.0 %copy-start.34 = (bf16[1,128,462]{1,0,2:T(2,128)(2,1)S(1)}, bf16[1,128,462]{1,0,2:T(2,128)(2,1)}, u32[]{:S(2)}) copy-start(bf16[1,128,462]{1,0,2:T(2,128)(2,1)} %get-tuple-element.14) | copy-start | bytes 354820
  58.4 36.0 %copy-start.33 = (bf16[1,128,462]{1,0,2:T(2,128)(2,1)S(1)}, bf16[1,128,462]{1,0,2:T(2,128)(2,1)}, u32[]{:S(2)}) copy-start(bf16[1,128,462]{1,0,2:T(2,128)(2,1)} %get-tuple-element.6) | copy-start | bytes 354820
  58.5 13.0 %collective-permute-start.8 = (bf16[128,462]{0,1:T(8,128)(2,1)S(1)}, bf16[128,462]{0,1:T(8,128)(2,1)S(1)}, u32[]{:S(2)}, u32[]{:S(2)}) collective-permute-start(bf16[128,462]{0,1:T(8,128)(2,1)S(1)} %bitcast.381), channel_id=1, source_target_pairs={{0,480},{32,0},{64,32},{96,64},{128,96},{160,128},{192,160},{224,1... | collective-permute-start | bytes 354824 | tf_op jit(solution)/shard_map/ppermute | solution.py:75
  68.4 32.8 %copy-start.31 = (bf16[1,128,462]{1,0,2:T(2,128)(2,1)S(1)}, bf16[1,128,462]{1,0,2:T(2,128)(2,1)}, u32[]{:S(2)}) copy-start(bf16[1,128,462]{1,0,2:T(2,128)(2,1)} %get-tuple-element.5) | copy-start | bytes 354820
  69.5 7.5 %collective-permute-start.1 = (bf16[128,462]{0,1:T(8,128)(2,1)S(1)}, bf16[128,462]{0,1:T(8,128)(2,1)S(1)}, u32[]{:S(2)}, u32[]{:S(2)}) collective-permute-start(bf16[128,462]{0,1:T(8,128)(2,1)S(1)} %fusion.89), channel_id=1, source_target_pairs={{0,32},{32,64},{64,96},{96,128},{128,160},{160,192},{192,224},{224... | collective-permute-start | bytes 354824 | tf_op jit(solution)/shard_map/ppermute | solution.py:71
  71.5 34.7 %copy-start.30 = (bf16[1,128,462]{1,0,2:T(2,128)(2,1)S(1)}, bf16[1,128,462]{1,0,2:T(2,128)(2,1)}, u32[]{:S(2)}) copy-start(bf16[1,128,462]{1,0,2:T(2,128)(2,1)} %get-tuple-element.12) | copy-start | bytes 354820
  72.6 7.4 %collective-permute-start.9 = (bf16[128,462]{0,1:T(8,128)(2,1)S(1)}, bf16[128,462]{0,1:T(8,128)(2,1)S(1)}, u32[]{:S(2)}, u32[]{:S(2)}) collective-permute-start(bf16[128,462]{0,1:T(8,128)(2,1)S(1)} %fusion.82), channel_id=1, source_target_pairs={{0,480},{32,0},{64,32},{96,64},{128,96},{160,128},{192,160},{224,1... | collective-permute-start | bytes 354824 | tf_op jit(solution)/shard_map/ppermute | solution.py:75
  77.1 31.5 %copy-start.29 = (bf16[1,128,462]{1,0,2:T(2,128)(2,1)S(1)}, bf16[1,128,462]{1,0,2:T(2,128)(2,1)}, u32[]{:S(2)}) copy-start(bf16[1,128,462]{1,0,2:T(2,128)(2,1)} %get-tuple-element.19) | copy-start | bytes 354820
  78.1 7.5 %collective-permute-start.2 = (bf16[128,462]{0,1:T(8,128)(2,1)S(1)}, bf16[128,462]{0,1:T(8,128)(2,1)S(1)}, u32[]{:S(2)}, u32[]{:S(2)}) collective-permute-start(bf16[128,462]{0,1:T(8,128)(2,1)S(1)} %fusion.88), channel_id=1, source_target_pairs={{0,32},{32,64},{64,96},{96,128},{128,160},{160,192},{192,224},{224... | collective-permute-start | bytes 354824 | tf_op jit(solution)/shard_map/ppermute | solution.py:71
  81.0 6.6 %collective-permute-start.10 = (bf16[128,462]{0,1:T(8,128)(2,1)S(1)}, bf16[128,462]{0,1:T(8,128)(2,1)S(1)}, u32[]{:S(2)}, u32[]{:S(2)}) collective-permute-start(bf16[128,462]{0,1:T(8,128)(2,1)S(1)} %fusion.81), channel_id=1, source_target_pairs={{0,480},{32,0},{64,32},{96,64},{128,96},{160,128},{192,160},{224,1... | collective-permute-start | bytes 354824 | tf_op jit(solution)/shard_map/ppermute | solution.py:75
  85.7 6.8 %collective-permute-start.3 = (bf16[128,462]{0,1:T(8,128)(2,1)S(1)}, bf16[128,462]{0,1:T(8,128)(2,1)S(1)}, u32[]{:S(2)}, u32[]{:S(2)}) collective-permute-start(bf16[128,462]{0,1:T(8,128)(2,1)S(1)} %fusion.87), channel_id=1, source_target_pairs={{0,32},{32,64},{64,96},{96,128},{128,160},{160,192},{192,224},{224... | collective-permute-start | bytes 354824 | tf_op jit(solution)/shard_map/ppermute | solution.py:71
  87.6 6.8 %collective-permute-start.11 = (bf16[128,462]{0,1:T(8,128)(2,1)S(1)}, bf16[128,462]{0,1:T(8,128)(2,1)S(1)}, u32[]{:S(2)}, u32[]{:S(2)}) collective-permute-start(bf16[128,462]{0,1:T(8,128)(2,1)S(1)} %fusion.80), channel_id=1, source_target_pairs={{0,480},{32,0},{64,32},{96,64},{128,96},{160,128},{192,160},{224,1... | collective-permute-start | bytes 354824 | tf_op jit(solution)/shard_map/ppermute | solution.py:75
  92.5 6.8 %collective-permute-start.4 = (bf16[128,462]{0,1:T(8,128)(2,1)S(1)}, bf16[128,462]{0,1:T(8,128)(2,1)S(1)}, u32[]{:S(2)}, u32[]{:S(2)}) collective-permute-start(bf16[128,462]{0,1:T(8,128)(2,1)S(1)} %fusion.86), channel_id=1, source_target_pairs={{0,32},{32,64},{64,96},{96,128},{128,160},{160,192},{192,224},{224... | collective-permute-start | bytes 354824 | tf_op jit(solution)/shard_map/ppermute | solution.py:71
  94.5 6.8 %collective-permute-start.12 = (bf16[128,462]{0,1:T(8,128)(2,1)S(1)}, bf16[128,462]{0,1:T(8,128)(2,1)S(1)}, u32[]{:S(2)}, u32[]{:S(2)}) collective-permute-start(bf16[128,462]{0,1:T(8,128)(2,1)S(1)} %fusion.79), channel_id=1, source_target_pairs={{0,480},{32,0},{64,32},{96,64},{128,96},{160,128},{192,160},{224,1... | collective-permute-start | bytes 354824 | tf_op jit(solution)/shard_map/ppermute | solution.py:75
  99.3 6.8 %collective-permute-start.5 = (bf16[128,462]{0,1:T(8,128)(2,1)S(1)}, bf16[128,462]{0,1:T(8,128)(2,1)S(1)}, u32[]{:S(2)}, u32[]{:S(2)}) collective-permute-start(bf16[128,462]{0,1:T(8,128)(2,1)S(1)} %fusion.85), channel_id=1, source_target_pairs={{0,32},{32,64},{64,96},{96,128},{128,160},{160,192},{192,224},{224... | collective-permute-start | bytes 354824 | tf_op jit(solution)/shard_map/ppermute | solution.py:71
  101.3 7.3 %collective-permute-start.13 = (bf16[128,462]{0,1:T(8,128)(2,1)S(1)}, bf16[128,462]{0,1:T(8,128)(2,1)S(1)}, u32[]{:S(2)}, u32[]{:S(2)}) collective-permute-start(bf16[128,462]{0,1:T(8,128)(2,1)S(1)} %fusion.78), channel_id=1, source_target_pairs={{0,480},{32,0},{64,32},{96,64},{128,96},{160,128},{192,160},{224,1... | collective-permute-start | bytes 354824 | tf_op jit(solution)/shard_map/ppermute | solution.py:75
  106.2 8.1 %collective-permute-start.6 = (bf16[128,462]{0,1:T(8,128)(2,1)S(1)}, bf16[128,462]{0,1:T(8,128)(2,1)S(1)}, u32[]{:S(2)}, u32[]{:S(2)}) collective-permute-start(bf16[128,462]{0,1:T(8,128)(2,1)S(1)} %fusion.84), channel_id=1, source_target_pairs={{0,32},{32,64},{64,96},{96,128},{128,160},{160,192},{192,224},{224... | collective-permute-start | bytes 354824 | tf_op jit(solution)/shard_map/ppermute | solution.py:71
  109.2 8.1 %collective-permute-start.14 = (bf16[128,462]{0,1:T(8,128)(2,1)}, bf16[128,462]{0,1:T(8,128)(2,1)}, u32[]{:S(2)}, u32[]{:S(2)}) collective-permute-start(bf16[128,462]{0,1:T(8,128)(2,1)} %fusion.77), channel_id=1, source_target_pairs={{0,480},{32,0},{64,32},{96,64},{128,96},{160,128},{192,160},{224,1... | collective-permute-start | bytes 354824 | tf_op jit(solution)/shard_map/ppermute | solution.py:75
  115.0 8.0 %collective-permute-start.7 = (bf16[128,462]{0,1:T(8,128)(2,1)}, bf16[128,462]{0,1:T(8,128)(2,1)S(1)}, u32[]{:S(2)}, u32[]{:S(2)}) collective-permute-start(bf16[128,462]{0,1:T(8,128)(2,1)} %fusion.83), channel_id=1, source_target_pairs={{0,32},{32,64},{64,96},{96,128},{128,160},{160,192},{192,224},{224... | collective-permute-start | bytes 354824 | tf_op jit(solution)/shard_map/ppermute | solution.py:71
  116.9 25.8 %copy-start.1 = (bf16[512,462]{0,1:T(8,128)(2,1)S(1)}, bf16[512,462]{0,1:T(8,128)(2,1)}, u32[]{:S(2)}) copy-start(bf16[512,462]{0,1:T(8,128)(2,1)} %param.11) | copy-start | bytes 1419268
  124.9 15.8 %collective-permute-start.15 = (bf16[3,128,462]{1,2,0:T(8,128)(2,1)S(1)}, bf16[3,128,462]{1,2,0:T(8,128)(2,1)S(1)}, u32[]{:S(2)}, u32[]{:S(2)}) collective-permute-start(bf16[3,128,462]{1,2,0:T(8,128)(2,1)S(1)} %pad_maximum_fusion), channel_id=1, source_target_pairs={{0,32},{32,64},{64,96},{96,128},{128,160},{160,192},{192,224},{224... | collective-permute-start | bytes 1064456 | tf_op jit(solution)/shard_map/ppermute | solution.py:155
  126.8 8.9 %collective-permute-start.23 = (bf16[3,128,462]{1,2,0:T(8,128)(2,1)S(1)}, bf16[3,128,462]{1,2,0:T(8,128)(2,1)S(1)}, u32[]{:S(2)}, u32[]{:S(2)}) collective-permute-start(bf16[3,128,462]{1,2,0:T(8,128)(2,1)S(1)} %pad_maximum_fusion), channel_id=1, source_target_pairs={{0,480},{32,0},{64,32},{96,64},{128,96},{160,128},{192,160},{224,1... | collective-permute-start | bytes 1064456 | tf_op jit(solution)/shard_map/ppermute | solution.py:157
  135.7 10.9 %collective-permute-start.24 = (bf16[3,128,462]{1,2,0:T(8,128)(2,1)S(1)}, bf16[3,128,462]{1,2,0:T(8,128)(2,1)S(1)}, u32[]{:S(2)}, u32[]{:S(2)}) collective-permute-start(bf16[3,128,462]{1,2,0:T(8,128)(2,1)S(1)} %collective-permute-done.23), channel_id=1, source_target_pairs={{0,480},{32,0},{64,32},{96,64},{128,96},{160,128},{192,160},{224,1... | collective-permute-start | bytes 1064456 | tf_op jit(solution)/shard_map/ppermute | solution.py:157
  140.7 11.2 %collective-permute-start.16 = (bf16[3,128,462]{1,2,0:T(8,128)(2,1)S(1)}, bf16[3,128,462]{1,2,0:T(8,128)(2,1)S(1)}, u32[]{:S(2)}, u32[]{:S(2)}) collective-permute-start(bf16[3,128,462]{1,2,0:T(8,128)(2,1)S(1)} %collective-permute-done.15), channel_id=1, source_target_pairs={{0,32},{32,64},{64,96},{96,128},{128,160},{160,192},{192,224},{224... | collective-permute-start | bytes 1064456 | tf_op jit(solution)/shard_map/ppermute | solution.py:155
  146.6 10.3 %collective-permute-start.25 = (bf16[3,128,462]{1,2,0:T(8,128)(2,1)S(1)}, bf16[3,128,462]{1,2,0:T(8,128)(2,1)}, u32[]{:S(2)}, u32[]{:S(2)}) collective-permute-start(bf16[3,128,462]{1,2,0:T(8,128)(2,1)S(1)} %collective-permute-done.24), channel_id=1, source_target_pairs={{0,480},{32,0},{64,32},{96,64},{128,96},{160,128},{192,160},{224,1... | collective-permute-start | bytes 1064456 | tf_op jit(solution)/shard_map/ppermute | solution.py:157
  151.9 10.3 %collective-permute-start.17 = (bf16[3,128,462]{1,2,0:T(8,128)(2,1)S(1)}, bf16[3,128,462]{1,2,0:T(8,128)(2,1)}, u32[]{:S(2)}, u32[]{:S(2)}) collective-permute-start(bf16[3,128,462]{1,2,0:T(8,128)(2,1)S(1)} %collective-permute-done.16), channel_id=1, source_target_pairs={{0,32},{32,64},{64,96},{96,128},{128,160},{160,192},{192,224},{224... | collective-permute-start | bytes 1064456 | tf_op jit(solution)/shard_map/ppermute | solution.py:155
  156.9 25.0 %collective-permute-start.26 = (bf16[3,128,462]{1,2,0:T(8,128)(2,1)}, bf16[3,128,462]{1,2,0:T(8,128)(2,1)}, u32[]{:S(2)}, u32[]{:S(2)}) collective-permute-start(bf16[3,128,462]{1,2,0:T(8,128)(2,1)} %collective-permute-done.25), channel_id=1, source_target_pairs={{0,480},{32,0},{64,32},{96,64},{128,96},{160,128},{192,160},{224,1... | collective-permute-start | bytes 1064456 | tf_op jit(solution)/shard_map/ppermute | solution.py:157
  162.2 28.0 %collective-permute-start.18 = (bf16[3,128,462]{1,2,0:T(8,128)(2,1)}, bf16[3,128,462]{1,2,0:T(8,128)(2,1)}, u32[]{:S(2)}, u32[]{:S(2)}) collective-permute-start(bf16[3,128,462]{1,2,0:T(8,128)(2,1)} %collective-permute-done.17), channel_id=1, source_target_pairs={{0,32},{32,64},{64,96},{96,128},{128,160},{160,192},{192,224},{224... | collective-permute-start | bytes 1064456 | tf_op jit(solution)/shard_map/ppermute | solution.py:155
  181.9 11.4 %copy-start.7 = (f32[462,512]{1,0:T(8,128)S(1)}, f32[462,512]{1,0:T(8,128)}, u32[]{:S(2)}) copy-start(f32[462,512]{1,0:T(8,128)} %fusion.4) | copy-start | bytes 2838532
  181.9 16.2 %collective-permute-start.27 = (bf16[3,128,462]{1,2,0:T(8,128)(2,1)}, bf16[3,128,462]{1,2,0:T(8,128)(2,1)S(1)}, u32[]{:S(2)}, u32[]{:S(2)}) collective-permute-start(bf16[3,128,462]{1,2,0:T(8,128)(2,1)} %collective-permute-done.26), channel_id=1, source_target_pairs={{0,480},{32,0},{64,32},{96,64},{128,96},{160,128},{192,160},{224,1... | collective-permute-start | bytes 1064456 | tf_op jit(solution)/shard_map/ppermute | solution.py:157
  190.2 14.2 %collective-permute-start.19 = (bf16[3,128,462]{1,2,0:T(8,128)(2,1)}, bf16[3,128,462]{1,2,0:T(8,128)(2,1)S(1)}, u32[]{:S(2)}, u32[]{:S(2)}) collective-permute-start(bf16[3,128,462]{1,2,0:T(8,128)(2,1)} %collective-permute-done.18), channel_id=1, source_target_pairs={{0,32},{32,64},{64,96},{96,128},{128,160},{160,192},{192,224},{224... | collective-permute-start | bytes 1064456 | tf_op jit(solution)/shard_map/ppermute | solution.py:155
  198.1 12.0 %collective-permute-start.28 = (bf16[3,128,462]{1,2,0:T(8,128)(2,1)S(1)}, bf16[3,128,462]{1,2,0:T(8,128)(2,1)S(1)}, u32[]{:S(2)}, u32[]{:S(2)}) collective-permute-start(bf16[3,128,462]{1,2,0:T(8,128)(2,1)S(1)} %collective-permute-done.27), channel_id=1, source_target_pairs={{0,480},{32,0},{64,32},{96,64},{128,96},{160,128},{192,160},{224,1... | collective-permute-start | bytes 1064456 | tf_op jit(solution)/shard_map/ppermute | solution.py:157
  204.4 12.5 %collective-permute-start.20 = (bf16[3,128,462]{1,2,0:T(8,128)(2,1)S(1)}, bf16[3,128,462]{1,2,0:T(8,128)(2,1)S(1)}, u32[]{:S(2)}, u32[]{:S(2)}) collective-permute-start(bf16[3,128,462]{1,2,0:T(8,128)(2,1)S(1)} %collective-permute-done.19), channel_id=1, source_target_pairs={{0,32},{32,64},{64,96},{96,128},{128,160},{160,192},{192,224},{224... | collective-permute-start | bytes 1064456 | tf_op jit(solution)/shard_map/ppermute | solution.py:155
  210.1 18.9 %collective-permute-start.29 = (bf16[3,128,462]{1,2,0:T(8,128)(2,1)S(1)}, bf16[3,128,462]{1,2,0:T(8,128)(2,1)S(1)}, u32[]{:S(2)}, u32[]{:S(2)}) collective-permute-start(bf16[3,128,462]{1,2,0:T(8,128)(2,1)S(1)} %collective-permute-done.28), channel_id=1, source_target_pairs={{0,480},{32,0},{64,32},{96,64},{128,96},{160,128},{192,160},{224,1... | collective-permute-start | bytes 1064456 | tf_op jit(solution)/shard_map/ppermute | solution.py:157
  216.9 9.9 %collective-permute-start.21 = (bf16[3,128,462]{1,2,0:T(8,128)(2,1)S(1)}, bf16[3,128,462]{1,2,0:T(8,128)(2,1)S(1)}, u32[]{:S(2)}, u32[]{:S(2)}) collective-permute-start(bf16[3,128,462]{1,2,0:T(8,128)(2,1)S(1)} %collective-permute-done.20), channel_id=1, source_target_pairs={{0,32},{32,64},{64,96},{96,128},{128,160},{160,192},{192,224},{224... | collective-permute-start | bytes 1064456 | tf_op jit(solution)/shard_map/ppermute | solution.py:155
  226.8 9.3 %collective-permute-start.22 = (bf16[3,128,462]{1,2,0:T(8,128)(2,1)S(1)}, bf16[3,128,462]{1,2,0:T(8,128)(2,1)S(1)}, u32[]{:S(2)}, u32[]{:S(2)}) collective-permute-start(bf16[3,128,462]{1,2,0:T(8,128)(2,1)S(1)} %collective-permute-done.21), channel_id=1, source_target_pairs={{0,32},{32,64},{64,96},{96,128},{128,160},{160,192},{192,224},{224... | collective-permute-start | bytes 1064456 | tf_op jit(solution)/shard_map/ppermute | solution.py:155
  229.0 24.7 %copy-start.23 = (bf16[3,128,462]{1,2,0:T(8,128)(2,1)}, bf16[3,128,462]{1,2,0:T(8,128)(2,1)S(1)}, u32[]{:S(2)}) copy-start(bf16[3,128,462]{1,2,0:T(8,128)(2,1)S(1)} %collective-permute-done.29) | copy-start | bytes 1064452
  261.3 23.6 %copy-start.24 = (bf16[3,128,462]{1,2,0:T(8,128)(2,1)S(1)}, bf16[3,128,462]{1,2,0:T(8,128)(2,1)}, u32[]{:S(2)}) copy-start(bf16[3,128,462]{1,2,0:T(8,128)(2,1)} %copy-done.23) | copy-start | bytes 1064452
  261.3 52.4 %all-to-all-start.1 = ((bf16[32,64,512]{2,1,0:T(8,128)(2,1)}), bf16[32,64,512]{2,1,0:T(8,128)(2,1)}, u32[]{:S(2)}, u32[]{:S(2)}) async-start(bf16[32,64,512]{2,1,0:T(8,128)(2,1)} %broadcast_select_fusion), calls=%async_computation.1 | async-start | bytes 4194304 | tf_op jit(solution)/shard_map/all_to_all | solution.py:165
  (24 other events, 85.1 us)
Sparse Core Ops, SparseCore 0:
  24.2 61.8 all-gather.1

commit v5 on v3

--- a/solution.py
+++ b/solution.py
@@ -114,39 +114,43 @@
     )
 
 
-def shards(inputs, gate_pre, up_pre, w_gate, w_up, w_down, grad_out, n_row, n_x, n_y):
+def gather_col(x, n_col):
+    spread = jnp.broadcast_to(x[None], (n_col,) + x.shape)
+    return lax.all_to_all(spread, "col", 0, 0).reshape((n_col * x.shape[0],) + x.shape[1:])
+
+
+def shards(inputs, gate_pre, up_pre, w_gate, w_up, w_down, grad_out, n_row, n_col):
     tokens_row, hidden_units = gate_pre.shape
-    all_grad_out = lax.all_gather(grad_out, "col", axis=0, tiled=True)
-    all_inputs = lax.all_gather(inputs, "col", axis=0, tiled=True)
+    tokens_col, width = grad_out.shape
+    all_pre = lax.all_gather(jnp.stack([gate_pre, up_pre]), "row", axis=1, tiled=True)
+    all_grad_out = gather_col(grad_out, n_col)
+    all_inputs = gather_col(inputs, n_col)
     part = contract_cols(all_grad_out, w_down).astype(jnp.bfloat16)
     part = part.reshape((n_row, tokens_row, hidden_units))
-    own_grad = ring_reduce_scatter(part, "row", n_row, jnp.bfloat16)
-    own = jnp.stack(pointwise(gate_pre, up_pre, own_grad), axis=0)
-    gathered = ring_all_gather(own, "row", n_row).reshape(
-        (3, n_row * tokens_row, hidden_units)
+    own_grad = ring_reduce_scatter(part, "row", n_row, jnp.bfloat16).astype(jnp.bfloat16)
+    hidden_grad = ring_all_gather(own_grad[None], "row", n_row).reshape(
+        (n_row * tokens_row, hidden_units)
     )
-    hidden, gate_grad, up_grad = gathered[0], gathered[1], gathered[2]
+    hidden, gate_grad, up_grad = pointwise(
+        all_pre[0], all_pre[1], hidden_grad.astype(jnp.float32)
+    )
     grad_down = contract_rows(hidden, all_grad_out).astype(jnp.bfloat16)
     grad_gate = contract_rows(all_inputs, gate_grad).astype(jnp.bfloat16)
     grad_up = contract_rows(all_inputs, up_grad).astype(jnp.bfloat16)
-    grad_in_terms = (
+    terms = (
         contract_cols(gate_grad, w_gate) + contract_cols(up_grad, w_up)
     ).astype(jnp.bfloat16)
-    grad_in_terms = grad_in_terms.reshape((n_y * n_x, -1, grad_in_terms.shape[1]))
-    grad_in = col_reduce_scatter(grad_in_terms, n_x, n_y).astype(jnp.bfloat16)
+    received = lax.all_to_all(terms.reshape((n_col, tokens_col, width)), "col", 0, 0)
+    grad_in = received.astype(jnp.float32).sum(axis=0).astype(jnp.bfloat16)
     return (grad_in, grad_gate, grad_up, grad_down)
 
 
 def solution(mesh):
     n_row = mesh.shape["row"]
-    try:
-        n_x = len({d.coords[0] for d in mesh.devices.flat})
-    except AttributeError:
-        n_x = int(round((mesh.shape["col"] // 2) ** 0.5))
-    n_y = mesh.shape["col"] // (2 * n_x)
+    n_col = mesh.shape["col"]
 
     def body(*args):
-        return shards(*args, n_row=n_row, n_x=n_x, n_y=n_y)
+        return shards(*args, n_row=n_row, n_col=n_col)
 
     return jax.shard_map(
         body,

time: 346 us -> 281 us (0.81)
  waiting for transfers between devices: 131 us -> 62.6 us
  local copies, waits for them, and re-layouts: 39.9 us -> 24.9 us
  starting transfers between devices: 133 us -> 147 us
    all_gather x2 -> x1, waiting for transfers between devices: 67.5 us -> 0.01 us  [shards(): lax.all_gather(jnp.stack([gate_pre, up_pre]), 'row', axis=1, tiled=True)]
    all_to_all x0 -> x3, waiting for transfers between devices: none -> 41.4 us  [the longest x2 28 us: gather_col(): lax.all_to_all(spread, 'col', 0, 0)]
    all_to_all x0 -> x3, starting transfers between devices: none -> 38.3 us  [the longest x2 28.6 us: gather_col(): lax.all_to_all(spread, 'col', 0, 0)]
    ppermute x8, waiting for transfers between devices: 39.9 us -> 9.96 us  [ring_all_gather(): a = lax.ppermute(a, axis, up)]
    ppermute x1 -> x0, starting transfers between devices: 18.5 us -> none  [col_reduce_scatter(): summed = keep + lax.ppermute(give, 'col', pair)]
    unnamed x52, local copies, waits for them, and re-layouts: 25.4 us -> 12.8 us
    ppermute x12 -> x8, waiting for transfers between devices: 18.4 us -> 7.8 us  [ring_reduce_scatter(): a = lax.ppermute(a.astype(wire_dtype), axis, up).astype(jnp.float32)]
    ppermute x12 -> x8, starting transfers between devices: 26.2 us -> 16.1 us  [ring_reduce_scatter(): a = lax.ppermute(a.astype(wire_dtype), axis, up).astype(jnp.float32)]
  transfers between devices with their start and end apart: 39 -> 34, of which waited for: 21 -> 16; matrix products, arithmetic and copies ran while one was open for 15% -> 15% of each run, Pallas kernels for 0% -> 0%
where the time goes in v5:
time: 281 us; the launch traced here: 280 us
  starting transfers between devices  147 us (52%)
  waiting for transfers between devices  62.6 us (22%)
  local copies, waits for them, and re-layouts  24.9 us (9%)
  matrix products  16.4 us (6%)
  between operations  15 us (5%)
  other arithmetic  13.9 us (5%)
    ppermute x7, starting transfers between devices, ring_reduce_scatter(): b = lax.ppermute(b.astype(wire_dtype), axis, down).astype(jnp.float32)  39.5 us
    ppermute x7, starting transfers between devices, ring_all_gather(): b = lax.ppermute(b, axis, down)  34.4 us
    all_to_all x2, starting transfers between devices, gather_col(): lax.all_to_all(spread, 'col', 0, 0)  28.6 us
    all_to_all x2, waiting for transfers between devices, gather_col(): lax.all_to_all(spread, 'col', 0, 0)  28 us
    ppermute x8, starting transfers between devices, ring_all_gather(): a = lax.ppermute(a, axis, up)  18.6 us
    ppermute x8, starting transfers between devices, ring_reduce_scatter(): a = lax.ppermute(a.astype(wire_dtype), axis, up).astype(jnp.float32)  16.1 us
    all_to_all x1, waiting for transfers between devices, shards(): lax.all_to_all(terms.reshape((n_col, tokens_col, width)), 'col', 0, 0)  13.4 us
    unnamed x52, local copies, waits for them, and re-layouts  12.8 us
  transfers between devices with their start and end apart: 34, of which 16 were waited for; matrix products, arithmetic and copies ran while one was open for 15% of the time, Pallas kernels for 0%

profile of v5, /device:TPU:1, one launch (start us, length us, event | category | flops | bytes accessed | tf_op | source)
XLA Modules:
  0.0 279.9 jit_solution(17766005775549095391)
XLA Ops:
  7.2 2.5 broadcast_in_dim.36
  9.7 10.6 %all-to-all-start = ((bf16[32,64,512]{2,1,0:T(8,128)(2,1)}), bf16[32,64,512]{2,1,0:T(8,128)(2,1)S(1)}, u32[]{:S(2)}, u32[]{:S(2)}) async-start(bf16[32,64,512]{2,1,0:T(8,128)(2,1)} %broadcast_in_dim.36), calls=%async_computation | async-start | bytes 4194304 | tf_op jit(solution)/shard_map/all_to_all | solution.py:119
  20.6 28.0 %all-to-all-done = bf16[32,64,512]{2,1,0:T(8,128)(2,1)S(1)} async-done(((bf16[32,64,512]{2,1,0:T(8,128)(2,1)}), bf16[32,64,512]{2,1,0:T(8,128)(2,1)S(1)}, u32[]{:S(2)}, u32[]{:S(2)}) %all-to-all-start) | async-done | bytes 2097184 | tf_op jit(solution)/shard_map/all_to_all | solution.py:119
  50.9 4.7 %constant_dynamic-slice_fusion.15 = (bf16[1,128,462]{1,0,2:T(2,128)(2,1)S(1)}, bf16[1,128,462]{1,0,2:T(2,128)(2,1)S(1)}, bf16[1,128,462]{1,0,2:T(2,128)(2,1)S(1)...) fusion(bf16[16,128,462]{1,0,2:T(8,128)(2,1)S(1)} %slice_bitcast, ...), kind=kLoop, calls=%fused_computation.131 | loop fusion | bytes 3784768 | tf_op jit(solution)/shard_map/jit(dynamic_index_in_dim)/dynamic_slice | solution.py:64
  55.6 1.9 collective-permute-start
  58.3 9.5 %collective-permute-start.8 = (bf16[128,462]{0,1:T(8,128)(2,1)S(1)}, bf16[128,462]{0,1:T(8,128)(2,1)S(1)}, u32[]{:S(2)}, u32[]{:S(2)}) collective-permute-start(bf16[128,462]{0,1:T(8,128)(2,1)S(1)} %bitcast.262), channel_id=1, source_target_pairs={{0,480},{32,0},{64,32},{96,64},{128,96},{160,128},{192,160},{224,1... | collective-permute-start | bytes 354824 | tf_op jit(solution)/shard_map/ppermute | solution.py:75
  68.9 1.9 collective-permute-start.1
  71.8 4.6 %collective-permute-start.9 = (bf16[128,462]{0,1:T(8,128)(2,1)S(1)}, bf16[128,462]{0,1:T(8,128)(2,1)S(1)}, u32[]{:S(2)}, u32[]{:S(2)}) collective-permute-start(bf16[128,462]{0,1:T(8,128)(2,1)S(1)} %fusion.40), channel_id=1, source_target_pairs={{0,480},{32,0},{64,32},{96,64},{128,96},{160,128},{192,160},{224,1... | collective-permute-start | bytes 354824 | tf_op jit(solution)/shard_map/ppermute | solution.py:75
  77.3 1.9 collective-permute-start.2
  79.4 5.4 %collective-permute-start.10 = (bf16[128,462]{0,1:T(8,128)(2,1)S(1)}, bf16[128,462]{0,1:T(8,128)(2,1)S(1)}, u32[]{:S(2)}, u32[]{:S(2)}) collective-permute-start(bf16[128,462]{0,1:T(8,128)(2,1)S(1)} %fusion.39), channel_id=1, source_target_pairs={{0,480},{32,0},{64,32},{96,64},{128,96},{160,128},{192,160},{224,1... | collective-permute-start | bytes 354824 | tf_op jit(solution)/shard_map/ppermute | solution.py:75
  86.9 5.0 %collective-permute-start.11 = (bf16[128,462]{0,1:T(8,128)(2,1)S(1)}, bf16[128,462]{0,1:T(8,128)(2,1)S(1)}, u32[]{:S(2)}, u32[]{:S(2)}) collective-permute-start(bf16[128,462]{0,1:T(8,128)(2,1)S(1)} %fusion.38), channel_id=1, source_target_pairs={{0,480},{32,0},{64,32},{96,64},{128,96},{160,128},{192,160},{224,1... | collective-permute-start | bytes 354824 | tf_op jit(solution)/shard_map/ppermute | solution.py:75
  93.4 1.9 collective-permute-start.4
  95.4 4.6 %collective-permute-start.12 = (bf16[128,462]{0,1:T(8,128)(2,1)S(1)}, bf16[128,462]{0,1:T(8,128)(2,1)S(1)}, u32[]{:S(2)}, u32[]{:S(2)}) collective-permute-start(bf16[128,462]{0,1:T(8,128)(2,1)S(1)} %fusion.37), channel_id=1, source_target_pairs={{0,480},{32,0},{64,32},{96,64},{128,96},{160,128},{192,160},{224,1... | collective-permute-start | bytes 354824 | tf_op jit(solution)/shard_map/ppermute | solution.py:75
  100.3 2.7 collective-permute-start.5
  103.0 5.4 %collective-permute-start.13 = (bf16[128,462]{0,1:T(8,128)(2,1)S(1)}, bf16[128,462]{0,1:T(8,128)(2,1)S(1)}, u32[]{:S(2)}, u32[]{:S(2)}) collective-permute-start(bf16[128,462]{0,1:T(8,128)(2,1)S(1)} %fusion.36), channel_id=1, source_target_pairs={{0,480},{32,0},{64,32},{96,64},{128,96},{160,128},{192,160},{224,1... | collective-permute-start | bytes 354824 | tf_op jit(solution)/shard_map/ppermute | solution.py:75
  108.5 1.9 collective-permute-start.6
  111.6 5.0 %collective-permute-start.14 = (bf16[128,462]{0,1:T(8,128)(2,1)S(1)}, bf16[128,462]{0,1:T(8,128)(2,1)S(1)}, u32[]{:S(2)}, u32[]{:S(2)}) collective-permute-start(bf16[128,462]{0,1:T(8,128)(2,1)S(1)} %fusion.35), channel_id=1, source_target_pairs={{0,480},{32,0},{64,32},{96,64},{128,96},{160,128},{192,160},{224,1... | collective-permute-start | bytes 354824 | tf_op jit(solution)/shard_map/ppermute | solution.py:75
  117.6 1.9 collective-permute-start.7
  120.1 5.1 %collective-permute-done.7 = bf16[128,462]{0,1:T(8,128)(2,1)S(1)} collective-permute-done((bf16[128,462]{0,1:T(8,128)(2,1)S(1)}, bf16[128,462]{0,1:T(8,128)(2,1)S(1)}, u32[]{:S(2)}, u32[]{:S(2)}) %collective-permute-start.7) | collective-permute-done | bytes 118304 | tf_op jit(solution)/shard_map/ppermute | solution.py:71
  125.3 3.0 %collective-permute-start.15 = (bf16[1,128,462]{1,2,0:T(8,128)(2,1)S(1)}, bf16[1,128,462]{1,2,0:T(8,128)(2,1)S(1)}, u32[]{:S(2)}, u32[]{:S(2)}) collective-permute-start(bf16[1,128,462]{1,2,0:T(8,128)(2,1)S(1)} %bitcast.259), channel_id=1, source_target_pairs={{0,32},{32,64},{64,96},{96,128},{128,160},{160,192},{192,224},{224... | collective-permute-start | bytes 354824 | tf_op jit(solution)/shard_map/ppermute | solution.py:47
  128.3 6.3 %collective-permute-done.15 = bf16[1,128,462]{1,2,0:T(8,128)(2,1)S(1)} collective-permute-done((bf16[1,128,462]{1,2,0:T(8,128)(2,1)S(1)}, bf16[1,128,462]{1,2,0:T(8,128)(2,1)S(1)}, u32[]{:S(2)}, u32[]{:S(2)}) %collective-permute-start.15) | collective-permute-done | bytes 118304 | tf_op jit(solution)/shard_map/ppermute | solution.py:47
  134.6 2.4 collective-permute-start.16
  137.0 4.1 %collective-permute-start.23 = (bf16[1,128,462]{1,2,0:T(8,128)(2,1)S(1)}, bf16[1,128,462]{1,2,0:T(8,128)(2,1)S(1)}, u32[]{:S(2)}, u32[]{:S(2)}) collective-permute-start(bf16[1,128,462]{1,2,0:T(8,128)(2,1)S(1)} %bitcast.260), channel_id=1, source_target_pairs={{0,480},{32,0},{64,32},{96,64},{128,96},{160,128},{192,160},{224,1... | collective-permute-start | bytes 354824 | tf_op jit(solution)/shard_map/ppermute | solution.py:50
  141.4 3.5 %collective-permute-start.17 = (bf16[1,128,462]{1,2,0:T(8,128)(2,1)S(1)}, bf16[1,128,462]{1,2,0:T(8,128)(2,1)S(1)}, u32[]{:S(2)}, u32[]{:S(2)}) collective-permute-start(bf16[1,128,462]{1,2,0:T(8,128)(2,1)S(1)} %collective-permute-done.16), channel_id=1, source_target_pairs={{0,32},{32,64},{64,96},{96,128},{128,160},{160,192},{192,224},{224... | collective-permute-start | bytes 354824 | tf_op jit(solution)/shard_map/ppermute | solution.py:47
  144.9 5.2 %collective-permute-start.24 = (bf16[1,128,462]{1,2,0:T(8,128)(2,1)S(1)}, bf16[1,128,462]{1,2,0:T(8,128)(2,1)S(1)}, u32[]{:S(2)}, u32[]{:S(2)}) collective-permute-start(bf16[1,128,462]{1,2,0:T(8,128)(2,1)S(1)} %collective-permute-done.23), channel_id=1, source_target_pairs={{0,480},{32,0},{64,32},{96,64},{128,96},{160,128},{192,160},{224,1... | collective-permute-start | bytes 354824 | tf_op jit(solution)/shard_map/ppermute | solution.py:50
  150.2 3.0 %collective-permute-done.17 = bf16[1,128,462]{1,2,0:T(8,128)(2,1)S(1)} collective-permute-done((bf16[1,128,462]{1,2,0:T(8,128)(2,1)S(1)}, bf16[1,128,462]{1,2,0:T(8,128)(2,1)S(1)}, u32[]{:S(2)}, u32[]{:S(2)}) %collective-permute-start.17) | collective-permute-done | bytes 118304 | tf_op jit(solution)/shard_map/ppermute | solution.py:47
  155.1 4.6 %collective-permute-start.25 = (bf16[1,128,462]{1,2,0:T(8,128)(2,1)S(1)}, bf16[1,128,462]{1,2,0:T(8,128)(2,1)S(1)}, u32[]{:S(2)}, u32[]{:S(2)}) collective-permute-start(bf16[1,128,462]{1,2,0:T(8,128)(2,1)S(1)} %collective-permute-done.24), channel_id=1, source_target_pairs={{0,480},{32,0},{64,32},{96,64},{128,96},{160,128},{192,160},{224,1... | collective-permute-start | bytes 354824 | tf_op jit(solution)/shard_map/ppermute | solution.py:50
  160.0 2.1 collective-permute-start.19
  162.1 4.8 %collective-permute-start.26 = (bf16[1,128,462]{1,2,0:T(8,128)(2,1)S(1)}, bf16[1,128,462]{1,2,0:T(8,128)(2,1)S(1)}, u32[]{:S(2)}, u32[]{:S(2)}) collective-permute-start(bf16[1,128,462]{1,2,0:T(8,128)(2,1)S(1)} %collective-permute-done.25), channel_id=1, source_target_pairs={{0,480},{32,0},{64,32},{96,64},{128,96},{160,128},{192,160},{224,1... | collective-permute-start | bytes 354824 | tf_op jit(solution)/shard_map/ppermute | solution.py:50
  167.0 1.9 collective-permute-start.20
  170.5 18.0 %all-to-all-start.2 = ((bf16[32,64,512]{2,1,0:T(8,128)(2,1)}), bf16[32,64,512]{2,1,0:T(8,128)(2,1)}, u32[]{:S(2)}, u32[]{:S(2)}) async-start(bf16[32,64,512]{2,1,0:T(8,128)(2,1)} %broadcast_in_dim.41), calls=%async_computation.2 | async-start | bytes 4194304 | tf_op jit(solution)/shard_map/all_to_all | solution.py:119
  188.5 4.9 %collective-permute-start.27 = (bf16[1,128,462]{1,2,0:T(8,128)(2,1)S(1)}, bf16[1,128,462]{1,2,0:T(8,128)(2,1)S(1)}, u32[]{:S(2)}, u32[]{:S(2)}) collective-permute-start(bf16[1,128,462]{1,2,0:T(8,128)(2,1)S(1)} %collective-permute-done.26), channel_id=1, source_target_pairs={{0,480},{32,0},{64,32},{96,64},{128,96},{160,128},{192,160},{224,1... | collective-permute-start | bytes 354824 | tf_op jit(solution)/shard_map/ppermute | solution.py:50
  195.6 5.4 %collective-permute-start.28 = (bf16[1,128,462]{1,2,0:T(8,128)(2,1)S(1)}, bf16[1,128,462]{1,2,0:T(8,128)(2,1)S(1)}, u32[]{:S(2)}, u32[]{:S(2)}) collective-permute-start(bf16[1,128,462]{1,2,0:T(8,128)(2,1)S(1)} %collective-permute-done.27), channel_id=1, source_target_pairs={{0,480},{32,0},{64,32},{96,64},{128,96},{160,128},{192,160},{224,1... | collective-permute-start | bytes 354824 | tf_op jit(solution)/shard_map/ppermute | solution.py:50
  201.0 1.9 collective-permute-start.22
  203.0 5.4 %collective-permute-start.29 = (bf16[1,128,462]{1,2,0:T(8,128)(2,1)S(1)}, bf16[1,128,462]{1,2,0:T(8,128)(2,1)S(1)}, u32[]{:S(2)}, u32[]{:S(2)}) collective-permute-start(bf16[1,128,462]{1,2,0:T(8,128)(2,1)S(1)} %collective-permute-done.28), channel_id=1, source_target_pairs={{0,480},{32,0},{64,32},{96,64},{128,96},{160,128},{192,160},{224,1... | collective-permute-start | bytes 354824 | tf_op jit(solution)/shard_map/ppermute | solution.py:50
  211.3 2.4 gather_fusion
  216.3 3.0 %slice_convert_fusion = (f32[1,2048,462]{1,2,0:T(8,128)S(1)}, f32[1,2048,462]{1,2,0:T(8,128)S(1)}) fusion(bf16[2,2048,462]{1,2,0:T(8,128)(2,1)} %all-gather.2.cloned.1.call-done), kind=kLoop, calls=%fused_computation.32 | loop fusion | flops 1892352 | bytes 11354112 | tf_op jit(solution)/shard_map/convert_element_type | solution.py:21
  219.4 2.7 copy.134
  222.0 2.7 copy.135
  226.1 2.7 fusion.21
  228.8 3.3 %add_convert_fusion = bf16[2048,512]{1,0:T(8,128)(2,1)} fusion(f32[2048,512]{1,0:T(8,128)S(1)} %fusion.21, bf16[512,462]{0,1:T(8,128)(2,1)S(1)} %copy-done.12, bf16[2048,462]{0,1:T(8,128)(2,1)S(1)} %bitcast.255, pred[2048]{0:T(1024)(128)(4,1)S(1)} %broadcast_bitcast_fusion, bf16[2,2048,462]{1,2,0:T(8,128)(2,1)S(1)} %copy-done.2), kind=kOutput, calls=%fused_computation.5 | convolution fusion | flops 979496960 | bytes 10569728 | tf_op jit(solution)/shard_map/dot_general | solution.py:14
  232.2 9.7 %all-to-all-start.1 = ((bf16[32,64,512]{2,1,0:T(8,128)(2,1)}), bf16[32,64,512]{2,1,0:T(8,128)(2,1)}, u32[]{:S(2)}, u32[]{:S(2)}) async-start(bf16[32,64,512]{2,1,0:T(8,128)(2,1)} %bitcast.253), calls=%async_computation.1 | async-start | bytes 4194304 | tf_op jit(solution)/shard_map/all_to_all | solution.py:143
  241.9 4.3 %fusion.23 = (bf16[462,16,128]{2,1,0:T(8,128)(2,1)S(1)}, bf16[462,16,128]{2,1,0:T(8,128)(2,1)S(1)}) fusion(f32[464,16,128]{2,1,0:T(8,128)} %bitcast.244, bf16[16,128,462]{1,2,0:T(8,128)(2,1)S(1)} %gather_fusion, pred[16]{0:T(512)(128)(4,1)S(1)} %compare_and_fusion, f32[464,16,128]{2,1,0:T(8,128)} %bitcast.243), kind=kLoop, calls=%fused_computation.39 | loop fusion | flops 14192640 | bytes 13246480
  247.9 3.5 %fusion.32 = bf16[512,462]{0,1:T(8,128)(2,1)} fusion(bf16[2048,462]{0,1:T(8,128)(2,1)S(1)} %bitcast.256, bf16[2048,512]{1,0:T(8,128)(2,1)} %bitcast.46), kind=kOutput, calls=%fused_computation.50 | convolution fusion | flops 969120768 | bytes 4462592 | tf_op jit(solution)/shard_map/dot_general | solution.py:8
  251.4 3.7 %fusion.31 = bf16[512,462]{0,1:T(8,128)(2,1)} fusion(bf16[2048,462]{0,1:T(8,128)(2,1)S(1)} %bitcast.257, bf16[2048,512]{1,0:T(8,128)(2,1)} %bitcast.46), kind=kOutput, calls=%fused_computation.49 | convolution fusion | flops 969120768 | bytes 4462592 | tf_op jit(solution)/shard_map/dot_general | solution.py:8
  255.1 2.0 fusion.25
  257.1 13.4 %all-to-all-done.1 = bf16[32,64,512]{2,1,0:T(8,128)(2,1)} async-done(((bf16[32,64,512]{2,1,0:T(8,128)(2,1)}), bf16[32,64,512]{2,1,0:T(8,128)(2,1)}, u32[]{:S(2)}, u32[]{:S(2)}) %all-to-all-start.1) | async-done | bytes 2097184 | tf_op jit(solution)/shard_map/all_to_all | solution.py:143
  270.5 2.5 reduce_sum.12
  (108 shorter events, 27.6 us)
Async XLA Ops:
  7.2 217.6 %copy-start = (bf16[512,462]{0,1:T(8,128)(2,1)S(1)}, bf16[512,462]{0,1:T(8,128)(2,1)}, u32[]{:S(2)}) copy-start(bf16[512,462]{0,1:T(8,128)(2,1)} %param.10) | copy-start | bytes 1419268
  9.6 38.9 %copy-start.11 = (bf16[462,512]{1,0:T(8,128)(2,1)S(1)}, bf16[462,512]{1,0:T(8,128)(2,1)}, u32[]{:S(2)}) copy-start(bf16[462,512]{1,0:T(8,128)(2,1)} %param.12) | copy-start | bytes 1419268
  9.7 38.9 %all-to-all-start = ((bf16[32,64,512]{2,1,0:T(8,128)(2,1)}), bf16[32,64,512]{2,1,0:T(8,128)(2,1)S(1)}, u32[]{:S(2)}, u32[]{:S(2)}) async-start(bf16[32,64,512]{2,1,0:T(8,128)(2,1)} %broadcast_in_dim.36), calls=%async_computation | async-start | bytes 4194304 | tf_op jit(solution)/shard_map/all_to_all | solution.py:119
  20.3 196.1 %all-gather.2.cloned.1.call-start = ((), (), s32[]{:S(2)}) async-start(), calls=%async_computation.3 | async-start | bytes 4038656 | tf_op jit(solution)/shard_map/all_gather | solution.py:125
  48.6 1.4 copy-start.5
  50.8 6.7 %copy-start.8 = (bf16[128,462]{0,1:T(8,128)(2,1)S(1)}, bf16[128,462]{0,1:T(8,128)(2,1)}, u32[]{:S(2)}) copy-start(bf16[128,462]{0,1:T(8,128)(2,1)} %param.9) | copy-start | bytes 354820
  50.9 6.7 %copy-start.9 = (bf16[128,462]{0,1:T(8,128)(2,1)S(1)}, bf16[128,462]{0,1:T(8,128)(2,1)}, u32[]{:S(2)}) copy-start(bf16[128,462]{0,1:T(8,128)(2,1)} %param.8) | copy-start | bytes 354820
  55.6 12.2 %collective-permute-start = (bf16[128,462]{0,1:T(8,128)(2,1)S(1)}, bf16[128,462]{0,1:T(8,128)(2,1)}, u32[]{:S(2)}, u32[]{:S(2)}) collective-permute-start(bf16[128,462]{0,1:T(8,128)(2,1)S(1)} %bitcast.261), channel_id=1, source_target_pairs={{0,32},{32,64},{64,96},{96,128},{128,160},{160,192},{192,224},{224... | collective-permute-start | bytes 354824 | tf_op jit(solution)/shard_map/ppermute | solution.py:71
  58.3 12.5 %collective-permute-start.8 = (bf16[128,462]{0,1:T(8,128)(2,1)S(1)}, bf16[128,462]{0,1:T(8,128)(2,1)S(1)}, u32[]{:S(2)}, u32[]{:S(2)}) collective-permute-start(bf16[128,462]{0,1:T(8,128)(2,1)S(1)} %bitcast.262), channel_id=1, source_target_pairs={{0,480},{32,0},{64,32},{96,64},{128,96},{160,128},{192,160},{224,1... | collective-permute-start | bytes 354824 | tf_op jit(solution)/shard_map/ppermute | solution.py:75
  68.9 7.5 %collective-permute-start.1 = (bf16[128,462]{0,1:T(8,128)(2,1)S(1)}, bf16[128,462]{0,1:T(8,128)(2,1)S(1)}, u32[]{:S(2)}, u32[]{:S(2)}) collective-permute-start(bf16[128,462]{0,1:T(8,128)(2,1)S(1)} %fusion.47), channel_id=1, source_target_pairs={{0,32},{32,64},{64,96},{96,128},{128,160},{160,192},{192,224},{224... | collective-permute-start | bytes 354824 | tf_op jit(solution)/shard_map/ppermute | solution.py:71
  71.8 7.6 %collective-permute-start.9 = (bf16[128,462]{0,1:T(8,128)(2,1)S(1)}, bf16[128,462]{0,1:T(8,128)(2,1)S(1)}, u32[]{:S(2)}, u32[]{:S(2)}) collective-permute-start(bf16[128,462]{0,1:T(8,128)(2,1)S(1)} %fusion.40), channel_id=1, source_target_pairs={{0,480},{32,0},{64,32},{96,64},{128,96},{160,128},{192,160},{224,1... | collective-permute-start | bytes 354824 | tf_op jit(solution)/shard_map/ppermute | solution.py:75
  77.3 7.4 %collective-permute-start.2 = (bf16[128,462]{0,1:T(8,128)(2,1)S(1)}, bf16[128,462]{0,1:T(8,128)(2,1)S(1)}, u32[]{:S(2)}, u32[]{:S(2)}) collective-permute-start(bf16[128,462]{0,1:T(8,128)(2,1)S(1)} %fusion.46), channel_id=1, source_target_pairs={{0,32},{32,64},{64,96},{96,128},{128,160},{160,192},{192,224},{224... | collective-permute-start | bytes 354824 | tf_op jit(solution)/shard_map/ppermute | solution.py:71
  79.4 7.5 %collective-permute-start.10 = (bf16[128,462]{0,1:T(8,128)(2,1)S(1)}, bf16[128,462]{0,1:T(8,128)(2,1)S(1)}, u32[]{:S(2)}, u32[]{:S(2)}) collective-permute-start(bf16[128,462]{0,1:T(8,128)(2,1)S(1)} %fusion.39), channel_id=1, source_target_pairs={{0,480},{32,0},{64,32},{96,64},{128,96},{160,128},{192,160},{224,1... | collective-permute-start | bytes 354824 | tf_op jit(solution)/shard_map/ppermute | solution.py:75
  84.8 8.6 %collective-permute-start.3 = (bf16[128,462]{0,1:T(8,128)(2,1)S(1)}, bf16[128,462]{0,1:T(8,128)(2,1)S(1)}, u32[]{:S(2)}, u32[]{:S(2)}) collective-permute-start(bf16[128,462]{0,1:T(8,128)(2,1)S(1)} %fusion.45), channel_id=1, source_target_pairs={{0,32},{32,64},{64,96},{96,128},{128,160},{160,192},{192,224},{224... | collective-permute-start | bytes 354824 | tf_op jit(solution)/shard_map/ppermute | solution.py:71
  86.9 8.5 %collective-permute-start.11 = (bf16[128,462]{0,1:T(8,128)(2,1)S(1)}, bf16[128,462]{0,1:T(8,128)(2,1)S(1)}, u32[]{:S(2)}, u32[]{:S(2)}) collective-permute-start(bf16[128,462]{0,1:T(8,128)(2,1)S(1)} %fusion.38), channel_id=1, source_target_pairs={{0,480},{32,0},{64,32},{96,64},{128,96},{160,128},{192,160},{224,1... | collective-permute-start | bytes 354824 | tf_op jit(solution)/shard_map/ppermute | solution.py:75
  93.4 75.5 %copy-start.10 = (bf16[64,512]{1,0:T(8,128)(2,1)S(1)}, bf16[64,512]{1,0:T(8,128)(2,1)}, u32[]{:S(2)}) copy-start(bf16[64,512]{1,0:T(8,128)(2,1)} %param.7) | copy-start | bytes 196612
  93.4 6.8 %collective-permute-start.4 = (bf16[128,462]{0,1:T(8,128)(2,1)S(1)}, bf16[128,462]{0,1:T(8,128)(2,1)S(1)}, u32[]{:S(2)}, u32[]{:S(2)}) collective-permute-start(bf16[128,462]{0,1:T(8,128)(2,1)S(1)} %fusion.44), channel_id=1, source_target_pairs={{0,32},{32,64},{64,96},{96,128},{128,160},{160,192},{192,224},{224... | collective-permute-start | bytes 354824 | tf_op jit(solution)/shard_map/ppermute | solution.py:71
  95.4 7.6 %collective-permute-start.12 = (bf16[128,462]{0,1:T(8,128)(2,1)S(1)}, bf16[128,462]{0,1:T(8,128)(2,1)S(1)}, u32[]{:S(2)}, u32[]{:S(2)}) collective-permute-start(bf16[128,462]{0,1:T(8,128)(2,1)S(1)} %fusion.37), channel_id=1, source_target_pairs={{0,480},{32,0},{64,32},{96,64},{128,96},{160,128},{192,160},{224,1... | collective-permute-start | bytes 354824 | tf_op jit(solution)/shard_map/ppermute | solution.py:75
  100.3 8.2 %collective-permute-start.5 = (bf16[128,462]{0,1:T(8,128)(2,1)S(1)}, bf16[128,462]{0,1:T(8,128)(2,1)S(1)}, u32[]{:S(2)}, u32[]{:S(2)}) collective-permute-start(bf16[128,462]{0,1:T(8,128)(2,1)S(1)} %fusion.43), channel_id=1, source_target_pairs={{0,32},{32,64},{64,96},{96,128},{128,160},{160,192},{192,224},{224... | collective-permute-start | bytes 354824 | tf_op jit(solution)/shard_map/ppermute | solution.py:71
  103.0 8.6 %collective-permute-start.13 = (bf16[128,462]{0,1:T(8,128)(2,1)S(1)}, bf16[128,462]{0,1:T(8,128)(2,1)S(1)}, u32[]{:S(2)}, u32[]{:S(2)}) collective-permute-start(bf16[128,462]{0,1:T(8,128)(2,1)S(1)} %fusion.36), channel_id=1, source_target_pairs={{0,480},{32,0},{64,32},{96,64},{128,96},{160,128},{192,160},{224,1... | collective-permute-start | bytes 354824 | tf_op jit(solution)/shard_map/ppermute | solution.py:75
  108.5 9.1 %collective-permute-start.6 = (bf16[128,462]{0,1:T(8,128)(2,1)S(1)}, bf16[128,462]{0,1:T(8,128)(2,1)S(1)}, u32[]{:S(2)}, u32[]{:S(2)}) collective-permute-start(bf16[128,462]{0,1:T(8,128)(2,1)S(1)} %fusion.42), channel_id=1, source_target_pairs={{0,32},{32,64},{64,96},{96,128},{128,160},{160,192},{192,224},{224... | collective-permute-start | bytes 354824 | tf_op jit(solution)/shard_map/ppermute | solution.py:71
  111.6 8.5 %collective-permute-start.14 = (bf16[128,462]{0,1:T(8,128)(2,1)S(1)}, bf16[128,462]{0,1:T(8,128)(2,1)S(1)}, u32[]{:S(2)}, u32[]{:S(2)}) collective-permute-start(bf16[128,462]{0,1:T(8,128)(2,1)S(1)} %fusion.35), channel_id=1, source_target_pairs={{0,480},{32,0},{64,32},{96,64},{128,96},{160,128},{192,160},{224,1... | collective-permute-start | bytes 354824 | tf_op jit(solution)/shard_map/ppermute | solution.py:75
  117.6 7.6 %collective-permute-start.7 = (bf16[128,462]{0,1:T(8,128)(2,1)S(1)}, bf16[128,462]{0,1:T(8,128)(2,1)S(1)}, u32[]{:S(2)}, u32[]{:S(2)}) collective-permute-start(bf16[128,462]{0,1:T(8,128)(2,1)S(1)} %fusion.41), channel_id=1, source_target_pairs={{0,32},{32,64},{64,96},{96,128},{128,160},{160,192},{192,224},{224... | collective-permute-start | bytes 354824 | tf_op jit(solution)/shard_map/ppermute | solution.py:71
  125.3 9.4 %collective-permute-start.15 = (bf16[1,128,462]{1,2,0:T(8,128)(2,1)S(1)}, bf16[1,128,462]{1,2,0:T(8,128)(2,1)S(1)}, u32[]{:S(2)}, u32[]{:S(2)}) collective-permute-start(bf16[1,128,462]{1,2,0:T(8,128)(2,1)S(1)} %bitcast.259), channel_id=1, source_target_pairs={{0,32},{32,64},{64,96},{96,128},{128,160},{160,192},{192,224},{224... | collective-permute-start | bytes 354824 | tf_op jit(solution)/shard_map/ppermute | solution.py:47
  134.6 6.8 %collective-permute-start.16 = (bf16[1,128,462]{1,2,0:T(8,128)(2,1)S(1)}, bf16[1,128,462]{1,2,0:T(8,128)(2,1)S(1)}, u32[]{:S(2)}, u32[]{:S(2)}) collective-permute-start(bf16[1,128,462]{1,2,0:T(8,128)(2,1)S(1)} %collective-permute-done.15), channel_id=1, source_target_pairs={{0,32},{32,64},{64,96},{96,128},{128,160},{160,192},{192,224},{224... | collective-permute-start | bytes 354824 | tf_op jit(solution)/shard_map/ppermute | solution.py:47
  137.0 7.9 %collective-permute-start.23 = (bf16[1,128,462]{1,2,0:T(8,128)(2,1)S(1)}, bf16[1,128,462]{1,2,0:T(8,128)(2,1)S(1)}, u32[]{:S(2)}, u32[]{:S(2)}) collective-permute-start(bf16[1,128,462]{1,2,0:T(8,128)(2,1)S(1)} %bitcast.260), channel_id=1, source_target_pairs={{0,480},{32,0},{64,32},{96,64},{128,96},{160,128},{192,160},{224,1... | collective-permute-start | bytes 354824 | tf_op jit(solution)/shard_map/ppermute | solution.py:50
  141.4 11.8 %collective-permute-start.17 = (bf16[1,128,462]{1,2,0:T(8,128)(2,1)S(1)}, bf16[1,128,462]{1,2,0:T(8,128)(2,1)S(1)}, u32[]{:S(2)}, u32[]{:S(2)}) collective-permute-start(bf16[1,128,462]{1,2,0:T(8,128)(2,1)S(1)} %collective-permute-done.16), channel_id=1, source_target_pairs={{0,32},{32,64},{64,96},{96,128},{128,160},{160,192},{192,224},{224... | collective-permute-start | bytes 354824 | tf_op jit(solution)/shard_map/ppermute | solution.py:47
  144.9 10.2 %collective-permute-start.24 = (bf16[1,128,462]{1,2,0:T(8,128)(2,1)S(1)}, bf16[1,128,462]{1,2,0:T(8,128)(2,1)S(1)}, u32[]{:S(2)}, u32[]{:S(2)}) collective-permute-start(bf16[1,128,462]{1,2,0:T(8,128)(2,1)S(1)} %collective-permute-done.23), channel_id=1, source_target_pairs={{0,480},{32,0},{64,32},{96,64},{128,96},{160,128},{192,160},{224,1... | collective-permute-start | bytes 354824 | tf_op jit(solution)/shard_map/ppermute | solution.py:50
  153.2 6.8 %collective-permute-start.18 = (bf16[1,128,462]{1,2,0:T(8,128)(2,1)S(1)}, bf16[1,128,462]{1,2,0:T(8,128)(2,1)S(1)}, u32[]{:S(2)}, u32[]{:S(2)}) collective-permute-start(bf16[1,128,462]{1,2,0:T(8,128)(2,1)S(1)} %collective-permute-done.17), channel_id=1, source_target_pairs={{0,32},{32,64},{64,96},{96,128},{128,160},{160,192},{192,224},{224... | collective-permute-start | bytes 354824 | tf_op jit(solution)/shard_map/ppermute | solution.py:47
  155.1 7.0 %collective-permute-start.25 = (bf16[1,128,462]{1,2,0:T(8,128)(2,1)S(1)}, bf16[1,128,462]{1,2,0:T(8,128)(2,1)S(1)}, u32[]{:S(2)}, u32[]{:S(2)}) collective-permute-start(bf16[1,128,462]{1,2,0:T(8,128)(2,1)S(1)} %collective-permute-done.24), channel_id=1, source_target_pairs={{0,480},{32,0},{64,32},{96,64},{128,96},{160,128},{192,160},{224,1... | collective-permute-start | bytes 354824 | tf_op jit(solution)/shard_map/ppermute | solution.py:50
  160.0 7.0 %collective-permute-start.19 = (bf16[1,128,462]{1,2,0:T(8,128)(2,1)S(1)}, bf16[1,128,462]{1,2,0:T(8,128)(2,1)S(1)}, u32[]{:S(2)}, u32[]{:S(2)}) collective-permute-start(bf16[1,128,462]{1,2,0:T(8,128)(2,1)S(1)} %collective-permute-done.18), channel_id=1, source_target_pairs={{0,32},{32,64},{64,96},{96,128},{128,160},{160,192},{192,224},{224... | collective-permute-start | bytes 354824 | tf_op jit(solution)/shard_map/ppermute | solution.py:47
  162.1 26.4 %collective-permute-start.26 = (bf16[1,128,462]{1,2,0:T(8,128)(2,1)S(1)}, bf16[1,128,462]{1,2,0:T(8,128)(2,1)S(1)}, u32[]{:S(2)}, u32[]{:S(2)}) collective-permute-start(bf16[1,128,462]{1,2,0:T(8,128)(2,1)S(1)} %collective-permute-done.25), channel_id=1, source_target_pairs={{0,480},{32,0},{64,32},{96,64},{128,96},{160,128},{192,160},{224,1... | collective-permute-start | bytes 354824 | tf_op jit(solution)/shard_map/ppermute | solution.py:50
  167.0 26.4 %collective-permute-start.20 = (bf16[1,128,462]{1,2,0:T(8,128)(2,1)S(1)}, bf16[1,128,462]{1,2,0:T(8,128)(2,1)S(1)}, u32[]{:S(2)}, u32[]{:S(2)}) collective-permute-start(bf16[1,128,462]{1,2,0:T(8,128)(2,1)S(1)} %collective-permute-done.19), channel_id=1, source_target_pairs={{0,32},{32,64},{64,96},{96,128},{128,160},{160,192},{192,224},{224... | collective-permute-start | bytes 354824 | tf_op jit(solution)/shard_map/ppermute | solution.py:47
  170.5 61.7 %all-to-all-start.2 = ((bf16[32,64,512]{2,1,0:T(8,128)(2,1)}), bf16[32,64,512]{2,1,0:T(8,128)(2,1)}, u32[]{:S(2)}, u32[]{:S(2)}) async-start(bf16[32,64,512]{2,1,0:T(8,128)(2,1)} %broadcast_in_dim.41), calls=%async_computation.2 | async-start | bytes 4194304 | tf_op jit(solution)/shard_map/all_to_all | solution.py:119
  188.5 7.1 %collective-permute-start.27 = (bf16[1,128,462]{1,2,0:T(8,128)(2,1)S(1)}, bf16[1,128,462]{1,2,0:T(8,128)(2,1)S(1)}, u32[]{:S(2)}, u32[]{:S(2)}) collective-permute-start(bf16[1,128,462]{1,2,0:T(8,128)(2,1)S(1)} %collective-permute-done.26), channel_id=1, source_target_pairs={{0,480},{32,0},{64,32},{96,64},{128,96},{160,128},{192,160},{224,1... | collective-permute-start | bytes 354824 | tf_op jit(solution)/shard_map/ppermute | solution.py:50
  193.3 7.7 %collective-permute-start.21 = (bf16[1,128,462]{1,2,0:T(8,128)(2,1)S(1)}, bf16[1,128,462]{1,2,0:T(8,128)(2,1)S(1)}, u32[]{:S(2)}, u32[]{:S(2)}) collective-permute-start(bf16[1,128,462]{1,2,0:T(8,128)(2,1)S(1)} %collective-permute-done.20), channel_id=1, source_target_pairs={{0,32},{32,64},{64,96},{96,128},{128,160},{160,192},{192,224},{224... | collective-permute-start | bytes 354824 | tf_op jit(solution)/shard_map/ppermute | solution.py:47
  195.6 7.4 %collective-permute-start.28 = (bf16[1,128,462]{1,2,0:T(8,128)(2,1)S(1)}, bf16[1,128,462]{1,2,0:T(8,128)(2,1)S(1)}, u32[]{:S(2)}, u32[]{:S(2)}) collective-permute-start(bf16[1,128,462]{1,2,0:T(8,128)(2,1)S(1)} %collective-permute-done.27), channel_id=1, source_target_pairs={{0,480},{32,0},{64,32},{96,64},{128,96},{160,128},{192,160},{224,1... | collective-permute-start | bytes 354824 | tf_op jit(solution)/shard_map/ppermute | solution.py:50
  201.0 7.4 %collective-permute-start.22 = (bf16[1,128,462]{1,2,0:T(8,128)(2,1)S(1)}, bf16[1,128,462]{1,2,0:T(8,128)(2,1)S(1)}, u32[]{:S(2)}, u32[]{:S(2)}) collective-permute-start(bf16[1,128,462]{1,2,0:T(8,128)(2,1)S(1)} %collective-permute-done.21), channel_id=1, source_target_pairs={{0,32},{32,64},{64,96},{96,128},{128,160},{160,192},{192,224},{224... | collective-permute-start | bytes 354824 | tf_op jit(solution)/shard_map/ppermute | solution.py:47
  203.0 7.0 %collective-permute-start.29 = (bf16[1,128,462]{1,2,0:T(8,128)(2,1)S(1)}, bf16[1,128,462]{1,2,0:T(8,128)(2,1)S(1)}, u32[]{:S(2)}, u32[]{:S(2)}) collective-permute-start(bf16[1,128,462]{1,2,0:T(8,128)(2,1)S(1)} %collective-permute-done.28), channel_id=1, source_target_pairs={{0,480},{32,0},{64,32},{96,64},{128,96},{160,128},{192,160},{224,1... | collective-permute-start | bytes 354824 | tf_op jit(solution)/shard_map/ppermute | solution.py:50
  210.0 1.3 copy-start.4
  222.0 2.9 %copy-start.2 = (bf16[2,2048,462]{1,2,0:T(8,128)(2,1)S(1)}, bf16[2,2048,462]{1,2,0:T(8,128)(2,1)}, u32[]{:S(2)}) copy-start(bf16[2,2048,462]{1,2,0:T(8,128)(2,1)} %all-gather.2.cloned.1.call-done) | copy-start | bytes 11354116
  222.0 4.0 %copy-start.7 = (bf16[58,8,16,128]{3,1,2,0:T(8,128)(2,1)S(1)}, bf16[58,8,16,128]{3,1,2,0:T(8,128)(2,1)}, u32[]{:S(2)}) copy-start(bf16[58,8,16,128]{3,1,2,0:T(8,128)(2,1)} %copy.133) | copy-start | bytes 5701636
  226.1 2.7 copy-start.12
  232.2 38.3 %all-to-all-start.1 = ((bf16[32,64,512]{2,1,0:T(8,128)(2,1)}), bf16[32,64,512]{2,1,0:T(8,128)(2,1)}, u32[]{:S(2)}, u32[]{:S(2)}) async-start(bf16[32,64,512]{2,1,0:T(8,128)(2,1)} %bitcast.253), calls=%async_computation.1 | async-start | bytes 4194304 | tf_op jit(solution)/shard_map/all_to_all | solution.py:143
  251.4 3.7 %copy-start.3 = (bf16[2,2048,462]{1,2,0:T(8,128)(2,1)S(1)}, bf16[2,2048,462]{1,2,0:T(8,128)(2,1)}, u32[]{:S(2)}) copy-start(bf16[2,2048,462]{1,2,0:T(8,128)(2,1)} %all-gather.2.cloned.1.call-done) | copy-start | bytes 11354116
  251.4 3.7 %copy-start.6 = (bf16[32,64,512]{2,1,0:T(8,128)(2,1)S(1)}, bf16[32,64,512]{2,1,0:T(8,128)(2,1)}, u32[]{:S(2)}) copy-start(bf16[32,64,512]{2,1,0:T(8,128)(2,1)} %copy-done.5) | copy-start | bytes 6291460
  255.1 17.9 %copy-start.1 = (bf16[512,462]{0,1:T(8,128)(2,1)S(1)}, bf16[512,462]{0,1:T(8,128)(2,1)}, u32[]{:S(2)}) copy-start(bf16[512,462]{0,1:T(8,128)(2,1)} %param.10) | copy-start | bytes 1419268
Sparse Core Ops, SparseCore 0:
  58.4 93.7 all-gather.1

commit v6 on v5

--- a/solution.py
+++ b/solution.py
@@ -122,10 +122,15 @@
 def shards(inputs, gate_pre, up_pre, w_gate, w_up, w_down, grad_out, n_row, n_col):
     tokens_row, hidden_units = gate_pre.shape
     tokens_col, width = grad_out.shape
+    half = width // 2
+    out_a = gather_col(grad_out[:, :half], n_col)
+    out_b = lax.all_gather(grad_out[:, half:], "col", axis=0, tiled=True)
     all_pre = lax.all_gather(jnp.stack([gate_pre, up_pre]), "row", axis=1, tiled=True)
-    all_grad_out = gather_col(grad_out, n_col)
-    all_inputs = gather_col(inputs, n_col)
-    part = contract_cols(all_grad_out, w_down).astype(jnp.bfloat16)
+    all_inputs = lax.all_gather(inputs, "col", axis=0, tiled=True)
+    part = (
+        contract_cols(out_a, w_down[:, :half]) + contract_cols(out_b, w_down[:, half:])
+    ).astype(jnp.bfloat16)
+    all_grad_out = jnp.concatenate([out_a, out_b], axis=1)
     part = part.reshape((n_row, tokens_row, hidden_units))
     own_grad = ring_reduce_scatter(part, "row", n_row, jnp.bfloat16).astype(jnp.bfloat16)
     hidden_grad = ring_all_gather(own_grad[None], "row", n_row).reshape(

time: 281 us -> 298 us (1.060)
  waiting for transfers between devices: 62.6 us -> 104 us
  starting transfers between devices: 147 us -> 133 us
  local copies, waits for them, and re-layouts: 24.9 us -> 16.3 us
  other arithmetic: 13.9 us -> 8.39 us
    all_gather x0 -> x2, waiting for transfers between devices: none -> 57.2 us  [the longest x1 33.5 us: shards(): out_b = lax.all_gather(grad_out[:, half:], 'col', axis=0, tiled=True)]
    all_to_all x2 -> x1, starting transfers between devices: 28.6 us -> 10.4 us  [gather_col(): lax.all_to_all(spread, 'col', 0, 0)]
    all_to_all x1, starting transfers between devices: 9.74 us -> 23.7 us  [shards(): lax.all_to_all(terms.reshape((n_col, tokens_col, width)), 'col', 0, 0)]
    all_to_all x1, waiting for transfers between devices: 13.4 us -> 0.01 us  [shards(): lax.all_to_all(terms.reshape((n_col, tokens_col, width)), 'col', 0, 0)]
    all_to_all x2 -> x1, waiting for transfers between devices: 28 us -> 16.9 us  [gather_col(): lax.all_to_all(spread, 'col', 0, 0)]
    ppermute x7, starting transfers between devices: 39.5 us -> 31.6 us  [ring_reduce_scatter(): b = lax.ppermute(b.astype(wire_dtype), axis, down).astype(jnp.float32)]
    unnamed x52 -> x40, local copies, waits for them, and re-layouts: 12.8 us -> 5.76 us
    ppermute x8, waiting for transfers between devices: 7.8 us -> 14.4 us  [ring_reduce_scatter(): a = lax.ppermute(a.astype(wire_dtype), axis, up).astype(jnp.float32)]
  transfers between devices with their start and end apart: 34 -> 35, of which waited for: 16 -> 19; matrix products, arithmetic and copies ran while one was open for 15% -> 12% of each run, Pallas kernels for 0% -> 0%
where the time goes in v6:
time: 298 us; the launch traced here: 294 us
  starting transfers between devices  133 us (45%)
  waiting for transfers between devices  104 us (35%)
  matrix products  18.1 us (6%)
  local copies, waits for them, and re-layouts  16.3 us (5%)
  between operations  14.7 us (5%)
  other arithmetic  8.39 us (3%)
    all_gather x1, waiting for transfers between devices, shards(): out_b = lax.all_gather(grad_out[:, half:], 'col', axis=0, tiled=True)  33.5 us
    ppermute x7, starting transfers between devices, ring_all_gather(): b = lax.ppermute(b, axis, down)  33.3 us
    ppermute x7, starting transfers between devices, ring_reduce_scatter(): b = lax.ppermute(b.astype(wire_dtype), axis, down).astype(jnp.float32)  31.6 us
    all_gather x1, waiting for transfers between devices, shards(): all_inputs = lax.all_gather(inputs, 'col', axis=0, tiled=True)  23.7 us
    all_to_all x1, starting transfers between devices, shards(): lax.all_to_all(terms.reshape((n_col, tokens_col, width)), 'col', 0, 0)  23.7 us
    ppermute x8, starting transfers between devices, ring_reduce_scatter(): a = lax.ppermute(a.astype(wire_dtype), axis, up).astype(jnp.float32)  17.7 us
    all_to_all x1, waiting for transfers between devices, gather_col(): lax.all_to_all(spread, 'col', 0, 0)  16.9 us
    ppermute x8, starting transfers between devices, ring_all_gather(): a = lax.ppermute(a, axis, up)  16 us
  transfers between devices with their start and end apart: 35, of which 19 were waited for; matrix products, arithmetic and copies ran while one was open for 12% of the time, Pallas kernels for 0%

profile of v6, /device:TPU:1, one launch (start us, length us, event | category | flops | bytes accessed | tf_op | source)
XLA Modules:
  0.0 294.0 jit_solution(963662543818817152)
XLA Ops:
  11.6 10.4 %all-to-all-start = ((bf16[32,64,256]{2,1,0:T(8,128)(2,1)}), bf16[32,64,256]{2,1,0:T(8,128)(2,1)S(1)}, u32[]{:S(2)}, u32[]{:S(2)}) async-start(bf16[32,64,256]{2,1,0:T(8,128)(2,1)} %broadcast_in_dim.26), calls=%async_computation | async-start | bytes 2097152 | tf_op jit(solution)/shard_map/all_to_all | solution.py:119
  22.3 16.9 %all-to-all-done = bf16[32,64,256]{2,1,0:T(8,128)(2,1)S(1)} async-done(((bf16[32,64,256]{2,1,0:T(8,128)(2,1)}), bf16[32,64,256]{2,1,0:T(8,128)(2,1)S(1)}, u32[]{:S(2)}, u32[]{:S(2)}) %all-to-all-start) | async-done | bytes 1048608 | tf_op jit(solution)/shard_map/all_to_all | solution.py:119
  39.2 2.5 fusion.37
  41.7 33.5 %all-gather.4.cloned.1.call-done = bf16[2048,256]{1,0:T(8,128)(2,1)} async-done(((bf16[64,256]{1,0:T(8,128)(2,1)}), bf16[2048,256]{1,0:T(8,128)(2,1)}) %all-gather.4.cloned.1.call-update) | async-done | bytes 1048592 | tf_op jit(solution)/shard_map/all_gather | solution.py:127
  75.2 3.1 %add_convert_fusion.1 = bf16[2048,462]{0,1:T(8,128)(2,1)S(1)} fusion(f32[2048,462]{0,1:T(8,128)} %fusion.37, bf16[2048,256]{1,0:T(8,128)(2,1)} %all-gather.4.cloned.1.call-done, bf16[462,512]{1,0:T(8,128)(2,1)S(1)} %copy-done.7), kind=kOutput, calls=%fused_computation.17 | convolution fusion | flops 486334464 | bytes 6963200 | tf_op jit(solution)/shard_map/dot_general | solution.py:14
  79.2 4.6 %constant_dynamic-slice_fusion.15 = (bf16[1,128,462]{1,0,2:T(2,128)(2,1)S(1)}, bf16[1,128,462]{1,0,2:T(2,128)(2,1)S(1)}, bf16[1,128,462]{1,0,2:T(2,128)(2,1)S(1)...) fusion(bf16[16,128,462]{1,0,2:T(8,128)(2,1)S(1)} %slice_bitcast, ...), kind=kLoop, calls=%fused_computation.113 | loop fusion | bytes 3784768 | tf_op jit(solution)/shard_map/jit(dynamic_index_in_dim)/dynamic_slice | solution.py:64
  83.9 3.2 %collective-permute-start = (bf16[128,462]{0,1:T(8,128)(2,1)S(1)}, bf16[128,462]{0,1:T(8,128)(2,1)S(1)}, u32[]{:S(2)}, u32[]{:S(2)}) collective-permute-start(bf16[128,462]{0,1:T(8,128)(2,1)S(1)} %bitcast.183), channel_id=1, source_target_pairs={{0,32},{32,64},{64,96},{96,128},{128,160},{160,192},{192,224},{224... | collective-permute-start | bytes 354824 | tf_op jit(solution)/shard_map/ppermute | solution.py:71
  87.1 4.4 %collective-permute-start.8 = (bf16[128,462]{0,1:T(8,128)(2,1)S(1)}, bf16[128,462]{0,1:T(8,128)(2,1)S(1)}, u32[]{:S(2)}, u32[]{:S(2)}) collective-permute-start(bf16[128,462]{0,1:T(8,128)(2,1)S(1)} %bitcast.182), channel_id=1, source_target_pairs={{0,480},{32,0},{64,32},{96,64},{128,96},{160,128},{192,160},{224,1... | collective-permute-start | bytes 354824 | tf_op jit(solution)/shard_map/ppermute | solution.py:75
  92.9 1.9 collective-permute-start.1
  94.9 4.6 %collective-permute-start.9 = (bf16[128,462]{0,1:T(8,128)(2,1)S(1)}, bf16[128,462]{0,1:T(8,128)(2,1)S(1)}, u32[]{:S(2)}, u32[]{:S(2)}) collective-permute-start(bf16[128,462]{0,1:T(8,128)(2,1)S(1)} %fusion.26), channel_id=1, source_target_pairs={{0,480},{32,0},{64,32},{96,64},{128,96},{160,128},{192,160},{224,1... | collective-permute-start | bytes 354824 | tf_op jit(solution)/shard_map/ppermute | solution.py:75
  99.5 3.0 %collective-permute-done.1 = bf16[128,462]{0,1:T(8,128)(2,1)S(1)} collective-permute-done((bf16[128,462]{0,1:T(8,128)(2,1)S(1)}, bf16[128,462]{0,1:T(8,128)(2,1)S(1)}, u32[]{:S(2)}, u32[]{:S(2)}) %collective-permute-start.1) | collective-permute-done | bytes 118304 | tf_op jit(solution)/shard_map/ppermute | solution.py:71
  102.5 1.9 collective-permute-start.2
  104.5 4.6 %collective-permute-start.10 = (bf16[128,462]{0,1:T(8,128)(2,1)S(1)}, bf16[128,462]{0,1:T(8,128)(2,1)S(1)}, u32[]{:S(2)}, u32[]{:S(2)}) collective-permute-start(bf16[128,462]{0,1:T(8,128)(2,1)S(1)} %fusion.25), channel_id=1, source_target_pairs={{0,480},{32,0},{64,32},{96,64},{128,96},{160,128},{192,160},{224,1... | collective-permute-start | bytes 354824 | tf_op jit(solution)/shard_map/ppermute | solution.py:75
  109.5 1.9 collective-permute-start.3
  112.1 4.3 %collective-permute-start.11 = (bf16[128,462]{0,1:T(8,128)(2,1)S(1)}, bf16[128,462]{0,1:T(8,128)(2,1)S(1)}, u32[]{:S(2)}, u32[]{:S(2)}) collective-permute-start(bf16[128,462]{0,1:T(8,128)(2,1)S(1)} %fusion.24), channel_id=1, source_target_pairs={{0,480},{32,0},{64,32},{96,64},{128,96},{160,128},{192,160},{224,1... | collective-permute-start | bytes 354824 | tf_op jit(solution)/shard_map/ppermute | solution.py:75
  118.1 1.9 collective-permute-start.4
  120.1 4.6 %collective-permute-start.12 = (bf16[128,462]{0,1:T(8,128)(2,1)S(1)}, bf16[128,462]{0,1:T(8,128)(2,1)S(1)}, u32[]{:S(2)}, u32[]{:S(2)}) collective-permute-start(bf16[128,462]{0,1:T(8,128)(2,1)S(1)} %fusion.23), channel_id=1, source_target_pairs={{0,480},{32,0},{64,32},{96,64},{128,96},{160,128},{192,160},{224,1... | collective-permute-start | bytes 354824 | tf_op jit(solution)/shard_map/ppermute | solution.py:75
  125.0 3.0 %collective-permute-start.5 = (bf16[128,462]{0,1:T(8,128)(2,1)S(1)}, bf16[128,462]{0,1:T(8,128)(2,1)S(1)}, u32[]{:S(2)}, u32[]{:S(2)}) collective-permute-start(bf16[128,462]{0,1:T(8,128)(2,1)S(1)} %fusion.29), channel_id=1, source_target_pairs={{0,32},{32,64},{64,96},{96,128},{128,160},{160,192},{192,224},{224... | collective-permute-start | bytes 354824 | tf_op jit(solution)/shard_map/ppermute | solution.py:71
  129.1 5.1 %collective-permute-start.13 = (bf16[128,462]{0,1:T(8,128)(2,1)S(1)}, bf16[128,462]{0,1:T(8,128)(2,1)S(1)}, u32[]{:S(2)}, u32[]{:S(2)}) collective-permute-start(bf16[128,462]{0,1:T(8,128)(2,1)S(1)} %fusion.22), channel_id=1, source_target_pairs={{0,480},{32,0},{64,32},{96,64},{128,96},{160,128},{192,160},{224,1... | collective-permute-start | bytes 354824 | tf_op jit(solution)/shard_map/ppermute | solution.py:75
  134.2 1.9 collective-permute-start.6
  136.8 4.2 %collective-permute-start.14 = (bf16[128,462]{0,1:T(8,128)(2,1)S(1)}, bf16[128,462]{0,1:T(8,128)(2,1)S(1)}, u32[]{:S(2)}, u32[]{:S(2)}) collective-permute-start(bf16[128,462]{0,1:T(8,128)(2,1)S(1)} %fusion.21), channel_id=1, source_target_pairs={{0,480},{32,0},{64,32},{96,64},{128,96},{160,128},{192,160},{224,1... | collective-permute-start | bytes 354824 | tf_op jit(solution)/shard_map/ppermute | solution.py:75
  141.0 2.6 collective-permute-done.6
  143.6 1.9 collective-permute-start.7
  145.5 5.1 %collective-permute-done.7 = bf16[128,462]{0,1:T(8,128)(2,1)S(1)} collective-permute-done((bf16[128,462]{0,1:T(8,128)(2,1)S(1)}, bf16[128,462]{0,1:T(8,128)(2,1)S(1)}, u32[]{:S(2)}, u32[]{:S(2)}) %collective-permute-start.7) | collective-permute-done | bytes 118304 | tf_op jit(solution)/shard_map/ppermute | solution.py:71
  150.7 1.9 collective-permute-start.15
  152.6 6.5 %collective-permute-done.15 = bf16[1,128,462]{1,2,0:T(8,128)(2,1)S(1)} collective-permute-done((bf16[1,128,462]{1,2,0:T(8,128)(2,1)S(1)}, bf16[1,128,462]{1,2,0:T(8,128)(2,1)S(1)}, u32[]{:S(2)}, u32[]{:S(2)}) %collective-permute-start.15) | collective-permute-done | bytes 118304 | tf_op jit(solution)/shard_map/ppermute | solution.py:47
  159.2 1.9 collective-permute-start.16
  161.1 4.6 %collective-permute-start.23 = (bf16[1,128,462]{1,2,0:T(8,128)(2,1)S(1)}, bf16[1,128,462]{1,2,0:T(8,128)(2,1)S(1)}, u32[]{:S(2)}, u32[]{:S(2)}) collective-permute-start(bf16[1,128,462]{1,2,0:T(8,128)(2,1)S(1)} %bitcast.181), channel_id=1, source_target_pairs={{0,480},{32,0},{64,32},{96,64},{128,96},{160,128},{192,160},{224,1... | collective-permute-start | bytes 354824 | tf_op jit(solution)/shard_map/ppermute | solution.py:50
  165.7 2.6 collective-permute-done.16
  168.2 2.0 collective-permute-start.17
  170.3 4.4 %collective-permute-start.24 = (bf16[1,128,462]{1,2,0:T(8,128)(2,1)S(1)}, bf16[1,128,462]{1,2,0:T(8,128)(2,1)S(1)}, u32[]{:S(2)}, u32[]{:S(2)}) collective-permute-start(bf16[1,128,462]{1,2,0:T(8,128)(2,1)S(1)} %collective-permute-done.23), channel_id=1, source_target_pairs={{0,480},{32,0},{64,32},{96,64},{128,96},{160,128},{192,160},{224,1... | collective-permute-start | bytes 354824 | tf_op jit(solution)/shard_map/ppermute | solution.py:50
  175.1 2.4 collective-permute-start.18
  177.5 4.9 %collective-permute-start.25 = (bf16[1,128,462]{1,2,0:T(8,128)(2,1)S(1)}, bf16[1,128,462]{1,2,0:T(8,128)(2,1)S(1)}, u32[]{:S(2)}, u32[]{:S(2)}) collective-permute-start(bf16[1,128,462]{1,2,0:T(8,128)(2,1)S(1)} %collective-permute-done.24), channel_id=1, source_target_pairs={{0,480},{32,0},{64,32},{96,64},{128,96},{160,128},{192,160},{224,1... | collective-permute-start | bytes 354824 | tf_op jit(solution)/shard_map/ppermute | solution.py:50
  182.4 2.0 collective-permute-start.19
  184.5 4.7 %collective-permute-start.26 = (bf16[1,128,462]{1,2,0:T(8,128)(2,1)S(1)}, bf16[1,128,462]{1,2,0:T(8,128)(2,1)S(1)}, u32[]{:S(2)}, u32[]{:S(2)}) collective-permute-start(bf16[1,128,462]{1,2,0:T(8,128)(2,1)S(1)} %collective-permute-done.25), channel_id=1, source_target_pairs={{0,480},{32,0},{64,32},{96,64},{128,96},{160,128},{192,160},{224,1... | collective-permute-start | bytes 354824 | tf_op jit(solution)/shard_map/ppermute | solution.py:50
  192.5 4.8 %collective-permute-start.27 = (bf16[1,128,462]{1,2,0:T(8,128)(2,1)S(1)}, bf16[1,128,462]{1,2,0:T(8,128)(2,1)S(1)}, u32[]{:S(2)}, u32[]{:S(2)}) collective-permute-start(bf16[1,128,462]{1,2,0:T(8,128)(2,1)S(1)} %collective-permute-done.26), channel_id=1, source_target_pairs={{0,480},{32,0},{64,32},{96,64},{128,96},{160,128},{192,160},{224,1... | collective-permute-start | bytes 354824 | tf_op jit(solution)/shard_map/ppermute | solution.py:50
  200.0 4.8 %collective-permute-start.28 = (bf16[1,128,462]{1,2,0:T(8,128)(2,1)S(1)}, bf16[1,128,462]{1,2,0:T(8,128)(2,1)S(1)}, u32[]{:S(2)}, u32[]{:S(2)}) collective-permute-start(bf16[1,128,462]{1,2,0:T(8,128)(2,1)S(1)} %collective-permute-done.27), channel_id=1, source_target_pairs={{0,480},{32,0},{64,32},{96,64},{128,96},{160,128},{192,160},{224,1... | collective-permute-start | bytes 354824 | tf_op jit(solution)/shard_map/ppermute | solution.py:50
  204.8 1.9 collective-permute-start.22
  206.8 5.0 %collective-permute-start.29 = (bf16[1,128,462]{1,2,0:T(8,128)(2,1)S(1)}, bf16[1,128,462]{1,2,0:T(8,128)(2,1)S(1)}, u32[]{:S(2)}, u32[]{:S(2)}) collective-permute-start(bf16[1,128,462]{1,2,0:T(8,128)(2,1)S(1)} %collective-permute-done.28), channel_id=1, source_target_pairs={{0,480},{32,0},{64,32},{96,64},{128,96},{160,128},{192,160},{224,1... | collective-permute-start | bytes 354824 | tf_op jit(solution)/shard_map/ppermute | solution.py:50
  214.7 2.4 gather_fusion
  219.7 3.7 %fusion.3 = bf16[2048,462]{0,1:T(8,128)(2,1)S(1)} fusion(bf16[2,2048,462]{1,2,0:T(8,128)(2,1)} %all-gather.6.cloned.1.call-done, bf16[2048,462]{0,1:T(8,128)(2,1)} %bitcast.171, pred[2048]{0:T(1024)(128)(4,1)S(1)} %broadcast_bitcast_fusion), kind=kLoop, calls=%fused_computation.11 | loop fusion | flops 13246464 | bytes 7571456 | tf_op jit(solution)/shard_map/convert_element_type | solution.py:28
  226.2 3.4 %add_convert_fusion = bf16[2048,512]{1,0:T(8,128)(2,1)} fusion(f32[2048,512]{1,0:T(8,128)S(1)} %fusion.47, bf16[512,462]{0,1:T(8,128)(2,1)S(1)} %copy-done.9, bf16[2048,462]{0,1:T(8,128)(2,1)S(1)} %bitcast.172, pred[2048]{0:T(1024)(128)(4,1)S(1)} %broadcast_bitcast_fusion, bf16[2,2048,462]{1,2,0:T(8,128)(2,1)S(1)} %copy-done.3), kind=kOutput, calls=%fused_computation.7 | convolution fusion | flops 979496960 | bytes 10569728 | tf_op jit(solution)/shard_map/dot_general | solution.py:14
  229.6 23.7 %all-to-all-start.1 = ((bf16[32,64,512]{2,1,0:T(8,128)(2,1)}), bf16[32,64,512]{2,1,0:T(8,128)(2,1)}, u32[]{:S(2)}, u32[]{:S(2)}) async-start(bf16[32,64,512]{2,1,0:T(8,128)(2,1)} %bitcast.179), calls=%async_computation.1 | async-start | bytes 4194304 | tf_op jit(solution)/shard_map/all_to_all | solution.py:148
  253.3 23.7 %all-gather.8.cloned.1.call-done = bf16[2048,512]{1,0:T(8,128)(2,1)} async-done(((bf16[64,512]{1,0:T(8,128)(2,1)}), bf16[2048,512]{1,0:T(8,128)(2,1)}) %all-gather.8.cloned.1.call-update) | async-done | bytes 2097168 | tf_op jit(solution)/shard_map/all_gather | solution.py:129
  277.0 3.7 %fusion.19 = bf16[512,462]{0,1:T(8,128)(2,1)} fusion(bf16[2048,462]{0,1:T(8,128)(2,1)S(1)} %fusion.3, bf16[2048,512]{1,0:T(8,128)(2,1)} %all-gather.8.cloned.1.call-done), kind=kOutput, calls=%fused_computation.30 | convolution fusion | flops 969120768 | bytes 4462592 | tf_op jit(solution)/shard_map/dot_general | solution.py:8
  280.6 2.0 fusion.14
  282.8 2.1 fusion.20
  284.9 2.5 reduce_sum.12
  (100 shorter events, 26.4 us)
Async XLA Ops:
  7.2 216.3 %copy-start = (bf16[512,462]{0,1:T(8,128)(2,1)S(1)}, bf16[512,462]{0,1:T(8,128)(2,1)}, u32[]{:S(2)}) copy-start(bf16[512,462]{0,1:T(8,128)(2,1)} %param.10) | copy-start | bytes 1419268
  7.2 68.1 %all-gather.4.cloned.1.call-start = ((), (), s32[]{:S(2)}) async-start(), calls=%async_computation.2 | async-start | bytes 1081344 | tf_op jit(solution)/shard_map/all_gather | solution.py:127
  8.7 211.1 %all-gather.6.cloned.1.call-start = ((), (), s32[]{:S(2)}) async-start(), calls=%async_computation.3 | async-start | bytes 4038656 | tf_op jit(solution)/shard_map/all_gather | solution.py:128
  10.4 28.7 %copy-start.7 = (bf16[462,512]{1,0:T(8,128)(2,1)S(1)}, bf16[462,512]{1,0:T(8,128)(2,1)}, u32[]{:S(2)}) copy-start(bf16[462,512]{1,0:T(8,128)(2,1)} %param.12) | copy-start | bytes 1419268
  11.6 27.6 %all-to-all-start = ((bf16[32,64,256]{2,1,0:T(8,128)(2,1)}), bf16[32,64,256]{2,1,0:T(8,128)(2,1)S(1)}, u32[]{:S(2)}, u32[]{:S(2)}) async-start(bf16[32,64,256]{2,1,0:T(8,128)(2,1)} %broadcast_in_dim.26), calls=%async_computation | async-start | bytes 2097152 | tf_op jit(solution)/shard_map/all_to_all | solution.py:119
  22.0 255.0 %all-gather.8.cloned.1.call-start = ((), (), s32[]{:S(2)}) async-start(), calls=%async_computation.4 | async-start | bytes 2162688 | tf_op jit(solution)/shard_map/all_gather | solution.py:129
  83.9 9.0 %collective-permute-start = (bf16[128,462]{0,1:T(8,128)(2,1)S(1)}, bf16[128,462]{0,1:T(8,128)(2,1)S(1)}, u32[]{:S(2)}, u32[]{:S(2)}) collective-permute-start(bf16[128,462]{0,1:T(8,128)(2,1)S(1)} %bitcast.183), channel_id=1, source_target_pairs={{0,32},{32,64},{64,96},{96,128},{128,160},{160,192},{192,224},{224... | collective-permute-start | bytes 354824 | tf_op jit(solution)/shard_map/ppermute | solution.py:71
  87.1 7.7 %collective-permute-start.8 = (bf16[128,462]{0,1:T(8,128)(2,1)S(1)}, bf16[128,462]{0,1:T(8,128)(2,1)S(1)}, u32[]{:S(2)}, u32[]{:S(2)}) collective-permute-start(bf16[128,462]{0,1:T(8,128)(2,1)S(1)} %bitcast.182), channel_id=1, source_target_pairs={{0,480},{32,0},{64,32},{96,64},{128,96},{160,128},{192,160},{224,1... | collective-permute-start | bytes 354824 | tf_op jit(solution)/shard_map/ppermute | solution.py:75
  92.9 9.6 %collective-permute-start.1 = (bf16[128,462]{0,1:T(8,128)(2,1)S(1)}, bf16[128,462]{0,1:T(8,128)(2,1)S(1)}, u32[]{:S(2)}, u32[]{:S(2)}) collective-permute-start(bf16[128,462]{0,1:T(8,128)(2,1)S(1)} %fusion.33), channel_id=1, source_target_pairs={{0,32},{32,64},{64,96},{96,128},{128,160},{160,192},{192,224},{224... | collective-permute-start | bytes 354824 | tf_op jit(solution)/shard_map/ppermute | solution.py:71
  94.9 9.6 %collective-permute-start.9 = (bf16[128,462]{0,1:T(8,128)(2,1)S(1)}, bf16[128,462]{0,1:T(8,128)(2,1)S(1)}, u32[]{:S(2)}, u32[]{:S(2)}) collective-permute-start(bf16[128,462]{0,1:T(8,128)(2,1)S(1)} %fusion.26), channel_id=1, source_target_pairs={{0,480},{32,0},{64,32},{96,64},{128,96},{160,128},{192,160},{224,1... | collective-permute-start | bytes 354824 | tf_op jit(solution)/shard_map/ppermute | solution.py:75
  102.5 6.9 %collective-permute-start.2 = (bf16[128,462]{0,1:T(8,128)(2,1)S(1)}, bf16[128,462]{0,1:T(8,128)(2,1)S(1)}, u32[]{:S(2)}, u32[]{:S(2)}) collective-permute-start(bf16[128,462]{0,1:T(8,128)(2,1)S(1)} %fusion.32), channel_id=1, source_target_pairs={{0,32},{32,64},{64,96},{96,128},{128,160},{160,192},{192,224},{224... | collective-permute-start | bytes 354824 | tf_op jit(solution)/shard_map/ppermute | solution.py:71
  104.5 7.5 %collective-permute-start.10 = (bf16[128,462]{0,1:T(8,128)(2,1)S(1)}, bf16[128,462]{0,1:T(8,128)(2,1)S(1)}, u32[]{:S(2)}, u32[]{:S(2)}) collective-permute-start(bf16[128,462]{0,1:T(8,128)(2,1)S(1)} %fusion.25), channel_id=1, source_target_pairs={{0,480},{32,0},{64,32},{96,64},{128,96},{160,128},{192,160},{224,1... | collective-permute-start | bytes 354824 | tf_op jit(solution)/shard_map/ppermute | solution.py:75
  109.5 8.6 %collective-permute-start.3 = (bf16[128,462]{0,1:T(8,128)(2,1)S(1)}, bf16[128,462]{0,1:T(8,128)(2,1)S(1)}, u32[]{:S(2)}, u32[]{:S(2)}) collective-permute-start(bf16[128,462]{0,1:T(8,128)(2,1)S(1)} %fusion.31), channel_id=1, source_target_pairs={{0,32},{32,64},{64,96},{96,128},{128,160},{160,192},{192,224},{224... | collective-permute-start | bytes 354824 | tf_op jit(solution)/shard_map/ppermute | solution.py:71
  112.1 8.0 %collective-permute-start.11 = (bf16[128,462]{0,1:T(8,128)(2,1)S(1)}, bf16[128,462]{0,1:T(8,128)(2,1)S(1)}, u32[]{:S(2)}, u32[]{:S(2)}) collective-permute-start(bf16[128,462]{0,1:T(8,128)(2,1)S(1)} %fusion.24), channel_id=1, source_target_pairs={{0,480},{32,0},{64,32},{96,64},{128,96},{160,128},{192,160},{224,1... | collective-permute-start | bytes 354824 | tf_op jit(solution)/shard_map/ppermute | solution.py:75
  118.1 6.8 %collective-permute-start.4 = (bf16[128,462]{0,1:T(8,128)(2,1)S(1)}, bf16[128,462]{0,1:T(8,128)(2,1)S(1)}, u32[]{:S(2)}, u32[]{:S(2)}) collective-permute-start(bf16[128,462]{0,1:T(8,128)(2,1)S(1)} %fusion.30), channel_id=1, source_target_pairs={{0,32},{32,64},{64,96},{96,128},{128,160},{160,192},{192,224},{224... | collective-permute-start | bytes 354824 | tf_op jit(solution)/shard_map/ppermute | solution.py:71
  120.1 8.9 %collective-permute-start.12 = (bf16[128,462]{0,1:T(8,128)(2,1)S(1)}, bf16[128,462]{0,1:T(8,128)(2,1)S(1)}, u32[]{:S(2)}, u32[]{:S(2)}) collective-permute-start(bf16[128,462]{0,1:T(8,128)(2,1)S(1)} %fusion.23), channel_id=1, source_target_pairs={{0,480},{32,0},{64,32},{96,64},{128,96},{160,128},{192,160},{224,1... | collective-permute-start | bytes 354824 | tf_op jit(solution)/shard_map/ppermute | solution.py:75
  125.0 9.2 %collective-permute-start.5 = (bf16[128,462]{0,1:T(8,128)(2,1)S(1)}, bf16[128,462]{0,1:T(8,128)(2,1)S(1)}, u32[]{:S(2)}, u32[]{:S(2)}) collective-permute-start(bf16[128,462]{0,1:T(8,128)(2,1)S(1)} %fusion.29), channel_id=1, source_target_pairs={{0,32},{32,64},{64,96},{96,128},{128,160},{160,192},{192,224},{224... | collective-permute-start | bytes 354824 | tf_op jit(solution)/shard_map/ppermute | solution.py:71
  129.1 7.7 %collective-permute-start.13 = (bf16[128,462]{0,1:T(8,128)(2,1)S(1)}, bf16[128,462]{0,1:T(8,128)(2,1)S(1)}, u32[]{:S(2)}, u32[]{:S(2)}) collective-permute-start(bf16[128,462]{0,1:T(8,128)(2,1)S(1)} %fusion.22), channel_id=1, source_target_pairs={{0,480},{32,0},{64,32},{96,64},{128,96},{160,128},{192,160},{224,1... | collective-permute-start | bytes 354824 | tf_op jit(solution)/shard_map/ppermute | solution.py:75
  134.2 9.4 %collective-permute-start.6 = (bf16[128,462]{0,1:T(8,128)(2,1)S(1)}, bf16[128,462]{0,1:T(8,128)(2,1)S(1)}, u32[]{:S(2)}, u32[]{:S(2)}) collective-permute-start(bf16[128,462]{0,1:T(8,128)(2,1)S(1)} %fusion.28), channel_id=1, source_target_pairs={{0,32},{32,64},{64,96},{96,128},{128,160},{160,192},{192,224},{224... | collective-permute-start | bytes 354824 | tf_op jit(solution)/shard_map/ppermute | solution.py:71
  136.8 8.7 %collective-permute-start.14 = (bf16[128,462]{0,1:T(8,128)(2,1)S(1)}, bf16[128,462]{0,1:T(8,128)(2,1)S(1)}, u32[]{:S(2)}, u32[]{:S(2)}) collective-permute-start(bf16[128,462]{0,1:T(8,128)(2,1)S(1)} %fusion.21), channel_id=1, source_target_pairs={{0,480},{32,0},{64,32},{96,64},{128,96},{160,128},{192,160},{224,1... | collective-permute-start | bytes 354824 | tf_op jit(solution)/shard_map/ppermute | solution.py:75
  143.6 7.1 %collective-permute-start.7 = (bf16[128,462]{0,1:T(8,128)(2,1)S(1)}, bf16[128,462]{0,1:T(8,128)(2,1)S(1)}, u32[]{:S(2)}, u32[]{:S(2)}) collective-permute-start(bf16[128,462]{0,1:T(8,128)(2,1)S(1)} %fusion.27), channel_id=1, source_target_pairs={{0,32},{32,64},{64,96},{96,128},{128,160},{160,192},{192,224},{224... | collective-permute-start | bytes 354824 | tf_op jit(solution)/shard_map/ppermute | solution.py:71
  150.7 8.4 %collective-permute-start.15 = (bf16[1,128,462]{1,2,0:T(8,128)(2,1)S(1)}, bf16[1,128,462]{1,2,0:T(8,128)(2,1)S(1)}, u32[]{:S(2)}, u32[]{:S(2)}) collective-permute-start(bf16[1,128,462]{1,2,0:T(8,128)(2,1)S(1)} %bitcast.180), channel_id=1, source_target_pairs={{0,32},{32,64},{64,96},{96,128},{128,160},{160,192},{192,224},{224... | collective-permute-start | bytes 354824 | tf_op jit(solution)/shard_map/ppermute | solution.py:47
  159.2 9.1 %collective-permute-start.16 = (bf16[1,128,462]{1,2,0:T(8,128)(2,1)S(1)}, bf16[1,128,462]{1,2,0:T(8,128)(2,1)S(1)}, u32[]{:S(2)}, u32[]{:S(2)}) collective-permute-start(bf16[1,128,462]{1,2,0:T(8,128)(2,1)S(1)} %collective-permute-done.15), channel_id=1, source_target_pairs={{0,32},{32,64},{64,96},{96,128},{128,160},{160,192},{192,224},{224... | collective-permute-start | bytes 354824 | tf_op jit(solution)/shard_map/ppermute | solution.py:47
  161.1 9.2 %collective-permute-start.23 = (bf16[1,128,462]{1,2,0:T(8,128)(2,1)S(1)}, bf16[1,128,462]{1,2,0:T(8,128)(2,1)S(1)}, u32[]{:S(2)}, u32[]{:S(2)}) collective-permute-start(bf16[1,128,462]{1,2,0:T(8,128)(2,1)S(1)} %bitcast.181), channel_id=1, source_target_pairs={{0,480},{32,0},{64,32},{96,64},{128,96},{160,128},{192,160},{224,1... | collective-permute-start | bytes 354824 | tf_op jit(solution)/shard_map/ppermute | solution.py:50
  168.2 6.9 %collective-permute-start.17 = (bf16[1,128,462]{1,2,0:T(8,128)(2,1)S(1)}, bf16[1,128,462]{1,2,0:T(8,128)(2,1)S(1)}, u32[]{:S(2)}, u32[]{:S(2)}) collective-permute-start(bf16[1,128,462]{1,2,0:T(8,128)(2,1)S(1)} %collective-permute-done.16), channel_id=1, source_target_pairs={{0,32},{32,64},{64,96},{96,128},{128,160},{160,192},{192,224},{224... | collective-permute-start | bytes 354824 | tf_op jit(solution)/shard_map/ppermute | solution.py:47
  170.3 7.2 %collective-permute-start.24 = (bf16[1,128,462]{1,2,0:T(8,128)(2,1)S(1)}, bf16[1,128,462]{1,2,0:T(8,128)(2,1)S(1)}, u32[]{:S(2)}, u32[]{:S(2)}) collective-permute-start(bf16[1,128,462]{1,2,0:T(8,128)(2,1)S(1)} %collective-permute-done.23), channel_id=1, source_target_pairs={{0,480},{32,0},{64,32},{96,64},{128,96},{160,128},{192,160},{224,1... | collective-permute-start | bytes 354824 | tf_op jit(solution)/shard_map/ppermute | solution.py:50
  175.1 7.3 %collective-permute-start.18 = (bf16[1,128,462]{1,2,0:T(8,128)(2,1)S(1)}, bf16[1,128,462]{1,2,0:T(8,128)(2,1)S(1)}, u32[]{:S(2)}, u32[]{:S(2)}) collective-permute-start(bf16[1,128,462]{1,2,0:T(8,128)(2,1)S(1)} %collective-permute-done.17), channel_id=1, source_target_pairs={{0,32},{32,64},{64,96},{96,128},{128,160},{160,192},{192,224},{224... | collective-permute-start | bytes 354824 | tf_op jit(solution)/shard_map/ppermute | solution.py:47
  177.5 6.9 %collective-permute-start.25 = (bf16[1,128,462]{1,2,0:T(8,128)(2,1)S(1)}, bf16[1,128,462]{1,2,0:T(8,128)(2,1)S(1)}, u32[]{:S(2)}, u32[]{:S(2)}) collective-permute-start(bf16[1,128,462]{1,2,0:T(8,128)(2,1)S(1)} %collective-permute-done.24), channel_id=1, source_target_pairs={{0,480},{32,0},{64,32},{96,64},{128,96},{160,128},{192,160},{224,1... | collective-permute-start | bytes 354824 | tf_op jit(solution)/shard_map/ppermute | solution.py:50
  182.4 8.0 %collective-permute-start.19 = (bf16[1,128,462]{1,2,0:T(8,128)(2,1)S(1)}, bf16[1,128,462]{1,2,0:T(8,128)(2,1)S(1)}, u32[]{:S(2)}, u32[]{:S(2)}) collective-permute-start(bf16[1,128,462]{1,2,0:T(8,128)(2,1)S(1)} %collective-permute-done.18), channel_id=1, source_target_pairs={{0,32},{32,64},{64,96},{96,128},{128,160},{160,192},{192,224},{224... | collective-permute-start | bytes 354824 | tf_op jit(solution)/shard_map/ppermute | solution.py:47
  184.5 8.0 %collective-permute-start.26 = (bf16[1,128,462]{1,2,0:T(8,128)(2,1)S(1)}, bf16[1,128,462]{1,2,0:T(8,128)(2,1)S(1)}, u32[]{:S(2)}, u32[]{:S(2)}) collective-permute-start(bf16[1,128,462]{1,2,0:T(8,128)(2,1)S(1)} %collective-permute-done.25), channel_id=1, source_target_pairs={{0,480},{32,0},{64,32},{96,64},{128,96},{160,128},{192,160},{224,1... | collective-permute-start | bytes 354824 | tf_op jit(solution)/shard_map/ppermute | solution.py:50
  190.5 7.5 %collective-permute-start.20 = (bf16[1,128,462]{1,2,0:T(8,128)(2,1)S(1)}, bf16[1,128,462]{1,2,0:T(8,128)(2,1)S(1)}, u32[]{:S(2)}, u32[]{:S(2)}) collective-permute-start(bf16[1,128,462]{1,2,0:T(8,128)(2,1)S(1)} %collective-permute-done.19), channel_id=1, source_target_pairs={{0,32},{32,64},{64,96},{96,128},{128,160},{160,192},{192,224},{224... | collective-permute-start | bytes 354824 | tf_op jit(solution)/shard_map/ppermute | solution.py:47
  192.5 7.5 %collective-permute-start.27 = (bf16[1,128,462]{1,2,0:T(8,128)(2,1)S(1)}, bf16[1,128,462]{1,2,0:T(8,128)(2,1)S(1)}, u32[]{:S(2)}, u32[]{:S(2)}) collective-permute-start(bf16[1,128,462]{1,2,0:T(8,128)(2,1)S(1)} %collective-permute-done.26), channel_id=1, source_target_pairs={{0,480},{32,0},{64,32},{96,64},{128,96},{160,128},{192,160},{224,1... | collective-permute-start | bytes 354824 | tf_op jit(solution)/shard_map/ppermute | solution.py:50
  198.0 6.8 %collective-permute-start.21 = (bf16[1,128,462]{1,2,0:T(8,128)(2,1)S(1)}, bf16[1,128,462]{1,2,0:T(8,128)(2,1)S(1)}, u32[]{:S(2)}, u32[]{:S(2)}) collective-permute-start(bf16[1,128,462]{1,2,0:T(8,128)(2,1)S(1)} %collective-permute-done.20), channel_id=1, source_target_pairs={{0,32},{32,64},{64,96},{96,128},{128,160},{160,192},{192,224},{224... | collective-permute-start | bytes 354824 | tf_op jit(solution)/shard_map/ppermute | solution.py:47
  200.0 6.8 %collective-permute-start.28 = (bf16[1,128,462]{1,2,0:T(8,128)(2,1)S(1)}, bf16[1,128,462]{1,2,0:T(8,128)(2,1)S(1)}, u32[]{:S(2)}, u32[]{:S(2)}) collective-permute-start(bf16[1,128,462]{1,2,0:T(8,128)(2,1)S(1)} %collective-permute-done.27), channel_id=1, source_target_pairs={{0,480},{32,0},{64,32},{96,64},{128,96},{160,128},{192,160},{224,1... | collective-permute-start | bytes 354824 | tf_op jit(solution)/shard_map/ppermute | solution.py:50
  204.8 7.0 %collective-permute-start.22 = (bf16[1,128,462]{1,2,0:T(8,128)(2,1)S(1)}, bf16[1,128,462]{1,2,0:T(8,128)(2,1)S(1)}, u32[]{:S(2)}, u32[]{:S(2)}) collective-permute-start(bf16[1,128,462]{1,2,0:T(8,128)(2,1)S(1)} %collective-permute-done.21), channel_id=1, source_target_pairs={{0,32},{32,64},{64,96},{96,128},{128,160},{160,192},{192,224},{224... | collective-permute-start | bytes 354824 | tf_op jit(solution)/shard_map/ppermute | solution.py:47
  206.8 6.6 %collective-permute-start.29 = (bf16[1,128,462]{1,2,0:T(8,128)(2,1)S(1)}, bf16[1,128,462]{1,2,0:T(8,128)(2,1)S(1)}, u32[]{:S(2)}, u32[]{:S(2)}) collective-permute-start(bf16[1,128,462]{1,2,0:T(8,128)(2,1)S(1)} %collective-permute-done.28), channel_id=1, source_target_pairs={{0,480},{32,0},{64,32},{96,64},{128,96},{160,128},{192,160},{224,1... | collective-permute-start | bytes 354824 | tf_op jit(solution)/shard_map/ppermute | solution.py:50
  213.4 1.3 copy-start.5
  223.4 1.5 copy-start.1
  223.5 2.6 copy-start.3
  223.5 2.7 copy-start.9
  229.6 55.3 %all-to-all-start.1 = ((bf16[32,64,512]{2,1,0:T(8,128)(2,1)}), bf16[32,64,512]{2,1,0:T(8,128)(2,1)}, u32[]{:S(2)}, u32[]{:S(2)}) async-start(bf16[32,64,512]{2,1,0:T(8,128)(2,1)} %bitcast.179), calls=%async_computation.1 | async-start | bytes 4194304 | tf_op jit(solution)/shard_map/all_to_all | solution.py:148
  277.0 3.7 %copy-start.4 = (bf16[2,2048,462]{1,2,0:T(8,128)(2,1)S(1)}, bf16[2,2048,462]{1,2,0:T(8,128)(2,1)}, u32[]{:S(2)}) copy-start(bf16[2,2048,462]{1,2,0:T(8,128)(2,1)} %all-gather.6.cloned.1.call-done) | copy-start | bytes 11354116
  277.0 3.7 %copy-start.6 = (bf16[2048,256]{1,0:T(8,128)(2,1)S(1)}, bf16[2048,256]{1,0:T(8,128)(2,1)}, u32[]{:S(2)}) copy-start(bf16[2048,256]{1,0:T(8,128)(2,1)} %all-gather.4.cloned.1.call-done) | copy-start | bytes 3145732
  280.6 2.0 copy-start.2
  280.6 2.2 copy-start.8
Sparse Core Ops, SparseCore 0:
  11.7 63.4 all-gather.3
  77.8 92.4 all-gather.5
  192.5 84.3 all-gather.7

commit v7 on v5

--- a/solution.py
+++ b/solution.py
@@ -115,8 +115,13 @@
 
 
 def gather_col(x, n_col):
-    spread = jnp.broadcast_to(x[None], (n_col,) + x.shape)
-    return lax.all_to_all(spread, "col", 0, 0).reshape((n_col * x.shape[0],) + x.shape[1:])
+    core = lax.axis_index("col") % 2
+    other = lax.ppermute(x, "col", [(j, j ^ 1) for j in range(n_col)])
+    chip = jnp.where(core == 0, jnp.concatenate([x, other]), jnp.concatenate([other, x]))
+    groups = [[j for j in range(n_col) if j % 2 == k] for k in (0, 1)]
+    spread = jnp.broadcast_to(chip[None], (n_col // 2,) + chip.shape)
+    gathered = lax.all_to_all(spread, "col", 0, 0, axis_index_groups=groups)
+    return gathered.reshape((n_col * x.shape[0],) + x.shape[1:])
 
 
 def shards(inputs, gate_pre, up_pre, w_gate, w_up, w_down, grad_out, n_row, n_col):
@@ -124,7 +129,7 @@
     tokens_col, width = grad_out.shape
     all_pre = lax.all_gather(jnp.stack([gate_pre, up_pre]), "row", axis=1, tiled=True)
     all_grad_out = gather_col(grad_out, n_col)
-    all_inputs = gather_col(inputs, n_col)
+    all_inputs = lax.all_gather(inputs, "col", axis=0, tiled=True)
     part = contract_cols(all_grad_out, w_down).astype(jnp.bfloat16)
     part = part.reshape((n_row, tokens_row, hidden_units))
     own_grad = ring_reduce_scatter(part, "row", n_row, jnp.bfloat16).astype(jnp.bfloat16)

time: 281 us -> 273 us (0.972); the launches traced: 280 us -> 268 us
  waiting for transfers between devices: 62.6 us -> 81.7 us
  starting transfers between devices: 147 us -> 133 us
  local copies, waits for them, and re-layouts: 24.9 us -> 15.4 us
  other arithmetic: 13.9 us -> 9.34 us
    all_to_all x2 -> x1, starting transfers between devices: 28.6 us -> 3.85 us  [gather_col(): gathered = lax.all_to_all(spread, 'col', 0, 0, axis_index_groups=groups)]
    all_gather x0 -> x1, waiting for transfers between devices: none -> 22.4 us  [shards(): all_inputs = lax.all_gather(inputs, 'col', axis=0, tiled=True)]
    all_to_all x1, waiting for transfers between devices: 13.4 us -> 0.01 us  [shards(): lax.all_to_all(terms.reshape((n_col, tokens_col, width)), 'col', 0, 0)]
    all_to_all x1, starting transfers between devices: 9.74 us -> 21.3 us  [shards(): lax.all_to_all(terms.reshape((n_col, tokens_col, width)), 'col', 0, 0)]
    ppermute x0 -> x1, starting transfers between devices: none -> 8.88 us  [gather_col(): other = lax.ppermute(x, 'col', [(j, j ^ 1) for j in range(n_col)])]
    ppermute x8, waiting for transfers between devices: 7.8 us -> 16 us  [ring_reduce_scatter(): a = lax.ppermute(a.astype(wire_dtype), axis, up).astype(jnp.float32)]
    unnamed x52 -> x42, local copies, waits for them, and re-layouts: 12.8 us -> 5.99 us
    all_to_all x2 -> x1, waiting for transfers between devices: 28 us -> 33.4 us  [gather_col(): gathered = lax.all_to_all(spread, 'col', 0, 0, axis_index_groups=groups)]
  transfers between devices with their start and end apart: 34 -> 35, of which waited for: 16 -> 18; matrix products, arithmetic and copies ran while one was open for 15% -> 12% of each run, Pallas kernels for 0% -> 0%
where the time goes in v7:
time: 273 us; the launch traced here: 268 us
  starting transfers between devices  133 us (49%)
  waiting for transfers between devices  81.7 us (30%)
  local copies, waits for them, and re-layouts  15.4 us (6%)
  between operations  15 us (5%)
  matrix products  13.6 us (5%)
  other arithmetic  9.34 us (3%)
    ppermute x7, starting transfers between devices, ring_reduce_scatter(): b = lax.ppermute(b.astype(wire_dtype), axis, down).astype(jnp.float32)  35.8 us
    all_to_all x1, waiting for transfers between devices, gather_col(): gathered = lax.all_to_all(spread, 'col', 0, 0, axis_index_groups=groups)  33.4 us
    ppermute x7, starting transfers between devices, ring_all_gather(): b = lax.ppermute(b, axis, down)  32.2 us
    all_gather x1, waiting for transfers between devices, shards(): all_inputs = lax.all_gather(inputs, 'col', axis=0, tiled=True)  22.4 us
    all_to_all x1, starting transfers between devices, shards(): lax.all_to_all(terms.reshape((n_col, tokens_col, width)), 'col', 0, 0)  21.3 us
    ppermute x8, waiting for transfers between devices, ring_reduce_scatter(): a = lax.ppermute(a.astype(wire_dtype), axis, up).astype(jnp.float32)  16 us
    ppermute x8, starting transfers between devices, ring_reduce_scatter(): a = lax.ppermute(a.astype(wire_dtype), axis, up).astype(jnp.float32)  15.4 us
    ppermute x8, starting transfers between devices, ring_all_gather(): a = lax.ppermute(a, axis, up)  15.3 us
  transfers between devices with their start and end apart: 35, of which 18 were waited for; matrix products, arithmetic and copies ran while one was open for 12% of the time, Pallas kernels for 0%

profile of v7, /device:TPU:1, one launch (start us, length us, event | category | flops | bytes accessed | tf_op | source)
XLA Modules:
  0.0 267.9 jit_solution(2542671597599000898)
XLA Ops:
  7.2 8.9 %collective-permute-start = (bf16[64,512]{1,0:T(8,128)(2,1)}, bf16[64,512]{1,0:T(8,128)(2,1)S(1)}, u32[]{:S(2)}, u32[]{:S(2)}) collective-permute-start(bf16[64,512]{1,0:T(8,128)(2,1)} %param.13), channel_id=1, source_target_pairs={{0,1},{1,0},{2,3},{3,2},{4,5},{5,4},{6,7},{7,6},{8,9},{9,8},{10,11... | collective-permute-start | bytes 196616 | tf_op jit(solution)/shard_map/ppermute | solution.py:119
  20.3 3.8 %all-to-all-start = ((bf16[16,128,512]{2,1,0:T(8,128)(2,1)}), bf16[16,128,512]{2,1,0:T(8,128)(2,1)S(1)}, u32[]{:S(2)}, u32[]{:S(2)}) async-start(bf16[16,128,512]{2,1,0:T(8,128)(2,1)} %broadcast_in_dim.26), calls=%async_computation | async-start | bytes 4194304 | tf_op jit(solution)/shard_map/all_to_all | solution.py:123
  24.5 33.4 %all-to-all-done = bf16[16,128,512]{2,1,0:T(8,128)(2,1)S(1)} async-done(((bf16[16,128,512]{2,1,0:T(8,128)(2,1)}), bf16[16,128,512]{2,1,0:T(8,128)(2,1)S(1)}, u32[]{:S(2)}, u32[]{:S(2)}) %all-to-all-start) | async-done | bytes 2097184 | tf_op jit(solution)/shard_map/all_to_all | solution.py:123
  60.2 4.5 %constant_dynamic-slice_fusion.15 = (bf16[1,128,462]{1,0,2:T(2,128)(2,1)S(1)}, bf16[1,128,462]{1,0,2:T(2,128)(2,1)S(1)}, bf16[1,128,462]{1,0,2:T(2,128)(2,1)S(1)...) fusion(bf16[16,128,462]{1,0,2:T(8,128)(2,1)S(1)} %slice_bitcast, ...), kind=kLoop, calls=%fused_computation.116 | loop fusion | bytes 3784768 | tf_op jit(solution)/shard_map/jit(dynamic_index_in_dim)/dynamic_slice | solution.py:64
  64.7 1.9 collective-permute-start.1
  66.6 8.4 %collective-permute-start.9 = (bf16[128,462]{0,1:T(8,128)(2,1)S(1)}, bf16[128,462]{0,1:T(8,128)(2,1)S(1)}, u32[]{:S(2)}, u32[]{:S(2)}) collective-permute-start(bf16[128,462]{0,1:T(8,128)(2,1)S(1)} %bitcast.192), channel_id=1, source_target_pairs={{0,480},{32,0},{64,32},{96,64},{128,96},{160,128},{192,160},{224,1... | collective-permute-start | bytes 354824 | tf_op jit(solution)/shard_map/ppermute | solution.py:75
  75.0 2.9 %collective-permute-done.1 = bf16[128,462]{0,1:T(8,128)(2,1)S(1)} collective-permute-done((bf16[128,462]{0,1:T(8,128)(2,1)S(1)}, bf16[128,462]{0,1:T(8,128)(2,1)S(1)}, u32[]{:S(2)}, u32[]{:S(2)}) %collective-permute-start.1) | collective-permute-done | bytes 118304 | tf_op jit(solution)/shard_map/ppermute | solution.py:71
  78.0 1.9 collective-permute-start.2
  80.0 4.6 %collective-permute-start.10 = (bf16[128,462]{0,1:T(8,128)(2,1)S(1)}, bf16[128,462]{0,1:T(8,128)(2,1)S(1)}, u32[]{:S(2)}, u32[]{:S(2)}) collective-permute-start(bf16[128,462]{0,1:T(8,128)(2,1)S(1)} %fusion.30), channel_id=1, source_target_pairs={{0,480},{32,0},{64,32},{96,64},{128,96},{160,128},{192,160},{224,1... | collective-permute-start | bytes 354824 | tf_op jit(solution)/shard_map/ppermute | solution.py:75
  84.6 3.5 %collective-permute-done.2 = bf16[128,462]{0,1:T(8,128)(2,1)S(1)} collective-permute-done((bf16[128,462]{0,1:T(8,128)(2,1)S(1)}, bf16[128,462]{0,1:T(8,128)(2,1)S(1)}, u32[]{:S(2)}, u32[]{:S(2)}) %collective-permute-start.2) | collective-permute-done | bytes 118304 | tf_op jit(solution)/shard_map/ppermute | solution.py:71
  88.1 1.9 collective-permute-start.3
  90.1 4.6 %collective-permute-start.11 = (bf16[128,462]{0,1:T(8,128)(2,1)S(1)}, bf16[128,462]{0,1:T(8,128)(2,1)S(1)}, u32[]{:S(2)}, u32[]{:S(2)}) collective-permute-start(bf16[128,462]{0,1:T(8,128)(2,1)S(1)} %fusion.29), channel_id=1, source_target_pairs={{0,480},{32,0},{64,32},{96,64},{128,96},{160,128},{192,160},{224,1... | collective-permute-start | bytes 354824 | tf_op jit(solution)/shard_map/ppermute | solution.py:75
  94.7 2.2 collective-permute-done.3
  96.9 1.9 collective-permute-start.4
  98.9 4.6 %collective-permute-start.12 = (bf16[128,462]{0,1:T(8,128)(2,1)S(1)}, bf16[128,462]{0,1:T(8,128)(2,1)S(1)}, u32[]{:S(2)}, u32[]{:S(2)}) collective-permute-start(bf16[128,462]{0,1:T(8,128)(2,1)S(1)} %fusion.28), channel_id=1, source_target_pairs={{0,480},{32,0},{64,32},{96,64},{128,96},{160,128},{192,160},{224,1... | collective-permute-start | bytes 354824 | tf_op jit(solution)/shard_map/ppermute | solution.py:75
  104.8 1.9 collective-permute-start.5
  106.8 4.6 %collective-permute-start.13 = (bf16[128,462]{0,1:T(8,128)(2,1)S(1)}, bf16[128,462]{0,1:T(8,128)(2,1)S(1)}, u32[]{:S(2)}, u32[]{:S(2)}) collective-permute-start(bf16[128,462]{0,1:T(8,128)(2,1)S(1)} %fusion.27), channel_id=1, source_target_pairs={{0,480},{32,0},{64,32},{96,64},{128,96},{160,128},{192,160},{224,1... | collective-permute-start | bytes 354824 | tf_op jit(solution)/shard_map/ppermute | solution.py:75
  112.1 1.9 collective-permute-start.6
  114.1 4.6 %collective-permute-start.14 = (bf16[128,462]{0,1:T(8,128)(2,1)S(1)}, bf16[128,462]{0,1:T(8,128)(2,1)S(1)}, u32[]{:S(2)}, u32[]{:S(2)}) collective-permute-start(bf16[128,462]{0,1:T(8,128)(2,1)S(1)} %fusion.26), channel_id=1, source_target_pairs={{0,480},{32,0},{64,32},{96,64},{128,96},{160,128},{192,160},{224,1... | collective-permute-start | bytes 354824 | tf_op jit(solution)/shard_map/ppermute | solution.py:75
  119.0 1.9 collective-permute-start.7
  120.9 4.6 %collective-permute-start.15 = (bf16[128,462]{0,1:T(8,128)(2,1)S(1)}, bf16[128,462]{0,1:T(8,128)(2,1)S(1)}, u32[]{:S(2)}, u32[]{:S(2)}) collective-permute-start(bf16[128,462]{0,1:T(8,128)(2,1)S(1)} %fusion.25), channel_id=1, source_target_pairs={{0,480},{32,0},{64,32},{96,64},{128,96},{160,128},{192,160},{224,1... | collective-permute-start | bytes 354824 | tf_op jit(solution)/shard_map/ppermute | solution.py:75
  125.8 1.9 collective-permute-start.8
  127.7 4.9 %collective-permute-done.8 = bf16[128,462]{0,1:T(8,128)(2,1)S(1)} collective-permute-done((bf16[128,462]{0,1:T(8,128)(2,1)S(1)}, bf16[128,462]{0,1:T(8,128)(2,1)S(1)}, u32[]{:S(2)}, u32[]{:S(2)}) %collective-permute-start.8) | collective-permute-done | bytes 118304 | tf_op jit(solution)/shard_map/ppermute | solution.py:71
  132.6 1.9 collective-permute-start.16
  134.6 5.0 %collective-permute-done.16 = bf16[1,128,462]{1,2,0:T(8,128)(2,1)S(1)} collective-permute-done((bf16[1,128,462]{1,2,0:T(8,128)(2,1)S(1)}, bf16[1,128,462]{1,2,0:T(8,128)(2,1)S(1)}, u32[]{:S(2)}, u32[]{:S(2)}) %collective-permute-start.16) | collective-permute-done | bytes 118304 | tf_op jit(solution)/shard_map/ppermute | solution.py:47
  139.6 1.9 collective-permute-start.17
  141.5 4.6 %collective-permute-start.24 = (bf16[1,128,462]{1,2,0:T(8,128)(2,1)S(1)}, bf16[1,128,462]{1,2,0:T(8,128)(2,1)S(1)}, u32[]{:S(2)}, u32[]{:S(2)}) collective-permute-start(bf16[1,128,462]{1,2,0:T(8,128)(2,1)S(1)} %bitcast.191), channel_id=1, source_target_pairs={{0,480},{32,0},{64,32},{96,64},{128,96},{160,128},{192,160},{224,1... | collective-permute-start | bytes 354824 | tf_op jit(solution)/shard_map/ppermute | solution.py:50
  147.8 1.9 collective-permute-start.18
  149.7 4.6 %collective-permute-start.25 = (bf16[1,128,462]{1,2,0:T(8,128)(2,1)S(1)}, bf16[1,128,462]{1,2,0:T(8,128)(2,1)S(1)}, u32[]{:S(2)}, u32[]{:S(2)}) collective-permute-start(bf16[1,128,462]{1,2,0:T(8,128)(2,1)S(1)} %collective-permute-done.24), channel_id=1, source_target_pairs={{0,480},{32,0},{64,32},{96,64},{128,96},{160,128},{192,160},{224,1... | collective-permute-start | bytes 354824 | tf_op jit(solution)/shard_map/ppermute | solution.py:50
  155.2 1.9 collective-permute-start.19
  157.1 4.6 %collective-permute-start.26 = (bf16[1,128,462]{1,2,0:T(8,128)(2,1)S(1)}, bf16[1,128,462]{1,2,0:T(8,128)(2,1)S(1)}, u32[]{:S(2)}, u32[]{:S(2)}) collective-permute-start(bf16[1,128,462]{1,2,0:T(8,128)(2,1)S(1)} %collective-permute-done.25), channel_id=1, source_target_pairs={{0,480},{32,0},{64,32},{96,64},{128,96},{160,128},{192,160},{224,1... | collective-permute-start | bytes 354824 | tf_op jit(solution)/shard_map/ppermute | solution.py:50
  162.0 1.9 collective-permute-start.20
  163.9 4.6 %collective-permute-start.27 = (bf16[1,128,462]{1,2,0:T(8,128)(2,1)S(1)}, bf16[1,128,462]{1,2,0:T(8,128)(2,1)S(1)}, u32[]{:S(2)}, u32[]{:S(2)}) collective-permute-start(bf16[1,128,462]{1,2,0:T(8,128)(2,1)S(1)} %collective-permute-done.26), channel_id=1, source_target_pairs={{0,480},{32,0},{64,32},{96,64},{128,96},{160,128},{192,160},{224,1... | collective-permute-start | bytes 354824 | tf_op jit(solution)/shard_map/ppermute | solution.py:50
  168.8 1.9 collective-permute-start.21
  170.7 4.6 %collective-permute-start.28 = (bf16[1,128,462]{1,2,0:T(8,128)(2,1)S(1)}, bf16[1,128,462]{1,2,0:T(8,128)(2,1)S(1)}, u32[]{:S(2)}, u32[]{:S(2)}) collective-permute-start(bf16[1,128,462]{1,2,0:T(8,128)(2,1)S(1)} %collective-permute-done.27), channel_id=1, source_target_pairs={{0,480},{32,0},{64,32},{96,64},{128,96},{160,128},{192,160},{224,1... | collective-permute-start | bytes 354824 | tf_op jit(solution)/shard_map/ppermute | solution.py:50
  175.5 1.9 collective-permute-start.22
  177.5 4.6 %collective-permute-start.29 = (bf16[1,128,462]{1,2,0:T(8,128)(2,1)S(1)}, bf16[1,128,462]{1,2,0:T(8,128)(2,1)S(1)}, u32[]{:S(2)}, u32[]{:S(2)}) collective-permute-start(bf16[1,128,462]{1,2,0:T(8,128)(2,1)S(1)} %collective-permute-done.28), channel_id=1, source_target_pairs={{0,480},{32,0},{64,32},{96,64},{128,96},{160,128},{192,160},{224,1... | collective-permute-start | bytes 354824 | tf_op jit(solution)/shard_map/ppermute | solution.py:50
  182.3 1.9 collective-permute-start.23
  184.3 4.8 %collective-permute-start.30 = (bf16[1,128,462]{1,2,0:T(8,128)(2,1)S(1)}, bf16[1,128,462]{1,2,0:T(8,128)(2,1)S(1)}, u32[]{:S(2)}, u32[]{:S(2)}) collective-permute-start(bf16[1,128,462]{1,2,0:T(8,128)(2,1)S(1)} %collective-permute-done.29), channel_id=1, source_target_pairs={{0,480},{32,0},{64,32},{96,64},{128,96},{160,128},{192,160},{224,1... | collective-permute-start | bytes 354824 | tf_op jit(solution)/shard_map/ppermute | solution.py:50
  192.0 2.4 gather_fusion
  197.0 3.7 %fusion.5 = bf16[2048,462]{0,1:T(8,128)(2,1)S(1)} fusion(bf16[2,2048,462]{1,2,0:T(8,128)(2,1)} %all-gather.3.cloned.1.call-done, bf16[2048,462]{0,1:T(8,128)(2,1)} %bitcast.179, pred[2048]{0:T(1024)(128)(4,1)S(1)} %broadcast_bitcast_fusion), kind=kLoop, calls=%fused_computation.14 | loop fusion | flops 13246464 | bytes 7571456 | tf_op jit(solution)/shard_map/convert_element_type | solution.py:28
  203.5 3.4 %add_convert_fusion = bf16[2048,512]{1,0:T(8,128)(2,1)} fusion(f32[2048,512]{1,0:T(8,128)S(1)} %fusion.46, bf16[512,462]{0,1:T(8,128)(2,1)S(1)} %copy-done.10, bf16[2048,462]{0,1:T(8,128)(2,1)S(1)} %bitcast.180, pred[2048]{0:T(1024)(128)(4,1)S(1)} %broadcast_bitcast_fusion, bf16[2,2048,462]{1,2,0:T(8,128)(2,1)S(1)} %copy-done.3), kind=kOutput, calls=%fused_computation.11 | convolution fusion | flops 979496960 | bytes 10569728 | tf_op jit(solution)/shard_map/dot_general | solution.py:14
  206.8 21.3 %all-to-all-start.1 = ((bf16[32,64,512]{2,1,0:T(8,128)(2,1)}), bf16[32,64,512]{2,1,0:T(8,128)(2,1)}, u32[]{:S(2)}, u32[]{:S(2)}) async-start(bf16[32,64,512]{2,1,0:T(8,128)(2,1)} %bitcast.188), calls=%async_computation.1 | async-start | bytes 4194304 | tf_op jit(solution)/shard_map/all_to_all | solution.py:148
  228.2 22.4 %all-gather.5.cloned.1.call-done = bf16[2048,512]{1,0:T(8,128)(2,1)} async-done(((bf16[64,512]{1,0:T(8,128)(2,1)}), bf16[2048,512]{1,0:T(8,128)(2,1)}) %all-gather.5.cloned.1.call-update) | async-done | bytes 2097168 | tf_op jit(solution)/shard_map/all_gather | solution.py:132
  250.6 3.7 %fusion.23 = bf16[512,462]{0,1:T(8,128)(2,1)} fusion(bf16[2048,462]{0,1:T(8,128)(2,1)S(1)} %fusion.5, bf16[2048,512]{1,0:T(8,128)(2,1)} %all-gather.5.cloned.1.call-done), kind=kOutput, calls=%fused_computation.35 | convolution fusion | flops 969120768 | bytes 4462592 | tf_op jit(solution)/shard_map/dot_general | solution.py:8
  254.2 2.0 fusion.20
  256.4 2.1 fusion.24
  258.5 2.5 reduce_sum.12
  (100 shorter events, 21.6 us)
Async XLA Ops:
  7.2 193.6 %copy-start = (bf16[512,462]{0,1:T(8,128)(2,1)S(1)}, bf16[512,462]{0,1:T(8,128)(2,1)}, u32[]{:S(2)}) copy-start(bf16[512,462]{0,1:T(8,128)(2,1)} %param.10) | copy-start | bytes 1419268
  7.2 189.9 %all-gather.3.cloned.1.call-start = ((), (), s32[]{:S(2)}) async-start(), calls=%async_computation.2 | async-start | bytes 4038656 | tf_op jit(solution)/shard_map/all_gather | solution.py:130
  7.2 10.6 %collective-permute-start = (bf16[64,512]{1,0:T(8,128)(2,1)}, bf16[64,512]{1,0:T(8,128)(2,1)S(1)}, u32[]{:S(2)}, u32[]{:S(2)}) collective-permute-start(bf16[64,512]{1,0:T(8,128)(2,1)} %param.13), channel_id=1, source_target_pairs={{0,1},{1,0},{2,3},{3,2},{4,5},{5,4},{6,7},{7,6},{8,9},{9,8},{10,11... | collective-permute-start | bytes 196616 | tf_op jit(solution)/shard_map/ppermute | solution.py:119
  20.3 37.5 %copy-start.9 = (bf16[462,512]{1,0:T(8,128)(2,1)S(1)}, bf16[462,512]{1,0:T(8,128)(2,1)}, u32[]{:S(2)}) copy-start(bf16[462,512]{1,0:T(8,128)(2,1)} %param.12) | copy-start | bytes 1419268
  20.3 37.5 %all-to-all-start = ((bf16[16,128,512]{2,1,0:T(8,128)(2,1)}), bf16[16,128,512]{2,1,0:T(8,128)(2,1)S(1)}, u32[]{:S(2)}, u32[]{:S(2)}) async-start(bf16[16,128,512]{2,1,0:T(8,128)(2,1)} %broadcast_in_dim.26), calls=%async_computation | async-start | bytes 4194304 | tf_op jit(solution)/shard_map/all_to_all | solution.py:123
  24.2 226.3 %all-gather.5.cloned.1.call-start = ((), (), s32[]{:S(2)}) async-start(), calls=%async_computation.3 | async-start | bytes 2162688 | tf_op jit(solution)/shard_map/all_gather | solution.py:132
  57.9 1.4 copy-start.6
  64.7 13.3 %collective-permute-start.1 = (bf16[128,462]{0,1:T(8,128)(2,1)S(1)}, bf16[128,462]{0,1:T(8,128)(2,1)S(1)}, u32[]{:S(2)}, u32[]{:S(2)}) collective-permute-start(bf16[128,462]{0,1:T(8,128)(2,1)S(1)} %bitcast.193), channel_id=1, source_target_pairs={{0,32},{32,64},{64,96},{96,128},{128,160},{160,192},{192,224},{224... | collective-permute-start | bytes 354824 | tf_op jit(solution)/shard_map/ppermute | solution.py:71
  66.6 13.3 %collective-permute-start.9 = (bf16[128,462]{0,1:T(8,128)(2,1)S(1)}, bf16[128,462]{0,1:T(8,128)(2,1)S(1)}, u32[]{:S(2)}, u32[]{:S(2)}) collective-permute-start(bf16[128,462]{0,1:T(8,128)(2,1)S(1)} %bitcast.192), channel_id=1, source_target_pairs={{0,480},{32,0},{64,32},{96,64},{128,96},{160,128},{192,160},{224,1... | collective-permute-start | bytes 354824 | tf_op jit(solution)/shard_map/ppermute | solution.py:75
  78.0 10.1 %collective-permute-start.2 = (bf16[128,462]{0,1:T(8,128)(2,1)S(1)}, bf16[128,462]{0,1:T(8,128)(2,1)S(1)}, u32[]{:S(2)}, u32[]{:S(2)}) collective-permute-start(bf16[128,462]{0,1:T(8,128)(2,1)S(1)} %fusion.37), channel_id=1, source_target_pairs={{0,32},{32,64},{64,96},{96,128},{128,160},{160,192},{192,224},{224... | collective-permute-start | bytes 354824 | tf_op jit(solution)/shard_map/ppermute | solution.py:71
  80.0 10.1 %collective-permute-start.10 = (bf16[128,462]{0,1:T(8,128)(2,1)S(1)}, bf16[128,462]{0,1:T(8,128)(2,1)S(1)}, u32[]{:S(2)}, u32[]{:S(2)}) collective-permute-start(bf16[128,462]{0,1:T(8,128)(2,1)S(1)} %fusion.30), channel_id=1, source_target_pairs={{0,480},{32,0},{64,32},{96,64},{128,96},{160,128},{192,160},{224,1... | collective-permute-start | bytes 354824 | tf_op jit(solution)/shard_map/ppermute | solution.py:75
  88.1 8.7 %collective-permute-start.3 = (bf16[128,462]{0,1:T(8,128)(2,1)S(1)}, bf16[128,462]{0,1:T(8,128)(2,1)S(1)}, u32[]{:S(2)}, u32[]{:S(2)}) collective-permute-start(bf16[128,462]{0,1:T(8,128)(2,1)S(1)} %fusion.36), channel_id=1, source_target_pairs={{0,32},{32,64},{64,96},{96,128},{128,160},{160,192},{192,224},{224... | collective-permute-start | bytes 354824 | tf_op jit(solution)/shard_map/ppermute | solution.py:71
  90.1 8.7 %collective-permute-start.11 = (bf16[128,462]{0,1:T(8,128)(2,1)S(1)}, bf16[128,462]{0,1:T(8,128)(2,1)S(1)}, u32[]{:S(2)}, u32[]{:S(2)}) collective-permute-start(bf16[128,462]{0,1:T(8,128)(2,1)S(1)} %fusion.29), channel_id=1, source_target_pairs={{0,480},{32,0},{64,32},{96,64},{128,96},{160,128},{192,160},{224,1... | collective-permute-start | bytes 354824 | tf_op jit(solution)/shard_map/ppermute | solution.py:75
  96.9 7.9 %collective-permute-start.4 = (bf16[128,462]{0,1:T(8,128)(2,1)S(1)}, bf16[128,462]{0,1:T(8,128)(2,1)S(1)}, u32[]{:S(2)}, u32[]{:S(2)}) collective-permute-start(bf16[128,462]{0,1:T(8,128)(2,1)S(1)} %fusion.35), channel_id=1, source_target_pairs={{0,32},{32,64},{64,96},{96,128},{128,160},{160,192},{192,224},{224... | collective-permute-start | bytes 354824 | tf_op jit(solution)/shard_map/ppermute | solution.py:71
  98.9 7.9 %collective-permute-start.12 = (bf16[128,462]{0,1:T(8,128)(2,1)S(1)}, bf16[128,462]{0,1:T(8,128)(2,1)S(1)}, u32[]{:S(2)}, u32[]{:S(2)}) collective-permute-start(bf16[128,462]{0,1:T(8,128)(2,1)S(1)} %fusion.28), channel_id=1, source_target_pairs={{0,480},{32,0},{64,32},{96,64},{128,96},{160,128},{192,160},{224,1... | collective-permute-start | bytes 354824 | tf_op jit(solution)/shard_map/ppermute | solution.py:75
  104.8 7.3 %collective-permute-start.5 = (bf16[128,462]{0,1:T(8,128)(2,1)S(1)}, bf16[128,462]{0,1:T(8,128)(2,1)S(1)}, u32[]{:S(2)}, u32[]{:S(2)}) collective-permute-start(bf16[128,462]{0,1:T(8,128)(2,1)S(1)} %fusion.34), channel_id=1, source_target_pairs={{0,32},{32,64},{64,96},{96,128},{128,160},{160,192},{192,224},{224... | collective-permute-start | bytes 354824 | tf_op jit(solution)/shard_map/ppermute | solution.py:71
  106.8 7.2 %collective-permute-start.13 = (bf16[128,462]{0,1:T(8,128)(2,1)S(1)}, bf16[128,462]{0,1:T(8,128)(2,1)S(1)}, u32[]{:S(2)}, u32[]{:S(2)}) collective-permute-start(bf16[128,462]{0,1:T(8,128)(2,1)S(1)} %fusion.27), channel_id=1, source_target_pairs={{0,480},{32,0},{64,32},{96,64},{128,96},{160,128},{192,160},{224,1... | collective-permute-start | bytes 354824 | tf_op jit(solution)/shard_map/ppermute | solution.py:75
  112.1 6.8 %collective-permute-start.6 = (bf16[128,462]{0,1:T(8,128)(2,1)S(1)}, bf16[128,462]{0,1:T(8,128)(2,1)S(1)}, u32[]{:S(2)}, u32[]{:S(2)}) collective-permute-start(bf16[128,462]{0,1:T(8,128)(2,1)S(1)} %fusion.33), channel_id=1, source_target_pairs={{0,32},{32,64},{64,96},{96,128},{128,160},{160,192},{192,224},{224... | collective-permute-start | bytes 354824 | tf_op jit(solution)/shard_map/ppermute | solution.py:71
  114.1 6.8 %collective-permute-start.14 = (bf16[128,462]{0,1:T(8,128)(2,1)S(1)}, bf16[128,462]{0,1:T(8,128)(2,1)S(1)}, u32[]{:S(2)}, u32[]{:S(2)}) collective-permute-start(bf16[128,462]{0,1:T(8,128)(2,1)S(1)} %fusion.26), channel_id=1, source_target_pairs={{0,480},{32,0},{64,32},{96,64},{128,96},{160,128},{192,160},{224,1... | collective-permute-start | bytes 354824 | tf_op jit(solution)/shard_map/ppermute | solution.py:75
  119.0 6.8 %collective-permute-start.7 = (bf16[128,462]{0,1:T(8,128)(2,1)S(1)}, bf16[128,462]{0,1:T(8,128)(2,1)S(1)}, u32[]{:S(2)}, u32[]{:S(2)}) collective-permute-start(bf16[128,462]{0,1:T(8,128)(2,1)S(1)} %fusion.32), channel_id=1, source_target_pairs={{0,32},{32,64},{64,96},{96,128},{128,160},{160,192},{192,224},{224... | collective-permute-start | bytes 354824 | tf_op jit(solution)/shard_map/ppermute | solution.py:71
  120.9 6.8 %collective-permute-start.15 = (bf16[128,462]{0,1:T(8,128)(2,1)S(1)}, bf16[128,462]{0,1:T(8,128)(2,1)S(1)}, u32[]{:S(2)}, u32[]{:S(2)}) collective-permute-start(bf16[128,462]{0,1:T(8,128)(2,1)S(1)} %fusion.25), channel_id=1, source_target_pairs={{0,480},{32,0},{64,32},{96,64},{128,96},{160,128},{192,160},{224,1... | collective-permute-start | bytes 354824 | tf_op jit(solution)/shard_map/ppermute | solution.py:75
  125.8 6.8 %collective-permute-start.8 = (bf16[128,462]{0,1:T(8,128)(2,1)S(1)}, bf16[128,462]{0,1:T(8,128)(2,1)S(1)}, u32[]{:S(2)}, u32[]{:S(2)}) collective-permute-start(bf16[128,462]{0,1:T(8,128)(2,1)S(1)} %fusion.31), channel_id=1, source_target_pairs={{0,32},{32,64},{64,96},{96,128},{128,160},{160,192},{192,224},{224... | collective-permute-start | bytes 354824 | tf_op jit(solution)/shard_map/ppermute | solution.py:71
  132.6 7.0 %collective-permute-start.16 = (bf16[1,128,462]{1,2,0:T(8,128)(2,1)S(1)}, bf16[1,128,462]{1,2,0:T(8,128)(2,1)S(1)}, u32[]{:S(2)}, u32[]{:S(2)}) collective-permute-start(bf16[1,128,462]{1,2,0:T(8,128)(2,1)S(1)} %bitcast.190), channel_id=1, source_target_pairs={{0,32},{32,64},{64,96},{96,128},{128,160},{160,192},{192,224},{224... | collective-permute-start | bytes 354824 | tf_op jit(solution)/shard_map/ppermute | solution.py:47
  139.6 8.2 %collective-permute-start.17 = (bf16[1,128,462]{1,2,0:T(8,128)(2,1)S(1)}, bf16[1,128,462]{1,2,0:T(8,128)(2,1)S(1)}, u32[]{:S(2)}, u32[]{:S(2)}) collective-permute-start(bf16[1,128,462]{1,2,0:T(8,128)(2,1)S(1)} %collective-permute-done.16), channel_id=1, source_target_pairs={{0,32},{32,64},{64,96},{96,128},{128,160},{160,192},{192,224},{224... | collective-permute-start | bytes 354824 | tf_op jit(solution)/shard_map/ppermute | solution.py:47
  141.5 8.2 %collective-permute-start.24 = (bf16[1,128,462]{1,2,0:T(8,128)(2,1)S(1)}, bf16[1,128,462]{1,2,0:T(8,128)(2,1)S(1)}, u32[]{:S(2)}, u32[]{:S(2)}) collective-permute-start(bf16[1,128,462]{1,2,0:T(8,128)(2,1)S(1)} %bitcast.191), channel_id=1, source_target_pairs={{0,480},{32,0},{64,32},{96,64},{128,96},{160,128},{192,160},{224,1... | collective-permute-start | bytes 354824 | tf_op jit(solution)/shard_map/ppermute | solution.py:50
  147.8 7.4 %collective-permute-start.18 = (bf16[1,128,462]{1,2,0:T(8,128)(2,1)S(1)}, bf16[1,128,462]{1,2,0:T(8,128)(2,1)S(1)}, u32[]{:S(2)}, u32[]{:S(2)}) collective-permute-start(bf16[1,128,462]{1,2,0:T(8,128)(2,1)S(1)} %collective-permute-done.17), channel_id=1, source_target_pairs={{0,32},{32,64},{64,96},{96,128},{128,160},{160,192},{192,224},{224... | collective-permute-start | bytes 354824 | tf_op jit(solution)/shard_map/ppermute | solution.py:47
  149.7 7.4 %collective-permute-start.25 = (bf16[1,128,462]{1,2,0:T(8,128)(2,1)S(1)}, bf16[1,128,462]{1,2,0:T(8,128)(2,1)S(1)}, u32[]{:S(2)}, u32[]{:S(2)}) collective-permute-start(bf16[1,128,462]{1,2,0:T(8,128)(2,1)S(1)} %collective-permute-done.24), channel_id=1, source_target_pairs={{0,480},{32,0},{64,32},{96,64},{128,96},{160,128},{192,160},{224,1... | collective-permute-start | bytes 354824 | tf_op jit(solution)/shard_map/ppermute | solution.py:50
  155.2 6.8 %collective-permute-start.19 = (bf16[1,128,462]{1,2,0:T(8,128)(2,1)S(1)}, bf16[1,128,462]{1,2,0:T(8,128)(2,1)S(1)}, u32[]{:S(2)}, u32[]{:S(2)}) collective-permute-start(bf16[1,128,462]{1,2,0:T(8,128)(2,1)S(1)} %collective-permute-done.18), channel_id=1, source_target_pairs={{0,32},{32,64},{64,96},{96,128},{128,160},{160,192},{192,224},{224... | collective-permute-start | bytes 354824 | tf_op jit(solution)/shard_map/ppermute | solution.py:47
  157.1 6.8 %collective-permute-start.26 = (bf16[1,128,462]{1,2,0:T(8,128)(2,1)S(1)}, bf16[1,128,462]{1,2,0:T(8,128)(2,1)S(1)}, u32[]{:S(2)}, u32[]{:S(2)}) collective-permute-start(bf16[1,128,462]{1,2,0:T(8,128)(2,1)S(1)} %collective-permute-done.25), channel_id=1, source_target_pairs={{0,480},{32,0},{64,32},{96,64},{128,96},{160,128},{192,160},{224,1... | collective-permute-start | bytes 354824 | tf_op jit(solution)/shard_map/ppermute | solution.py:50
  162.0 6.8 %collective-permute-start.20 = (bf16[1,128,462]{1,2,0:T(8,128)(2,1)S(1)}, bf16[1,128,462]{1,2,0:T(8,128)(2,1)S(1)}, u32[]{:S(2)}, u32[]{:S(2)}) collective-permute-start(bf16[1,128,462]{1,2,0:T(8,128)(2,1)S(1)} %collective-permute-done.19), channel_id=1, source_target_pairs={{0,32},{32,64},{64,96},{96,128},{128,160},{160,192},{192,224},{224... | collective-permute-start | bytes 354824 | tf_op jit(solution)/shard_map/ppermute | solution.py:47
  163.9 6.8 %collective-permute-start.27 = (bf16[1,128,462]{1,2,0:T(8,128)(2,1)S(1)}, bf16[1,128,462]{1,2,0:T(8,128)(2,1)S(1)}, u32[]{:S(2)}, u32[]{:S(2)}) collective-permute-start(bf16[1,128,462]{1,2,0:T(8,128)(2,1)S(1)} %collective-permute-done.26), channel_id=1, source_target_pairs={{0,480},{32,0},{64,32},{96,64},{128,96},{160,128},{192,160},{224,1... | collective-permute-start | bytes 354824 | tf_op jit(solution)/shard_map/ppermute | solution.py:50
  168.8 6.8 %collective-permute-start.21 = (bf16[1,128,462]{1,2,0:T(8,128)(2,1)S(1)}, bf16[1,128,462]{1,2,0:T(8,128)(2,1)S(1)}, u32[]{:S(2)}, u32[]{:S(2)}) collective-permute-start(bf16[1,128,462]{1,2,0:T(8,128)(2,1)S(1)} %collective-permute-done.20), channel_id=1, source_target_pairs={{0,32},{32,64},{64,96},{96,128},{128,160},{160,192},{192,224},{224... | collective-permute-start | bytes 354824 | tf_op jit(solution)/shard_map/ppermute | solution.py:47
  170.7 6.8 %collective-permute-start.28 = (bf16[1,128,462]{1,2,0:T(8,128)(2,1)S(1)}, bf16[1,128,462]{1,2,0:T(8,128)(2,1)S(1)}, u32[]{:S(2)}, u32[]{:S(2)}) collective-permute-start(bf16[1,128,462]{1,2,0:T(8,128)(2,1)S(1)} %collective-permute-done.27), channel_id=1, source_target_pairs={{0,480},{32,0},{64,32},{96,64},{128,96},{160,128},{192,160},{224,1... | collective-permute-start | bytes 354824 | tf_op jit(solution)/shard_map/ppermute | solution.py:50
  175.5 6.8 %collective-permute-start.22 = (bf16[1,128,462]{1,2,0:T(8,128)(2,1)S(1)}, bf16[1,128,462]{1,2,0:T(8,128)(2,1)S(1)}, u32[]{:S(2)}, u32[]{:S(2)}) collective-permute-start(bf16[1,128,462]{1,2,0:T(8,128)(2,1)S(1)} %collective-permute-done.21), channel_id=1, source_target_pairs={{0,32},{32,64},{64,96},{96,128},{128,160},{160,192},{192,224},{224... | collective-permute-start | bytes 354824 | tf_op jit(solution)/shard_map/ppermute | solution.py:47
  177.5 6.7 %collective-permute-start.29 = (bf16[1,128,462]{1,2,0:T(8,128)(2,1)S(1)}, bf16[1,128,462]{1,2,0:T(8,128)(2,1)S(1)}, u32[]{:S(2)}, u32[]{:S(2)}) collective-permute-start(bf16[1,128,462]{1,2,0:T(8,128)(2,1)S(1)} %collective-permute-done.28), channel_id=1, source_target_pairs={{0,480},{32,0},{64,32},{96,64},{128,96},{160,128},{192,160},{224,1... | collective-permute-start | bytes 354824 | tf_op jit(solution)/shard_map/ppermute | solution.py:50
  182.3 6.8 %collective-permute-start.23 = (bf16[1,128,462]{1,2,0:T(8,128)(2,1)S(1)}, bf16[1,128,462]{1,2,0:T(8,128)(2,1)S(1)}, u32[]{:S(2)}, u32[]{:S(2)}) collective-permute-start(bf16[1,128,462]{1,2,0:T(8,128)(2,1)S(1)} %collective-permute-done.22), channel_id=1, source_target_pairs={{0,32},{32,64},{64,96},{96,128},{128,160},{160,192},{192,224},{224... | collective-permute-start | bytes 354824 | tf_op jit(solution)/shard_map/ppermute | solution.py:47
  184.3 6.4 %collective-permute-start.30 = (bf16[1,128,462]{1,2,0:T(8,128)(2,1)S(1)}, bf16[1,128,462]{1,2,0:T(8,128)(2,1)S(1)}, u32[]{:S(2)}, u32[]{:S(2)}) collective-permute-start(bf16[1,128,462]{1,2,0:T(8,128)(2,1)S(1)} %collective-permute-done.29), channel_id=1, source_target_pairs={{0,480},{32,0},{64,32},{96,64},{128,96},{160,128},{192,160},{224,1... | collective-permute-start | bytes 354824 | tf_op jit(solution)/shard_map/ppermute | solution.py:50
  190.7 1.3 copy-start.5
  200.8 1.5 copy-start.1
  200.8 2.7 copy-start.3
  200.8 2.7 %copy-start.10 = (bf16[512,462]{0,1:T(8,128)(2,1)S(1)}, bf16[512,462]{0,1:T(8,128)(2,1)}, u32[]{:S(2)}) copy-start(bf16[512,462]{0,1:T(8,128)(2,1)} %param.11) | copy-start | bytes 1419268
  206.8 51.7 %all-to-all-start.1 = ((bf16[32,64,512]{2,1,0:T(8,128)(2,1)}), bf16[32,64,512]{2,1,0:T(8,128)(2,1)}, u32[]{:S(2)}, u32[]{:S(2)}) async-start(bf16[32,64,512]{2,1,0:T(8,128)(2,1)} %bitcast.188), calls=%async_computation.1 | async-start | bytes 4194304 | tf_op jit(solution)/shard_map/all_to_all | solution.py:148
  250.5 3.7 %copy-start.4 = (bf16[2,2048,462]{1,2,0:T(8,128)(2,1)S(1)}, bf16[2,2048,462]{1,2,0:T(8,128)(2,1)}, u32[]{:S(2)}) copy-start(bf16[2,2048,462]{1,2,0:T(8,128)(2,1)} %all-gather.3.cloned.1.call-done) | copy-start | bytes 11354116
  250.5 3.7 %copy-start.7 = (bf16[16,128,512]{2,1,0:T(8,128)(2,1)S(1)}, bf16[16,128,512]{2,1,0:T(8,128)(2,1)}, u32[]{:S(2)}) copy-start(bf16[16,128,512]{2,1,0:T(8,128)(2,1)} %copy-done.6) | copy-start | bytes 6291460
  254.2 2.0 copy-start.2
  254.2 2.2 copy-start.8
Sparse Core Ops, SparseCore 0:
  17.9 84.9 all-gather.2
  170.8 79.6 all-gather.4

commit v8 on v7

--- a/solution.py
+++ b/solution.py
@@ -114,6 +114,11 @@
     )
 
 
+def gather_col_flat(x, n_col):
+    spread = jnp.broadcast_to(x[None], (n_col,) + x.shape)
+    return lax.all_to_all(spread, "col", 0, 0).reshape((n_col * x.shape[0],) + x.shape[1:])
+
+
 def gather_col(x, n_col):
     core = lax.axis_index("col") % 2
     other = lax.ppermute(x, "col", [(j, j ^ 1) for j in range(n_col)])
@@ -128,7 +133,7 @@
     tokens_row, hidden_units = gate_pre.shape
     tokens_col, width = grad_out.shape
     all_pre = lax.all_gather(jnp.stack([gate_pre, up_pre]), "row", axis=1, tiled=True)
-    all_grad_out = gather_col(grad_out, n_col)
+    all_grad_out = gather_col_flat(grad_out, n_col)
     all_inputs = lax.all_gather(inputs, "col", axis=0, tiled=True)
     part = contract_cols(all_grad_out, w_down).astype(jnp.bfloat16)
     part = part.reshape((n_row, tokens_row, hidden_units))
@@ -140,12 +145,13 @@
         all_pre[0], all_pre[1], hidden_grad.astype(jnp.float32)
     )
     grad_down = contract_rows(hidden, all_grad_out).astype(jnp.bfloat16)
-    grad_gate = contract_rows(all_inputs, gate_grad).astype(jnp.bfloat16)
-    grad_up = contract_rows(all_inputs, up_grad).astype(jnp.bfloat16)
     terms = (
         contract_cols(gate_grad, w_gate) + contract_cols(up_grad, w_up)
     ).astype(jnp.bfloat16)
     received = lax.all_to_all(terms.reshape((n_col, tokens_col, width)), "col", 0, 0)
+    received, all_inputs = lax.optimization_barrier((received, all_inputs))
+    grad_gate = contract_rows(all_inputs, gate_grad).astype(jnp.bfloat16)
+    grad_up = contract_rows(all_inputs, up_grad).astype(jnp.bfloat16)
     grad_in = received.astype(jnp.float32).sum(axis=0).astype(jnp.bfloat16)
     return (grad_in, grad_gate, grad_up, grad_down)
 

time: 273 us -> 271 us (level); the launches traced: 268 us -> 269 us
  matrix products: 13.6 us -> 18.4 us
  waiting for transfers between devices: 81.7 us -> 78.7 us
    all_to_all x1, waiting for transfers between devices: 0.01 us -> 9.4 us  [shards(): lax.all_to_all(terms.reshape((n_col, tokens_col, width)), 'col', 0, 0)]
    ppermute x1 -> x0, starting transfers between devices: 8.88 us -> none  [gather_col(): other = lax.ppermute(x, 'col', [(j, j ^ 1) for j in range(n_col)])]
    all_to_all x1, starting transfers between devices: 3.85 us -> 10.6 us  [gather_col_flat(): lax.all_to_all(spread, 'col', 0, 0)]
    all_gather x1, waiting for transfers between devices: 22.4 us -> 15.9 us  [shards(): all_inputs = lax.all_gather(inputs, 'col', axis=0, tiled=True)]
    all_to_all x1, waiting for transfers between devices: 33.4 us -> 28 us  [gather_col_flat(): lax.all_to_all(spread, 'col', 0, 0)]
    dot_general x3, matrix products: 7.79 us -> 12.6 us  [contract_rows(): lax.dot_general(left, right, (((0,), (0,)), ((), ())), preferred_element_...]
    unnamed x42 -> x36, local copies, waits for them, and re-layouts: 5.99 us -> 5.79 us
  transfers between devices with their start and end apart: 35 -> 34, of which waited for: 18 -> 20; matrix products, arithmetic and copies ran while one was open for 12% -> 10% of each run, Pallas kernels for 0% -> 0%
where the time goes in v8:
time: 271 us; the launch traced here: 269 us
  starting transfers between devices  133 us (49%)
  waiting for transfers between devices  78.7 us (29%)
  matrix products  18.4 us (7%)
  local copies, waits for them, and re-layouts  16.2 us (6%)
  between operations  14.9 us (5%)
  other arithmetic  8.57 us (3%)
    ppermute x7, starting transfers between devices, ring_reduce_scatter(): b = lax.ppermute(b.astype(wire_dtype), axis, down).astype(jnp.float32)  38.5 us
    ppermute x7, starting transfers between devices, ring_all_gather(): b = lax.ppermute(b, axis, down)  32.3 us
    all_to_all x1, waiting for transfers between devices, gather_col_flat(): lax.all_to_all(spread, 'col', 0, 0)  28 us
    all_to_all x1, starting transfers between devices, shards(): lax.all_to_all(terms.reshape((n_col, tokens_col, width)), 'col', 0, 0)  20.5 us
    all_gather x1, waiting for transfers between devices, shards(): all_inputs = lax.all_gather(inputs, 'col', axis=0, tiled=True)  15.9 us
    ppermute x8, starting transfers between devices, ring_reduce_scatter(): a = lax.ppermute(a.astype(wire_dtype), axis, up).astype(jnp.float32)  15.4 us
    ppermute x8, starting transfers between devices, ring_all_gather(): a = lax.ppermute(a, axis, up)  15.3 us
    ppermute x8, waiting for transfers between devices, ring_reduce_scatter(): a = lax.ppermute(a.astype(wire_dtype), axis, up).astype(jnp.float32)  14 us
  transfers between devices with their start and end apart: 34, of which 20 were waited for; matrix products, arithmetic and copies ran while one was open for 10% of the time, Pallas kernels for 0%

profile of v8, /device:TPU:1, one launch (start us, length us, event | category | flops | bytes accessed | tf_op | source)
XLA Modules:
  0.0 269.4 jit_solution(3944099900243515238)
XLA Ops:
  9.0 2.4 broadcast_in_dim.26
  11.4 10.6 %all-to-all-start = ((bf16[32,64,512]{2,1,0:T(8,128)(2,1)}), bf16[32,64,512]{2,1,0:T(8,128)(2,1)S(1)}, u32[]{:S(2)}, u32[]{:S(2)}) async-start(bf16[32,64,512]{2,1,0:T(8,128)(2,1)} %broadcast_in_dim.26), calls=%async_computation | async-start | bytes 4194304 | tf_op jit(solution)/shard_map/all_to_all | solution.py:119
  22.3 28.0 %all-to-all-done = bf16[32,64,512]{2,1,0:T(8,128)(2,1)S(1)} async-done(((bf16[32,64,512]{2,1,0:T(8,128)(2,1)}), bf16[32,64,512]{2,1,0:T(8,128)(2,1)S(1)}, u32[]{:S(2)}, u32[]{:S(2)}) %all-to-all-start) | async-done | bytes 2097184 | tf_op jit(solution)/shard_map/all_to_all | solution.py:119
  52.6 4.6 %constant_dynamic-slice_fusion.15 = (bf16[1,128,462]{1,0,2:T(2,128)(2,1)S(1)}, bf16[1,128,462]{1,0,2:T(2,128)(2,1)S(1)}, bf16[1,128,462]{1,0,2:T(2,128)(2,1)S(1)...) fusion(bf16[16,128,462]{1,0,2:T(8,128)(2,1)S(1)} %slice_bitcast, ...), kind=kLoop, calls=%fused_computation.113 | loop fusion | bytes 3784768 | tf_op jit(solution)/shard_map/jit(dynamic_index_in_dim)/dynamic_slice | solution.py:64
  57.3 1.9 collective-permute-start
  59.2 9.5 %collective-permute-start.8 = (bf16[128,462]{0,1:T(8,128)(2,1)S(1)}, bf16[128,462]{0,1:T(8,128)(2,1)S(1)}, u32[]{:S(2)}, u32[]{:S(2)}) collective-permute-start(bf16[128,462]{0,1:T(8,128)(2,1)S(1)} %bitcast.188), channel_id=1, source_target_pairs={{0,480},{32,0},{64,32},{96,64},{128,96},{160,128},{192,160},{224,1... | collective-permute-start | bytes 354824 | tf_op jit(solution)/shard_map/ppermute | solution.py:75
  68.7 3.3 %collective-permute-done = bf16[128,462]{0,1:T(8,128)(2,1)S(1)} collective-permute-done((bf16[128,462]{0,1:T(8,128)(2,1)S(1)}, bf16[128,462]{0,1:T(8,128)(2,1)S(1)}, u32[]{:S(2)}, u32[]{:S(2)}) %collective-permute-start) | collective-permute-done | bytes 118304 | tf_op jit(solution)/shard_map/ppermute | solution.py:71
  72.1 1.9 collective-permute-start.1
  74.0 4.6 %collective-permute-start.9 = (bf16[128,462]{0,1:T(8,128)(2,1)S(1)}, bf16[128,462]{0,1:T(8,128)(2,1)S(1)}, u32[]{:S(2)}, u32[]{:S(2)}) collective-permute-start(bf16[128,462]{0,1:T(8,128)(2,1)S(1)} %fusion.28), channel_id=1, source_target_pairs={{0,480},{32,0},{64,32},{96,64},{128,96},{160,128},{192,160},{224,1... | collective-permute-start | bytes 354824 | tf_op jit(solution)/shard_map/ppermute | solution.py:75
  78.6 2.7 %collective-permute-done.1 = bf16[128,462]{0,1:T(8,128)(2,1)S(1)} collective-permute-done((bf16[128,462]{0,1:T(8,128)(2,1)S(1)}, bf16[128,462]{0,1:T(8,128)(2,1)S(1)}, u32[]{:S(2)}, u32[]{:S(2)}) %collective-permute-start.1) | collective-permute-done | bytes 118304 | tf_op jit(solution)/shard_map/ppermute | solution.py:71
  81.4 1.9 collective-permute-start.2
  83.3 4.6 %collective-permute-start.10 = (bf16[128,462]{0,1:T(8,128)(2,1)S(1)}, bf16[128,462]{0,1:T(8,128)(2,1)S(1)}, u32[]{:S(2)}, u32[]{:S(2)}) collective-permute-start(bf16[128,462]{0,1:T(8,128)(2,1)S(1)} %fusion.27), channel_id=1, source_target_pairs={{0,480},{32,0},{64,32},{96,64},{128,96},{160,128},{192,160},{224,1... | collective-permute-start | bytes 354824 | tf_op jit(solution)/shard_map/ppermute | solution.py:75
  88.2 1.9 collective-permute-start.3
  90.5 5.4 %collective-permute-start.11 = (bf16[128,462]{0,1:T(8,128)(2,1)S(1)}, bf16[128,462]{0,1:T(8,128)(2,1)S(1)}, u32[]{:S(2)}, u32[]{:S(2)}) collective-permute-start(bf16[128,462]{0,1:T(8,128)(2,1)S(1)} %fusion.26), channel_id=1, source_target_pairs={{0,480},{32,0},{64,32},{96,64},{128,96},{160,128},{192,160},{224,1... | collective-permute-start | bytes 354824 | tf_op jit(solution)/shard_map/ppermute | solution.py:75
  97.4 1.9 collective-permute-start.4
  99.3 5.1 %collective-permute-start.12 = (bf16[128,462]{0,1:T(8,128)(2,1)S(1)}, bf16[128,462]{0,1:T(8,128)(2,1)S(1)}, u32[]{:S(2)}, u32[]{:S(2)}) collective-permute-start(bf16[128,462]{0,1:T(8,128)(2,1)S(1)} %fusion.25), channel_id=1, source_target_pairs={{0,480},{32,0},{64,32},{96,64},{128,96},{160,128},{192,160},{224,1... | collective-permute-start | bytes 354824 | tf_op jit(solution)/shard_map/ppermute | solution.py:75
  104.5 2.0 collective-permute-start.5
  106.6 4.7 %collective-permute-start.13 = (bf16[128,462]{0,1:T(8,128)(2,1)S(1)}, bf16[128,462]{0,1:T(8,128)(2,1)S(1)}, u32[]{:S(2)}, u32[]{:S(2)}) collective-permute-start(bf16[128,462]{0,1:T(8,128)(2,1)S(1)} %fusion.24), channel_id=1, source_target_pairs={{0,480},{32,0},{64,32},{96,64},{128,96},{160,128},{192,160},{224,1... | collective-permute-start | bytes 354824 | tf_op jit(solution)/shard_map/ppermute | solution.py:75
  112.4 1.9 collective-permute-start.6
  114.4 4.6 %collective-permute-start.14 = (bf16[128,462]{0,1:T(8,128)(2,1)S(1)}, bf16[128,462]{0,1:T(8,128)(2,1)S(1)}, u32[]{:S(2)}, u32[]{:S(2)}) collective-permute-start(bf16[128,462]{0,1:T(8,128)(2,1)S(1)} %fusion.23), channel_id=1, source_target_pairs={{0,480},{32,0},{64,32},{96,64},{128,96},{160,128},{192,160},{224,1... | collective-permute-start | bytes 354824 | tf_op jit(solution)/shard_map/ppermute | solution.py:75
  119.2 1.9 collective-permute-start.7
  121.2 5.1 %collective-permute-done.7 = bf16[128,462]{0,1:T(8,128)(2,1)S(1)} collective-permute-done((bf16[128,462]{0,1:T(8,128)(2,1)S(1)}, bf16[128,462]{0,1:T(8,128)(2,1)S(1)}, u32[]{:S(2)}, u32[]{:S(2)}) %collective-permute-start.7) | collective-permute-done | bytes 118304 | tf_op jit(solution)/shard_map/ppermute | solution.py:71
  126.3 1.9 collective-permute-start.15
  128.2 6.3 %collective-permute-done.15 = bf16[1,128,462]{1,2,0:T(8,128)(2,1)S(1)} collective-permute-done((bf16[1,128,462]{1,2,0:T(8,128)(2,1)S(1)}, bf16[1,128,462]{1,2,0:T(8,128)(2,1)S(1)}, u32[]{:S(2)}, u32[]{:S(2)}) %collective-permute-start.15) | collective-permute-done | bytes 118304 | tf_op jit(solution)/shard_map/ppermute | solution.py:47
  134.6 1.9 collective-permute-start.16
  136.5 4.6 %collective-permute-start.23 = (bf16[1,128,462]{1,2,0:T(8,128)(2,1)S(1)}, bf16[1,128,462]{1,2,0:T(8,128)(2,1)S(1)}, u32[]{:S(2)}, u32[]{:S(2)}) collective-permute-start(bf16[1,128,462]{1,2,0:T(8,128)(2,1)S(1)} %bitcast.187), channel_id=1, source_target_pairs={{0,480},{32,0},{64,32},{96,64},{128,96},{160,128},{192,160},{224,1... | collective-permute-start | bytes 354824 | tf_op jit(solution)/shard_map/ppermute | solution.py:50
  141.9 1.9 collective-permute-start.17
  143.8 4.6 %collective-permute-start.24 = (bf16[1,128,462]{1,2,0:T(8,128)(2,1)S(1)}, bf16[1,128,462]{1,2,0:T(8,128)(2,1)S(1)}, u32[]{:S(2)}, u32[]{:S(2)}) collective-permute-start(bf16[1,128,462]{1,2,0:T(8,128)(2,1)S(1)} %collective-permute-done.23), channel_id=1, source_target_pairs={{0,480},{32,0},{64,32},{96,64},{128,96},{160,128},{192,160},{224,1... | collective-permute-start | bytes 354824 | tf_op jit(solution)/shard_map/ppermute | solution.py:50
  148.6 1.9 collective-permute-start.18
  150.6 4.6 %collective-permute-start.25 = (bf16[1,128,462]{1,2,0:T(8,128)(2,1)S(1)}, bf16[1,128,462]{1,2,0:T(8,128)(2,1)S(1)}, u32[]{:S(2)}, u32[]{:S(2)}) collective-permute-start(bf16[1,128,462]{1,2,0:T(8,128)(2,1)S(1)} %collective-permute-done.24), channel_id=1, source_target_pairs={{0,480},{32,0},{64,32},{96,64},{128,96},{160,128},{192,160},{224,1... | collective-permute-start | bytes 354824 | tf_op jit(solution)/shard_map/ppermute | solution.py:50
  155.4 1.9 collective-permute-start.19
  157.4 4.6 %collective-permute-start.26 = (bf16[1,128,462]{1,2,0:T(8,128)(2,1)S(1)}, bf16[1,128,462]{1,2,0:T(8,128)(2,1)S(1)}, u32[]{:S(2)}, u32[]{:S(2)}) collective-permute-start(bf16[1,128,462]{1,2,0:T(8,128)(2,1)S(1)} %collective-permute-done.25), channel_id=1, source_target_pairs={{0,480},{32,0},{64,32},{96,64},{128,96},{160,128},{192,160},{224,1... | collective-permute-start | bytes 354824 | tf_op jit(solution)/shard_map/ppermute | solution.py:50
  162.2 1.9 collective-permute-start.20
  164.2 4.6 %collective-permute-start.27 = (bf16[1,128,462]{1,2,0:T(8,128)(2,1)S(1)}, bf16[1,128,462]{1,2,0:T(8,128)(2,1)S(1)}, u32[]{:S(2)}, u32[]{:S(2)}) collective-permute-start(bf16[1,128,462]{1,2,0:T(8,128)(2,1)S(1)} %collective-permute-done.26), channel_id=1, source_target_pairs={{0,480},{32,0},{64,32},{96,64},{128,96},{160,128},{192,160},{224,1... | collective-permute-start | bytes 354824 | tf_op jit(solution)/shard_map/ppermute | solution.py:50
  169.0 1.9 collective-permute-start.21
  171.0 4.6 %collective-permute-start.28 = (bf16[1,128,462]{1,2,0:T(8,128)(2,1)S(1)}, bf16[1,128,462]{1,2,0:T(8,128)(2,1)S(1)}, u32[]{:S(2)}, u32[]{:S(2)}) collective-permute-start(bf16[1,128,462]{1,2,0:T(8,128)(2,1)S(1)} %collective-permute-done.27), channel_id=1, source_target_pairs={{0,480},{32,0},{64,32},{96,64},{128,96},{160,128},{192,160},{224,1... | collective-permute-start | bytes 354824 | tf_op jit(solution)/shard_map/ppermute | solution.py:50
  175.8 1.9 collective-permute-start.22
  177.7 4.8 %collective-permute-start.29 = (bf16[1,128,462]{1,2,0:T(8,128)(2,1)S(1)}, bf16[1,128,462]{1,2,0:T(8,128)(2,1)S(1)}, u32[]{:S(2)}, u32[]{:S(2)}) collective-permute-start(bf16[1,128,462]{1,2,0:T(8,128)(2,1)S(1)} %collective-permute-done.28), channel_id=1, source_target_pairs={{0,480},{32,0},{64,32},{96,64},{128,96},{160,128},{192,160},{224,1... | collective-permute-start | bytes 354824 | tf_op jit(solution)/shard_map/ppermute | solution.py:50
  186.7 2.4 gather_fusion
  191.8 3.7 %fusion.5 = bf16[2048,462]{0,1:T(8,128)(2,1)S(1)} fusion(bf16[2,2048,462]{1,2,0:T(8,128)(2,1)} %all-gather.3.cloned.1.call-done, bf16[2048,462]{0,1:T(8,128)(2,1)} %bitcast.175, pred[2048]{0:T(1024)(128)(4,1)S(1)} %broadcast_bitcast_fusion), kind=kLoop, calls=%fused_computation.14 | loop fusion | flops 13246464 | bytes 7571456 | tf_op jit(solution)/shard_map/convert_element_type | solution.py:28
  198.2 3.3 %add_convert_fusion = bf16[2048,512]{1,0:T(8,128)(2,1)} fusion(f32[2048,512]{1,0:T(8,128)S(1)} %fusion.44, bf16[512,462]{0,1:T(8,128)(2,1)S(1)} %copy-done.7, bf16[2048,462]{0,1:T(8,128)(2,1)S(1)} %bitcast.176, pred[2048]{0:T(1024)(128)(4,1)S(1)} %broadcast_bitcast_fusion, bf16[2,2048,462]{1,2,0:T(8,128)(2,1)S(1)} %copy-done.3), kind=kOutput, calls=%fused_computation.11 | convolution fusion | flops 979496960 | bytes 10569728 | tf_op jit(solution)/shard_map/dot_general | solution.py:14
  201.5 20.5 %all-to-all-start.1 = ((bf16[32,64,512]{2,1,0:T(8,128)(2,1)}), bf16[32,64,512]{2,1,0:T(8,128)(2,1)}, u32[]{:S(2)}, u32[]{:S(2)}) async-start(bf16[32,64,512]{2,1,0:T(8,128)(2,1)} %bitcast.184), calls=%async_computation.1 | async-start | bytes 4194304 | tf_op jit(solution)/shard_map/all_to_all | solution.py:151
  222.1 4.8 %fusion.20 = bf16[462,512]{1,0:T(8,128)(2,1)} fusion(bf16[2048,512]{1,0:T(8,128)(2,1)} %bitcast.183, bf16[2,2048,462]{1,2,0:T(8,128)(2,1)} %all-gather.3.cloned.1.call-done), kind=kOutput, calls=%fused_computation.32 | convolution fusion | flops 976690176 | bytes 6354944 | tf_op jit(solution)/shard_map/dot_general | solution.py:8
  226.9 15.9 %all-gather.5.cloned.1.call-done = bf16[2048,512]{1,0:T(8,128)(2,1)} async-done(((bf16[64,512]{1,0:T(8,128)(2,1)}), bf16[2048,512]{1,0:T(8,128)(2,1)}) %all-gather.5.cloned.1.call-update) | async-done | bytes 2097168 | tf_op jit(solution)/shard_map/all_gather | solution.py:137
  242.8 9.4 %all-to-all-done.1 = bf16[32,64,512]{2,1,0:T(8,128)(2,1)} async-done(((bf16[32,64,512]{2,1,0:T(8,128)(2,1)}), bf16[32,64,512]{2,1,0:T(8,128)(2,1)}, u32[]{:S(2)}, u32[]{:S(2)}) %all-to-all-start.1) | async-done | bytes 2097184 | tf_op jit(solution)/shard_map/all_to_all | solution.py:151
  252.2 3.5 %convolution_convert_fusion.2 = bf16[512,462]{0,1:T(8,128)(2,1)} fusion(bf16[2048,512]{1,0:T(8,128)(2,1)} %all-gather.5.cloned.1.call-done, bf16[2048,462]{0,1:T(8,128)(2,1)S(1)} %fusion.5), kind=kOutput, calls=%fused_computation.34 | convolution fusion | flops 969120768 | bytes 4462592 | tf_op jit(solution)/shard_map/dot_general | solution.py:8
  255.7 2.7 reduce_sum.12
  258.4 4.2 %convolution_convert_fusion.1 = bf16[512,462]{0,1:T(8,128)(2,1)} fusion(bf16[2048,512]{1,0:T(8,128)(2,1)} %all-gather.5.cloned.1.call-done, bf16[2048,462]{0,1:T(8,128)(2,1)S(1)} %bitcast.177, pred[2048]{0:T(1024)(128)(4,1)S(1)} %broadcast_bitcast_fusion, bf16[2,2048,462]{1,2,0:T(8,128)(2,1)} %all-gather.3.cloned.1.call-done), kind=kOutput, calls=%fused_computation.33 | convolution fusion | flops 977636352 | bytes 6365184 | tf_op jit(solution)/shard_map/dot_general | solution.py:8
  (91 shorter events, 19.4 us)
Async XLA Ops:
  7.2 188.3 %copy-start = (bf16[512,462]{0,1:T(8,128)(2,1)S(1)}, bf16[512,462]{0,1:T(8,128)(2,1)}, u32[]{:S(2)}) copy-start(bf16[512,462]{0,1:T(8,128)(2,1)} %param.10) | copy-start | bytes 1419268
  7.2 184.6 %all-gather.3.cloned.1.call-start = ((), (), s32[]{:S(2)}) async-start(), calls=%async_computation.2 | async-start | bytes 4038656 | tf_op jit(solution)/shard_map/all_gather | solution.py:135
  11.4 39.0 %copy-start.6 = (bf16[462,512]{1,0:T(8,128)(2,1)S(1)}, bf16[462,512]{1,0:T(8,128)(2,1)}, u32[]{:S(2)}) copy-start(bf16[462,512]{1,0:T(8,128)(2,1)} %param.12) | copy-start | bytes 1419268
  11.4 38.9 %all-to-all-start = ((bf16[32,64,512]{2,1,0:T(8,128)(2,1)}), bf16[32,64,512]{2,1,0:T(8,128)(2,1)S(1)}, u32[]{:S(2)}, u32[]{:S(2)}) async-start(bf16[32,64,512]{2,1,0:T(8,128)(2,1)} %broadcast_in_dim.26), calls=%async_computation | async-start | bytes 4194304 | tf_op jit(solution)/shard_map/all_to_all | solution.py:119
  22.0 220.8 %all-gather.5.cloned.1.call-start = ((), (), s32[]{:S(2)}) async-start(), calls=%async_computation.3 | async-start | bytes 2162688 | tf_op jit(solution)/shard_map/all_gather | solution.py:137
  50.3 1.4 copy-start.5
  57.3 14.8 %collective-permute-start = (bf16[128,462]{0,1:T(8,128)(2,1)S(1)}, bf16[128,462]{0,1:T(8,128)(2,1)S(1)}, u32[]{:S(2)}, u32[]{:S(2)}) collective-permute-start(bf16[128,462]{0,1:T(8,128)(2,1)S(1)} %bitcast.189), channel_id=1, source_target_pairs={{0,32},{32,64},{64,96},{96,128},{128,160},{160,192},{192,224},{224... | collective-permute-start | bytes 354824 | tf_op jit(solution)/shard_map/ppermute | solution.py:71
  59.2 14.8 %collective-permute-start.8 = (bf16[128,462]{0,1:T(8,128)(2,1)S(1)}, bf16[128,462]{0,1:T(8,128)(2,1)S(1)}, u32[]{:S(2)}, u32[]{:S(2)}) collective-permute-start(bf16[128,462]{0,1:T(8,128)(2,1)S(1)} %bitcast.188), channel_id=1, source_target_pairs={{0,480},{32,0},{64,32},{96,64},{128,96},{160,128},{192,160},{224,1... | collective-permute-start | bytes 354824 | tf_op jit(solution)/shard_map/ppermute | solution.py:75
  72.1 9.3 %collective-permute-start.1 = (bf16[128,462]{0,1:T(8,128)(2,1)S(1)}, bf16[128,462]{0,1:T(8,128)(2,1)S(1)}, u32[]{:S(2)}, u32[]{:S(2)}) collective-permute-start(bf16[128,462]{0,1:T(8,128)(2,1)S(1)} %fusion.35), channel_id=1, source_target_pairs={{0,32},{32,64},{64,96},{96,128},{128,160},{160,192},{192,224},{224... | collective-permute-start | bytes 354824 | tf_op jit(solution)/shard_map/ppermute | solution.py:71
  74.0 9.2 %collective-permute-start.9 = (bf16[128,462]{0,1:T(8,128)(2,1)S(1)}, bf16[128,462]{0,1:T(8,128)(2,1)S(1)}, u32[]{:S(2)}, u32[]{:S(2)}) collective-permute-start(bf16[128,462]{0,1:T(8,128)(2,1)S(1)} %fusion.28), channel_id=1, source_target_pairs={{0,480},{32,0},{64,32},{96,64},{128,96},{160,128},{192,160},{224,1... | collective-permute-start | bytes 354824 | tf_op jit(solution)/shard_map/ppermute | solution.py:75
  81.4 6.8 %collective-permute-start.2 = (bf16[128,462]{0,1:T(8,128)(2,1)S(1)}, bf16[128,462]{0,1:T(8,128)(2,1)S(1)}, u32[]{:S(2)}, u32[]{:S(2)}) collective-permute-start(bf16[128,462]{0,1:T(8,128)(2,1)S(1)} %fusion.34), channel_id=1, source_target_pairs={{0,32},{32,64},{64,96},{96,128},{128,160},{160,192},{192,224},{224... | collective-permute-start | bytes 354824 | tf_op jit(solution)/shard_map/ppermute | solution.py:71
  83.3 7.2 %collective-permute-start.10 = (bf16[128,462]{0,1:T(8,128)(2,1)S(1)}, bf16[128,462]{0,1:T(8,128)(2,1)S(1)}, u32[]{:S(2)}, u32[]{:S(2)}) collective-permute-start(bf16[128,462]{0,1:T(8,128)(2,1)S(1)} %fusion.27), channel_id=1, source_target_pairs={{0,480},{32,0},{64,32},{96,64},{128,96},{160,128},{192,160},{224,1... | collective-permute-start | bytes 354824 | tf_op jit(solution)/shard_map/ppermute | solution.py:75
  88.2 9.2 %collective-permute-start.3 = (bf16[128,462]{0,1:T(8,128)(2,1)S(1)}, bf16[128,462]{0,1:T(8,128)(2,1)S(1)}, u32[]{:S(2)}, u32[]{:S(2)}) collective-permute-start(bf16[128,462]{0,1:T(8,128)(2,1)S(1)} %fusion.33), channel_id=1, source_target_pairs={{0,32},{32,64},{64,96},{96,128},{128,160},{160,192},{192,224},{224... | collective-permute-start | bytes 354824 | tf_op jit(solution)/shard_map/ppermute | solution.py:71
  90.5 8.8 %collective-permute-start.11 = (bf16[128,462]{0,1:T(8,128)(2,1)S(1)}, bf16[128,462]{0,1:T(8,128)(2,1)S(1)}, u32[]{:S(2)}, u32[]{:S(2)}) collective-permute-start(bf16[128,462]{0,1:T(8,128)(2,1)S(1)} %fusion.26), channel_id=1, source_target_pairs={{0,480},{32,0},{64,32},{96,64},{128,96},{160,128},{192,160},{224,1... | collective-permute-start | bytes 354824 | tf_op jit(solution)/shard_map/ppermute | solution.py:75
  97.4 7.1 %collective-permute-start.4 = (bf16[128,462]{0,1:T(8,128)(2,1)S(1)}, bf16[128,462]{0,1:T(8,128)(2,1)S(1)}, u32[]{:S(2)}, u32[]{:S(2)}) collective-permute-start(bf16[128,462]{0,1:T(8,128)(2,1)S(1)} %fusion.32), channel_id=1, source_target_pairs={{0,32},{32,64},{64,96},{96,128},{128,160},{160,192},{192,224},{224... | collective-permute-start | bytes 354824 | tf_op jit(solution)/shard_map/ppermute | solution.py:71
  99.3 7.2 %collective-permute-start.12 = (bf16[128,462]{0,1:T(8,128)(2,1)S(1)}, bf16[128,462]{0,1:T(8,128)(2,1)S(1)}, u32[]{:S(2)}, u32[]{:S(2)}) collective-permute-start(bf16[128,462]{0,1:T(8,128)(2,1)S(1)} %fusion.25), channel_id=1, source_target_pairs={{0,480},{32,0},{64,32},{96,64},{128,96},{160,128},{192,160},{224,1... | collective-permute-start | bytes 354824 | tf_op jit(solution)/shard_map/ppermute | solution.py:75
  104.5 7.8 %collective-permute-start.5 = (bf16[128,462]{0,1:T(8,128)(2,1)S(1)}, bf16[128,462]{0,1:T(8,128)(2,1)S(1)}, u32[]{:S(2)}, u32[]{:S(2)}) collective-permute-start(bf16[128,462]{0,1:T(8,128)(2,1)S(1)} %fusion.31), channel_id=1, source_target_pairs={{0,32},{32,64},{64,96},{96,128},{128,160},{160,192},{192,224},{224... | collective-permute-start | bytes 354824 | tf_op jit(solution)/shard_map/ppermute | solution.py:71
  106.6 7.8 %collective-permute-start.13 = (bf16[128,462]{0,1:T(8,128)(2,1)S(1)}, bf16[128,462]{0,1:T(8,128)(2,1)S(1)}, u32[]{:S(2)}, u32[]{:S(2)}) collective-permute-start(bf16[128,462]{0,1:T(8,128)(2,1)S(1)} %fusion.24), channel_id=1, source_target_pairs={{0,480},{32,0},{64,32},{96,64},{128,96},{160,128},{192,160},{224,1... | collective-permute-start | bytes 354824 | tf_op jit(solution)/shard_map/ppermute | solution.py:75
  112.4 6.8 %collective-permute-start.6 = (bf16[128,462]{0,1:T(8,128)(2,1)S(1)}, bf16[128,462]{0,1:T(8,128)(2,1)S(1)}, u32[]{:S(2)}, u32[]{:S(2)}) collective-permute-start(bf16[128,462]{0,1:T(8,128)(2,1)S(1)} %fusion.30), channel_id=1, source_target_pairs={{0,32},{32,64},{64,96},{96,128},{128,160},{160,192},{192,224},{224... | collective-permute-start | bytes 354824 | tf_op jit(solution)/shard_map/ppermute | solution.py:71
  114.4 6.8 %collective-permute-start.14 = (bf16[128,462]{0,1:T(8,128)(2,1)S(1)}, bf16[128,462]{0,1:T(8,128)(2,1)S(1)}, u32[]{:S(2)}, u32[]{:S(2)}) collective-permute-start(bf16[128,462]{0,1:T(8,128)(2,1)S(1)} %fusion.23), channel_id=1, source_target_pairs={{0,480},{32,0},{64,32},{96,64},{128,96},{160,128},{192,160},{224,1... | collective-permute-start | bytes 354824 | tf_op jit(solution)/shard_map/ppermute | solution.py:75
  119.2 7.0 %collective-permute-start.7 = (bf16[128,462]{0,1:T(8,128)(2,1)S(1)}, bf16[128,462]{0,1:T(8,128)(2,1)S(1)}, u32[]{:S(2)}, u32[]{:S(2)}) collective-permute-start(bf16[128,462]{0,1:T(8,128)(2,1)S(1)} %fusion.29), channel_id=1, source_target_pairs={{0,32},{32,64},{64,96},{96,128},{128,160},{160,192},{192,224},{224... | collective-permute-start | bytes 354824 | tf_op jit(solution)/shard_map/ppermute | solution.py:71
  126.3 8.2 %collective-permute-start.15 = (bf16[1,128,462]{1,2,0:T(8,128)(2,1)S(1)}, bf16[1,128,462]{1,2,0:T(8,128)(2,1)S(1)}, u32[]{:S(2)}, u32[]{:S(2)}) collective-permute-start(bf16[1,128,462]{1,2,0:T(8,128)(2,1)S(1)} %bitcast.186), channel_id=1, source_target_pairs={{0,32},{32,64},{64,96},{96,128},{128,160},{160,192},{192,224},{224... | collective-permute-start | bytes 354824 | tf_op jit(solution)/shard_map/ppermute | solution.py:47
  134.6 7.3 %collective-permute-start.16 = (bf16[1,128,462]{1,2,0:T(8,128)(2,1)S(1)}, bf16[1,128,462]{1,2,0:T(8,128)(2,1)S(1)}, u32[]{:S(2)}, u32[]{:S(2)}) collective-permute-start(bf16[1,128,462]{1,2,0:T(8,128)(2,1)S(1)} %collective-permute-done.15), channel_id=1, source_target_pairs={{0,32},{32,64},{64,96},{96,128},{128,160},{160,192},{192,224},{224... | collective-permute-start | bytes 354824 | tf_op jit(solution)/shard_map/ppermute | solution.py:47
  136.5 7.3 %collective-permute-start.23 = (bf16[1,128,462]{1,2,0:T(8,128)(2,1)S(1)}, bf16[1,128,462]{1,2,0:T(8,128)(2,1)S(1)}, u32[]{:S(2)}, u32[]{:S(2)}) collective-permute-start(bf16[1,128,462]{1,2,0:T(8,128)(2,1)S(1)} %bitcast.187), channel_id=1, source_target_pairs={{0,480},{32,0},{64,32},{96,64},{128,96},{160,128},{192,160},{224,1... | collective-permute-start | bytes 354824 | tf_op jit(solution)/shard_map/ppermute | solution.py:50
  141.9 6.8 %collective-permute-start.17 = (bf16[1,128,462]{1,2,0:T(8,128)(2,1)S(1)}, bf16[1,128,462]{1,2,0:T(8,128)(2,1)S(1)}, u32[]{:S(2)}, u32[]{:S(2)}) collective-permute-start(bf16[1,128,462]{1,2,0:T(8,128)(2,1)S(1)} %collective-permute-done.16), channel_id=1, source_target_pairs={{0,32},{32,64},{64,96},{96,128},{128,160},{160,192},{192,224},{224... | collective-permute-start | bytes 354824 | tf_op jit(solution)/shard_map/ppermute | solution.py:47
  143.8 6.8 %collective-permute-start.24 = (bf16[1,128,462]{1,2,0:T(8,128)(2,1)S(1)}, bf16[1,128,462]{1,2,0:T(8,128)(2,1)S(1)}, u32[]{:S(2)}, u32[]{:S(2)}) collective-permute-start(bf16[1,128,462]{1,2,0:T(8,128)(2,1)S(1)} %collective-permute-done.23), channel_id=1, source_target_pairs={{0,480},{32,0},{64,32},{96,64},{128,96},{160,128},{192,160},{224,1... | collective-permute-start | bytes 354824 | tf_op jit(solution)/shard_map/ppermute | solution.py:50
  148.6 6.8 %collective-permute-start.18 = (bf16[1,128,462]{1,2,0:T(8,128)(2,1)S(1)}, bf16[1,128,462]{1,2,0:T(8,128)(2,1)S(1)}, u32[]{:S(2)}, u32[]{:S(2)}) collective-permute-start(bf16[1,128,462]{1,2,0:T(8,128)(2,1)S(1)} %collective-permute-done.17), channel_id=1, source_target_pairs={{0,32},{32,64},{64,96},{96,128},{128,160},{160,192},{192,224},{224... | collective-permute-start | bytes 354824 | tf_op jit(solution)/shard_map/ppermute | solution.py:47
  150.6 6.8 %collective-permute-start.25 = (bf16[1,128,462]{1,2,0:T(8,128)(2,1)S(1)}, bf16[1,128,462]{1,2,0:T(8,128)(2,1)S(1)}, u32[]{:S(2)}, u32[]{:S(2)}) collective-permute-start(bf16[1,128,462]{1,2,0:T(8,128)(2,1)S(1)} %collective-permute-done.24), channel_id=1, source_target_pairs={{0,480},{32,0},{64,32},{96,64},{128,96},{160,128},{192,160},{224,1... | collective-permute-start | bytes 354824 | tf_op jit(solution)/shard_map/ppermute | solution.py:50
  155.4 6.8 %collective-permute-start.19 = (bf16[1,128,462]{1,2,0:T(8,128)(2,1)S(1)}, bf16[1,128,462]{1,2,0:T(8,128)(2,1)S(1)}, u32[]{:S(2)}, u32[]{:S(2)}) collective-permute-start(bf16[1,128,462]{1,2,0:T(8,128)(2,1)S(1)} %collective-permute-done.18), channel_id=1, source_target_pairs={{0,32},{32,64},{64,96},{96,128},{128,160},{160,192},{192,224},{224... | collective-permute-start | bytes 354824 | tf_op jit(solution)/shard_map/ppermute | solution.py:47
  157.4 6.8 %collective-permute-start.26 = (bf16[1,128,462]{1,2,0:T(8,128)(2,1)S(1)}, bf16[1,128,462]{1,2,0:T(8,128)(2,1)S(1)}, u32[]{:S(2)}, u32[]{:S(2)}) collective-permute-start(bf16[1,128,462]{1,2,0:T(8,128)(2,1)S(1)} %collective-permute-done.25), channel_id=1, source_target_pairs={{0,480},{32,0},{64,32},{96,64},{128,96},{160,128},{192,160},{224,1... | collective-permute-start | bytes 354824 | tf_op jit(solution)/shard_map/ppermute | solution.py:50
  162.2 6.8 %collective-permute-start.20 = (bf16[1,128,462]{1,2,0:T(8,128)(2,1)S(1)}, bf16[1,128,462]{1,2,0:T(8,128)(2,1)S(1)}, u32[]{:S(2)}, u32[]{:S(2)}) collective-permute-start(bf16[1,128,462]{1,2,0:T(8,128)(2,1)S(1)} %collective-permute-done.19), channel_id=1, source_target_pairs={{0,32},{32,64},{64,96},{96,128},{128,160},{160,192},{192,224},{224... | collective-permute-start | bytes 354824 | tf_op jit(solution)/shard_map/ppermute | solution.py:47
  164.2 6.8 %collective-permute-start.27 = (bf16[1,128,462]{1,2,0:T(8,128)(2,1)S(1)}, bf16[1,128,462]{1,2,0:T(8,128)(2,1)S(1)}, u32[]{:S(2)}, u32[]{:S(2)}) collective-permute-start(bf16[1,128,462]{1,2,0:T(8,128)(2,1)S(1)} %collective-permute-done.26), channel_id=1, source_target_pairs={{0,480},{32,0},{64,32},{96,64},{128,96},{160,128},{192,160},{224,1... | collective-permute-start | bytes 354824 | tf_op jit(solution)/shard_map/ppermute | solution.py:50
  169.0 6.8 %collective-permute-start.21 = (bf16[1,128,462]{1,2,0:T(8,128)(2,1)S(1)}, bf16[1,128,462]{1,2,0:T(8,128)(2,1)S(1)}, u32[]{:S(2)}, u32[]{:S(2)}) collective-permute-start(bf16[1,128,462]{1,2,0:T(8,128)(2,1)S(1)} %collective-permute-done.20), channel_id=1, source_target_pairs={{0,32},{32,64},{64,96},{96,128},{128,160},{160,192},{192,224},{224... | collective-permute-start | bytes 354824 | tf_op jit(solution)/shard_map/ppermute | solution.py:47
  171.0 6.7 %collective-permute-start.28 = (bf16[1,128,462]{1,2,0:T(8,128)(2,1)S(1)}, bf16[1,128,462]{1,2,0:T(8,128)(2,1)S(1)}, u32[]{:S(2)}, u32[]{:S(2)}) collective-permute-start(bf16[1,128,462]{1,2,0:T(8,128)(2,1)S(1)} %collective-permute-done.27), channel_id=1, source_target_pairs={{0,480},{32,0},{64,32},{96,64},{128,96},{160,128},{192,160},{224,1... | collective-permute-start | bytes 354824 | tf_op jit(solution)/shard_map/ppermute | solution.py:50
  175.8 7.8 %collective-permute-start.22 = (bf16[1,128,462]{1,2,0:T(8,128)(2,1)S(1)}, bf16[1,128,462]{1,2,0:T(8,128)(2,1)S(1)}, u32[]{:S(2)}, u32[]{:S(2)}) collective-permute-start(bf16[1,128,462]{1,2,0:T(8,128)(2,1)S(1)} %collective-permute-done.21), channel_id=1, source_target_pairs={{0,32},{32,64},{64,96},{96,128},{128,160},{160,192},{192,224},{224... | collective-permute-start | bytes 354824 | tf_op jit(solution)/shard_map/ppermute | solution.py:47
  177.7 7.7 %collective-permute-start.29 = (bf16[1,128,462]{1,2,0:T(8,128)(2,1)S(1)}, bf16[1,128,462]{1,2,0:T(8,128)(2,1)S(1)}, u32[]{:S(2)}, u32[]{:S(2)}) collective-permute-start(bf16[1,128,462]{1,2,0:T(8,128)(2,1)S(1)} %collective-permute-done.28), channel_id=1, source_target_pairs={{0,480},{32,0},{64,32},{96,64},{128,96},{160,128},{192,160},{224,1... | collective-permute-start | bytes 354824 | tf_op jit(solution)/shard_map/ppermute | solution.py:50
  185.4 1.3 copy-start.4
  195.5 1.5 copy-start.1
  195.5 2.6 copy-start.3
  195.5 2.7 copy-start.7
  201.5 50.7 %all-to-all-start.1 = ((bf16[32,64,512]{2,1,0:T(8,128)(2,1)}), bf16[32,64,512]{2,1,0:T(8,128)(2,1)}, u32[]{:S(2)}, u32[]{:S(2)}) async-start(bf16[32,64,512]{2,1,0:T(8,128)(2,1)} %bitcast.184), calls=%async_computation.1 | async-start | bytes 4194304 | tf_op jit(solution)/shard_map/all_to_all | solution.py:151
  255.7 2.7 copy-start.2
Sparse Core Ops, SparseCore 0:
  10.6 92.1 all-gather.2
  164.3 78.4 all-gather.4

commit v9 on v8

--- a/solution.py
+++ b/solution.py
@@ -138,6 +138,7 @@
     part = contract_cols(all_grad_out, w_down).astype(jnp.bfloat16)
     part = part.reshape((n_row, tokens_row, hidden_units))
     own_grad = ring_reduce_scatter(part, "row", n_row, jnp.bfloat16).astype(jnp.bfloat16)
+    own_grad, all_inputs = lax.optimization_barrier((own_grad, all_inputs))
     hidden_grad = ring_all_gather(own_grad[None], "row", n_row).reshape(
         (n_row * tokens_row, hidden_units)
     )

time: 271 us -> 276 us (1.018)
  waiting for transfers between devices: 78.7 us -> 82.3 us
    all_gather x1, waiting for transfers between devices: 15.9 us -> 0.02 us  [shards(): all_inputs = lax.all_gather(inputs, 'col', axis=0, tiled=True)]
    all_to_all x1, waiting for transfers between devices: 9.4 us -> 24 us  [shards(): lax.all_to_all(terms.reshape((n_col, tokens_col, width)), 'col', 0, 0)]
    ppermute x8, waiting for transfers between devices: 9.35 us -> 15 us  [ring_all_gather(): a = lax.ppermute(a, axis, up)]
    ppermute x8, waiting for transfers between devices: 14 us -> 10.6 us  [ring_reduce_scatter(): a = lax.ppermute(a.astype(wire_dtype), axis, up).astype(jnp.float32)]
    unnamed x36 -> x40, local copies, waits for them, and re-layouts: 5.79 us -> 5.79 us
  transfers between devices with their start and end apart: 34 -> 34, of which waited for: 20 -> 19; matrix products, arithmetic and copies ran while one was open for 10% -> 9% of each run, Pallas kernels for 0% -> 0%
where the time goes in v9:
time: 276 us; the launch traced here: 275 us
  starting transfers between devices  132 us (48%)
  waiting for transfers between devices  82.3 us (30%)
  matrix products  18.3 us (7%)
  local copies, waits for them, and re-layouts  16.3 us (6%)
  between operations  15 us (5%)
  other arithmetic  10.5 us (4%)
    ppermute x7, starting transfers between devices, ring_reduce_scatter(): b = lax.ppermute(b.astype(wire_dtype), axis, down).astype(jnp.float32)  37.6 us
    ppermute x7, starting transfers between devices, ring_all_gather(): b = lax.ppermute(b, axis, down)  32.7 us
    all_to_all x1, waiting for transfers between devices, gather_col_flat(): lax.all_to_all(spread, 'col', 0, 0)  29 us
    all_to_all x1, waiting for transfers between devices, shards(): lax.all_to_all(terms.reshape((n_col, tokens_col, width)), 'col', 0, 0)  24 us
    all_to_all x1, starting transfers between devices, shards(): lax.all_to_all(terms.reshape((n_col, tokens_col, width)), 'col', 0, 0)  19.9 us
    ppermute x8, starting transfers between devices, ring_all_gather(): a = lax.ppermute(a, axis, up)  15.9 us
    ppermute x8, starting transfers between devices, ring_reduce_scatter(): a = lax.ppermute(a.astype(wire_dtype), axis, up).astype(jnp.float32)  15.5 us
    ppermute x8, waiting for transfers between devices, ring_all_gather(): a = lax.ppermute(a, axis, up)  15 us
  transfers between devices with their start and end apart: 34, of which 19 were waited for; matrix products, arithmetic and copies ran while one was open for 9% of the time, Pallas kernels for 0%

profile of v9, /device:TPU:1, one launch (start us, length us, event | category | flops | bytes accessed | tf_op | source)
XLA Modules:
  0.0 274.6 jit_solution(17041345415265195395)
XLA Ops:
  7.9 2.4 broadcast_in_dim.26
  10.3 10.6 %all-to-all-start = ((bf16[32,64,512]{2,1,0:T(8,128)(2,1)}), bf16[32,64,512]{2,1,0:T(8,128)(2,1)S(1)}, u32[]{:S(2)}, u32[]{:S(2)}) async-start(bf16[32,64,512]{2,1,0:T(8,128)(2,1)} %broadcast_in_dim.26), calls=%async_computation | async-start | bytes 4194304 | tf_op jit(solution)/shard_map/all_to_all | solution.py:119
  21.3 29.0 %all-to-all-done = bf16[32,64,512]{2,1,0:T(8,128)(2,1)S(1)} async-done(((bf16[32,64,512]{2,1,0:T(8,128)(2,1)}), bf16[32,64,512]{2,1,0:T(8,128)(2,1)S(1)}, u32[]{:S(2)}, u32[]{:S(2)}) %all-to-all-start) | async-done | bytes 2097184 | tf_op jit(solution)/shard_map/all_to_all | solution.py:119
  52.5 4.7 %constant_dynamic-slice_fusion.15 = (bf16[1,128,462]{1,0,2:T(2,128)(2,1)S(1)}, bf16[1,128,462]{1,0,2:T(2,128)(2,1)S(1)}, bf16[1,128,462]{1,0,2:T(2,128)(2,1)S(1)...) fusion(bf16[16,128,462]{1,0,2:T(8,128)(2,1)S(1)} %slice_bitcast, ...), kind=kLoop, calls=%fused_computation.113 | loop fusion | bytes 3784768 | tf_op jit(solution)/shard_map/jit(dynamic_index_in_dim)/dynamic_slice | solution.py:64
  57.3 1.9 collective-permute-start
  60.0 9.3 %collective-permute-start.8 = (bf16[128,462]{0,1:T(8,128)(2,1)S(1)}, bf16[128,462]{0,1:T(8,128)(2,1)S(1)}, u32[]{:S(2)}, u32[]{:S(2)}) collective-permute-start(bf16[128,462]{0,1:T(8,128)(2,1)S(1)} %bitcast.189), channel_id=1, source_target_pairs={{0,480},{32,0},{64,32},{96,64},{128,96},{160,128},{192,160},{224,1... | collective-permute-start | bytes 354824 | tf_op jit(solution)/shard_map/ppermute | solution.py:75
  70.4 1.9 collective-permute-start.1
  73.3 4.6 %collective-permute-start.9 = (bf16[128,462]{0,1:T(8,128)(2,1)S(1)}, bf16[128,462]{0,1:T(8,128)(2,1)S(1)}, u32[]{:S(2)}, u32[]{:S(2)}) collective-permute-start(bf16[128,462]{0,1:T(8,128)(2,1)S(1)} %fusion.28), channel_id=1, source_target_pairs={{0,480},{32,0},{64,32},{96,64},{128,96},{160,128},{192,160},{224,1... | collective-permute-start | bytes 354824 | tf_op jit(solution)/shard_map/ppermute | solution.py:75
  78.9 1.9 collective-permute-start.2
  80.9 4.6 %collective-permute-start.10 = (bf16[128,462]{0,1:T(8,128)(2,1)S(1)}, bf16[128,462]{0,1:T(8,128)(2,1)S(1)}, u32[]{:S(2)}, u32[]{:S(2)}) collective-permute-start(bf16[128,462]{0,1:T(8,128)(2,1)S(1)} %fusion.27), channel_id=1, source_target_pairs={{0,480},{32,0},{64,32},{96,64},{128,96},{160,128},{192,160},{224,1... | collective-permute-start | bytes 354824 | tf_op jit(solution)/shard_map/ppermute | solution.py:75
  85.7 1.9 collective-permute-start.3
  87.7 4.6 %collective-permute-start.11 = (bf16[128,462]{0,1:T(8,128)(2,1)S(1)}, bf16[128,462]{0,1:T(8,128)(2,1)S(1)}, u32[]{:S(2)}, u32[]{:S(2)}) collective-permute-start(bf16[128,462]{0,1:T(8,128)(2,1)S(1)} %fusion.26), channel_id=1, source_target_pairs={{0,480},{32,0},{64,32},{96,64},{128,96},{160,128},{192,160},{224,1... | collective-permute-start | bytes 354824 | tf_op jit(solution)/shard_map/ppermute | solution.py:75
  92.5 1.9 collective-permute-start.4
  94.5 4.6 %collective-permute-start.12 = (bf16[128,462]{0,1:T(8,128)(2,1)S(1)}, bf16[128,462]{0,1:T(8,128)(2,1)S(1)}, u32[]{:S(2)}, u32[]{:S(2)}) collective-permute-start(bf16[128,462]{0,1:T(8,128)(2,1)S(1)} %fusion.25), channel_id=1, source_target_pairs={{0,480},{32,0},{64,32},{96,64},{128,96},{160,128},{192,160},{224,1... | collective-permute-start | bytes 354824 | tf_op jit(solution)/shard_map/ppermute | solution.py:75
  99.4 1.9 collective-permute-start.5
  102.5 5.4 %collective-permute-start.13 = (bf16[128,462]{0,1:T(8,128)(2,1)S(1)}, bf16[128,462]{0,1:T(8,128)(2,1)S(1)}, u32[]{:S(2)}, u32[]{:S(2)}) collective-permute-start(bf16[128,462]{0,1:T(8,128)(2,1)S(1)} %fusion.24), channel_id=1, source_target_pairs={{0,480},{32,0},{64,32},{96,64},{128,96},{160,128},{192,160},{224,1... | collective-permute-start | bytes 354824 | tf_op jit(solution)/shard_map/ppermute | solution.py:75
  109.0 1.9 collective-permute-start.6
  111.0 4.6 %collective-permute-start.14 = (bf16[128,462]{0,1:T(8,128)(2,1)S(1)}, bf16[128,462]{0,1:T(8,128)(2,1)S(1)}, u32[]{:S(2)}, u32[]{:S(2)}) collective-permute-start(bf16[128,462]{0,1:T(8,128)(2,1)S(1)} %fusion.23), channel_id=1, source_target_pairs={{0,480},{32,0},{64,32},{96,64},{128,96},{160,128},{192,160},{224,1... | collective-permute-start | bytes 354824 | tf_op jit(solution)/shard_map/ppermute | solution.py:75
  115.5 2.7 collective-permute-done.6
  118.3 2.1 collective-permute-start.7
  120.3 6.2 %collective-permute-done.7 = bf16[128,462]{0,1:T(8,128)(2,1)S(1)} collective-permute-done((bf16[128,462]{0,1:T(8,128)(2,1)S(1)}, bf16[128,462]{0,1:T(8,128)(2,1)S(1)}, u32[]{:S(2)}, u32[]{:S(2)}) %collective-permute-start.7) | collective-permute-done | bytes 118304 | tf_op jit(solution)/shard_map/ppermute | solution.py:71
  126.7 2.5 collective-permute-start.15
  129.2 6.6 %collective-permute-done.15 = bf16[1,128,462]{1,2,0:T(8,128)(2,1)S(1)} collective-permute-done((bf16[1,128,462]{1,2,0:T(8,128)(2,1)S(1)}, bf16[1,128,462]{1,2,0:T(8,128)(2,1)S(1)}, u32[]{:S(2)}, u32[]{:S(2)}) %collective-permute-start.15) | collective-permute-done | bytes 118304 | tf_op jit(solution)/shard_map/ppermute | solution.py:47
  135.8 1.9 collective-permute-start.16
  137.7 4.6 %collective-permute-start.23 = (bf16[1,128,462]{1,2,0:T(8,128)(2,1)S(1)}, bf16[1,128,462]{1,2,0:T(8,128)(2,1)S(1)}, u32[]{:S(2)}, u32[]{:S(2)}) collective-permute-start(bf16[1,128,462]{1,2,0:T(8,128)(2,1)S(1)} %bitcast.187), channel_id=1, source_target_pairs={{0,480},{32,0},{64,32},{96,64},{128,96},{160,128},{192,160},{224,1... | collective-permute-start | bytes 354824 | tf_op jit(solution)/shard_map/ppermute | solution.py:50
  142.3 2.3 collective-permute-done.16
  144.6 1.9 collective-permute-start.17
  146.5 4.6 %collective-permute-start.24 = (bf16[1,128,462]{1,2,0:T(8,128)(2,1)S(1)}, bf16[1,128,462]{1,2,0:T(8,128)(2,1)S(1)}, u32[]{:S(2)}, u32[]{:S(2)}) collective-permute-start(bf16[1,128,462]{1,2,0:T(8,128)(2,1)S(1)} %collective-permute-done.23), channel_id=1, source_target_pairs={{0,480},{32,0},{64,32},{96,64},{128,96},{160,128},{192,160},{224,1... | collective-permute-start | bytes 354824 | tf_op jit(solution)/shard_map/ppermute | solution.py:50
  152.5 1.9 collective-permute-start.18
  154.5 5.4 %collective-permute-start.25 = (bf16[1,128,462]{1,2,0:T(8,128)(2,1)S(1)}, bf16[1,128,462]{1,2,0:T(8,128)(2,1)S(1)}, u32[]{:S(2)}, u32[]{:S(2)}) collective-permute-start(bf16[1,128,462]{1,2,0:T(8,128)(2,1)S(1)} %collective-permute-done.24), channel_id=1, source_target_pairs={{0,480},{32,0},{64,32},{96,64},{128,96},{160,128},{192,160},{224,1... | collective-permute-start | bytes 354824 | tf_op jit(solution)/shard_map/ppermute | solution.py:50
  160.6 1.9 collective-permute-start.19
  162.5 4.6 %collective-permute-start.26 = (bf16[1,128,462]{1,2,0:T(8,128)(2,1)S(1)}, bf16[1,128,462]{1,2,0:T(8,128)(2,1)S(1)}, u32[]{:S(2)}, u32[]{:S(2)}) collective-permute-start(bf16[1,128,462]{1,2,0:T(8,128)(2,1)S(1)} %collective-permute-done.25), channel_id=1, source_target_pairs={{0,480},{32,0},{64,32},{96,64},{128,96},{160,128},{192,160},{224,1... | collective-permute-start | bytes 354824 | tf_op jit(solution)/shard_map/ppermute | solution.py:50
  168.3 1.9 collective-permute-start.20
  170.2 4.6 %collective-permute-start.27 = (bf16[1,128,462]{1,2,0:T(8,128)(2,1)S(1)}, bf16[1,128,462]{1,2,0:T(8,128)(2,1)S(1)}, u32[]{:S(2)}, u32[]{:S(2)}) collective-permute-start(bf16[1,128,462]{1,2,0:T(8,128)(2,1)S(1)} %collective-permute-done.26), channel_id=1, source_target_pairs={{0,480},{32,0},{64,32},{96,64},{128,96},{160,128},{192,160},{224,1... | collective-permute-start | bytes 354824 | tf_op jit(solution)/shard_map/ppermute | solution.py:50
  174.8 2.7 collective-permute-done.20
  177.5 1.9 collective-permute-start.21
  179.5 4.6 %collective-permute-start.28 = (bf16[1,128,462]{1,2,0:T(8,128)(2,1)S(1)}, bf16[1,128,462]{1,2,0:T(8,128)(2,1)S(1)}, u32[]{:S(2)}, u32[]{:S(2)}) collective-permute-start(bf16[1,128,462]{1,2,0:T(8,128)(2,1)S(1)} %collective-permute-done.27), channel_id=1, source_target_pairs={{0,480},{32,0},{64,32},{96,64},{128,96},{160,128},{192,160},{224,1... | collective-permute-start | bytes 354824 | tf_op jit(solution)/shard_map/ppermute | solution.py:50
  184.2 1.9 collective-permute-start.22
  186.6 4.4 %collective-permute-start.29 = (bf16[1,128,462]{1,2,0:T(8,128)(2,1)S(1)}, bf16[1,128,462]{1,2,0:T(8,128)(2,1)S(1)}, u32[]{:S(2)}, u32[]{:S(2)}) collective-permute-start(bf16[1,128,462]{1,2,0:T(8,128)(2,1)S(1)} %collective-permute-done.28), channel_id=1, source_target_pairs={{0,480},{32,0},{64,32},{96,64},{128,96},{160,128},{192,160},{224,1... | collective-permute-start | bytes 354824 | tf_op jit(solution)/shard_map/ppermute | solution.py:50
  193.9 2.4 gather_fusion
  199.0 3.7 %fusion.5 = bf16[2048,462]{0,1:T(8,128)(2,1)S(1)} fusion(bf16[2,2048,462]{1,2,0:T(8,128)(2,1)} %all-gather.5.cloned.1.call-done, bf16[2048,462]{0,1:T(8,128)(2,1)} %bitcast.175, pred[2048]{0:T(1024)(128)(4,1)S(1)} %broadcast_bitcast_fusion), kind=kLoop, calls=%fused_computation.14 | loop fusion | flops 13246464 | bytes 7571456 | tf_op jit(solution)/shard_map/convert_element_type | solution.py:28
  205.4 3.4 %add_convert_fusion = bf16[2048,512]{1,0:T(8,128)(2,1)} fusion(f32[2048,512]{1,0:T(8,128)S(1)} %fusion.44, bf16[512,462]{0,1:T(8,128)(2,1)S(1)} %copy-done.9, bf16[2048,462]{0,1:T(8,128)(2,1)S(1)} %bitcast.176, pred[2048]{0:T(1024)(128)(4,1)S(1)} %broadcast_bitcast_fusion, bf16[2,2048,462]{1,2,0:T(8,128)(2,1)S(1)} %copy-done.3), kind=kOutput, calls=%fused_computation.11 | convolution fusion | flops 979496960 | bytes 10569728 | tf_op jit(solution)/shard_map/dot_general | solution.py:14
  208.7 19.9 %all-to-all-start.1 = ((bf16[32,64,512]{2,1,0:T(8,128)(2,1)}), bf16[32,64,512]{2,1,0:T(8,128)(2,1)}, u32[]{:S(2)}, u32[]{:S(2)}) async-start(bf16[32,64,512]{2,1,0:T(8,128)(2,1)} %bitcast.184), calls=%async_computation.1 | async-start | bytes 4194304 | tf_op jit(solution)/shard_map/all_to_all | solution.py:152
  228.6 4.7 %fusion.20 = bf16[462,512]{1,0:T(8,128)(2,1)} fusion(bf16[2048,512]{1,0:T(8,128)(2,1)} %bitcast.183, bf16[2,2048,462]{1,2,0:T(8,128)(2,1)} %all-gather.5.cloned.1.call-done), kind=kOutput, calls=%fused_computation.32 | convolution fusion | flops 976690176 | bytes 6354944 | tf_op jit(solution)/shard_map/dot_general | solution.py:8
  233.4 24.0 %all-to-all-done.1 = bf16[32,64,512]{2,1,0:T(8,128)(2,1)} async-done(((bf16[32,64,512]{2,1,0:T(8,128)(2,1)}), bf16[32,64,512]{2,1,0:T(8,128)(2,1)}, u32[]{:S(2)}, u32[]{:S(2)}) %all-to-all-start.1) | async-done | bytes 2097184 | tf_op jit(solution)/shard_map/all_to_all | solution.py:152
  257.4 3.5 %convolution_convert_fusion.2 = bf16[512,462]{0,1:T(8,128)(2,1)} fusion(bf16[2048,512]{1,0:T(8,128)(2,1)} %all-gather.3.cloned.1.call-done, bf16[2048,462]{0,1:T(8,128)(2,1)S(1)} %fusion.5), kind=kOutput, calls=%fused_computation.34 | convolution fusion | flops 969120768 | bytes 4462592 | tf_op jit(solution)/shard_map/dot_general | solution.py:8
  260.9 2.7 reduce_sum.12
  263.5 4.2 %convolution_convert_fusion.1 = bf16[512,462]{0,1:T(8,128)(2,1)} fusion(bf16[2048,512]{1,0:T(8,128)(2,1)} %all-gather.3.cloned.1.call-done, bf16[2048,462]{0,1:T(8,128)(2,1)S(1)} %bitcast.177, pred[2048]{0:T(1024)(128)(4,1)S(1)} %broadcast_bitcast_fusion, bf16[2,2048,462]{1,2,0:T(8,128)(2,1)} %all-gather.5.cloned.1.call-done), kind=kOutput, calls=%fused_computation.33 | convolution fusion | flops 977636352 | bytes 6365184 | tf_op jit(solution)/shard_map/dot_general | solution.py:8
  (95 shorter events, 22.2 us)
Async XLA Ops:
  7.2 195.5 %copy-start = (bf16[512,462]{0,1:T(8,128)(2,1)S(1)}, bf16[512,462]{0,1:T(8,128)(2,1)}, u32[]{:S(2)}) copy-start(bf16[512,462]{0,1:T(8,128)(2,1)} %param.10) | copy-start | bytes 1419268
  7.2 119.5 %all-gather.3.cloned.1.call-start = ((), (), s32[]{:S(2)}) async-start(), calls=%async_computation.2 | async-start | bytes 2162688 | tf_op jit(solution)/shard_map/all_gather | solution.py:137
  10.3 39.9 %copy-start.8 = (bf16[462,512]{1,0:T(8,128)(2,1)S(1)}, bf16[462,512]{1,0:T(8,128)(2,1)}, u32[]{:S(2)}) copy-start(bf16[462,512]{1,0:T(8,128)(2,1)} %param.12) | copy-start | bytes 1419268
  10.3 39.9 %all-to-all-start = ((bf16[32,64,512]{2,1,0:T(8,128)(2,1)}), bf16[32,64,512]{2,1,0:T(8,128)(2,1)S(1)}, u32[]{:S(2)}, u32[]{:S(2)}) async-start(bf16[32,64,512]{2,1,0:T(8,128)(2,1)} %broadcast_in_dim.26), calls=%async_computation | async-start | bytes 4194304 | tf_op jit(solution)/shard_map/all_to_all | solution.py:119
  21.0 178.0 %all-gather.5.cloned.1.call-start = ((), (), s32[]{:S(2)}) async-start(), calls=%async_computation.3 | async-start | bytes 4038656 | tf_op jit(solution)/shard_map/all_gather | solution.py:135
  50.3 1.4 copy-start.5
  52.5 6.7 %copy-start.6 = (bf16[128,462]{0,1:T(8,128)(2,1)S(1)}, bf16[128,462]{0,1:T(8,128)(2,1)}, u32[]{:S(2)}) copy-start(bf16[128,462]{0,1:T(8,128)(2,1)} %param.9) | copy-start | bytes 354820
  52.5 6.7 %copy-start.7 = (bf16[128,462]{0,1:T(8,128)(2,1)S(1)}, bf16[128,462]{0,1:T(8,128)(2,1)}, u32[]{:S(2)}) copy-start(bf16[128,462]{0,1:T(8,128)(2,1)} %param.8) | copy-start | bytes 354820
  57.3 12.0 %collective-permute-start = (bf16[128,462]{0,1:T(8,128)(2,1)S(1)}, bf16[128,462]{0,1:T(8,128)(2,1)}, u32[]{:S(2)}, u32[]{:S(2)}) collective-permute-start(bf16[128,462]{0,1:T(8,128)(2,1)S(1)} %bitcast.188), channel_id=1, source_target_pairs={{0,32},{32,64},{64,96},{96,128},{128,160},{160,192},{192,224},{224... | collective-permute-start | bytes 354824 | tf_op jit(solution)/shard_map/ppermute | solution.py:71
  60.0 12.3 %collective-permute-start.8 = (bf16[128,462]{0,1:T(8,128)(2,1)S(1)}, bf16[128,462]{0,1:T(8,128)(2,1)S(1)}, u32[]{:S(2)}, u32[]{:S(2)}) collective-permute-start(bf16[128,462]{0,1:T(8,128)(2,1)S(1)} %bitcast.189), channel_id=1, source_target_pairs={{0,480},{32,0},{64,32},{96,64},{128,96},{160,128},{192,160},{224,1... | collective-permute-start | bytes 354824 | tf_op jit(solution)/shard_map/ppermute | solution.py:75
  70.4 7.5 %collective-permute-start.1 = (bf16[128,462]{0,1:T(8,128)(2,1)S(1)}, bf16[128,462]{0,1:T(8,128)(2,1)S(1)}, u32[]{:S(2)}, u32[]{:S(2)}) collective-permute-start(bf16[128,462]{0,1:T(8,128)(2,1)S(1)} %fusion.35), channel_id=1, source_target_pairs={{0,32},{32,64},{64,96},{96,128},{128,160},{160,192},{192,224},{224... | collective-permute-start | bytes 354824 | tf_op jit(solution)/shard_map/ppermute | solution.py:71
  73.3 7.5 %collective-permute-start.9 = (bf16[128,462]{0,1:T(8,128)(2,1)S(1)}, bf16[128,462]{0,1:T(8,128)(2,1)S(1)}, u32[]{:S(2)}, u32[]{:S(2)}) collective-permute-start(bf16[128,462]{0,1:T(8,128)(2,1)S(1)} %fusion.28), channel_id=1, source_target_pairs={{0,480},{32,0},{64,32},{96,64},{128,96},{160,128},{192,160},{224,1... | collective-permute-start | bytes 354824 | tf_op jit(solution)/shard_map/ppermute | solution.py:75
  78.9 6.8 %collective-permute-start.2 = (bf16[128,462]{0,1:T(8,128)(2,1)S(1)}, bf16[128,462]{0,1:T(8,128)(2,1)S(1)}, u32[]{:S(2)}, u32[]{:S(2)}) collective-permute-start(bf16[128,462]{0,1:T(8,128)(2,1)S(1)} %fusion.34), channel_id=1, source_target_pairs={{0,32},{32,64},{64,96},{96,128},{128,160},{160,192},{192,224},{224... | collective-permute-start | bytes 354824 | tf_op jit(solution)/shard_map/ppermute | solution.py:71
  80.9 6.8 %collective-permute-start.10 = (bf16[128,462]{0,1:T(8,128)(2,1)S(1)}, bf16[128,462]{0,1:T(8,128)(2,1)S(1)}, u32[]{:S(2)}, u32[]{:S(2)}) collective-permute-start(bf16[128,462]{0,1:T(8,128)(2,1)S(1)} %fusion.27), channel_id=1, source_target_pairs={{0,480},{32,0},{64,32},{96,64},{128,96},{160,128},{192,160},{224,1... | collective-permute-start | bytes 354824 | tf_op jit(solution)/shard_map/ppermute | solution.py:75
  85.7 6.8 %collective-permute-start.3 = (bf16[128,462]{0,1:T(8,128)(2,1)S(1)}, bf16[128,462]{0,1:T(8,128)(2,1)S(1)}, u32[]{:S(2)}, u32[]{:S(2)}) collective-permute-start(bf16[128,462]{0,1:T(8,128)(2,1)S(1)} %fusion.33), channel_id=1, source_target_pairs={{0,32},{32,64},{64,96},{96,128},{128,160},{160,192},{192,224},{224... | collective-permute-start | bytes 354824 | tf_op jit(solution)/shard_map/ppermute | solution.py:71
  87.7 6.8 %collective-permute-start.11 = (bf16[128,462]{0,1:T(8,128)(2,1)S(1)}, bf16[128,462]{0,1:T(8,128)(2,1)S(1)}, u32[]{:S(2)}, u32[]{:S(2)}) collective-permute-start(bf16[128,462]{0,1:T(8,128)(2,1)S(1)} %fusion.26), channel_id=1, source_target_pairs={{0,480},{32,0},{64,32},{96,64},{128,96},{160,128},{192,160},{224,1... | collective-permute-start | bytes 354824 | tf_op jit(solution)/shard_map/ppermute | solution.py:75
  92.5 6.8 %collective-permute-start.4 = (bf16[128,462]{0,1:T(8,128)(2,1)S(1)}, bf16[128,462]{0,1:T(8,128)(2,1)S(1)}, u32[]{:S(2)}, u32[]{:S(2)}) collective-permute-start(bf16[128,462]{0,1:T(8,128)(2,1)S(1)} %fusion.32), channel_id=1, source_target_pairs={{0,32},{32,64},{64,96},{96,128},{128,160},{160,192},{192,224},{224... | collective-permute-start | bytes 354824 | tf_op jit(solution)/shard_map/ppermute | solution.py:71
  94.5 8.0 %collective-permute-start.12 = (bf16[128,462]{0,1:T(8,128)(2,1)S(1)}, bf16[128,462]{0,1:T(8,128)(2,1)S(1)}, u32[]{:S(2)}, u32[]{:S(2)}) collective-permute-start(bf16[128,462]{0,1:T(8,128)(2,1)S(1)} %fusion.25), channel_id=1, source_target_pairs={{0,480},{32,0},{64,32},{96,64},{128,96},{160,128},{192,160},{224,1... | collective-permute-start | bytes 354824 | tf_op jit(solution)/shard_map/ppermute | solution.py:75
  99.4 9.6 %collective-permute-start.5 = (bf16[128,462]{0,1:T(8,128)(2,1)S(1)}, bf16[128,462]{0,1:T(8,128)(2,1)S(1)}, u32[]{:S(2)}, u32[]{:S(2)}) collective-permute-start(bf16[128,462]{0,1:T(8,128)(2,1)S(1)} %fusion.31), channel_id=1, source_target_pairs={{0,32},{32,64},{64,96},{96,128},{128,160},{160,192},{192,224},{224... | collective-permute-start | bytes 354824 | tf_op jit(solution)/shard_map/ppermute | solution.py:71
  102.5 8.4 %collective-permute-start.13 = (bf16[128,462]{0,1:T(8,128)(2,1)S(1)}, bf16[128,462]{0,1:T(8,128)(2,1)S(1)}, u32[]{:S(2)}, u32[]{:S(2)}) collective-permute-start(bf16[128,462]{0,1:T(8,128)(2,1)S(1)} %fusion.24), channel_id=1, source_target_pairs={{0,480},{32,0},{64,32},{96,64},{128,96},{160,128},{192,160},{224,1... | collective-permute-start | bytes 354824 | tf_op jit(solution)/shard_map/ppermute | solution.py:75
  109.0 9.2 %collective-permute-start.6 = (bf16[128,462]{0,1:T(8,128)(2,1)S(1)}, bf16[128,462]{0,1:T(8,128)(2,1)S(1)}, u32[]{:S(2)}, u32[]{:S(2)}) collective-permute-start(bf16[128,462]{0,1:T(8,128)(2,1)S(1)} %fusion.30), channel_id=1, source_target_pairs={{0,32},{32,64},{64,96},{96,128},{128,160},{160,192},{192,224},{224... | collective-permute-start | bytes 354824 | tf_op jit(solution)/shard_map/ppermute | solution.py:71
  111.0 9.4 %collective-permute-start.14 = (bf16[128,462]{0,1:T(8,128)(2,1)S(1)}, bf16[128,462]{0,1:T(8,128)(2,1)S(1)}, u32[]{:S(2)}, u32[]{:S(2)}) collective-permute-start(bf16[128,462]{0,1:T(8,128)(2,1)S(1)} %fusion.23), channel_id=1, source_target_pairs={{0,480},{32,0},{64,32},{96,64},{128,96},{160,128},{192,160},{224,1... | collective-permute-start | bytes 354824 | tf_op jit(solution)/shard_map/ppermute | solution.py:75
  118.3 8.3 %collective-permute-start.7 = (bf16[128,462]{0,1:T(8,128)(2,1)S(1)}, bf16[128,462]{0,1:T(8,128)(2,1)S(1)}, u32[]{:S(2)}, u32[]{:S(2)}) collective-permute-start(bf16[128,462]{0,1:T(8,128)(2,1)S(1)} %fusion.29), channel_id=1, source_target_pairs={{0,32},{32,64},{64,96},{96,128},{128,160},{160,192},{192,224},{224... | collective-permute-start | bytes 354824 | tf_op jit(solution)/shard_map/ppermute | solution.py:71
  126.7 9.2 %collective-permute-start.15 = (bf16[1,128,462]{1,2,0:T(8,128)(2,1)S(1)}, bf16[1,128,462]{1,2,0:T(8,128)(2,1)S(1)}, u32[]{:S(2)}, u32[]{:S(2)}) collective-permute-start(bf16[1,128,462]{1,2,0:T(8,128)(2,1)S(1)} %bitcast.186), channel_id=1, source_target_pairs={{0,32},{32,64},{64,96},{96,128},{128,160},{160,192},{192,224},{224... | collective-permute-start | bytes 354824 | tf_op jit(solution)/shard_map/ppermute | solution.py:47
  135.8 8.8 %collective-permute-start.16 = (bf16[1,128,462]{1,2,0:T(8,128)(2,1)S(1)}, bf16[1,128,462]{1,2,0:T(8,128)(2,1)S(1)}, u32[]{:S(2)}, u32[]{:S(2)}) collective-permute-start(bf16[1,128,462]{1,2,0:T(8,128)(2,1)S(1)} %collective-permute-done.15), channel_id=1, source_target_pairs={{0,32},{32,64},{64,96},{96,128},{128,160},{160,192},{192,224},{224... | collective-permute-start | bytes 354824 | tf_op jit(solution)/shard_map/ppermute | solution.py:47
  137.7 8.8 %collective-permute-start.23 = (bf16[1,128,462]{1,2,0:T(8,128)(2,1)S(1)}, bf16[1,128,462]{1,2,0:T(8,128)(2,1)S(1)}, u32[]{:S(2)}, u32[]{:S(2)}) collective-permute-start(bf16[1,128,462]{1,2,0:T(8,128)(2,1)S(1)} %bitcast.187), channel_id=1, source_target_pairs={{0,480},{32,0},{64,32},{96,64},{128,96},{160,128},{192,160},{224,1... | collective-permute-start | bytes 354824 | tf_op jit(solution)/shard_map/ppermute | solution.py:50
  144.6 7.9 %collective-permute-start.17 = (bf16[1,128,462]{1,2,0:T(8,128)(2,1)S(1)}, bf16[1,128,462]{1,2,0:T(8,128)(2,1)S(1)}, u32[]{:S(2)}, u32[]{:S(2)}) collective-permute-start(bf16[1,128,462]{1,2,0:T(8,128)(2,1)S(1)} %collective-permute-done.16), channel_id=1, source_target_pairs={{0,32},{32,64},{64,96},{96,128},{128,160},{160,192},{192,224},{224... | collective-permute-start | bytes 354824 | tf_op jit(solution)/shard_map/ppermute | solution.py:47
  146.5 8.0 %collective-permute-start.24 = (bf16[1,128,462]{1,2,0:T(8,128)(2,1)S(1)}, bf16[1,128,462]{1,2,0:T(8,128)(2,1)S(1)}, u32[]{:S(2)}, u32[]{:S(2)}) collective-permute-start(bf16[1,128,462]{1,2,0:T(8,128)(2,1)S(1)} %collective-permute-done.23), channel_id=1, source_target_pairs={{0,480},{32,0},{64,32},{96,64},{128,96},{160,128},{192,160},{224,1... | collective-permute-start | bytes 354824 | tf_op jit(solution)/shard_map/ppermute | solution.py:50
  152.5 8.1 %collective-permute-start.18 = (bf16[1,128,462]{1,2,0:T(8,128)(2,1)S(1)}, bf16[1,128,462]{1,2,0:T(8,128)(2,1)S(1)}, u32[]{:S(2)}, u32[]{:S(2)}) collective-permute-start(bf16[1,128,462]{1,2,0:T(8,128)(2,1)S(1)} %collective-permute-done.17), channel_id=1, source_target_pairs={{0,32},{32,64},{64,96},{96,128},{128,160},{160,192},{192,224},{224... | collective-permute-start | bytes 354824 | tf_op jit(solution)/shard_map/ppermute | solution.py:47
  154.5 8.0 %collective-permute-start.25 = (bf16[1,128,462]{1,2,0:T(8,128)(2,1)S(1)}, bf16[1,128,462]{1,2,0:T(8,128)(2,1)S(1)}, u32[]{:S(2)}, u32[]{:S(2)}) collective-permute-start(bf16[1,128,462]{1,2,0:T(8,128)(2,1)S(1)} %collective-permute-done.24), channel_id=1, source_target_pairs={{0,480},{32,0},{64,32},{96,64},{128,96},{160,128},{192,160},{224,1... | collective-permute-start | bytes 354824 | tf_op jit(solution)/shard_map/ppermute | solution.py:50
  160.6 7.7 %collective-permute-start.19 = (bf16[1,128,462]{1,2,0:T(8,128)(2,1)S(1)}, bf16[1,128,462]{1,2,0:T(8,128)(2,1)S(1)}, u32[]{:S(2)}, u32[]{:S(2)}) collective-permute-start(bf16[1,128,462]{1,2,0:T(8,128)(2,1)S(1)} %collective-permute-done.18), channel_id=1, source_target_pairs={{0,32},{32,64},{64,96},{96,128},{128,160},{160,192},{192,224},{224... | collective-permute-start | bytes 354824 | tf_op jit(solution)/shard_map/ppermute | solution.py:47
  162.5 7.7 %collective-permute-start.26 = (bf16[1,128,462]{1,2,0:T(8,128)(2,1)S(1)}, bf16[1,128,462]{1,2,0:T(8,128)(2,1)S(1)}, u32[]{:S(2)}, u32[]{:S(2)}) collective-permute-start(bf16[1,128,462]{1,2,0:T(8,128)(2,1)S(1)} %collective-permute-done.25), channel_id=1, source_target_pairs={{0,480},{32,0},{64,32},{96,64},{128,96},{160,128},{192,160},{224,1... | collective-permute-start | bytes 354824 | tf_op jit(solution)/shard_map/ppermute | solution.py:50
  168.3 9.2 %collective-permute-start.20 = (bf16[1,128,462]{1,2,0:T(8,128)(2,1)S(1)}, bf16[1,128,462]{1,2,0:T(8,128)(2,1)S(1)}, u32[]{:S(2)}, u32[]{:S(2)}) collective-permute-start(bf16[1,128,462]{1,2,0:T(8,128)(2,1)S(1)} %collective-permute-done.19), channel_id=1, source_target_pairs={{0,32},{32,64},{64,96},{96,128},{128,160},{160,192},{192,224},{224... | collective-permute-start | bytes 354824 | tf_op jit(solution)/shard_map/ppermute | solution.py:47
  170.2 9.3 %collective-permute-start.27 = (bf16[1,128,462]{1,2,0:T(8,128)(2,1)S(1)}, bf16[1,128,462]{1,2,0:T(8,128)(2,1)S(1)}, u32[]{:S(2)}, u32[]{:S(2)}) collective-permute-start(bf16[1,128,462]{1,2,0:T(8,128)(2,1)S(1)} %collective-permute-done.26), channel_id=1, source_target_pairs={{0,480},{32,0},{64,32},{96,64},{128,96},{160,128},{192,160},{224,1... | collective-permute-start | bytes 354824 | tf_op jit(solution)/shard_map/ppermute | solution.py:50
  177.5 6.8 %collective-permute-start.21 = (bf16[1,128,462]{1,2,0:T(8,128)(2,1)S(1)}, bf16[1,128,462]{1,2,0:T(8,128)(2,1)S(1)}, u32[]{:S(2)}, u32[]{:S(2)}) collective-permute-start(bf16[1,128,462]{1,2,0:T(8,128)(2,1)S(1)} %collective-permute-done.20), channel_id=1, source_target_pairs={{0,32},{32,64},{64,96},{96,128},{128,160},{160,192},{192,224},{224... | collective-permute-start | bytes 354824 | tf_op jit(solution)/shard_map/ppermute | solution.py:47
  179.5 7.1 %collective-permute-start.28 = (bf16[1,128,462]{1,2,0:T(8,128)(2,1)S(1)}, bf16[1,128,462]{1,2,0:T(8,128)(2,1)S(1)}, u32[]{:S(2)}, u32[]{:S(2)}) collective-permute-start(bf16[1,128,462]{1,2,0:T(8,128)(2,1)S(1)} %collective-permute-done.27), channel_id=1, source_target_pairs={{0,480},{32,0},{64,32},{96,64},{128,96},{160,128},{192,160},{224,1... | collective-permute-start | bytes 354824 | tf_op jit(solution)/shard_map/ppermute | solution.py:50
  184.2 6.8 %collective-permute-start.22 = (bf16[1,128,462]{1,2,0:T(8,128)(2,1)S(1)}, bf16[1,128,462]{1,2,0:T(8,128)(2,1)S(1)}, u32[]{:S(2)}, u32[]{:S(2)}) collective-permute-start(bf16[1,128,462]{1,2,0:T(8,128)(2,1)S(1)} %collective-permute-done.21), channel_id=1, source_target_pairs={{0,32},{32,64},{64,96},{96,128},{128,160},{160,192},{192,224},{224... | collective-permute-start | bytes 354824 | tf_op jit(solution)/shard_map/ppermute | solution.py:47
  186.6 6.0 %collective-permute-start.29 = (bf16[1,128,462]{1,2,0:T(8,128)(2,1)S(1)}, bf16[1,128,462]{1,2,0:T(8,128)(2,1)S(1)}, u32[]{:S(2)}, u32[]{:S(2)}) collective-permute-start(bf16[1,128,462]{1,2,0:T(8,128)(2,1)S(1)} %collective-permute-done.28), channel_id=1, source_target_pairs={{0,480},{32,0},{64,32},{96,64},{128,96},{160,128},{192,160},{224,1... | collective-permute-start | bytes 354824 | tf_op jit(solution)/shard_map/ppermute | solution.py:50
  192.6 1.3 copy-start.4
  202.7 1.5 copy-start.1
  202.7 2.6 copy-start.3
  202.7 2.7 copy-start.9
  208.7 48.6 %all-to-all-start.1 = ((bf16[32,64,512]{2,1,0:T(8,128)(2,1)}), bf16[32,64,512]{2,1,0:T(8,128)(2,1)}, u32[]{:S(2)}, u32[]{:S(2)}) async-start(bf16[32,64,512]{2,1,0:T(8,128)(2,1)} %bitcast.184), calls=%async_computation.1 | async-start | bytes 4194304 | tf_op jit(solution)/shard_map/all_to_all | solution.py:152
  260.9 2.7 copy-start.2
Sparse Core Ops, SparseCore 0:
  11.1 70.5 all-gather.2
  84.3 96.3 all-gather.4

commit v10 on v8

--- a/solution.py
+++ b/solution.py
@@ -145,13 +145,12 @@
         all_pre[0], all_pre[1], hidden_grad.astype(jnp.float32)
     )
     grad_down = contract_rows(hidden, all_grad_out).astype(jnp.bfloat16)
+    grad_gate = contract_rows(all_inputs, gate_grad).astype(jnp.bfloat16)
+    grad_up = contract_rows(all_inputs, up_grad).astype(jnp.bfloat16)
     terms = (
         contract_cols(gate_grad, w_gate) + contract_cols(up_grad, w_up)
     ).astype(jnp.bfloat16)
     received = lax.all_to_all(terms.reshape((n_col, tokens_col, width)), "col", 0, 0)
-    received, all_inputs = lax.optimization_barrier((received, all_inputs))
-    grad_gate = contract_rows(all_inputs, gate_grad).astype(jnp.bfloat16)
-    grad_up = contract_rows(all_inputs, up_grad).astype(jnp.bfloat16)
     grad_in = received.astype(jnp.float32).sum(axis=0).astype(jnp.bfloat16)
     return (grad_in, grad_gate, grad_up, grad_down)
 

time: 271 us -> 267 us (0.985)
  the two profiles are of different devices: /device:TPU:1 before, /device:TPU:45 now
where the time goes in v10:
time: 267 us; the launch traced here: 266 us
  starting transfers between devices  128 us (48%)
  waiting for transfers between devices  85.3 us (32%)
  local copies, waits for them, and re-layouts  16.2 us (6%)
  between operations  14.9 us (6%)
  matrix products  13.6 us (5%)
  other arithmetic  8.43 us (3%)
    ppermute x7, starting transfers between devices, ring_all_gather(): b = lax.ppermute(b, axis, down)  31.8 us
    all_gather x1, waiting for transfers between devices, shards(): all_inputs = lax.all_gather(inputs, 'col', axis=0, tiled=True)  31.4 us
    ppermute x7, starting transfers between devices, ring_reduce_scatter(): b = lax.ppermute(b.astype(wire_dtype), axis, down).astype(jnp.float32)  31.2 us
    all_to_all x1, waiting for transfers between devices, gather_col_flat(): lax.all_to_all(spread, 'col', 0, 0)  25.1 us
    all_to_all x1, starting transfers between devices, shards(): lax.all_to_all(terms.reshape((n_col, tokens_col, width)), 'col', 0, 0)  24.3 us
    ppermute x8, starting transfers between devices, ring_reduce_scatter(): a = lax.ppermute(a.astype(wire_dtype), axis, up).astype(jnp.float32)  17.2 us
    ppermute x8, starting transfers between devices, ring_all_gather(): a = lax.ppermute(a, axis, up)  15.3 us
    ppermute x8, waiting for transfers between devices, ring_reduce_scatter(): a = lax.ppermute(a.astype(wire_dtype), axis, up).astype(jnp.float32)  15.1 us
  transfers between devices with their start and end apart: 34, of which 22 were waited for; matrix products, arithmetic and copies ran while one was open for 12% of the time, Pallas kernels for 0%

profile of v10, /device:TPU:45, one launch (start us, length us, event | category | flops | bytes accessed | tf_op | source)
XLA Modules:
  0.0 266.2 jit_solution(1201622438064049496)
XLA Ops:
  9.0 2.4 broadcast_in_dim.26
  11.4 7.9 %all-to-all-start = ((bf16[32,64,512]{2,1,0:T(8,128)(2,1)}), bf16[32,64,512]{2,1,0:T(8,128)(2,1)S(1)}, u32[]{:S(2)}, u32[]{:S(2)}) async-start(bf16[32,64,512]{2,1,0:T(8,128)(2,1)} %broadcast_in_dim.26), calls=%async_computation | async-start | bytes 4194304 | tf_op jit(solution)/shard_map/all_to_all | solution.py:119
  19.6 25.1 %all-to-all-done = bf16[32,64,512]{2,1,0:T(8,128)(2,1)S(1)} async-done(((bf16[32,64,512]{2,1,0:T(8,128)(2,1)}), bf16[32,64,512]{2,1,0:T(8,128)(2,1)S(1)}, u32[]{:S(2)}, u32[]{:S(2)}) %all-to-all-start) | async-done | bytes 2097184 | tf_op jit(solution)/shard_map/all_to_all | solution.py:119
  46.9 4.5 %constant_dynamic-slice_fusion.15 = (bf16[1,128,462]{1,0,2:T(2,128)(2,1)S(1)}, bf16[1,128,462]{1,0,2:T(2,128)(2,1)S(1)}, bf16[1,128,462]{1,0,2:T(2,128)(2,1)S(1)...) fusion(bf16[16,128,462]{1,0,2:T(8,128)(2,1)S(1)} %slice_bitcast, ...), kind=kLoop, calls=%fused_computation.115 | loop fusion | bytes 3784768 | tf_op jit(solution)/shard_map/jit(dynamic_index_in_dim)/dynamic_slice | solution.py:64
  51.4 3.5 %collective-permute-start = (bf16[128,462]{0,1:T(8,128)(2,1)S(1)}, bf16[128,462]{0,1:T(8,128)(2,1)S(1)}, u32[]{:S(2)}, u32[]{:S(2)}) collective-permute-start(bf16[128,462]{0,1:T(8,128)(2,1)S(1)} %bitcast.193), channel_id=1, source_target_pairs={{0,32},{32,64},{64,96},{96,128},{128,160},{160,192},{192,224},{224... | collective-permute-start | bytes 354824 | tf_op jit(solution)/shard_map/ppermute | solution.py:71
  55.0 2.1 collective-permute-start.8
  57.2 2.5 collective-permute-done
  59.7 2.0 collective-permute-start.1
  63.4 6.4 %collective-permute-start.9 = (bf16[128,462]{0,1:T(8,128)(2,1)S(1)}, bf16[128,462]{0,1:T(8,128)(2,1)S(1)}, u32[]{:S(2)}, u32[]{:S(2)}) collective-permute-start(bf16[128,462]{0,1:T(8,128)(2,1)S(1)} %fusion.30), channel_id=1, source_target_pairs={{0,480},{32,0},{64,32},{96,64},{128,96},{160,128},{192,160},{224,1... | collective-permute-start | bytes 354824 | tf_op jit(solution)/shard_map/ppermute | solution.py:75
  71.1 1.9 collective-permute-start.2
  73.3 4.2 %collective-permute-start.10 = (bf16[128,462]{0,1:T(8,128)(2,1)S(1)}, bf16[128,462]{0,1:T(8,128)(2,1)S(1)}, u32[]{:S(2)}, u32[]{:S(2)}) collective-permute-start(bf16[128,462]{0,1:T(8,128)(2,1)S(1)} %fusion.29), channel_id=1, source_target_pairs={{0,480},{32,0},{64,32},{96,64},{128,96},{160,128},{192,160},{224,1... | collective-permute-start | bytes 354824 | tf_op jit(solution)/shard_map/ppermute | solution.py:75
  77.9 1.9 collective-permute-start.3
  81.5 4.2 %collective-permute-start.11 = (bf16[128,462]{0,1:T(8,128)(2,1)S(1)}, bf16[128,462]{0,1:T(8,128)(2,1)S(1)}, u32[]{:S(2)}, u32[]{:S(2)}) collective-permute-start(bf16[128,462]{0,1:T(8,128)(2,1)S(1)} %fusion.28), channel_id=1, source_target_pairs={{0,480},{32,0},{64,32},{96,64},{128,96},{160,128},{192,160},{224,1... | collective-permute-start | bytes 354824 | tf_op jit(solution)/shard_map/ppermute | solution.py:75
  85.7 2.5 collective-permute-done.3
  88.3 1.9 collective-permute-start.4
  90.3 5.1 %collective-permute-start.12 = (bf16[128,462]{0,1:T(8,128)(2,1)S(1)}, bf16[128,462]{0,1:T(8,128)(2,1)S(1)}, u32[]{:S(2)}, u32[]{:S(2)}) collective-permute-start(bf16[128,462]{0,1:T(8,128)(2,1)S(1)} %fusion.27), channel_id=1, source_target_pairs={{0,480},{32,0},{64,32},{96,64},{128,96},{160,128},{192,160},{224,1... | collective-permute-start | bytes 354824 | tf_op jit(solution)/shard_map/ppermute | solution.py:75
  95.4 2.3 collective-permute-done.4
  97.7 1.9 collective-permute-start.5
  100.0 3.3 %collective-permute-start.13 = (bf16[128,462]{0,1:T(8,128)(2,1)S(1)}, bf16[128,462]{0,1:T(8,128)(2,1)S(1)}, u32[]{:S(2)}, u32[]{:S(2)}) collective-permute-start(bf16[128,462]{0,1:T(8,128)(2,1)S(1)} %fusion.26), channel_id=1, source_target_pairs={{0,480},{32,0},{64,32},{96,64},{128,96},{160,128},{192,160},{224,1... | collective-permute-start | bytes 354824 | tf_op jit(solution)/shard_map/ppermute | solution.py:75
  103.7 2.1 collective-permute-start.6
  105.9 5.9 %collective-permute-start.14 = (bf16[128,462]{0,1:T(8,128)(2,1)S(1)}, bf16[128,462]{0,1:T(8,128)(2,1)S(1)}, u32[]{:S(2)}, u32[]{:S(2)}) collective-permute-start(bf16[128,462]{0,1:T(8,128)(2,1)S(1)} %fusion.25), channel_id=1, source_target_pairs={{0,480},{32,0},{64,32},{96,64},{128,96},{160,128},{192,160},{224,1... | collective-permute-start | bytes 354824 | tf_op jit(solution)/shard_map/ppermute | solution.py:75
  111.8 1.9 collective-permute-start.7
  113.8 5.7 %collective-permute-done.7 = bf16[128,462]{0,1:T(8,128)(2,1)S(1)} collective-permute-done((bf16[128,462]{0,1:T(8,128)(2,1)S(1)}, bf16[128,462]{0,1:T(8,128)(2,1)S(1)}, u32[]{:S(2)}, u32[]{:S(2)}) %collective-permute-start.7) | collective-permute-done | bytes 118304 | tf_op jit(solution)/shard_map/ppermute | solution.py:71
  119.5 1.9 collective-permute-start.15
  121.4 4.9 %collective-permute-done.15 = bf16[1,128,462]{1,2,0:T(8,128)(2,1)S(1)} collective-permute-done((bf16[1,128,462]{1,2,0:T(8,128)(2,1)S(1)}, bf16[1,128,462]{1,2,0:T(8,128)(2,1)S(1)}, u32[]{:S(2)}, u32[]{:S(2)}) %collective-permute-start.15) | collective-permute-done | bytes 118304 | tf_op jit(solution)/shard_map/ppermute | solution.py:47
  126.3 1.9 collective-permute-start.16
  128.2 4.6 %collective-permute-start.23 = (bf16[1,128,462]{1,2,0:T(8,128)(2,1)S(1)}, bf16[1,128,462]{1,2,0:T(8,128)(2,1)S(1)}, u32[]{:S(2)}, u32[]{:S(2)}) collective-permute-start(bf16[1,128,462]{1,2,0:T(8,128)(2,1)S(1)} %bitcast.191), channel_id=1, source_target_pairs={{0,480},{32,0},{64,32},{96,64},{128,96},{160,128},{192,160},{224,1... | collective-permute-start | bytes 354824 | tf_op jit(solution)/shard_map/ppermute | solution.py:50
  133.5 1.9 collective-permute-start.17
  135.5 4.9 %collective-permute-start.24 = (bf16[1,128,462]{1,2,0:T(8,128)(2,1)S(1)}, bf16[1,128,462]{1,2,0:T(8,128)(2,1)S(1)}, u32[]{:S(2)}, u32[]{:S(2)}) collective-permute-start(bf16[1,128,462]{1,2,0:T(8,128)(2,1)S(1)} %collective-permute-done.23), channel_id=1, source_target_pairs={{0,480},{32,0},{64,32},{96,64},{128,96},{160,128},{192,160},{224,1... | collective-permute-start | bytes 354824 | tf_op jit(solution)/shard_map/ppermute | solution.py:50
  141.8 1.9 collective-permute-start.18
  143.8 4.3 %collective-permute-start.25 = (bf16[1,128,462]{1,2,0:T(8,128)(2,1)S(1)}, bf16[1,128,462]{1,2,0:T(8,128)(2,1)S(1)}, u32[]{:S(2)}, u32[]{:S(2)}) collective-permute-start(bf16[1,128,462]{1,2,0:T(8,128)(2,1)S(1)} %collective-permute-done.24), channel_id=1, source_target_pairs={{0,480},{32,0},{64,32},{96,64},{128,96},{160,128},{192,160},{224,1... | collective-permute-start | bytes 354824 | tf_op jit(solution)/shard_map/ppermute | solution.py:50
  148.7 1.9 collective-permute-start.19
  150.7 4.2 %collective-permute-start.26 = (bf16[1,128,462]{1,2,0:T(8,128)(2,1)S(1)}, bf16[1,128,462]{1,2,0:T(8,128)(2,1)S(1)}, u32[]{:S(2)}, u32[]{:S(2)}) collective-permute-start(bf16[1,128,462]{1,2,0:T(8,128)(2,1)S(1)} %collective-permute-done.25), channel_id=1, source_target_pairs={{0,480},{32,0},{64,32},{96,64},{128,96},{160,128},{192,160},{224,1... | collective-permute-start | bytes 354824 | tf_op jit(solution)/shard_map/ppermute | solution.py:50
  155.1 1.9 collective-permute-start.20
  157.1 4.6 %collective-permute-start.27 = (bf16[1,128,462]{1,2,0:T(8,128)(2,1)S(1)}, bf16[1,128,462]{1,2,0:T(8,128)(2,1)S(1)}, u32[]{:S(2)}, u32[]{:S(2)}) collective-permute-start(bf16[1,128,462]{1,2,0:T(8,128)(2,1)S(1)} %collective-permute-done.26), channel_id=1, source_target_pairs={{0,480},{32,0},{64,32},{96,64},{128,96},{160,128},{192,160},{224,1... | collective-permute-start | bytes 354824 | tf_op jit(solution)/shard_map/ppermute | solution.py:50
  161.9 1.9 collective-permute-start.21
  163.9 4.6 %collective-permute-start.28 = (bf16[1,128,462]{1,2,0:T(8,128)(2,1)S(1)}, bf16[1,128,462]{1,2,0:T(8,128)(2,1)S(1)}, u32[]{:S(2)}, u32[]{:S(2)}) collective-permute-start(bf16[1,128,462]{1,2,0:T(8,128)(2,1)S(1)} %collective-permute-done.27), channel_id=1, source_target_pairs={{0,480},{32,0},{64,32},{96,64},{128,96},{160,128},{192,160},{224,1... | collective-permute-start | bytes 354824 | tf_op jit(solution)/shard_map/ppermute | solution.py:50
  168.7 1.9 collective-permute-start.22
  170.6 4.8 %collective-permute-start.29 = (bf16[1,128,462]{1,2,0:T(8,128)(2,1)S(1)}, bf16[1,128,462]{1,2,0:T(8,128)(2,1)S(1)}, u32[]{:S(2)}, u32[]{:S(2)}) collective-permute-start(bf16[1,128,462]{1,2,0:T(8,128)(2,1)S(1)} %collective-permute-done.28), channel_id=1, source_target_pairs={{0,480},{32,0},{64,32},{96,64},{128,96},{160,128},{192,160},{224,1... | collective-permute-start | bytes 354824 | tf_op jit(solution)/shard_map/ppermute | solution.py:50
  178.3 2.4 gather_fusion
  183.4 3.7 %fusion.5 = bf16[2048,462]{0,1:T(8,128)(2,1)S(1)} fusion(bf16[2,2048,462]{1,2,0:T(8,128)(2,1)} %all-gather.3.cloned.1.call-done, bf16[2048,462]{0,1:T(8,128)(2,1)} %bitcast.179, pred[2048]{0:T(1024)(128)(4,1)S(1)} %broadcast_bitcast_fusion), kind=kLoop, calls=%fused_computation.14 | loop fusion | flops 13246464 | bytes 7571456 | tf_op jit(solution)/shard_map/convert_element_type | solution.py:28
  189.8 3.4 %add_convert_fusion = bf16[2048,512]{1,0:T(8,128)(2,1)} fusion(f32[2048,512]{1,0:T(8,128)S(1)} %fusion.46, bf16[512,462]{0,1:T(8,128)(2,1)S(1)} %copy-done.10, bf16[2048,462]{0,1:T(8,128)(2,1)S(1)} %bitcast.180, pred[2048]{0:T(1024)(128)(4,1)S(1)} %broadcast_bitcast_fusion, bf16[2,2048,462]{1,2,0:T(8,128)(2,1)S(1)} %copy-done.3), kind=kOutput, calls=%fused_computation.11 | convolution fusion | flops 979496960 | bytes 10569728 | tf_op jit(solution)/shard_map/dot_general | solution.py:14
  193.2 24.3 %all-to-all-start.1 = ((bf16[32,64,512]{2,1,0:T(8,128)(2,1)}), bf16[32,64,512]{2,1,0:T(8,128)(2,1)}, u32[]{:S(2)}, u32[]{:S(2)}) async-start(bf16[32,64,512]{2,1,0:T(8,128)(2,1)} %bitcast.188), calls=%async_computation.1 | async-start | bytes 4194304 | tf_op jit(solution)/shard_map/all_to_all | solution.py:153
  217.5 31.4 %all-gather.5.cloned.1.call-done = bf16[2048,512]{1,0:T(8,128)(2,1)} async-done(((bf16[64,512]{1,0:T(8,128)(2,1)}), bf16[2048,512]{1,0:T(8,128)(2,1)}) %all-gather.5.cloned.1.call-update) | async-done | bytes 2097168 | tf_op jit(solution)/shard_map/all_gather | solution.py:137
  248.9 3.7 %fusion.23 = bf16[512,462]{0,1:T(8,128)(2,1)} fusion(bf16[2048,462]{0,1:T(8,128)(2,1)S(1)} %fusion.5, bf16[2048,512]{1,0:T(8,128)(2,1)} %all-gather.5.cloned.1.call-done), kind=kOutput, calls=%fused_computation.35 | convolution fusion | flops 969120768 | bytes 4462592 | tf_op jit(solution)/shard_map/dot_general | solution.py:8
  252.6 2.0 fusion.20
  254.7 2.1 fusion.24
  256.8 2.5 reduce_sum.12
  (97 shorter events, 22.5 us)
Async XLA Ops:
  7.2 179.9 %copy-start = (bf16[512,462]{0,1:T(8,128)(2,1)S(1)}, bf16[512,462]{0,1:T(8,128)(2,1)}, u32[]{:S(2)}) copy-start(bf16[512,462]{0,1:T(8,128)(2,1)} %param.10) | copy-start | bytes 1419268
  7.2 176.2 %all-gather.3.cloned.1.call-start = ((), (), s32[]{:S(2)}) async-start(), calls=%async_computation.2 | async-start | bytes 4038656 | tf_op jit(solution)/shard_map/all_gather | solution.py:135
  11.4 33.3 %copy-start.9 = (bf16[462,512]{1,0:T(8,128)(2,1)S(1)}, bf16[462,512]{1,0:T(8,128)(2,1)}, u32[]{:S(2)}) copy-start(bf16[462,512]{1,0:T(8,128)(2,1)} %param.12) | copy-start | bytes 1419268
  11.4 33.3 %all-to-all-start = ((bf16[32,64,512]{2,1,0:T(8,128)(2,1)}), bf16[32,64,512]{2,1,0:T(8,128)(2,1)S(1)}, u32[]{:S(2)}, u32[]{:S(2)}) async-start(bf16[32,64,512]{2,1,0:T(8,128)(2,1)} %broadcast_in_dim.26), calls=%async_computation | async-start | bytes 4194304 | tf_op jit(solution)/shard_map/all_to_all | solution.py:119
  19.3 229.6 %all-gather.5.cloned.1.call-start = ((), (), s32[]{:S(2)}) async-start(), calls=%async_computation.3 | async-start | bytes 2162688 | tf_op jit(solution)/shard_map/all_gather | solution.py:137
  44.6 1.4 copy-start.6
  51.4 8.3 %collective-permute-start = (bf16[128,462]{0,1:T(8,128)(2,1)S(1)}, bf16[128,462]{0,1:T(8,128)(2,1)S(1)}, u32[]{:S(2)}, u32[]{:S(2)}) collective-permute-start(bf16[128,462]{0,1:T(8,128)(2,1)S(1)} %bitcast.193), channel_id=1, source_target_pairs={{0,32},{32,64},{64,96},{96,128},{128,160},{160,192},{192,224},{224... | collective-permute-start | bytes 354824 | tf_op jit(solution)/shard_map/ppermute | solution.py:71
  55.0 8.3 %collective-permute-start.8 = (bf16[128,462]{0,1:T(8,128)(2,1)S(1)}, bf16[128,462]{0,1:T(8,128)(2,1)S(1)}, u32[]{:S(2)}, u32[]{:S(2)}) collective-permute-start(bf16[128,462]{0,1:T(8,128)(2,1)S(1)} %bitcast.192), channel_id=1, source_target_pairs={{0,480},{32,0},{64,32},{96,64},{128,96},{160,128},{192,160},{224,1... | collective-permute-start | bytes 354824 | tf_op jit(solution)/shard_map/ppermute | solution.py:75
  59.7 11.3 %collective-permute-start.1 = (bf16[128,462]{0,1:T(8,128)(2,1)S(1)}, bf16[128,462]{0,1:T(8,128)(2,1)S(1)}, u32[]{:S(2)}, u32[]{:S(2)}) collective-permute-start(bf16[128,462]{0,1:T(8,128)(2,1)S(1)} %fusion.37), channel_id=1, source_target_pairs={{0,32},{32,64},{64,96},{96,128},{128,160},{160,192},{192,224},{224... | collective-permute-start | bytes 354824 | tf_op jit(solution)/shard_map/ppermute | solution.py:71
  63.4 9.9 %collective-permute-start.9 = (bf16[128,462]{0,1:T(8,128)(2,1)S(1)}, bf16[128,462]{0,1:T(8,128)(2,1)S(1)}, u32[]{:S(2)}, u32[]{:S(2)}) collective-permute-start(bf16[128,462]{0,1:T(8,128)(2,1)S(1)} %fusion.30), channel_id=1, source_target_pairs={{0,480},{32,0},{64,32},{96,64},{128,96},{160,128},{192,160},{224,1... | collective-permute-start | bytes 354824 | tf_op jit(solution)/shard_map/ppermute | solution.py:75
  71.1 6.8 %collective-permute-start.2 = (bf16[128,462]{0,1:T(8,128)(2,1)S(1)}, bf16[128,462]{0,1:T(8,128)(2,1)S(1)}, u32[]{:S(2)}, u32[]{:S(2)}) collective-permute-start(bf16[128,462]{0,1:T(8,128)(2,1)S(1)} %fusion.36), channel_id=1, source_target_pairs={{0,32},{32,64},{64,96},{96,128},{128,160},{160,192},{192,224},{224... | collective-permute-start | bytes 354824 | tf_op jit(solution)/shard_map/ppermute | solution.py:71
  73.3 8.2 %collective-permute-start.10 = (bf16[128,462]{0,1:T(8,128)(2,1)S(1)}, bf16[128,462]{0,1:T(8,128)(2,1)S(1)}, u32[]{:S(2)}, u32[]{:S(2)}) collective-permute-start(bf16[128,462]{0,1:T(8,128)(2,1)S(1)} %fusion.29), channel_id=1, source_target_pairs={{0,480},{32,0},{64,32},{96,64},{128,96},{160,128},{192,160},{224,1... | collective-permute-start | bytes 354824 | tf_op jit(solution)/shard_map/ppermute | solution.py:75
  77.9 10.4 %collective-permute-start.3 = (bf16[128,462]{0,1:T(8,128)(2,1)S(1)}, bf16[128,462]{0,1:T(8,128)(2,1)S(1)}, u32[]{:S(2)}, u32[]{:S(2)}) collective-permute-start(bf16[128,462]{0,1:T(8,128)(2,1)S(1)} %fusion.35), channel_id=1, source_target_pairs={{0,32},{32,64},{64,96},{96,128},{128,160},{160,192},{192,224},{224... | collective-permute-start | bytes 354824 | tf_op jit(solution)/shard_map/ppermute | solution.py:71
  81.5 8.7 %collective-permute-start.11 = (bf16[128,462]{0,1:T(8,128)(2,1)S(1)}, bf16[128,462]{0,1:T(8,128)(2,1)S(1)}, u32[]{:S(2)}, u32[]{:S(2)}) collective-permute-start(bf16[128,462]{0,1:T(8,128)(2,1)S(1)} %fusion.28), channel_id=1, source_target_pairs={{0,480},{32,0},{64,32},{96,64},{128,96},{160,128},{192,160},{224,1... | collective-permute-start | bytes 354824 | tf_op jit(solution)/shard_map/ppermute | solution.py:75
  88.3 9.4 %collective-permute-start.4 = (bf16[128,462]{0,1:T(8,128)(2,1)S(1)}, bf16[128,462]{0,1:T(8,128)(2,1)S(1)}, u32[]{:S(2)}, u32[]{:S(2)}) collective-permute-start(bf16[128,462]{0,1:T(8,128)(2,1)S(1)} %fusion.34), channel_id=1, source_target_pairs={{0,32},{32,64},{64,96},{96,128},{128,160},{160,192},{192,224},{224... | collective-permute-start | bytes 354824 | tf_op jit(solution)/shard_map/ppermute | solution.py:71
  90.3 9.7 %collective-permute-start.12 = (bf16[128,462]{0,1:T(8,128)(2,1)S(1)}, bf16[128,462]{0,1:T(8,128)(2,1)S(1)}, u32[]{:S(2)}, u32[]{:S(2)}) collective-permute-start(bf16[128,462]{0,1:T(8,128)(2,1)S(1)} %fusion.27), channel_id=1, source_target_pairs={{0,480},{32,0},{64,32},{96,64},{128,96},{160,128},{192,160},{224,1... | collective-permute-start | bytes 354824 | tf_op jit(solution)/shard_map/ppermute | solution.py:75
  97.7 6.0 %collective-permute-start.5 = (bf16[128,462]{0,1:T(8,128)(2,1)S(1)}, bf16[128,462]{0,1:T(8,128)(2,1)S(1)}, u32[]{:S(2)}, u32[]{:S(2)}) collective-permute-start(bf16[128,462]{0,1:T(8,128)(2,1)S(1)} %fusion.33), channel_id=1, source_target_pairs={{0,32},{32,64},{64,96},{96,128},{128,160},{160,192},{192,224},{224... | collective-permute-start | bytes 354824 | tf_op jit(solution)/shard_map/ppermute | solution.py:71
  100.0 5.8 %collective-permute-start.13 = (bf16[128,462]{0,1:T(8,128)(2,1)S(1)}, bf16[128,462]{0,1:T(8,128)(2,1)S(1)}, u32[]{:S(2)}, u32[]{:S(2)}) collective-permute-start(bf16[128,462]{0,1:T(8,128)(2,1)S(1)} %fusion.26), channel_id=1, source_target_pairs={{0,480},{32,0},{64,32},{96,64},{128,96},{160,128},{192,160},{224,1... | collective-permute-start | bytes 354824 | tf_op jit(solution)/shard_map/ppermute | solution.py:75
  103.7 8.0 %collective-permute-start.6 = (bf16[128,462]{0,1:T(8,128)(2,1)S(1)}, bf16[128,462]{0,1:T(8,128)(2,1)S(1)}, u32[]{:S(2)}, u32[]{:S(2)}) collective-permute-start(bf16[128,462]{0,1:T(8,128)(2,1)S(1)} %fusion.32), channel_id=1, source_target_pairs={{0,32},{32,64},{64,96},{96,128},{128,160},{160,192},{192,224},{224... | collective-permute-start | bytes 354824 | tf_op jit(solution)/shard_map/ppermute | solution.py:71
  105.9 7.8 %collective-permute-start.14 = (bf16[128,462]{0,1:T(8,128)(2,1)S(1)}, bf16[128,462]{0,1:T(8,128)(2,1)S(1)}, u32[]{:S(2)}, u32[]{:S(2)}) collective-permute-start(bf16[128,462]{0,1:T(8,128)(2,1)S(1)} %fusion.25), channel_id=1, source_target_pairs={{0,480},{32,0},{64,32},{96,64},{128,96},{160,128},{192,160},{224,1... | collective-permute-start | bytes 354824 | tf_op jit(solution)/shard_map/ppermute | solution.py:75
  111.8 7.6 %collective-permute-start.7 = (bf16[128,462]{0,1:T(8,128)(2,1)S(1)}, bf16[128,462]{0,1:T(8,128)(2,1)S(1)}, u32[]{:S(2)}, u32[]{:S(2)}) collective-permute-start(bf16[128,462]{0,1:T(8,128)(2,1)S(1)} %fusion.31), channel_id=1, source_target_pairs={{0,32},{32,64},{64,96},{96,128},{128,160},{160,192},{192,224},{224... | collective-permute-start | bytes 354824 | tf_op jit(solution)/shard_map/ppermute | solution.py:71
  119.5 6.8 %collective-permute-start.15 = (bf16[1,128,462]{1,2,0:T(8,128)(2,1)S(1)}, bf16[1,128,462]{1,2,0:T(8,128)(2,1)S(1)}, u32[]{:S(2)}, u32[]{:S(2)}) collective-permute-start(bf16[1,128,462]{1,2,0:T(8,128)(2,1)S(1)} %bitcast.190), channel_id=1, source_target_pairs={{0,32},{32,64},{64,96},{96,128},{128,160},{160,192},{192,224},{224... | collective-permute-start | bytes 354824 | tf_op jit(solution)/shard_map/ppermute | solution.py:47
  126.3 7.2 %collective-permute-start.16 = (bf16[1,128,462]{1,2,0:T(8,128)(2,1)S(1)}, bf16[1,128,462]{1,2,0:T(8,128)(2,1)S(1)}, u32[]{:S(2)}, u32[]{:S(2)}) collective-permute-start(bf16[1,128,462]{1,2,0:T(8,128)(2,1)S(1)} %collective-permute-done.15), channel_id=1, source_target_pairs={{0,32},{32,64},{64,96},{96,128},{128,160},{160,192},{192,224},{224... | collective-permute-start | bytes 354824 | tf_op jit(solution)/shard_map/ppermute | solution.py:47
  128.2 7.2 %collective-permute-start.23 = (bf16[1,128,462]{1,2,0:T(8,128)(2,1)S(1)}, bf16[1,128,462]{1,2,0:T(8,128)(2,1)S(1)}, u32[]{:S(2)}, u32[]{:S(2)}) collective-permute-start(bf16[1,128,462]{1,2,0:T(8,128)(2,1)S(1)} %bitcast.191), channel_id=1, source_target_pairs={{0,480},{32,0},{64,32},{96,64},{128,96},{160,128},{192,160},{224,1... | collective-permute-start | bytes 354824 | tf_op jit(solution)/shard_map/ppermute | solution.py:50
  133.5 8.3 %collective-permute-start.17 = (bf16[1,128,462]{1,2,0:T(8,128)(2,1)S(1)}, bf16[1,128,462]{1,2,0:T(8,128)(2,1)S(1)}, u32[]{:S(2)}, u32[]{:S(2)}) collective-permute-start(bf16[1,128,462]{1,2,0:T(8,128)(2,1)S(1)} %collective-permute-done.16), channel_id=1, source_target_pairs={{0,32},{32,64},{64,96},{96,128},{128,160},{160,192},{192,224},{224... | collective-permute-start | bytes 354824 | tf_op jit(solution)/shard_map/ppermute | solution.py:47
  135.5 8.3 %collective-permute-start.24 = (bf16[1,128,462]{1,2,0:T(8,128)(2,1)S(1)}, bf16[1,128,462]{1,2,0:T(8,128)(2,1)S(1)}, u32[]{:S(2)}, u32[]{:S(2)}) collective-permute-start(bf16[1,128,462]{1,2,0:T(8,128)(2,1)S(1)} %collective-permute-done.23), channel_id=1, source_target_pairs={{0,480},{32,0},{64,32},{96,64},{128,96},{160,128},{192,160},{224,1... | collective-permute-start | bytes 354824 | tf_op jit(solution)/shard_map/ppermute | solution.py:50
  141.8 6.9 %collective-permute-start.18 = (bf16[1,128,462]{1,2,0:T(8,128)(2,1)S(1)}, bf16[1,128,462]{1,2,0:T(8,128)(2,1)S(1)}, u32[]{:S(2)}, u32[]{:S(2)}) collective-permute-start(bf16[1,128,462]{1,2,0:T(8,128)(2,1)S(1)} %collective-permute-done.17), channel_id=1, source_target_pairs={{0,32},{32,64},{64,96},{96,128},{128,160},{160,192},{192,224},{224... | collective-permute-start | bytes 354824 | tf_op jit(solution)/shard_map/ppermute | solution.py:47
  143.8 6.9 %collective-permute-start.25 = (bf16[1,128,462]{1,2,0:T(8,128)(2,1)S(1)}, bf16[1,128,462]{1,2,0:T(8,128)(2,1)S(1)}, u32[]{:S(2)}, u32[]{:S(2)}) collective-permute-start(bf16[1,128,462]{1,2,0:T(8,128)(2,1)S(1)} %collective-permute-done.24), channel_id=1, source_target_pairs={{0,480},{32,0},{64,32},{96,64},{128,96},{160,128},{192,160},{224,1... | collective-permute-start | bytes 354824 | tf_op jit(solution)/shard_map/ppermute | solution.py:50
  148.7 6.4 %collective-permute-start.19 = (bf16[1,128,462]{1,2,0:T(8,128)(2,1)S(1)}, bf16[1,128,462]{1,2,0:T(8,128)(2,1)S(1)}, u32[]{:S(2)}, u32[]{:S(2)}) collective-permute-start(bf16[1,128,462]{1,2,0:T(8,128)(2,1)S(1)} %collective-permute-done.18), channel_id=1, source_target_pairs={{0,32},{32,64},{64,96},{96,128},{128,160},{160,192},{192,224},{224... | collective-permute-start | bytes 354824 | tf_op jit(solution)/shard_map/ppermute | solution.py:47
  150.7 6.4 %collective-permute-start.26 = (bf16[1,128,462]{1,2,0:T(8,128)(2,1)S(1)}, bf16[1,128,462]{1,2,0:T(8,128)(2,1)S(1)}, u32[]{:S(2)}, u32[]{:S(2)}) collective-permute-start(bf16[1,128,462]{1,2,0:T(8,128)(2,1)S(1)} %collective-permute-done.25), channel_id=1, source_target_pairs={{0,480},{32,0},{64,32},{96,64},{128,96},{160,128},{192,160},{224,1... | collective-permute-start | bytes 354824 | tf_op jit(solution)/shard_map/ppermute | solution.py:50
  155.1 6.8 %collective-permute-start.20 = (bf16[1,128,462]{1,2,0:T(8,128)(2,1)S(1)}, bf16[1,128,462]{1,2,0:T(8,128)(2,1)S(1)}, u32[]{:S(2)}, u32[]{:S(2)}) collective-permute-start(bf16[1,128,462]{1,2,0:T(8,128)(2,1)S(1)} %collective-permute-done.19), channel_id=1, source_target_pairs={{0,32},{32,64},{64,96},{96,128},{128,160},{160,192},{192,224},{224... | collective-permute-start | bytes 354824 | tf_op jit(solution)/shard_map/ppermute | solution.py:47
  157.1 6.8 %collective-permute-start.27 = (bf16[1,128,462]{1,2,0:T(8,128)(2,1)S(1)}, bf16[1,128,462]{1,2,0:T(8,128)(2,1)S(1)}, u32[]{:S(2)}, u32[]{:S(2)}) collective-permute-start(bf16[1,128,462]{1,2,0:T(8,128)(2,1)S(1)} %collective-permute-done.26), channel_id=1, source_target_pairs={{0,480},{32,0},{64,32},{96,64},{128,96},{160,128},{192,160},{224,1... | collective-permute-start | bytes 354824 | tf_op jit(solution)/shard_map/ppermute | solution.py:50
  161.9 6.8 %collective-permute-start.21 = (bf16[1,128,462]{1,2,0:T(8,128)(2,1)S(1)}, bf16[1,128,462]{1,2,0:T(8,128)(2,1)S(1)}, u32[]{:S(2)}, u32[]{:S(2)}) collective-permute-start(bf16[1,128,462]{1,2,0:T(8,128)(2,1)S(1)} %collective-permute-done.20), channel_id=1, source_target_pairs={{0,32},{32,64},{64,96},{96,128},{128,160},{160,192},{192,224},{224... | collective-permute-start | bytes 354824 | tf_op jit(solution)/shard_map/ppermute | solution.py:47
  163.9 6.7 %collective-permute-start.28 = (bf16[1,128,462]{1,2,0:T(8,128)(2,1)S(1)}, bf16[1,128,462]{1,2,0:T(8,128)(2,1)S(1)}, u32[]{:S(2)}, u32[]{:S(2)}) collective-permute-start(bf16[1,128,462]{1,2,0:T(8,128)(2,1)S(1)} %collective-permute-done.27), channel_id=1, source_target_pairs={{0,480},{32,0},{64,32},{96,64},{128,96},{160,128},{192,160},{224,1... | collective-permute-start | bytes 354824 | tf_op jit(solution)/shard_map/ppermute | solution.py:50
  168.7 6.8 %collective-permute-start.22 = (bf16[1,128,462]{1,2,0:T(8,128)(2,1)S(1)}, bf16[1,128,462]{1,2,0:T(8,128)(2,1)S(1)}, u32[]{:S(2)}, u32[]{:S(2)}) collective-permute-start(bf16[1,128,462]{1,2,0:T(8,128)(2,1)S(1)} %collective-permute-done.21), channel_id=1, source_target_pairs={{0,32},{32,64},{64,96},{96,128},{128,160},{160,192},{192,224},{224... | collective-permute-start | bytes 354824 | tf_op jit(solution)/shard_map/ppermute | solution.py:47
  170.6 6.4 %collective-permute-start.29 = (bf16[1,128,462]{1,2,0:T(8,128)(2,1)S(1)}, bf16[1,128,462]{1,2,0:T(8,128)(2,1)S(1)}, u32[]{:S(2)}, u32[]{:S(2)}) collective-permute-start(bf16[1,128,462]{1,2,0:T(8,128)(2,1)S(1)} %collective-permute-done.28), channel_id=1, source_target_pairs={{0,480},{32,0},{64,32},{96,64},{128,96},{160,128},{192,160},{224,1... | collective-permute-start | bytes 354824 | tf_op jit(solution)/shard_map/ppermute | solution.py:50
  177.0 1.3 copy-start.5
  187.1 1.5 copy-start.1
  187.1 2.6 copy-start.3
  187.1 2.7 %copy-start.10 = (bf16[512,462]{0,1:T(8,128)(2,1)S(1)}, bf16[512,462]{0,1:T(8,128)(2,1)}, u32[]{:S(2)}) copy-start(bf16[512,462]{0,1:T(8,128)(2,1)} %param.11) | copy-start | bytes 1419268
  193.2 63.7 %all-to-all-start.1 = ((bf16[32,64,512]{2,1,0:T(8,128)(2,1)}), bf16[32,64,512]{2,1,0:T(8,128)(2,1)}, u32[]{:S(2)}, u32[]{:S(2)}) async-start(bf16[32,64,512]{2,1,0:T(8,128)(2,1)} %bitcast.188), calls=%async_computation.1 | async-start | bytes 4194304 | tf_op jit(solution)/shard_map/all_to_all | solution.py:153
  248.9 3.7 %copy-start.4 = (bf16[2,2048,462]{1,2,0:T(8,128)(2,1)S(1)}, bf16[2,2048,462]{1,2,0:T(8,128)(2,1)}, u32[]{:S(2)}) copy-start(bf16[2,2048,462]{1,2,0:T(8,128)(2,1)} %all-gather.3.cloned.1.call-done) | copy-start | bytes 11354116
  248.9 3.7 %copy-start.7 = (bf16[32,64,512]{2,1,0:T(8,128)(2,1)S(1)}, bf16[32,64,512]{2,1,0:T(8,128)(2,1)}, u32[]{:S(2)}) copy-start(bf16[32,64,512]{2,1,0:T(8,128)(2,1)} %copy-done.6) | copy-start | bytes 6291460
  252.6 2.0 copy-start.2
  252.6 2.2 copy-start.8
Sparse Core Ops, SparseCore 0:
  10.6 92.7 all-gather.2
  157.2 91.6 all-gather.4
